TPU v7x, 32 devices: a whole 2x2x4 slice. The times are simulated.
32 devices in a mesh: row: 8 (over y, x, core), col: 4 (over z).
Axes of the slice: x: 2, y: 2, z: 4, core: 2. Of those that a mesh axis runs over, the one named last changes fastest.
Arguments:
- image: bfloat16 [512, 512, 128], P('row', 'col'), may hold values from -6 to 6
- raw_first: float32 [15, 15, 128], replicated, may hold values from -0.75 to 0.75
- sigma_first: float32 [128], replicated, may hold values from 2 to 10
- in_first: bfloat16 [128, 512], replicated, may hold values from -0.5 to 0.5
- out_first: bfloat16 [512, 128], replicated, may hold values from -0.25 to 0.25
- widen: bfloat16 [128, 256], replicated, may hold values from -0.75 to 0.75
- raw_second: float32 [15, 15, 256], replicated, may hold values from -0.75 to 0.75
- sigma_second: float32 [256], replicated, may hold values from 2 to 10
- in_second: bfloat16 [256, 1024], replicated, may hold values from -0.375 to 0.375
- out_second: bfloat16 [1024, 256], replicated, may hold values from -0.1875 to 0.1875
Outputs:
- encoded: bfloat16 [128, 128, 256], P('row', 'col')
All inputs are finite; a program needn't handle non-finite values.
Results may differ from a plain program's by a relative error of at most 0.0065.
Values may be sent and summed in bfloat16 or wider, within the bound.
No kernel may reach another device: no remote copies, remote signals or barrier semaphores. Data moves between devices by JAX's collectives and lax.ppermute only.
A program may use at most 64 MiB of HBM per device.

v0:
```python
import jax
import jax.numpy as jnp
from jax import lax
from jax.sharding import PartitionSpec as P


def padded_2(block, sides, width):
    for axis, dim in sides:
        count = lax.axis_size(axis)
        forward = [(i, i + 1) for i in range(count - 1)]
        backward = [(target, source) for source, target in forward]
        low = lax.ppermute(
            lax.slice_in_dim(block, block.shape[dim] - width, None, axis=dim), axis, forward
        )
        high = lax.ppermute(lax.slice_in_dim(block, 0, width, axis=dim), axis, backward)
        block = jnp.concatenate([low, block, high], axis=dim)
    return block


def masked_kernel(raw, sigma):
    offsets = jnp.arange(raw.shape[0]).astype(jnp.float32) - 7.0
    dist = offsets[:, None] ** 2 + offsets[None, :] ** 2
    mask = jnp.exp(-dist[:, :, None] / (2.0 * sigma[None, None, :] ** 2))
    return (raw * mask).astype(jnp.bfloat16)


def local_section(extended, raw, sigma, w_in, w_out):
    channels = extended.shape[2]
    kernel = masked_kernel(raw, sigma)
    conv_out = lax.conv_general_dilated(
        extended[None],
        kernel[:, :, None, :],
        (1, 1),
        "VALID",
        dimension_numbers=("NHWC", "HWIO", "NHWC"),
        feature_group_count=channels,
        preferred_element_type=jnp.float32,
    )[0]
    field = extended[7 : extended.shape[0] - 7, 7 : extended.shape[1] - 7]
    mean = jnp.mean(conv_out, axis=-1, keepdims=True)
    var = jnp.mean((conv_out - mean) ** 2, axis=-1, keepdims=True)
    normed = ((conv_out - mean) * lax.rsqrt(var + 1e-06)).astype(jnp.bfloat16)
    hidden = jax.nn.gelu(jnp.dot(normed, w_in, preferred_element_type=jnp.float32)).astype(
        jnp.bfloat16
    )
    mixed = jnp.dot(hidden, w_out, preferred_element_type=jnp.float32)
    return (field.astype(jnp.float32) + mixed).astype(jnp.bfloat16)


def blur_down(padded):
    rows = padded.shape[0] - 2
    cols = padded.shape[1] - 2
    padded = padded.astype(jnp.float32)
    upper = padded[0:rows].reshape(rows // 2, 2, cols + 2, -1)
    lower = padded[2 : rows + 2].reshape(rows // 2, 2, cols + 2, -1)
    vert = (upper[:, 0] + 3.0 * upper[:, 1] + 3.0 * lower[:, 0] + lower[:, 1]) / 8.0
    left = vert[:, 0:cols].reshape(rows // 2, cols // 2, 2, -1)
    right = vert[:, 2 : cols + 2].reshape(rows // 2, cols // 2, 2, -1)
    return (
        (left[:, :, 0] + 3.0 * left[:, :, 1] + 3.0 * right[:, :, 0] + right[:, :, 1]) / 8.0
    ).astype(jnp.bfloat16)


def on_device(
    image,
    raw_first,
    sigma_first,
    in_first,
    out_first,
    widen,
    raw_second,
    sigma_second,
    in_second,
    out_second,
):
    reach = 7
    extended = padded_2(image, (("row", 0), ("col", 1)), reach)
    first = local_section(extended, raw_first, sigma_first, in_first, out_first)
    first_cycle = padded_2(first, (("row", 0), ("col", 1)), 1)
    first_pooled = blur_down(first_cycle)
    widened = jnp.dot(first_pooled, widen, preferred_element_type=jnp.float32).astype(jnp.bfloat16)
    widened_ext = padded_2(widened, (("row", 0), ("col", 1)), reach)
    second = local_section(widened_ext, raw_second, sigma_second, in_second, out_second)
    second_cycle = padded_2(second, (("row", 0), ("col", 1)), 1)
    return blur_down(second_cycle)


def solution(mesh):
    placed = (P("row", "col", None), P(), P(), P(), P(), P(), P(), P(), P(), P())
    return jax.shard_map(
        on_device, mesh=mesh, in_specs=placed, out_specs=P("row", "col", None), check_vma=False
    )
```

profile of v0, /device:TPU:3, one launch (start us, length us, event | category | flops | bytes accessed | tf_op | source)
XLA Modules:
  0.0 528.5 jit_solution(8969613165531808596)
XLA Ops:
  0.0 1.1 fusion.98
  1.1 3.7 collective-permute-start
  4.8 1.9 collective-permute-start.1
  6.8 0.7 multiply_multiply_fusion.3
  7.5 0.3 collective-permute-done
  7.8 2.0 constant_dynamic-update-slice_fusion.1
  9.8 3.2 collective-permute-done.1
  13.2 3.2 collective-permute-start.2
  16.4 1.3 collective-permute-start.3
  17.8 1.1 collective-permute-done.2
  18.9 4.1 collective-permute-done.3
  23.0 1.3 maximum_bitcast_fusion
  24.4 0.7 copy.41
  25.1 0.5 pad.clone
  25.7 1.1 copy.16
  26.8 0.6 slice.164
  27.4 1.0 fusion.106
  28.4 323.0 %broadcast_select_fusion = f32[64,8,18,128]{3,1,2,0:T(8,128)S(1)} fusion(pred[8,18]{0,1:T(8,128)(4,1)S(1)} %copy-done.11, bf16[15,15,1,128]{3,1,0,2:T(8,128)(2,1)S(1)} %fusion.77, bf16[78,8,32,128]{3,1,2,0:T(8,128)(2,1)S(1)} %fusion.106), kind=kOutput, calls=%fused_computation.38 | convolution fusion | flops 532021248 | bytes 9888144 | tf_op jit(solution)/shard_map/conv_general_dilated | solution.py:30
  351.4 1.5 copy.18
  352.9 1.1 slice_reduce_fusion
  354.1 2.8 multiply_reduce_fusion
  356.9 4.6 multiply_convert_fusion
  361.5 9.0 %add_convert_fusion = bf16[64,128,128]{2,1,0:T(8,128)(2,1)S(1)} fusion(bf16[64,128,128]{2,1,0:T(8,128)(2,1)} %param.10, bf16[64,128,128]{2,0,1:T(8,128)(2,1)} %multiply_convert_fusion, bf16[512,128]{1,0:T(8,128)(2,1)S(1)} %copy-done.9, bf16[128,512]{1,0:T(8,128)(2,1)S(1)} %copy-done.10), kind=kOutput, calls=%fused_computation.27 | convolution fusion | flops 2188378112 | bytes 6553600 | tf_op jit(solution)/shard_map/dot_general | solution.py:46
  370.5 3.9 collective-permute-start.4
  374.4 1.9 collective-permute-start.5
  376.4 4.2 collective-permute-done.5
  380.6 3.2 collective-permute-start.6
  383.8 1.8 collective-permute-start.7
  385.7 2.8 collective-permute-done.7
  388.5 0.8 maximum_convert_fusion
  389.4 0.6 fusion.89
  390.0 0.6 fusion.90
  390.5 1.6 fusion.33
  392.1 0.6 fusion.96
  392.7 0.5 fusion.64
  393.2 0.3 copy-done.6
  393.6 0.4 convolution_convert_fusion
  394.0 3.3 collective-permute-start.8
  397.4 1.9 collective-permute-start.9
  399.3 2.2 collective-permute-done.8
  401.6 4.0 collective-permute-done.9
  405.7 3.2 collective-permute-start.10
  408.9 1.3 collective-permute-start.11
  410.3 1.1 collective-permute-done.10
  411.4 4.1 collective-permute-done.11
  415.5 1.1 maximum_bitcast_fusion.1
  416.6 86.1 %fusion.102 = (f32[32,64]{1,0:T(8,128)S(1)}, f32[1,32,64,256]{3,0,2,1:T(1,128)S(1)}) fusion(bf16[15,15,1,256]{3,1,0,2:T(8,128)(2,1)S(1)} %fusion.74, bf16[1,46,78,256]{3,2,1,0:T(8,128)(2,1)S(1)} %maximum_bitcast_fusion.1), kind=kOutput, calls=%fused_computation.140 | convolution fusion | flops 236451840 | bytes 4057600 | tf_op jit(solution)/shard_map/conv_general_dilated | solution.py:30
  502.7 0.6 multiply_reduce_fusion.1
  503.4 0.7 copy-done.1
  504.1 4.8 add_convert_fusion.1
  508.9 2.9 collective-permute-start.12
  511.8 1.9 collective-permute-start.13
  513.7 4.2 collective-permute-done.13
  518.0 1.6 collective-permute-start.14
  519.6 1.3 collective-permute-start.15
  520.9 3.4 collective-permute-done.15
  524.3 0.4 maximum_convert_fusion.1
  524.7 0.4 fusion.93
  525.2 0.2 fusion.94
  525.4 0.2 fusion.95
  525.6 1.4 fusion.45
  527.0 0.3 fusion.99
  527.2 0.2 fusion.65
  527.5 0.8 copy.31
  (44 shorter events, 0.7 us)
Async XLA Ops:
  0.0 504.1 %copy-start = (bf16[1024,256]{1,0:T(8,128)(2,1)S(1)}, bf16[1024,256]{1,0:T(8,128)(2,1)}, u32[]{:S(2)}) copy-start(bf16[1024,256]{1,0:T(8,128)(2,1)} %param.19) | copy-start | bytes 1572868
  1.1 6.6 %collective-permute-start = (bf16[7,128,128]{2,1,0:T(8,128)(2,1)S(1)}, bf16[7,128,128]{2,1,0:T(8,128)(2,1)S(1)}, u32[]{:S(2)}, u32[]{:S(2)}) collective-permute-start(bf16[7,128,128]{2,1,0:T(8,128)(2,1)S(1)} %get-tuple-element.26), channel_id=1, source_target_pairs={{0,4},{4,8},{8,12},{12,16},{16,20},{20,24},{24,28},{1,5},{5,9},{9,... | collective-permute-start | bytes 688136 | tf_op jit(solution)/shard_map/ppermute | solution.py:12
  4.8 8.2 %collective-permute-start.1 = (bf16[7,128,128]{2,1,0:T(8,128)(2,1)S(1)}, bf16[7,128,128]{2,1,0:T(8,128)(2,1)S(1)}, u32[]{:S(2)}, u32[]{:S(2)}) collective-permute-start(bf16[7,128,128]{2,1,0:T(8,128)(2,1)S(1)} %get-tuple-element.25), channel_id=1, source_target_pairs={{4,0},{8,4},{12,8},{16,12},{20,16},{24,20},{28,24},{5,1},{9,5},{13... | collective-permute-start | bytes 688136 | tf_op jit(solution)/shard_map/ppermute | solution.py:15
  7.5 10.2 %copy-start.4 = (f32[15,15]{1,0:T(8,128)}, f32[15,15]{1,0:T(8,128)S(1)}, u32[]{:S(2)}) copy-start(f32[15,15]{1,0:T(8,128)S(1)} %add_negate_fusion) | copy-start | bytes 2704
  7.8 9.9 %copy-start.3 = (f32[15,15,128]{2,1,0:T(8,128)S(1)}, f32[15,15,128]{2,1,0:T(8,128)}, u32[]{:S(2)}) copy-start(f32[15,15,128]{2,1,0:T(8,128)} %param.11) | copy-start | bytes 345604
  13.2 5.7 %collective-permute-start.2 = (bf16[78,7,128]{2,1,0:T(8,128)(2,1)S(1)}, bf16[78,7,128]{2,1,0:T(8,128)(2,1)S(1)}, u32[]{:S(2)}, u32[]{:S(2)}) collective-permute-start(bf16[78,7,128]{2,1,0:T(8,128)(2,1)S(1)} %get-tuple-element.11), channel_id=1, source_target_pairs={{0,1},{1,2},{2,3},{4,5},{5,6},{6,7},{8,9},{9,10},{10,11},{12,13},{... | collective-permute-start | bytes 419336 | tf_op jit(solution)/shard_map/ppermute | solution.py:12
  16.4 6.6 %collective-permute-start.3 = (bf16[78,7,128]{2,1,0:T(8,128)(2,1)S(1)}, bf16[78,7,128]{2,1,0:T(8,128)(2,1)S(1)}, u32[]{:S(2)}, u32[]{:S(2)}) collective-permute-start(bf16[78,7,128]{2,1,0:T(8,128)(2,1)S(1)} %get-tuple-element.12), channel_id=1, source_target_pairs={{1,0},{2,1},{3,2},{5,4},{6,5},{7,6},{9,8},{10,9},{11,10},{13,12},{... | collective-permute-start | bytes 419336 | tf_op jit(solution)/shard_map/ppermute | solution.py:15
  27.4 1.0 copy-start.11
  356.9 4.7 copy-start.9
  356.9 4.7 copy-start.10
  370.5 5.8 %collective-permute-start.4 = (bf16[1,128,128]{2,1,0:T(8,128)(2,1)S(1)}, bf16[1,128,128]{2,1,0:T(8,128)(2,1)S(1)}, u32[]{:S(2)}, u32[]{:S(2)}) collective-permute-start(bf16[1,128,128]{2,1,0:T(8,128)(2,1)S(1)} %get-tuple-element.23), channel_id=1, source_target_pairs={{0,4},{4,8},{8,12},{12,16},{16,20},{20,24},{24,28},{1,5},{5,9},{9,... | collective-permute-start | bytes 98312 | tf_op jit(solution)/shard_map/ppermute | solution.py:12
  374.4 6.1 %collective-permute-start.5 = (bf16[1,128,128]{2,1,0:T(8,128)(2,1)S(1)}, bf16[1,128,128]{2,1,0:T(8,128)(2,1)S(1)}, u32[]{:S(2)}, u32[]{:S(2)}) collective-permute-start(bf16[1,128,128]{2,1,0:T(8,128)(2,1)S(1)} %get-tuple-element.24), channel_id=1, source_target_pairs={{4,0},{8,4},{12,8},{16,12},{20,16},{24,20},{28,24},{5,1},{9,5},{13... | collective-permute-start | bytes 98312 | tf_op jit(solution)/shard_map/ppermute | solution.py:15
  380.6 5.0 collective-permute-start.6
  383.8 4.7 collective-permute-start.7
  392.7 0.8 copy-start.6
  392.7 6.6 %copy-start.7 = (f32[256]{0:T(256)S(1)}, f32[256]{0:T(256)}, u32[]{:S(2)}) copy-start(f32[256]{0:T(256)} %param.17) | copy-start | bytes 3076
  393.5 16.7 %copy-start.2 = (f32[15,15,256]{2,1,0:T(8,128)S(1)}, f32[15,15,256]{2,1,0:T(8,128)}, u32[]{:S(2)}) copy-start(f32[15,15,256]{2,1,0:T(8,128)} %param.16) | copy-start | bytes 691204
  393.5 16.7 %copy-start.5 = (f32[15,15]{1,0:T(8,128)S(1)}, f32[15,15]{1,0:T(8,128)}, u32[]{:S(2)}) copy-start(f32[15,15]{1,0:T(8,128)} %copy-done.4) | copy-start | bytes 2704
  394.0 7.5 %collective-permute-start.8 = (bf16[7,64,256]{2,1,0:T(8,128)(2,1)S(1)}, bf16[7,64,256]{2,1,0:T(8,128)(2,1)S(1)}, u32[]{:S(2)}, u32[]{:S(2)}) collective-permute-start(bf16[7,64,256]{2,1,0:T(8,128)(2,1)S(1)} %get-tuple-element.35), channel_id=1, source_target_pairs={{0,4},{4,8},{8,12},{12,16},{16,20},{20,24},{24,28},{1,5},{5,9},{9,... | collective-permute-start | bytes 688136 | tf_op jit(solution)/shard_map/ppermute | solution.py:12
  397.4 8.2 %collective-permute-start.9 = (bf16[7,64,256]{2,1,0:T(8,128)(2,1)S(1)}, bf16[7,64,256]{2,1,0:T(8,128)(2,1)S(1)}, u32[]{:S(2)}, u32[]{:S(2)}) collective-permute-start(bf16[7,64,256]{2,1,0:T(8,128)(2,1)S(1)} %get-tuple-element.36), channel_id=1, source_target_pairs={{4,0},{8,4},{12,8},{16,12},{20,16},{24,20},{28,24},{5,1},{9,5},{13... | collective-permute-start | bytes 688136 | tf_op jit(solution)/shard_map/ppermute | solution.py:15
  405.7 5.8 %collective-permute-start.10 = (bf16[46,7,256]{2,1,0:T(8,128)(2,1)S(1)}, bf16[46,7,256]{2,1,0:T(8,128)(2,1)S(1)}, u32[]{:S(2)}, u32[]{:S(2)}) collective-permute-start(bf16[46,7,256]{2,1,0:T(8,128)(2,1)S(1)} %get-tuple-element.27), channel_id=1, source_target_pairs={{0,1},{1,2},{2,3},{4,5},{5,6},{6,7},{8,9},{9,10},{10,11},{12,13},{... | collective-permute-start | bytes 494600 | tf_op jit(solution)/shard_map/ppermute | solution.py:12
  408.9 6.6 %collective-permute-start.11 = (bf16[46,7,256]{2,1,0:T(8,128)(2,1)S(1)}, bf16[46,7,256]{2,1,0:T(8,128)(2,1)S(1)}, u32[]{:S(2)}, u32[]{:S(2)}) collective-permute-start(bf16[46,7,256]{2,1,0:T(8,128)(2,1)S(1)} %get-tuple-element.28), channel_id=1, source_target_pairs={{1,0},{2,1},{3,2},{5,4},{6,5},{7,6},{9,8},{10,9},{11,10},{13,12},{... | collective-permute-start | bytes 494600 | tf_op jit(solution)/shard_map/ppermute | solution.py:15
  416.6 87.5 %copy-start.8 = (bf16[256,1024]{1,0:T(8,128)(2,1)S(1)}, bf16[256,1024]{1,0:T(8,128)(2,1)}, u32[]{:S(2)}) copy-start(bf16[256,1024]{1,0:T(8,128)(2,1)} %param.18) | copy-start | bytes 1572868
  502.7 1.4 copy-start.1
  508.9 4.8 collective-permute-start.12
  511.8 6.1 %collective-permute-start.13 = (bf16[1,64,256]{2,1,0:T(8,128)(2,1)S(1)}, bf16[1,64,256]{2,1,0:T(8,128)(2,1)S(1)}, u32[]{:S(2)}, u32[]{:S(2)}) collective-permute-start(bf16[1,64,256]{2,1,0:T(8,128)(2,1)S(1)} %get-tuple-element.34), channel_id=1, source_target_pairs={{4,0},{8,4},{12,8},{16,12},{20,16},{24,20},{28,24},{5,1},{9,5},{13... | collective-permute-start | bytes 98312 | tf_op jit(solution)/shard_map/ppermute | solution.py:15
  518.0 2.9 collective-permute-start.14
  519.6 4.7 collective-permute-start.15
where the time goes:
time: 534 us; the launch traced here: 528 us
  matrix products  423 us (79%)
  starting transfers between devices  38.4 us (7%)
  waiting for transfers between devices  34.8 us (7%)
  other arithmetic  18.8 us (4%)
  local copies, waits for them, and re-layouts  12.4 us (2%)
    conv_general_dilated x2, matrix products, local_section(): lax.conv_general_dilated(extended[None], kernel[:, :, None, :], (1, 1), '...  409 us
    ppermute x8, waiting for transfers between devices, padded_2(): lax.ppermute(lax.slice_in_dim(block, 0, width, axis=dim), axis, backward)  30.1 us
    ppermute x8, starting transfers between devices, padded_2(): lax.ppermute(lax.slice_in_dim(block, block.shape[dim] - width, None, axis...  25 us
    dot_general x2, matrix products, local_section(): mixed = jnp.dot(hidden, w_out, preferred_element_type=jnp.float32)  13.8 us
    ppermute x8, starting transfers between devices, padded_2(): lax.ppermute(lax.slice_in_dim(block, 0, width, axis=dim), axis, backward)  13.4 us
  transfers between devices with their start and end apart: 16, of which 12 were waited for; matrix products, arithmetic and copies ran while one was open for 1% of the time, Pallas kernels for 0%

commit v1 on v0

--- a/solution.py
+++ b/solution.py
@@ -1,6 +1,10 @@
+import functools
+
 import jax
 import jax.numpy as jnp
 from jax import lax
+from jax.experimental import pallas as pl
+from jax.experimental.pallas import tpu as pltpu
 from jax.sharding import PartitionSpec as P
 
 
@@ -24,18 +28,61 @@
     return (raw * mask).astype(jnp.bfloat16)
 
 
+def _dw_body(x_ref, k_ref, o_ref, xs_ref, *, taps, rows, cols, chans, rb):
+    nlb = chans // 128
+    njb = cols // 8
+    nrb = rows // rb
+    for b in range(taps):
+        def shift(r, c):
+            xs_ref[r] = x_ref[r, pl.ds(b, cols), :]
+            return c
+
+        lax.fori_loop(0, rows + taps - 1, shift, 0)
+        for lb in range(nlb):
+            lanes = pl.ds(lb * 128, 128)
+            ks = [k_ref[a, b, :, lanes] for a in range(taps)]
+
+            def body(i, c):
+                r0 = pl.multiple_of((i // njb) * rb, rb)
+                j0 = pl.multiple_of((i % njb) * 8, 8)
+                xs = xs_ref[pl.ds(r0, rb + taps - 1), pl.ds(j0, 8), lanes]
+                if b == 0:
+                    acc = jnp.zeros((rb, 8, 128), jnp.float32)
+                else:
+                    acc = o_ref[pl.ds(r0, rb), pl.ds(j0, 8), lanes]
+                for a in range(taps):
+                    acc = acc + xs[a : a + rb] * ks[a][None]
+                o_ref[pl.ds(r0, rb), pl.ds(j0, 8), lanes] = acc
+                return c
+
+            lax.fori_loop(0, nrb * njb, body, 0)
+
+
+def depthwise(extended, kernel):
+    taps = kernel.shape[0]
+    rows = extended.shape[0] - taps + 1
+    cols = extended.shape[1] - taps + 1
+    chans = extended.shape[2]
+    kb = jnp.broadcast_to(kernel.astype(jnp.float32)[:, :, None, :], (taps, taps, 8, chans))
+    body = functools.partial(_dw_body, taps=taps, rows=rows, cols=cols, chans=chans, rb=8)
+    vmem = pl.BlockSpec(memory_space=pltpu.VMEM)
+    return pl.pallas_call(
+        body,
+        out_shape=jax.ShapeDtypeStruct((rows, cols, chans), jnp.float32),
+        in_specs=[vmem, vmem],
+        out_specs=vmem,
+        scratch_shapes=[pltpu.VMEM((extended.shape[0], cols, chans), jnp.float32)],
+        cost_estimate=pl.CostEstimate(
+            flops=2 * rows * cols * chans * taps * taps,
+            transcendentals=0,
+            bytes_accessed=extended.size * 4 + rows * cols * chans * 4,
+        ),
+    )(extended.astype(jnp.float32), kb)
+
+
 def local_section(extended, raw, sigma, w_in, w_out):
-    channels = extended.shape[2]
     kernel = masked_kernel(raw, sigma)
-    conv_out = lax.conv_general_dilated(
-        extended[None],
-        kernel[:, :, None, :],
-        (1, 1),
-        "VALID",
-        dimension_numbers=("NHWC", "HWIO", "NHWC"),
-        feature_group_count=channels,
-        preferred_element_type=jnp.float32,
-    )[0]
+    conv_out = depthwise(extended, kernel)
     field = extended[7 : extended.shape[0] - 7, 7 : extended.shape[1] - 7]
     mean = jnp.mean(conv_out, axis=-1, keepdims=True)
     var = jnp.mean((conv_out - mean) ** 2, axis=-1, keepdims=True)

time: 534 us -> 289 us (0.54)
  matrix products: 423 us -> 14.7 us
  Pallas kernels: 0 us -> 164 us
  other arithmetic: 18.8 us -> 24.6 us
    conv_general_dilated x2 -> x0, matrix products: 409 us -> none  [local_section(): lax.conv_general_dilated(extended[None], kernel[:, :, None, :], (1, 1), '...]
    pallas_call x0 -> x2, Pallas kernels: none -> 164 us  [depthwise(): pl.pallas_call(body, out_shape=jax.ShapeDtypeStruct((rows, cols, chans),...]
where the time goes in v1:
time: 289 us; the launch traced here: 288 us
  Pallas kernels  164 us (57%)
  starting transfers between devices  38.3 us (13%)
  waiting for transfers between devices  34.9 us (12%)
  other arithmetic  24.6 us (9%)
  matrix products  14.7 us (5%)
  local copies, waits for them, and re-layouts  10.5 us (4%)
    pallas_call x2, Pallas kernels, depthwise(): pl.pallas_call(body, out_shape=jax.ShapeDtypeStruct((rows, cols, chans),...  164 us
    ppermute x8, waiting for transfers between devices, padded_2(): lax.ppermute(lax.slice_in_dim(block, 0, width, axis=dim), axis, backward)  30.2 us
    ppermute x8, starting transfers between devices, padded_2(): lax.ppermute(lax.slice_in_dim(block, block.shape[dim] - width, None, axis...  25 us
    dot_general x2, matrix products, local_section(): mixed = jnp.dot(hidden, w_out, preferred_element_type=jnp.float32)  14.3 us
    ppermute x8, starting transfers between devices, padded_2(): lax.ppermute(lax.slice_in_dim(block, 0, width, axis=dim), axis, backward)  13.3 us
    convert_element_type x2, other arithmetic, depthwise(): extended.astype(jnp.float32)  6.08 us
  transfers between devices with their start and end apart: 16, of which 12 were waited for; matrix products, arithmetic and copies ran while one was open for 1% of the time, Pallas kernels for 0%

profile of v1, /device:TPU:3, one launch (start us, length us, event | category | flops | bytes accessed | tf_op | source)
XLA Modules:
  0.0 287.8 jit_solution(906213316193663942)
XLA Ops:
  0.0 1.1 fusion.80
  1.1 3.7 %collective-permute-start = (bf16[7,128,128]{2,1,0:T(8,128)(2,1)S(1)}, bf16[7,128,128]{2,1,0:T(8,128)(2,1)S(1)}, u32[]{:S(2)}, u32[]{:S(2)}) collective-permute-start(bf16[7,128,128]{2,1,0:T(8,128)(2,1)S(1)} %get-tuple-element.26), channel_id=1, source_target_pairs={{0,4},{4,8},{8,12},{12,16},{16,20},{20,24},{24,28},{1,5},{5,9},{9,... | collective-permute-start | bytes 688136 | tf_op jit(solution)/shard_map/ppermute | solution.py:16
  4.8 1.9 collective-permute-start.1
  6.8 0.7 multiply_multiply_fusion.3
  7.5 0.3 collective-permute-done
  7.8 2.0 constant_dynamic-update-slice_fusion.1
  9.8 3.2 %collective-permute-done.1 = bf16[7,128,128]{2,1,0:T(8,128)(2,1)S(1)} collective-permute-done((bf16[7,128,128]{2,1,0:T(8,128)(2,1)S(1)}, bf16[7,128,128]{2,1,0:T(8,128)(2,1)S(1)}, u32[]{:S(2)}, u32[]{:S(2)}) %collective-permute-start.1) | collective-permute-done | bytes 229408 | tf_op jit(solution)/shard_map/ppermute | solution.py:19
  13.2 3.2 %collective-permute-start.2 = (bf16[78,7,128]{2,1,0:T(8,128)(2,1)S(1)}, bf16[78,7,128]{2,1,0:T(8,128)(2,1)S(1)}, u32[]{:S(2)}, u32[]{:S(2)}) collective-permute-start(bf16[78,7,128]{2,1,0:T(8,128)(2,1)S(1)} %get-tuple-element.11), channel_id=1, source_target_pairs={{0,1},{1,2},{2,3},{4,5},{5,6},{6,7},{8,9},{9,10},{10,11},{12,13},{... | collective-permute-start | bytes 419336 | tf_op jit(solution)/shard_map/ppermute | solution.py:16
  16.4 1.3 collective-permute-start.3
  17.7 0.1 fusion.62
  17.8 1.1 collective-permute-done.2
  18.9 4.1 %collective-permute-done.3 = bf16[78,7,128]{2,1,0:T(8,128)(2,1)S(1)} collective-permute-done((bf16[78,7,128]{2,1,0:T(8,128)(2,1)S(1)}, bf16[78,7,128]{2,1,0:T(8,128)(2,1)S(1)}, u32[]{:S(2)}, u32[]{:S(2)}) %collective-permute-start.3) | collective-permute-done | bytes 139808 | tf_op jit(solution)/shard_map/ppermute | solution.py:19
  23.0 3.6 %maximum_convert_fusion.x_ref = f32[78,142,128]{2,1,0:T(8,128)} fusion(bf16[78,7,128]{2,1,0:T(8,128)(2,1)S(1)} %collective-permute-done.3, bf16[78,128,128]{2,1,0:T(8,128)(2,1)S(1)} %constant_dynamic-update-slice_fusion, bf16[78,7,128]{2,1,0:T(8,128)(2,1)S(1)} %collective-permute-done.2), kind=kLoop, calls=%fused_computation.23 | loop fusion | flops 8506368 | bytes 8506368 | tf_op jit(solution)/shard_map/convert_element_type | solution.py:80
  26.6 1.0 broadcast_in_dim.4.k_ref
  27.6 106.7 %shard_map.100 = f32[64,128,128]{2,1,0:T(8,128)} custom-call(f32[78,142,128]{2,1,0:T(8,128)} %maximum_convert_fusion.x_ref, f32[15,15,8,128]{3,2,1,0:T(8,128)} %broadcast_in_dim.4.k_ref), custom_call_target="tpu_custom_call" | custom-call | flops 471859200 | bytes 9865216 | tf_op jit(solution)/shard_map/pallas_call | solution.py:69
  134.3 3.3 %reduce_sum.36 = f32[64,128]{1,0:T(8,128)S(1)} reduce(f32[64,128,128]{2,1,0:T(8,128)} %shard_map.100, f32[]{:T(128)} %constant.14.clone.1), dimensions={2}, to_apply=%region_0.0 | reduce | flops 1040384 | bytes 4227076 | tf_op jit(solution)/shard_map/reduce_sum | solution.py:87
  137.7 4.0 %multiply_reduce_fusion = f32[64,128]{1,0:T(8,128)S(1)} fusion(f32[64,128,128]{2,1,0:T(8,128)} %shard_map.100, f32[64,128]{1,0:T(8,128)S(1)} %broadcast_multiply_fusion), kind=kLoop, calls=%fused_computation.20 | loop fusion | flops 3137536 | bytes 4259840 | tf_op jit(solution)/shard_map/reduce_sum | solution.py:88
  141.8 8.9 %add_convert_fusion = bf16[64,128,128]{2,1,0:T(8,128)(2,1)S(1)} fusion(bf16[64,128,128]{2,1,0:T(8,128)(2,1)} %param.10, f32[64,128,128]{2,1,0:T(8,128)} %shard_map.100, f32[64,128]{1,0:T(8,128)S(1)} %add_rsqrt_fusion, f32[64,128]{1,0:T(8,128)S(1)} %broadcast_multiply_fusion, bf16[512,128]{1,0:T(8,128)(2,1)S(1)} %copy-done.8, bf16[128,512]{1,0:T(8,128)(2,1)S(1)} %copy-done.9), kind=kOutput, calls=%fused_computation.18 | convolution fusion | flops 2191523840 | bytes 8716288 | tf_op jit(solution)/shard_map/dot_general | solution.py:93
  150.7 3.9 %collective-permute-start.4 = (bf16[1,128,128]{2,1,0:T(8,128)(2,1)S(1)}, bf16[1,128,128]{2,1,0:T(8,128)(2,1)S(1)}, u32[]{:S(2)}, u32[]{:S(2)}) collective-permute-start(bf16[1,128,128]{2,1,0:T(8,128)(2,1)S(1)} %get-tuple-element.23), channel_id=1, source_target_pairs={{0,4},{4,8},{8,12},{12,16},{16,20},{20,24},{24,28},{1,5},{5,9},{9,... | collective-permute-start | bytes 98312 | tf_op jit(solution)/shard_map/ppermute | solution.py:16
  154.6 1.9 collective-permute-start.5
  156.5 4.2 %collective-permute-done.5 = bf16[1,128,128]{2,1,0:T(8,128)(2,1)S(1)} collective-permute-done((bf16[1,128,128]{2,1,0:T(8,128)(2,1)S(1)}, bf16[1,128,128]{2,1,0:T(8,128)(2,1)S(1)}, u32[]{:S(2)}, u32[]{:S(2)}) %collective-permute-start.5) | collective-permute-done | bytes 32800 | tf_op jit(solution)/shard_map/ppermute | solution.py:19
  160.8 3.2 %collective-permute-start.6 = (bf16[66,1,128]{2,1,0:T(2,128)(2,1)S(1)}, bf16[66,1,128]{2,1,0:T(2,128)(2,1)S(1)}, u32[]{:S(2)}, u32[]{:S(2)}) collective-permute-start(bf16[66,1,128]{2,1,0:T(2,128)(2,1)S(1)} %get-tuple-element.19), channel_id=1, source_target_pairs={{0,1},{1,2},{2,3},{4,5},{5,6},{6,7},{8,9},{9,10},{10,11},{12,13},{... | collective-permute-start | bytes 50696 | tf_op jit(solution)/shard_map/ppermute | solution.py:16
  164.0 1.5 collective-permute-start.7
  165.5 3.2 %collective-permute-done.7 = bf16[66,1,128]{2,1,0:T(2,128)(2,1)S(1)} collective-permute-done((bf16[66,1,128]{2,1,0:T(2,128)(2,1)S(1)}, bf16[66,1,128]{2,1,0:T(2,128)(2,1)S(1)}, u32[]{:S(2)}, u32[]{:S(2)}) %collective-permute-start.7) | collective-permute-done | bytes 16928 | tf_op jit(solution)/shard_map/ppermute | solution.py:19
  168.7 0.8 maximum_convert_fusion.1
  169.5 0.6 fusion.71
  170.1 0.6 fusion.72
  170.7 1.6 fusion.22
  172.2 0.6 fusion.78
  172.9 0.5 fusion.51
  173.4 0.3 copy-done.5
  173.7 0.4 convolution_convert_fusion
  174.2 3.3 %collective-permute-start.8 = (bf16[7,64,256]{2,1,0:T(8,128)(2,1)S(1)}, bf16[7,64,256]{2,1,0:T(8,128)(2,1)S(1)}, u32[]{:S(2)}, u32[]{:S(2)}) collective-permute-start(bf16[7,64,256]{2,1,0:T(8,128)(2,1)S(1)} %get-tuple-element.35), channel_id=1, source_target_pairs={{0,4},{4,8},{8,12},{12,16},{16,20},{20,24},{24,28},{1,5},{5,9},{9,... | collective-permute-start | bytes 688136 | tf_op jit(solution)/shard_map/ppermute | solution.py:16
  177.5 1.9 collective-permute-start.9
  179.5 2.2 collective-permute-done.8
  181.7 4.0 %collective-permute-done.9 = bf16[7,64,256]{2,1,0:T(8,128)(2,1)S(1)} collective-permute-done((bf16[7,64,256]{2,1,0:T(8,128)(2,1)S(1)}, bf16[7,64,256]{2,1,0:T(8,128)(2,1)S(1)}, u32[]{:S(2)}, u32[]{:S(2)}) %collective-permute-start.9) | collective-permute-done | bytes 229408 | tf_op jit(solution)/shard_map/ppermute | solution.py:19
  185.8 3.2 %collective-permute-start.10 = (bf16[46,7,256]{2,1,0:T(8,128)(2,1)S(1)}, bf16[46,7,256]{2,1,0:T(8,128)(2,1)S(1)}, u32[]{:S(2)}, u32[]{:S(2)}) collective-permute-start(bf16[46,7,256]{2,1,0:T(8,128)(2,1)S(1)} %get-tuple-element.27), channel_id=1, source_target_pairs={{0,1},{1,2},{2,3},{4,5},{5,6},{6,7},{8,9},{9,10},{10,11},{12,13},{... | collective-permute-start | bytes 494600 | tf_op jit(solution)/shard_map/ppermute | solution.py:16
  189.0 1.3 collective-permute-start.11
  190.3 0.1 fusion.60
  190.5 1.1 collective-permute-done.10
  191.6 4.1 %collective-permute-done.11 = bf16[46,7,256]{2,1,0:T(8,128)(2,1)S(1)} collective-permute-done((bf16[46,7,256]{2,1,0:T(8,128)(2,1)S(1)}, bf16[46,7,256]{2,1,0:T(8,128)(2,1)S(1)}, u32[]{:S(2)}, u32[]{:S(2)}) %collective-permute-start.11) | collective-permute-done | bytes 164896 | tf_op jit(solution)/shard_map/ppermute | solution.py:19
  195.7 2.5 maximum_convert_fusion.2.x_ref
  198.2 1.4 broadcast_in_dim.5.k_ref
  199.5 57.7 %shard_map.101 = f32[32,64,256]{2,1,0:T(8,128)} custom-call(f32[46,78,256]{2,1,0:T(8,128)} %maximum_convert_fusion.2.x_ref, f32[15,15,8,256]{3,2,1,0:T(8,128)} %broadcast_in_dim.5.k_ref), custom_call_target="tpu_custom_call" | custom-call | flops 235929600 | bytes 5771264 | tf_op jit(solution)/shard_map/pallas_call | solution.py:69
  257.2 2.1 reduce_sum.38
  259.3 0.1 copy-done.1
  259.4 0.6 multiply_reduce_fusion.1
  260.1 5.4 %add_convert_fusion.1 = bf16[32,64,256]{2,1,0:T(8,128)(2,1)} fusion(bf16[32,64,256]{2,1,0:T(8,128)(2,1)} %copy-done.2, f32[32,64,256]{2,1,0:T(8,128)S(1)} %copy-done.1, f32[32,64]{1,0:T(8,128)S(1)} %add_rsqrt_fusion.1, f32[32,64]{1,0:T(8,128)S(1)} %broadcast_multiply_fusion.1, bf16[1024,256]{1,0:T(8,128)(2,1)S(1)} %copy-done, ...), kind=kOutput, calls=%fused_computation.33 | convolution fusion | flops 2169503744 | bytes 5259264 | tf_op jit(solution)/shard_map/dot_general | solution.py:93
  265.4 0.8 fusion.82
  266.2 2.8 collective-permute-start.12
  269.1 1.9 collective-permute-start.13
  271.0 4.2 %collective-permute-done.13 = bf16[1,64,256]{2,1,0:T(8,128)(2,1)S(1)} collective-permute-done((bf16[1,64,256]{2,1,0:T(8,128)(2,1)S(1)}, bf16[1,64,256]{2,1,0:T(8,128)(2,1)S(1)}, u32[]{:S(2)}, u32[]{:S(2)}) %collective-permute-start.13) | collective-permute-done | bytes 32800 | tf_op jit(solution)/shard_map/ppermute | solution.py:19
  275.2 1.0 pad_maximum_fusion.5
  276.2 1.6 collective-permute-start.14
  277.9 1.5 collective-permute-start.15
  279.4 3.1 %collective-permute-done.15 = bf16[34,1,256]{2,1,0:T(2,128)(2,1)S(1)} collective-permute-done((bf16[34,1,256]{2,1,0:T(2,128)(2,1)S(1)}, bf16[34,1,256]{2,1,0:T(2,128)(2,1)S(1)}, u32[]{:S(2)}, u32[]{:S(2)}) %collective-permute-start.15) | collective-permute-done | bytes 17440 | tf_op jit(solution)/shard_map/ppermute | solution.py:19
  282.6 1.8 maximum_convert_fusion.3
  284.3 0.4 fusion.75
  284.7 0.2 fusion.76
  284.9 0.2 fusion.77
  285.1 1.4 fusion.32
  286.5 0.3 fusion.81
  286.8 0.2 fusion.52
  287.0 0.8 copy.20
  (36 shorter events, 0.4 us)
Async XLA Ops:
  0.0 260.1 %copy-start = (bf16[1024,256]{1,0:T(8,128)(2,1)S(1)}, bf16[1024,256]{1,0:T(8,128)(2,1)}, u32[]{:S(2)}) copy-start(bf16[1024,256]{1,0:T(8,128)(2,1)} %param.19) | copy-start | bytes 1572868
  1.1 6.6 %collective-permute-start = (bf16[7,128,128]{2,1,0:T(8,128)(2,1)S(1)}, bf16[7,128,128]{2,1,0:T(8,128)(2,1)S(1)}, u32[]{:S(2)}, u32[]{:S(2)}) collective-permute-start(bf16[7,128,128]{2,1,0:T(8,128)(2,1)S(1)} %get-tuple-element.26), channel_id=1, source_target_pairs={{0,4},{4,8},{8,12},{12,16},{16,20},{20,24},{24,28},{1,5},{5,9},{9,... | collective-permute-start | bytes 688136 | tf_op jit(solution)/shard_map/ppermute | solution.py:16
  4.8 8.2 %collective-permute-start.1 = (bf16[7,128,128]{2,1,0:T(8,128)(2,1)S(1)}, bf16[7,128,128]{2,1,0:T(8,128)(2,1)S(1)}, u32[]{:S(2)}, u32[]{:S(2)}) collective-permute-start(bf16[7,128,128]{2,1,0:T(8,128)(2,1)S(1)} %get-tuple-element.25), channel_id=1, source_target_pairs={{4,0},{8,4},{12,8},{16,12},{20,16},{24,20},{28,24},{5,1},{9,5},{13... | collective-permute-start | bytes 688136 | tf_op jit(solution)/shard_map/ppermute | solution.py:19
  7.8 9.9 %copy-start.4 = (f32[15,15,128]{2,1,0:T(8,128)S(1)}, f32[15,15,128]{2,1,0:T(8,128)}, u32[]{:S(2)}) copy-start(f32[15,15,128]{2,1,0:T(8,128)} %param.11) | copy-start | bytes 345604
  13.2 5.7 %collective-permute-start.2 = (bf16[78,7,128]{2,1,0:T(8,128)(2,1)S(1)}, bf16[78,7,128]{2,1,0:T(8,128)(2,1)S(1)}, u32[]{:S(2)}, u32[]{:S(2)}) collective-permute-start(bf16[78,7,128]{2,1,0:T(8,128)(2,1)S(1)} %get-tuple-element.11), channel_id=1, source_target_pairs={{0,1},{1,2},{2,3},{4,5},{5,6},{6,7},{8,9},{9,10},{10,11},{12,13},{... | collective-permute-start | bytes 419336 | tf_op jit(solution)/shard_map/ppermute | solution.py:16
  16.4 6.6 %collective-permute-start.3 = (bf16[78,7,128]{2,1,0:T(8,128)(2,1)S(1)}, bf16[78,7,128]{2,1,0:T(8,128)(2,1)S(1)}, u32[]{:S(2)}, u32[]{:S(2)}) collective-permute-start(bf16[78,7,128]{2,1,0:T(8,128)(2,1)S(1)} %get-tuple-element.12), channel_id=1, source_target_pairs={{1,0},{2,1},{3,2},{5,4},{6,5},{7,6},{9,8},{10,9},{11,10},{13,12},{... | collective-permute-start | bytes 419336 | tf_op jit(solution)/shard_map/ppermute | solution.py:19
  137.7 4.1 %copy-start.8 = (bf16[512,128]{1,0:T(8,128)(2,1)S(1)}, bf16[512,128]{1,0:T(8,128)(2,1)}, u32[]{:S(2)}) copy-start(bf16[512,128]{1,0:T(8,128)(2,1)} %param.14) | copy-start | bytes 393220
  137.7 4.1 %copy-start.9 = (bf16[128,512]{1,0:T(8,128)(2,1)S(1)}, bf16[128,512]{1,0:T(8,128)(2,1)}, u32[]{:S(2)}) copy-start(bf16[128,512]{1,0:T(8,128)(2,1)} %param.13) | copy-start | bytes 393220
  150.7 5.8 %collective-permute-start.4 = (bf16[1,128,128]{2,1,0:T(8,128)(2,1)S(1)}, bf16[1,128,128]{2,1,0:T(8,128)(2,1)S(1)}, u32[]{:S(2)}, u32[]{:S(2)}) collective-permute-start(bf16[1,128,128]{2,1,0:T(8,128)(2,1)S(1)} %get-tuple-element.23), channel_id=1, source_target_pairs={{0,4},{4,8},{8,12},{12,16},{16,20},{20,24},{24,28},{1,5},{5,9},{9,... | collective-permute-start | bytes 98312 | tf_op jit(solution)/shard_map/ppermute | solution.py:16
  154.6 6.1 %collective-permute-start.5 = (bf16[1,128,128]{2,1,0:T(8,128)(2,1)S(1)}, bf16[1,128,128]{2,1,0:T(8,128)(2,1)S(1)}, u32[]{:S(2)}, u32[]{:S(2)}) collective-permute-start(bf16[1,128,128]{2,1,0:T(8,128)(2,1)S(1)} %get-tuple-element.24), channel_id=1, source_target_pairs={{4,0},{8,4},{12,8},{16,12},{20,16},{24,20},{28,24},{5,1},{9,5},{13... | collective-permute-start | bytes 98312 | tf_op jit(solution)/shard_map/ppermute | solution.py:19
  160.8 4.7 %collective-permute-start.6 = (bf16[66,1,128]{2,1,0:T(2,128)(2,1)S(1)}, bf16[66,1,128]{2,1,0:T(2,128)(2,1)S(1)}, u32[]{:S(2)}, u32[]{:S(2)}) collective-permute-start(bf16[66,1,128]{2,1,0:T(2,128)(2,1)S(1)} %get-tuple-element.19), channel_id=1, source_target_pairs={{0,1},{1,2},{2,3},{4,5},{5,6},{6,7},{8,9},{9,10},{10,11},{12,13},{... | collective-permute-start | bytes 50696 | tf_op jit(solution)/shard_map/ppermute | solution.py:16
  164.0 4.7 %collective-permute-start.7 = (bf16[66,1,128]{2,1,0:T(2,128)(2,1)S(1)}, bf16[66,1,128]{2,1,0:T(2,128)(2,1)S(1)}, u32[]{:S(2)}, u32[]{:S(2)}) collective-permute-start(bf16[66,1,128]{2,1,0:T(2,128)(2,1)S(1)} %get-tuple-element.20), channel_id=1, source_target_pairs={{1,0},{2,1},{3,2},{5,4},{6,5},{7,6},{9,8},{10,9},{11,10},{13,12},{... | collective-permute-start | bytes 50696 | tf_op jit(solution)/shard_map/ppermute | solution.py:19
  172.8 0.8 copy-start.5
  172.9 6.6 %copy-start.6 = (f32[256]{0:T(256)S(1)}, f32[256]{0:T(256)}, u32[]{:S(2)}) copy-start(f32[256]{0:T(256)} %param.17) | copy-start | bytes 3076
  173.7 16.6 %copy-start.3 = (f32[15,15,256]{2,1,0:T(8,128)S(1)}, f32[15,15,256]{2,1,0:T(8,128)}, u32[]{:S(2)}) copy-start(f32[15,15,256]{2,1,0:T(8,128)} %param.16) | copy-start | bytes 691204
  174.1 24.0 %copy-start.2 = (bf16[32,64,256]{2,1,0:T(8,128)(2,1)}, bf16[32,64,256]{2,1,0:T(8,128)(2,1)S(1)}, u32[]{:S(2)}) copy-start(bf16[32,64,256]{2,1,0:T(8,128)(2,1)S(1)} %convolution_convert_fusion) | copy-start | bytes 3145732
  174.2 7.5 %collective-permute-start.8 = (bf16[7,64,256]{2,1,0:T(8,128)(2,1)S(1)}, bf16[7,64,256]{2,1,0:T(8,128)(2,1)S(1)}, u32[]{:S(2)}, u32[]{:S(2)}) collective-permute-start(bf16[7,64,256]{2,1,0:T(8,128)(2,1)S(1)} %get-tuple-element.35), channel_id=1, source_target_pairs={{0,4},{4,8},{8,12},{12,16},{16,20},{20,24},{24,28},{1,5},{5,9},{9,... | collective-permute-start | bytes 688136 | tf_op jit(solution)/shard_map/ppermute | solution.py:16
  177.5 8.2 %collective-permute-start.9 = (bf16[7,64,256]{2,1,0:T(8,128)(2,1)S(1)}, bf16[7,64,256]{2,1,0:T(8,128)(2,1)S(1)}, u32[]{:S(2)}, u32[]{:S(2)}) collective-permute-start(bf16[7,64,256]{2,1,0:T(8,128)(2,1)S(1)} %get-tuple-element.36), channel_id=1, source_target_pairs={{4,0},{8,4},{12,8},{16,12},{20,16},{24,20},{28,24},{5,1},{9,5},{13... | collective-permute-start | bytes 688136 | tf_op jit(solution)/shard_map/ppermute | solution.py:19
  185.8 5.7 %collective-permute-start.10 = (bf16[46,7,256]{2,1,0:T(8,128)(2,1)S(1)}, bf16[46,7,256]{2,1,0:T(8,128)(2,1)S(1)}, u32[]{:S(2)}, u32[]{:S(2)}) collective-permute-start(bf16[46,7,256]{2,1,0:T(8,128)(2,1)S(1)} %get-tuple-element.27), channel_id=1, source_target_pairs={{0,1},{1,2},{2,3},{4,5},{5,6},{6,7},{8,9},{9,10},{10,11},{12,13},{... | collective-permute-start | bytes 494600 | tf_op jit(solution)/shard_map/ppermute | solution.py:16
  189.0 6.6 %collective-permute-start.11 = (bf16[46,7,256]{2,1,0:T(8,128)(2,1)S(1)}, bf16[46,7,256]{2,1,0:T(8,128)(2,1)S(1)}, u32[]{:S(2)}, u32[]{:S(2)}) collective-permute-start(bf16[46,7,256]{2,1,0:T(8,128)(2,1)S(1)} %get-tuple-element.28), channel_id=1, source_target_pairs={{1,0},{2,1},{3,2},{5,4},{6,5},{7,6},{9,8},{10,9},{11,10},{13,12},{... | collective-permute-start | bytes 494600 | tf_op jit(solution)/shard_map/ppermute | solution.py:19
  257.2 2.2 copy-start.1
  257.2 2.9 %copy-start.7 = (bf16[256,1024]{1,0:T(8,128)(2,1)S(1)}, bf16[256,1024]{1,0:T(8,128)(2,1)}, u32[]{:S(2)}) copy-start(bf16[256,1024]{1,0:T(8,128)(2,1)} %param.18) | copy-start | bytes 1572868
  266.2 4.8 %collective-permute-start.12 = (bf16[1,64,256]{2,1,0:T(8,128)(2,1)S(1)}, bf16[1,64,256]{2,1,0:T(8,128)(2,1)S(1)}, u32[]{:S(2)}, u32[]{:S(2)}) collective-permute-start(bf16[1,64,256]{2,1,0:T(8,128)(2,1)S(1)} %get-tuple-element.33), channel_id=1, source_target_pairs={{0,4},{4,8},{8,12},{12,16},{16,20},{20,24},{24,28},{1,5},{5,9},{9,... | collective-permute-start | bytes 98312 | tf_op jit(solution)/shard_map/ppermute | solution.py:16
  269.1 6.1 %collective-permute-start.13 = (bf16[1,64,256]{2,1,0:T(8,128)(2,1)S(1)}, bf16[1,64,256]{2,1,0:T(8,128)(2,1)S(1)}, u32[]{:S(2)}, u32[]{:S(2)}) collective-permute-start(bf16[1,64,256]{2,1,0:T(8,128)(2,1)S(1)} %get-tuple-element.34), channel_id=1, source_target_pairs={{4,0},{8,4},{12,8},{16,12},{20,16},{24,20},{28,24},{5,1},{9,5},{13... | collective-permute-start | bytes 98312 | tf_op jit(solution)/shard_map/ppermute | solution.py:19
  276.2 3.2 %collective-permute-start.14 = (bf16[34,1,256]{2,1,0:T(2,128)(2,1)S(1)}, bf16[34,1,256]{2,1,0:T(2,128)(2,1)S(1)}, u32[]{:S(2)}, u32[]{:S(2)}) collective-permute-start(bf16[34,1,256]{2,1,0:T(2,128)(2,1)S(1)} %get-tuple-element.29), channel_id=1, source_target_pairs={{0,1},{1,2},{2,3},{4,5},{5,6},{6,7},{8,9},{9,10},{10,11},{12,13},{... | collective-permute-start | bytes 52232 | tf_op jit(solution)/shard_map/ppermute | solution.py:16
  277.9 4.7 %collective-permute-start.15 = (bf16[34,1,256]{2,1,0:T(2,128)(2,1)S(1)}, bf16[34,1,256]{2,1,0:T(2,128)(2,1)S(1)}, u32[]{:S(2)}, u32[]{:S(2)}) collective-permute-start(bf16[34,1,256]{2,1,0:T(2,128)(2,1)S(1)} %get-tuple-element.30), channel_id=1, source_target_pairs={{1,0},{2,1},{3,2},{5,4},{6,5},{7,6},{9,8},{10,9},{11,10},{13,12},{... | collective-permute-start | bytes 52232 | tf_op jit(solution)/shard_map/ppermute | solution.py:19

commit v2 on v1

--- a/solution.py
+++ b/solution.py
@@ -50,12 +50,19 @@
                     acc = jnp.zeros((rb, 8, 128), jnp.float32)
                 else:
                     acc = o_ref[pl.ds(r0, rb), pl.ds(j0, 8), lanes]
-                for a in range(taps):
-                    acc = acc + xs[a : a + rb] * ks[a][None]
+                terms = [xs[a : a + rb] * ks[a][None] for a in range(taps)]
+                for g in range(0, taps, 5):
+                    group = terms[g : g + 5]
+                    while len(group) > 1:
+                        group = [
+                            group[i] + group[i + 1] if i + 1 < len(group) else group[i]
+                            for i in range(0, len(group), 2)
+                        ]
+                    acc = acc + group[0]
                 o_ref[pl.ds(r0, rb), pl.ds(j0, 8), lanes] = acc
                 return c
 
-            lax.fori_loop(0, nrb * njb, body, 0)
+            lax.fori_loop(0, nrb * njb, body, 0, unroll=2)
 
 
 def depthwise(extended, kernel):

time: 289 us -> 279 us (0.965)
  Pallas kernels: 164 us -> 155 us
    pallas_call x2, Pallas kernels: 164 us -> 155 us  [depthwise(): pl.pallas_call(body, out_shape=jax.ShapeDtypeStruct((rows, cols, chans),...]
where the time goes in v2:
time: 279 us; the launch traced here: 278 us
  Pallas kernels  155 us (56%)
  starting transfers between devices  38.1 us (14%)
  waiting for transfers between devices  35.2 us (13%)
  other arithmetic  24.6 us (9%)
  matrix products  14.7 us (5%)
  local copies, waits for them, and re-layouts  10.5 us (4%)
    pallas_call x2, Pallas kernels, depthwise(): pl.pallas_call(body, out_shape=jax.ShapeDtypeStruct((rows, cols, chans),...  155 us
    ppermute x8, waiting for transfers between devices, padded_2(): lax.ppermute(lax.slice_in_dim(block, 0, width, axis=dim), axis, backward)  30.4 us
    ppermute x8, starting transfers between devices, padded_2(): lax.ppermute(lax.slice_in_dim(block, block.shape[dim] - width, None, axis...  25 us
    dot_general x2, matrix products, local_section(): mixed = jnp.dot(hidden, w_out, preferred_element_type=jnp.float32)  14.3 us
    ppermute x8, starting transfers between devices, padded_2(): lax.ppermute(lax.slice_in_dim(block, 0, width, axis=dim), axis, backward)  13 us
    convert_element_type x2, other arithmetic, depthwise(): extended.astype(jnp.float32)  6.08 us
  transfers between devices with their start and end apart: 16, of which 12 were waited for; matrix products, arithmetic and copies ran while one was open for 1% of the time, Pallas kernels for 0%

profile of v2, /device:TPU:3, one launch (start us, length us, event | category | flops | bytes accessed | tf_op | source)
XLA Modules:
  0.0 278.2 jit_solution(13566687550779702395)
XLA Ops:
  0.0 1.1 fusion.80
  1.1 3.7 %collective-permute-start = (bf16[7,128,128]{2,1,0:T(8,128)(2,1)S(1)}, bf16[7,128,128]{2,1,0:T(8,128)(2,1)S(1)}, u32[]{:S(2)}, u32[]{:S(2)}) collective-permute-start(bf16[7,128,128]{2,1,0:T(8,128)(2,1)S(1)} %get-tuple-element.26), channel_id=1, source_target_pairs={{0,4},{4,8},{8,12},{12,16},{16,20},{20,24},{24,28},{1,5},{5,9},{9,... | collective-permute-start | bytes 688136 | tf_op jit(solution)/shard_map/ppermute | solution.py:16
  4.8 1.9 collective-permute-start.1
  6.8 0.7 multiply_multiply_fusion.3
  7.5 0.3 collective-permute-done
  7.8 2.0 constant_dynamic-update-slice_fusion.1
  9.8 3.2 %collective-permute-done.1 = bf16[7,128,128]{2,1,0:T(8,128)(2,1)S(1)} collective-permute-done((bf16[7,128,128]{2,1,0:T(8,128)(2,1)S(1)}, bf16[7,128,128]{2,1,0:T(8,128)(2,1)S(1)}, u32[]{:S(2)}, u32[]{:S(2)}) %collective-permute-start.1) | collective-permute-done | bytes 229408 | tf_op jit(solution)/shard_map/ppermute | solution.py:19
  13.2 3.2 %collective-permute-start.2 = (bf16[78,7,128]{2,1,0:T(8,128)(2,1)S(1)}, bf16[78,7,128]{2,1,0:T(8,128)(2,1)S(1)}, u32[]{:S(2)}, u32[]{:S(2)}) collective-permute-start(bf16[78,7,128]{2,1,0:T(8,128)(2,1)S(1)} %get-tuple-element.11), channel_id=1, source_target_pairs={{0,1},{1,2},{2,3},{4,5},{5,6},{6,7},{8,9},{9,10},{10,11},{12,13},{... | collective-permute-start | bytes 419336 | tf_op jit(solution)/shard_map/ppermute | solution.py:16
  16.4 1.3 collective-permute-start.3
  17.7 0.1 fusion.62
  17.8 1.1 collective-permute-done.2
  18.9 4.1 %collective-permute-done.3 = bf16[78,7,128]{2,1,0:T(8,128)(2,1)S(1)} collective-permute-done((bf16[78,7,128]{2,1,0:T(8,128)(2,1)S(1)}, bf16[78,7,128]{2,1,0:T(8,128)(2,1)S(1)}, u32[]{:S(2)}, u32[]{:S(2)}) %collective-permute-start.3) | collective-permute-done | bytes 139808 | tf_op jit(solution)/shard_map/ppermute | solution.py:19
  23.0 3.6 %maximum_convert_fusion.x_ref = f32[78,142,128]{2,1,0:T(8,128)} fusion(bf16[78,7,128]{2,1,0:T(8,128)(2,1)S(1)} %collective-permute-done.3, bf16[78,128,128]{2,1,0:T(8,128)(2,1)S(1)} %constant_dynamic-update-slice_fusion, bf16[78,7,128]{2,1,0:T(8,128)(2,1)S(1)} %collective-permute-done.2), kind=kLoop, calls=%fused_computation.23 | loop fusion | flops 8506368 | bytes 8506368 | tf_op jit(solution)/shard_map/convert_element_type | solution.py:87
  26.6 1.0 broadcast_in_dim.4.k_ref
  27.6 100.6 %shard_map.100 = f32[64,128,128]{2,1,0:T(8,128)} custom-call(f32[78,142,128]{2,1,0:T(8,128)} %maximum_convert_fusion.x_ref, f32[15,15,8,128]{3,2,1,0:T(8,128)} %broadcast_in_dim.4.k_ref), custom_call_target="tpu_custom_call" | custom-call | flops 471859200 | bytes 9865216 | tf_op jit(solution)/shard_map/pallas_call | solution.py:76
  128.2 3.3 %reduce_sum.36 = f32[64,128]{1,0:T(8,128)S(1)} reduce(f32[64,128,128]{2,1,0:T(8,128)} %shard_map.100, f32[]{:T(128)} %constant.14.clone.1), dimensions={2}, to_apply=%region_0.0 | reduce | flops 1040384 | bytes 4227076 | tf_op jit(solution)/shard_map/reduce_sum | solution.py:94
  131.6 4.0 %multiply_reduce_fusion = f32[64,128]{1,0:T(8,128)S(1)} fusion(f32[64,128,128]{2,1,0:T(8,128)} %shard_map.100, f32[64,128]{1,0:T(8,128)S(1)} %broadcast_multiply_fusion), kind=kLoop, calls=%fused_computation.20 | loop fusion | flops 3137536 | bytes 4259840 | tf_op jit(solution)/shard_map/reduce_sum | solution.py:95
  135.6 8.9 %add_convert_fusion = bf16[64,128,128]{2,1,0:T(8,128)(2,1)S(1)} fusion(bf16[64,128,128]{2,1,0:T(8,128)(2,1)} %param.10, f32[64,128,128]{2,1,0:T(8,128)} %shard_map.100, f32[64,128]{1,0:T(8,128)S(1)} %add_rsqrt_fusion, f32[64,128]{1,0:T(8,128)S(1)} %broadcast_multiply_fusion, bf16[512,128]{1,0:T(8,128)(2,1)S(1)} %copy-done.8, bf16[128,512]{1,0:T(8,128)(2,1)S(1)} %copy-done.9), kind=kOutput, calls=%fused_computation.18 | convolution fusion | flops 2191523840 | bytes 8716288 | tf_op jit(solution)/shard_map/dot_general | solution.py:100
  144.5 3.9 %collective-permute-start.4 = (bf16[1,128,128]{2,1,0:T(8,128)(2,1)S(1)}, bf16[1,128,128]{2,1,0:T(8,128)(2,1)S(1)}, u32[]{:S(2)}, u32[]{:S(2)}) collective-permute-start(bf16[1,128,128]{2,1,0:T(8,128)(2,1)S(1)} %get-tuple-element.23), channel_id=1, source_target_pairs={{0,4},{4,8},{8,12},{12,16},{16,20},{20,24},{24,28},{1,5},{5,9},{9,... | collective-permute-start | bytes 98312 | tf_op jit(solution)/shard_map/ppermute | solution.py:16
  148.5 1.9 collective-permute-start.5
  150.4 4.2 %collective-permute-done.5 = bf16[1,128,128]{2,1,0:T(8,128)(2,1)S(1)} collective-permute-done((bf16[1,128,128]{2,1,0:T(8,128)(2,1)S(1)}, bf16[1,128,128]{2,1,0:T(8,128)(2,1)S(1)}, u32[]{:S(2)}, u32[]{:S(2)}) %collective-permute-start.5) | collective-permute-done | bytes 32800 | tf_op jit(solution)/shard_map/ppermute | solution.py:19
  154.6 3.2 %collective-permute-start.6 = (bf16[66,1,128]{2,1,0:T(2,128)(2,1)S(1)}, bf16[66,1,128]{2,1,0:T(2,128)(2,1)S(1)}, u32[]{:S(2)}, u32[]{:S(2)}) collective-permute-start(bf16[66,1,128]{2,1,0:T(2,128)(2,1)S(1)} %get-tuple-element.19), channel_id=1, source_target_pairs={{0,1},{1,2},{2,3},{4,5},{5,6},{6,7},{8,9},{9,10},{10,11},{12,13},{... | collective-permute-start | bytes 50696 | tf_op jit(solution)/shard_map/ppermute | solution.py:16
  157.8 1.5 collective-permute-start.7
  159.3 3.2 %collective-permute-done.7 = bf16[66,1,128]{2,1,0:T(2,128)(2,1)S(1)} collective-permute-done((bf16[66,1,128]{2,1,0:T(2,128)(2,1)S(1)}, bf16[66,1,128]{2,1,0:T(2,128)(2,1)S(1)}, u32[]{:S(2)}, u32[]{:S(2)}) %collective-permute-start.7) | collective-permute-done | bytes 16928 | tf_op jit(solution)/shard_map/ppermute | solution.py:19
  162.5 0.8 maximum_convert_fusion.1
  163.4 0.6 fusion.71
  164.0 0.6 fusion.72
  164.5 1.6 fusion.22
  166.1 0.6 fusion.78
  166.7 0.5 fusion.51
  167.2 0.3 copy-done.5
  167.6 0.4 convolution_convert_fusion
  168.0 3.3 %collective-permute-start.8 = (bf16[7,64,256]{2,1,0:T(8,128)(2,1)S(1)}, bf16[7,64,256]{2,1,0:T(8,128)(2,1)S(1)}, u32[]{:S(2)}, u32[]{:S(2)}) collective-permute-start(bf16[7,64,256]{2,1,0:T(8,128)(2,1)S(1)} %get-tuple-element.35), channel_id=1, source_target_pairs={{0,4},{4,8},{8,12},{12,16},{16,20},{20,24},{24,28},{1,5},{5,9},{9,... | collective-permute-start | bytes 688136 | tf_op jit(solution)/shard_map/ppermute | solution.py:16
  171.4 1.9 collective-permute-start.9
  173.3 2.2 collective-permute-done.8
  175.6 4.0 %collective-permute-done.9 = bf16[7,64,256]{2,1,0:T(8,128)(2,1)S(1)} collective-permute-done((bf16[7,64,256]{2,1,0:T(8,128)(2,1)S(1)}, bf16[7,64,256]{2,1,0:T(8,128)(2,1)S(1)}, u32[]{:S(2)}, u32[]{:S(2)}) %collective-permute-start.9) | collective-permute-done | bytes 229408 | tf_op jit(solution)/shard_map/ppermute | solution.py:19
  179.7 3.2 %collective-permute-start.10 = (bf16[46,7,256]{2,1,0:T(8,128)(2,1)S(1)}, bf16[46,7,256]{2,1,0:T(8,128)(2,1)S(1)}, u32[]{:S(2)}, u32[]{:S(2)}) collective-permute-start(bf16[46,7,256]{2,1,0:T(8,128)(2,1)S(1)} %get-tuple-element.27), channel_id=1, source_target_pairs={{0,1},{1,2},{2,3},{4,5},{5,6},{6,7},{8,9},{9,10},{10,11},{12,13},{... | collective-permute-start | bytes 494600 | tf_op jit(solution)/shard_map/ppermute | solution.py:16
  182.9 1.3 collective-permute-start.11
  184.2 0.1 fusion.60
  184.3 1.1 collective-permute-done.10
  185.4 4.1 %collective-permute-done.11 = bf16[46,7,256]{2,1,0:T(8,128)(2,1)S(1)} collective-permute-done((bf16[46,7,256]{2,1,0:T(8,128)(2,1)S(1)}, bf16[46,7,256]{2,1,0:T(8,128)(2,1)S(1)}, u32[]{:S(2)}, u32[]{:S(2)}) %collective-permute-start.11) | collective-permute-done | bytes 164896 | tf_op jit(solution)/shard_map/ppermute | solution.py:19
  189.5 2.5 maximum_convert_fusion.2.x_ref
  192.0 1.4 broadcast_in_dim.5.k_ref
  193.4 54.2 %shard_map.101 = f32[32,64,256]{2,1,0:T(8,128)} custom-call(f32[46,78,256]{2,1,0:T(8,128)} %maximum_convert_fusion.2.x_ref, f32[15,15,8,256]{3,2,1,0:T(8,128)} %broadcast_in_dim.5.k_ref), custom_call_target="tpu_custom_call" | custom-call | flops 235929600 | bytes 5771264 | tf_op jit(solution)/shard_map/pallas_call | solution.py:76
  247.5 2.1 reduce_sum.38
  249.7 0.1 copy-done.1
  249.8 0.6 multiply_reduce_fusion.1
  250.4 5.4 %add_convert_fusion.1 = bf16[32,64,256]{2,1,0:T(8,128)(2,1)} fusion(bf16[32,64,256]{2,1,0:T(8,128)(2,1)} %copy-done.2, f32[32,64,256]{2,1,0:T(8,128)S(1)} %copy-done.1, f32[32,64]{1,0:T(8,128)S(1)} %add_rsqrt_fusion.1, f32[32,64]{1,0:T(8,128)S(1)} %broadcast_multiply_fusion.1, bf16[1024,256]{1,0:T(8,128)(2,1)S(1)} %copy-done, ...), kind=kOutput, calls=%fused_computation.33 | convolution fusion | flops 2169503744 | bytes 5259264 | tf_op jit(solution)/shard_map/dot_general | solution.py:100
  255.8 0.8 fusion.82
  256.6 2.9 %collective-permute-start.12 = (bf16[1,64,256]{2,1,0:T(8,128)(2,1)S(1)}, bf16[1,64,256]{2,1,0:T(8,128)(2,1)S(1)}, u32[]{:S(2)}, u32[]{:S(2)}) collective-permute-start(bf16[1,64,256]{2,1,0:T(8,128)(2,1)S(1)} %get-tuple-element.33), channel_id=1, source_target_pairs={{0,4},{4,8},{8,12},{12,16},{16,20},{20,24},{24,28},{1,5},{5,9},{9,... | collective-permute-start | bytes 98312 | tf_op jit(solution)/shard_map/ppermute | solution.py:16
  259.4 1.9 collective-permute-start.13
  261.4 4.2 %collective-permute-done.13 = bf16[1,64,256]{2,1,0:T(8,128)(2,1)S(1)} collective-permute-done((bf16[1,64,256]{2,1,0:T(8,128)(2,1)S(1)}, bf16[1,64,256]{2,1,0:T(8,128)(2,1)S(1)}, u32[]{:S(2)}, u32[]{:S(2)}) %collective-permute-start.13) | collective-permute-done | bytes 32800 | tf_op jit(solution)/shard_map/ppermute | solution.py:19
  265.6 1.0 pad_maximum_fusion.5
  266.6 1.6 collective-permute-start.14
  268.3 1.3 collective-permute-start.15
  269.6 3.4 %collective-permute-done.15 = bf16[34,1,256]{2,1,0:T(2,128)(2,1)S(1)} collective-permute-done((bf16[34,1,256]{2,1,0:T(2,128)(2,1)S(1)}, bf16[34,1,256]{2,1,0:T(2,128)(2,1)S(1)}, u32[]{:S(2)}, u32[]{:S(2)}) %collective-permute-start.15) | collective-permute-done | bytes 17440 | tf_op jit(solution)/shard_map/ppermute | solution.py:19
  272.9 1.8 maximum_convert_fusion.3
  274.7 0.4 fusion.75
  275.1 0.2 fusion.76
  275.3 0.2 fusion.77
  275.5 1.4 fusion.32
  276.9 0.3 fusion.81
  277.2 0.2 fusion.52
  277.4 0.8 copy.20
  (36 shorter events, 0.4 us)
Async XLA Ops:
  0.0 250.4 %copy-start = (bf16[1024,256]{1,0:T(8,128)(2,1)S(1)}, bf16[1024,256]{1,0:T(8,128)(2,1)}, u32[]{:S(2)}) copy-start(bf16[1024,256]{1,0:T(8,128)(2,1)} %param.19) | copy-start | bytes 1572868
  1.1 6.6 %collective-permute-start = (bf16[7,128,128]{2,1,0:T(8,128)(2,1)S(1)}, bf16[7,128,128]{2,1,0:T(8,128)(2,1)S(1)}, u32[]{:S(2)}, u32[]{:S(2)}) collective-permute-start(bf16[7,128,128]{2,1,0:T(8,128)(2,1)S(1)} %get-tuple-element.26), channel_id=1, source_target_pairs={{0,4},{4,8},{8,12},{12,16},{16,20},{20,24},{24,28},{1,5},{5,9},{9,... | collective-permute-start | bytes 688136 | tf_op jit(solution)/shard_map/ppermute | solution.py:16
  4.8 8.2 %collective-permute-start.1 = (bf16[7,128,128]{2,1,0:T(8,128)(2,1)S(1)}, bf16[7,128,128]{2,1,0:T(8,128)(2,1)S(1)}, u32[]{:S(2)}, u32[]{:S(2)}) collective-permute-start(bf16[7,128,128]{2,1,0:T(8,128)(2,1)S(1)} %get-tuple-element.25), channel_id=1, source_target_pairs={{4,0},{8,4},{12,8},{16,12},{20,16},{24,20},{28,24},{5,1},{9,5},{13... | collective-permute-start | bytes 688136 | tf_op jit(solution)/shard_map/ppermute | solution.py:19
  7.8 9.9 %copy-start.4 = (f32[15,15,128]{2,1,0:T(8,128)S(1)}, f32[15,15,128]{2,1,0:T(8,128)}, u32[]{:S(2)}) copy-start(f32[15,15,128]{2,1,0:T(8,128)} %param.11) | copy-start | bytes 345604
  13.2 5.7 %collective-permute-start.2 = (bf16[78,7,128]{2,1,0:T(8,128)(2,1)S(1)}, bf16[78,7,128]{2,1,0:T(8,128)(2,1)S(1)}, u32[]{:S(2)}, u32[]{:S(2)}) collective-permute-start(bf16[78,7,128]{2,1,0:T(8,128)(2,1)S(1)} %get-tuple-element.11), channel_id=1, source_target_pairs={{0,1},{1,2},{2,3},{4,5},{5,6},{6,7},{8,9},{9,10},{10,11},{12,13},{... | collective-permute-start | bytes 419336 | tf_op jit(solution)/shard_map/ppermute | solution.py:16
  16.4 6.6 %collective-permute-start.3 = (bf16[78,7,128]{2,1,0:T(8,128)(2,1)S(1)}, bf16[78,7,128]{2,1,0:T(8,128)(2,1)S(1)}, u32[]{:S(2)}, u32[]{:S(2)}) collective-permute-start(bf16[78,7,128]{2,1,0:T(8,128)(2,1)S(1)} %get-tuple-element.12), channel_id=1, source_target_pairs={{1,0},{2,1},{3,2},{5,4},{6,5},{7,6},{9,8},{10,9},{11,10},{13,12},{... | collective-permute-start | bytes 419336 | tf_op jit(solution)/shard_map/ppermute | solution.py:19
  131.5 4.1 %copy-start.8 = (bf16[512,128]{1,0:T(8,128)(2,1)S(1)}, bf16[512,128]{1,0:T(8,128)(2,1)}, u32[]{:S(2)}) copy-start(bf16[512,128]{1,0:T(8,128)(2,1)} %param.14) | copy-start | bytes 393220
  131.5 4.1 %copy-start.9 = (bf16[128,512]{1,0:T(8,128)(2,1)S(1)}, bf16[128,512]{1,0:T(8,128)(2,1)}, u32[]{:S(2)}) copy-start(bf16[128,512]{1,0:T(8,128)(2,1)} %param.13) | copy-start | bytes 393220
  144.5 5.8 %collective-permute-start.4 = (bf16[1,128,128]{2,1,0:T(8,128)(2,1)S(1)}, bf16[1,128,128]{2,1,0:T(8,128)(2,1)S(1)}, u32[]{:S(2)}, u32[]{:S(2)}) collective-permute-start(bf16[1,128,128]{2,1,0:T(8,128)(2,1)S(1)} %get-tuple-element.23), channel_id=1, source_target_pairs={{0,4},{4,8},{8,12},{12,16},{16,20},{20,24},{24,28},{1,5},{5,9},{9,... | collective-permute-start | bytes 98312 | tf_op jit(solution)/shard_map/ppermute | solution.py:16
  148.5 6.1 %collective-permute-start.5 = (bf16[1,128,128]{2,1,0:T(8,128)(2,1)S(1)}, bf16[1,128,128]{2,1,0:T(8,128)(2,1)S(1)}, u32[]{:S(2)}, u32[]{:S(2)}) collective-permute-start(bf16[1,128,128]{2,1,0:T(8,128)(2,1)S(1)} %get-tuple-element.24), channel_id=1, source_target_pairs={{4,0},{8,4},{12,8},{16,12},{20,16},{24,20},{28,24},{5,1},{9,5},{13... | collective-permute-start | bytes 98312 | tf_op jit(solution)/shard_map/ppermute | solution.py:19
  154.6 4.7 %collective-permute-start.6 = (bf16[66,1,128]{2,1,0:T(2,128)(2,1)S(1)}, bf16[66,1,128]{2,1,0:T(2,128)(2,1)S(1)}, u32[]{:S(2)}, u32[]{:S(2)}) collective-permute-start(bf16[66,1,128]{2,1,0:T(2,128)(2,1)S(1)} %get-tuple-element.19), channel_id=1, source_target_pairs={{0,1},{1,2},{2,3},{4,5},{5,6},{6,7},{8,9},{9,10},{10,11},{12,13},{... | collective-permute-start | bytes 50696 | tf_op jit(solution)/shard_map/ppermute | solution.py:16
  157.8 4.7 %collective-permute-start.7 = (bf16[66,1,128]{2,1,0:T(2,128)(2,1)S(1)}, bf16[66,1,128]{2,1,0:T(2,128)(2,1)S(1)}, u32[]{:S(2)}, u32[]{:S(2)}) collective-permute-start(bf16[66,1,128]{2,1,0:T(2,128)(2,1)S(1)} %get-tuple-element.20), channel_id=1, source_target_pairs={{1,0},{2,1},{3,2},{5,4},{6,5},{7,6},{9,8},{10,9},{11,10},{13,12},{... | collective-permute-start | bytes 50696 | tf_op jit(solution)/shard_map/ppermute | solution.py:19
  166.7 0.8 copy-start.5
  166.7 6.6 %copy-start.6 = (f32[256]{0:T(256)S(1)}, f32[256]{0:T(256)}, u32[]{:S(2)}) copy-start(f32[256]{0:T(256)} %param.17) | copy-start | bytes 3076
  167.5 16.7 %copy-start.3 = (f32[15,15,256]{2,1,0:T(8,128)S(1)}, f32[15,15,256]{2,1,0:T(8,128)}, u32[]{:S(2)}) copy-start(f32[15,15,256]{2,1,0:T(8,128)} %param.16) | copy-start | bytes 691204
  168.0 24.0 %copy-start.2 = (bf16[32,64,256]{2,1,0:T(8,128)(2,1)}, bf16[32,64,256]{2,1,0:T(8,128)(2,1)S(1)}, u32[]{:S(2)}) copy-start(bf16[32,64,256]{2,1,0:T(8,128)(2,1)S(1)} %convolution_convert_fusion) | copy-start | bytes 3145732
  168.0 7.5 %collective-permute-start.8 = (bf16[7,64,256]{2,1,0:T(8,128)(2,1)S(1)}, bf16[7,64,256]{2,1,0:T(8,128)(2,1)S(1)}, u32[]{:S(2)}, u32[]{:S(2)}) collective-permute-start(bf16[7,64,256]{2,1,0:T(8,128)(2,1)S(1)} %get-tuple-element.35), channel_id=1, source_target_pairs={{0,4},{4,8},{8,12},{12,16},{16,20},{20,24},{24,28},{1,5},{5,9},{9,... | collective-permute-start | bytes 688136 | tf_op jit(solution)/shard_map/ppermute | solution.py:16
  171.4 8.2 %collective-permute-start.9 = (bf16[7,64,256]{2,1,0:T(8,128)(2,1)S(1)}, bf16[7,64,256]{2,1,0:T(8,128)(2,1)S(1)}, u32[]{:S(2)}, u32[]{:S(2)}) collective-permute-start(bf16[7,64,256]{2,1,0:T(8,128)(2,1)S(1)} %get-tuple-element.36), channel_id=1, source_target_pairs={{4,0},{8,4},{12,8},{16,12},{20,16},{24,20},{28,24},{5,1},{9,5},{13... | collective-permute-start | bytes 688136 | tf_op jit(solution)/shard_map/ppermute | solution.py:19
  179.7 5.8 %collective-permute-start.10 = (bf16[46,7,256]{2,1,0:T(8,128)(2,1)S(1)}, bf16[46,7,256]{2,1,0:T(8,128)(2,1)S(1)}, u32[]{:S(2)}, u32[]{:S(2)}) collective-permute-start(bf16[46,7,256]{2,1,0:T(8,128)(2,1)S(1)} %get-tuple-element.27), channel_id=1, source_target_pairs={{0,1},{1,2},{2,3},{4,5},{5,6},{6,7},{8,9},{9,10},{10,11},{12,13},{... | collective-permute-start | bytes 494600 | tf_op jit(solution)/shard_map/ppermute | solution.py:16
  182.9 6.6 %collective-permute-start.11 = (bf16[46,7,256]{2,1,0:T(8,128)(2,1)S(1)}, bf16[46,7,256]{2,1,0:T(8,128)(2,1)S(1)}, u32[]{:S(2)}, u32[]{:S(2)}) collective-permute-start(bf16[46,7,256]{2,1,0:T(8,128)(2,1)S(1)} %get-tuple-element.28), channel_id=1, source_target_pairs={{1,0},{2,1},{3,2},{5,4},{6,5},{7,6},{9,8},{10,9},{11,10},{13,12},{... | collective-permute-start | bytes 494600 | tf_op jit(solution)/shard_map/ppermute | solution.py:19
  247.5 2.2 copy-start.1
  247.5 2.9 %copy-start.7 = (bf16[256,1024]{1,0:T(8,128)(2,1)S(1)}, bf16[256,1024]{1,0:T(8,128)(2,1)}, u32[]{:S(2)}) copy-start(bf16[256,1024]{1,0:T(8,128)(2,1)} %param.18) | copy-start | bytes 1572868
  256.6 4.8 %collective-permute-start.12 = (bf16[1,64,256]{2,1,0:T(8,128)(2,1)S(1)}, bf16[1,64,256]{2,1,0:T(8,128)(2,1)S(1)}, u32[]{:S(2)}, u32[]{:S(2)}) collective-permute-start(bf16[1,64,256]{2,1,0:T(8,128)(2,1)S(1)} %get-tuple-element.33), channel_id=1, source_target_pairs={{0,4},{4,8},{8,12},{12,16},{16,20},{20,24},{24,28},{1,5},{5,9},{9,... | collective-permute-start | bytes 98312 | tf_op jit(solution)/shard_map/ppermute | solution.py:16
  259.4 6.1 %collective-permute-start.13 = (bf16[1,64,256]{2,1,0:T(8,128)(2,1)S(1)}, bf16[1,64,256]{2,1,0:T(8,128)(2,1)S(1)}, u32[]{:S(2)}, u32[]{:S(2)}) collective-permute-start(bf16[1,64,256]{2,1,0:T(8,128)(2,1)S(1)} %get-tuple-element.34), channel_id=1, source_target_pairs={{4,0},{8,4},{12,8},{16,12},{20,16},{24,20},{28,24},{5,1},{9,5},{13... | collective-permute-start | bytes 98312 | tf_op jit(solution)/shard_map/ppermute | solution.py:19
  266.6 2.9 %collective-permute-start.14 = (bf16[34,1,256]{2,1,0:T(2,128)(2,1)S(1)}, bf16[34,1,256]{2,1,0:T(2,128)(2,1)S(1)}, u32[]{:S(2)}, u32[]{:S(2)}) collective-permute-start(bf16[34,1,256]{2,1,0:T(2,128)(2,1)S(1)} %get-tuple-element.29), channel_id=1, source_target_pairs={{0,1},{1,2},{2,3},{4,5},{5,6},{6,7},{8,9},{9,10},{10,11},{12,13},{... | collective-permute-start | bytes 52232 | tf_op jit(solution)/shard_map/ppermute | solution.py:16
  268.3 4.7 %collective-permute-start.15 = (bf16[34,1,256]{2,1,0:T(2,128)(2,1)S(1)}, bf16[34,1,256]{2,1,0:T(2,128)(2,1)S(1)}, u32[]{:S(2)}, u32[]{:S(2)}) collective-permute-start(bf16[34,1,256]{2,1,0:T(2,128)(2,1)S(1)} %get-tuple-element.30), channel_id=1, source_target_pairs={{1,0},{2,1},{3,2},{5,4},{6,5},{7,6},{9,8},{10,9},{11,10},{13,12},{... | collective-permute-start | bytes 52232 | tf_op jit(solution)/shard_map/ppermute | solution.py:19

commit v3 on v2

--- a/solution.py
+++ b/solution.py
@@ -65,31 +65,37 @@
             lax.fori_loop(0, nrb * njb, body, 0, unroll=2)
 
 
-def depthwise(extended, kernel):
+def depthwise(extended, kernel, rb):
     taps = kernel.shape[0]
     rows = extended.shape[0] - taps + 1
     cols = extended.shape[1] - taps + 1
     chans = extended.shape[2]
+    rows_p = -(-rows // rb) * rb
+    cols_p = -(-cols // 8) * 8
+    padded = jnp.pad(
+        extended.astype(jnp.float32), ((0, rows_p - rows), (0, cols_p - cols), (0, 0))
+    )
     kb = jnp.broadcast_to(kernel.astype(jnp.float32)[:, :, None, :], (taps, taps, 8, chans))
-    body = functools.partial(_dw_body, taps=taps, rows=rows, cols=cols, chans=chans, rb=8)
+    body = functools.partial(_dw_body, taps=taps, rows=rows_p, cols=cols_p, chans=chans, rb=rb)
     vmem = pl.BlockSpec(memory_space=pltpu.VMEM)
-    return pl.pallas_call(
+    out = pl.pallas_call(
         body,
-        out_shape=jax.ShapeDtypeStruct((rows, cols, chans), jnp.float32),
+        out_shape=jax.ShapeDtypeStruct((rows_p, cols_p, chans), jnp.float32),
         in_specs=[vmem, vmem],
         out_specs=vmem,
-        scratch_shapes=[pltpu.VMEM((extended.shape[0], cols, chans), jnp.float32)],
+        scratch_shapes=[pltpu.VMEM((padded.shape[0], cols_p, chans), jnp.float32)],
         cost_estimate=pl.CostEstimate(
-            flops=2 * rows * cols * chans * taps * taps,
+            flops=2 * rows_p * cols_p * chans * taps * taps,
             transcendentals=0,
-            bytes_accessed=extended.size * 4 + rows * cols * chans * 4,
+            bytes_accessed=padded.size * 4 + rows_p * cols_p * chans * 4,
         ),
-    )(extended.astype(jnp.float32), kb)
+    )(padded, kb)
+    return out[:rows, :cols]
 
 
-def local_section(extended, raw, sigma, w_in, w_out):
+def local_section(extended, raw, sigma, w_in, w_out, rb):
     kernel = masked_kernel(raw, sigma)
-    conv_out = depthwise(extended, kernel)
+    conv_out = depthwise(extended, kernel, rb)
     field = extended[7 : extended.shape[0] - 7, 7 : extended.shape[1] - 7]
     mean = jnp.mean(conv_out, axis=-1, keepdims=True)
     var = jnp.mean((conv_out - mean) ** 2, axis=-1, keepdims=True)
@@ -98,7 +104,19 @@
         jnp.bfloat16
     )
     mixed = jnp.dot(hidden, w_out, preferred_element_type=jnp.float32)
-    return (field.astype(jnp.float32) + mixed).astype(jnp.bfloat16)
+    out = (field.astype(jnp.float32) + mixed).astype(jnp.bfloat16)
+    return zero_outer_edge(out)
+
+
+def zero_outer_edge(block):
+    keep = None
+    for axis, dim in (("row", 0), ("col", 1)):
+        index = lax.axis_index(axis)
+        last = lax.axis_size(axis) - 1
+        pos = lax.broadcasted_iota(jnp.int32, block.shape[:2], dim)
+        ok = ((pos != 0) | (index != 0)) & ((pos != block.shape[dim] - 1) | (index != last))
+        keep = ok if keep is None else keep & ok
+    return jnp.where(keep[:, :, None], block, jnp.zeros_like(block))
 
 
 def blur_down(padded):
@@ -127,15 +145,13 @@
     in_second,
     out_second,
 ):
-    reach = 7
+    reach = 8
     extended = padded_2(image, (("row", 0), ("col", 1)), reach)
-    first = local_section(extended, raw_first, sigma_first, in_first, out_first)
-    first_cycle = padded_2(first, (("row", 0), ("col", 1)), 1)
+    first_cycle = local_section(extended, raw_first, sigma_first, in_first, out_first, 6)
     first_pooled = blur_down(first_cycle)
     widened = jnp.dot(first_pooled, widen, preferred_element_type=jnp.float32).astype(jnp.bfloat16)
     widened_ext = padded_2(widened, (("row", 0), ("col", 1)), reach)
-    second = local_section(widened_ext, raw_second, sigma_second, in_second, out_second)
-    second_cycle = padded_2(second, (("row", 0), ("col", 1)), 1)
+    second_cycle = local_section(widened_ext, raw_second, sigma_second, in_second, out_second, 6)
     return blur_down(second_cycle)
 
 

time: 279 us -> 282 us (1.011)
  Pallas kernels: 155 us -> 177 us
  starting transfers between devices: 38.1 us -> 20.1 us
  waiting for transfers between devices: 35.2 us -> 19 us
  matrix products: 14.7 us -> 21.3 us
  local copies, waits for them, and re-layouts: 10.5 us -> 15.5 us
  other arithmetic: 24.6 us -> 28.2 us
    pallas_call x2, Pallas kernels: 155 us -> 177 us  [depthwise(): pl.pallas_call(body, out_shape=jax.ShapeDtypeStruct((rows_p, cols_p, chan...]
    ppermute x8 -> x4, waiting for transfers between devices: 30.4 us -> 15.1 us  [padded_2(): lax.ppermute(lax.slice_in_dim(block, 0, width, axis=dim), axis, backward)]
    ppermute x8 -> x4, starting transfers between devices: 25 us -> 13.7 us  [padded_2(): lax.ppermute(lax.slice_in_dim(block, block.shape[dim] - width, None, axis...]
    convert_element_type x4 -> x0, other arithmetic: 8.69 us -> none  [the longest x2 6.08 us: depthwise(): extended.astype(jnp.float32)]
    ppermute x8 -> x4, starting transfers between devices: 13 us -> 6.43 us  [padded_2(): lax.ppermute(lax.slice_in_dim(block, 0, width, axis=dim), axis, backward)]
    dot_general x2, matrix products: 14.3 us -> 20.8 us  [local_section(): mixed = jnp.dot(hidden, w_out, preferred_element_type=jnp.float32)]
    slice x2, local copies, waits for them, and re-layouts: 0.97 us -> 6.9 us  [blur_down(): upper = padded[0:rows].reshape(rows // 2, 2, cols + 2, -1)]
    pad x0 -> x2, other arithmetic: none -> 5.7 us  [depthwise(): jnp.pad(extended.astype(jnp.float32), ((0, rows_p - rows), (0, cols_p - c...]
  transfers between devices with their start and end apart: 16 -> 8, of which waited for: 12 -> 7; matrix products, arithmetic and copies ran while one was open for 1% -> 2% of each run, Pallas kernels for 0% -> 0%
where the time goes in v3:
time: 282 us
  Pallas kernels  177 us (63%)
  other arithmetic  28.2 us (10%)
  matrix products  21.3 us (8%)
  starting transfers between devices  20.1 us (7%)
  waiting for transfers between devices  19 us (7%)
  local copies, waits for them, and re-layouts  15.5 us (5%)
    pallas_call x2, Pallas kernels, depthwise(): pl.pallas_call(body, out_shape=jax.ShapeDtypeStruct((rows_p, cols_p, chan...  177 us
    dot_general x2, matrix products, local_section(): mixed = jnp.dot(hidden, w_out, preferred_element_type=jnp.float32)  20.8 us
    ppermute x4, waiting for transfers between devices, padded_2(): lax.ppermute(lax.slice_in_dim(block, 0, width, axis=dim), axis, backward)  15.1 us
    ppermute x4, starting transfers between devices, padded_2(): lax.ppermute(lax.slice_in_dim(block, block.shape[dim] - width, None, axis...  13.7 us
    reduce_sum x2, other arithmetic, local_section(): mean = jnp.mean(conv_out, axis=-1, keepdims=True)  7.26 us
    slice x2, local copies, waits for them, and re-layouts, blur_down(): upper = padded[0:rows].reshape(rows // 2, 2, cols + 2, -1)  6.9 us
    reduce_sum x2, other arithmetic, local_section(): var = jnp.mean((conv_out - mean) ** 2, axis=-1, keepdims=True)  6.64 us
    ppermute x4, starting transfers between devices, padded_2(): lax.ppermute(lax.slice_in_dim(block, 0, width, axis=dim), axis, backward)  6.43 us
  transfers between devices with their start and end apart: 8, of which 7 were waited for; matrix products, arithmetic and copies ran while one was open for 2% of the time, Pallas kernels for 0%

profile of v3, /device:TPU:3, one launch (start us, length us, event | category | flops | bytes accessed | tf_op | source)
XLA Modules:
  0.0 281.8 jit_solution(13001714146567348985)
XLA Ops:
  0.0 0.0 copy-start
  0.0 1.1 fusion.83
  1.1 3.7 %collective-permute-start = (bf16[8,128,128]{2,1,0:T(8,128)(2,1)S(1)}, bf16[8,128,128]{2,1,0:T(8,128)(2,1)S(1)}, u32[]{:S(2)}, u32[]{:S(2)}) collective-permute-start(bf16[8,128,128]{2,1,0:T(8,128)(2,1)S(1)} %get-tuple-element.22), channel_id=1, source_target_pairs={{0,4},{4,8},{8,12},{12,16},{16,20},{20,24},{24,28},{1,5},{5,9},{9,... | collective-permute-start | bytes 786440 | tf_op jit(solution)/shard_map/ppermute | solution.py:16
  4.8 1.9 collective-permute-start.1
  6.8 0.1 add_negate_fusion
  6.9 0.7 broadcast_and_fusion
  7.5 0.7 multiply_multiply_fusion.3
  8.2 1.0 fusion.66
  9.2 0.0 collective-permute-done
  9.2 0.0 copy-start.7
  9.3 2.0 constant_dynamic-update-slice_fusion.1
  11.2 2.2 collective-permute-done.1
  13.5 3.2 %collective-permute-start.2 = (bf16[80,8,128]{2,1,0:T(8,128)(2,1)S(1)}, bf16[80,8,128]{2,1,0:T(8,128)(2,1)S(1)}, u32[]{:S(2)}, u32[]{:S(2)}) collective-permute-start(bf16[80,8,128]{2,1,0:T(8,128)(2,1)S(1)} %get-tuple-element.11), channel_id=1, source_target_pairs={{0,1},{1,2},{2,3},{4,5},{5,6},{6,7},{8,9},{9,10},{10,11},{12,13},{... | collective-permute-start | bytes 491528 | tf_op jit(solution)/shard_map/ppermute | solution.py:16
  16.7 1.3 collective-permute-start.3
  18.0 0.0 copy-done.7
  18.0 0.6 multiply_multiply_fusion.2
  18.6 0.6 or_and_fusion.3
  19.2 0.4 collective-permute-done.2
  19.7 4.1 %collective-permute-done.3 = bf16[80,8,128]{2,1,0:T(8,128)(2,1)S(1)} collective-permute-done((bf16[80,8,128]{2,1,0:T(8,128)(2,1)S(1)}, bf16[80,8,128]{2,1,0:T(8,128)(2,1)S(1)}, u32[]{:S(2)}, u32[]{:S(2)}) %collective-permute-start.3) | collective-permute-done | bytes 163872 | tf_op jit(solution)/shard_map/ppermute | solution.py:19
  23.8 0.3 pad_maximum_fusion
  24.0 3.1 %pad_convert_fusion.x_ref = f32[80,150,128]{2,1,0:T(8,128)} fusion(bf16[80,144,128]{2,1,0:T(8,128)(2,1)S(1)} %pad_maximum_fusion), kind=kLoop, calls=%fused_computation.25 | loop fusion | flops 1536000 | bytes 9093120 | tf_op jit(solution)/shard_map/jit(_pad)/pad | solution.py:75
  27.1 1.0 broadcast_in_dim.23.k_ref
  28.1 110.0 %shard_map.100 = f32[66,136,128]{2,1,0:T(8,128)} custom-call(f32[80,150,128]{2,1,0:T(8,128)} %pad_convert_fusion.x_ref, f32[15,15,8,128]{3,2,1,0:T(8,128)} %broadcast_in_dim.23.k_ref), custom_call_target="tpu_custom_call" | custom-call | flops 517017600 | bytes 10739712 | tf_op jit(solution)/shard_map/pallas_call | solution.py:81
  138.1 4.8 %slice_reduce_fusion = f32[66,130]{1,0:T(8,128)S(1)} fusion(f32[66,136,128]{2,1,0:T(8,128)} %shard_map.100), kind=kLoop, calls=%fused_computation.23 | loop fusion | flops 1089660 | bytes 4427280 | tf_op jit(solution)/shard_map/reduce_sum | solution.py:100
  142.9 0.0 copy-done.1
  142.9 3.9 %multiply_reduce_fusion = f32[66,130]{1,0:T(8,128)S(1)} fusion(f32[66,136,128]{2,1,0:T(8,128)S(1)} %copy-done.1, f32[66,130]{1,0:T(8,128)S(1)} %broadcast_multiply_fusion), kind=kLoop, calls=%fused_computation.21 | loop fusion | flops 3286140 | bytes 4461600 | tf_op jit(solution)/shard_map/reduce_sum | solution.py:101
  146.9 0.7 add_rsqrt_fusion
  147.5 13.3 %fusion.22 = f32[66,130,128]{2,1,0:T(8,128)} fusion(bf16[80,144,128]{2,1,0:T(8,128)(2,1)S(1)} %pad_maximum_fusion, pred[66,130]{1,0:T(8,128)(4,1)} %broadcast_and_fusion, f32[66,136,128]{2,1,0:T(8,128)} %shard_map.100, f32[66,130]{1,0:T(8,128)} %add_rsqrt_fusion, f32[66,130]{1,0:T(8,128)S(1)} %broadcast_multiply_fusion, bf16[512,128]{1,0:T(8,128)(2,1)} %param.14, ...), kind=kOutput, calls=%fused_computation.34 | convolution fusion | flops 2297518080 | bytes 11524516 | tf_op jit(solution)/shard_map/dot_general | solution.py:106
  160.8 4.2 %fusion.75 = (f32[64,130,128]{2,1,0:T(8,128)S(1)}, f32[64,130,128]{2,1,0:T(8,128)S(1)}) fusion(f32[66,130,128]{2,1,0:T(8,128)} %fusion.22), kind=kLoop, calls=%fused_computation.115 | loop fusion | bytes 17039360 | tf_op jit(solution)/shard_map/slice | solution.py:126
  165.0 0.6 fusion.76
  165.6 1.6 fusion.28
  167.1 0.6 fusion.82
  167.7 0.0 copy-start.5
  167.7 0.5 fusion.55
  168.3 0.3 copy-done.5
  168.6 0.4 convolution_convert_fusion
  169.1 3.6 %collective-permute-start.4 = (bf16[8,64,256]{2,1,0:T(8,128)(2,1)S(1)}, bf16[8,64,256]{2,1,0:T(8,128)(2,1)S(1)}, u32[]{:S(2)}, u32[]{:S(2)}) collective-permute-start(bf16[8,64,256]{2,1,0:T(8,128)(2,1)S(1)} %get-tuple-element.27), channel_id=1, source_target_pairs={{0,4},{4,8},{8,12},{12,16},{16,20},{20,24},{24,28},{1,5},{5,9},{9,... | collective-permute-start | bytes 786440 | tf_op jit(solution)/shard_map/ppermute | solution.py:16
  172.6 1.9 collective-permute-start.5
  174.6 0.0 copy-done.4
  174.6 0.1 fusion.64
  174.7 1.8 collective-permute-done.4
  176.6 4.7 %collective-permute-done.5 = bf16[8,64,256]{2,1,0:T(8,128)(2,1)S(1)} collective-permute-done((bf16[8,64,256]{2,1,0:T(8,128)(2,1)S(1)}, bf16[8,64,256]{2,1,0:T(8,128)(2,1)S(1)}, u32[]{:S(2)}, u32[]{:S(2)}) %collective-permute-start.5) | collective-permute-done | bytes 262176 | tf_op jit(solution)/shard_map/ppermute | solution.py:19
  181.3 3.2 %collective-permute-start.6 = (bf16[48,8,256]{2,1,0:T(8,128)(2,1)S(1)}, bf16[48,8,256]{2,1,0:T(8,128)(2,1)S(1)}, u32[]{:S(2)}, u32[]{:S(2)}) collective-permute-start(bf16[48,8,256]{2,1,0:T(8,128)(2,1)S(1)} %get-tuple-element.23), channel_id=1, source_target_pairs={{0,1},{1,2},{2,3},{4,5},{5,6},{6,7},{8,9},{9,10},{10,11},{12,13},{... | collective-permute-start | bytes 589832 | tf_op jit(solution)/shard_map/ppermute | solution.py:16
  184.5 1.3 collective-permute-start.7
  185.8 0.1 broadcast_and_fusion.1
  185.9 1.7 collective-permute-done.6
  187.5 4.1 %collective-permute-done.7 = bf16[48,8,256]{2,1,0:T(8,128)(2,1)S(1)} collective-permute-done((bf16[48,8,256]{2,1,0:T(8,128)(2,1)S(1)}, bf16[48,8,256]{2,1,0:T(8,128)(2,1)S(1)}, u32[]{:S(2)}, u32[]{:S(2)}) %collective-permute-start.7) | collective-permute-done | bytes 196640 | tf_op jit(solution)/shard_map/ppermute | solution.py:19
  191.7 0.1 pad_maximum_fusion.1
  191.8 2.6 pad_convert_fusion.1.x_ref
  194.4 0.1 copy-done.3
  194.5 1.3 broadcast_in_dim.25.k_ref
  195.9 67.3 %shard_map.101 = f32[36,72,256]{2,1,0:T(8,128)} custom-call(f32[50,86,256]{2,1,0:T(8,128)} %pad_convert_fusion.1.x_ref, f32[15,15,8,256]{3,2,1,0:T(8,128)} %broadcast_in_dim.25.k_ref), custom_call_target="tpu_custom_call" | custom-call | flops 298598400 | bytes 7057408 | tf_op jit(solution)/shard_map/pallas_call | solution.py:81
  263.2 2.5 slice_reduce_fusion.1
  265.7 2.7 multiply_reduce_fusion.1
  268.4 0.0 copy-done
  268.4 0.0 copy-done.2
  268.4 7.6 %select_convert_fusion = f32[34,66,256]{2,1,0:T(8,128)} fusion(pred[34,66]{1,0:T(8,128)(4,1)S(1)} %broadcast_and_fusion.1, f32[36,72,256]{2,1,0:T(8,128)S(1)} %copy-done.2, f32[34,66]{1,0:T(8,128)S(1)} %add_rsqrt_fusion.1, f32[34,66]{1,0:T(8,128)S(1)} %broadcast_multiply_fusion.1, bf16[48,80,256]{2,1,0:T(8,128)(2,1)} %copy-done.3, ...), kind=kOutput, calls=%fused_computation.47 | convolution fusion | flops 2378280960 | bytes 7048192 | tf_op jit(solution)/shard_map/dot_general | solution.py:106
  276.0 2.7 fusion.79
  278.7 0.2 fusion.80
  278.9 0.2 fusion.81
  279.1 1.4 fusion.40
  280.5 0.3 fusion.84
  280.8 0.2 fusion.56
  281.0 0.8 copy.20
  (20 shorter events, 0.2 us)
Async XLA Ops:
  0.0 268.4 %copy-start = (bf16[1024,256]{1,0:T(8,128)(2,1)S(1)}, bf16[1024,256]{1,0:T(8,128)(2,1)}, u32[]{:S(2)}) copy-start(bf16[1024,256]{1,0:T(8,128)(2,1)} %param.19) | copy-start | bytes 1572868
  1.1 8.1 %collective-permute-start = (bf16[8,128,128]{2,1,0:T(8,128)(2,1)S(1)}, bf16[8,128,128]{2,1,0:T(8,128)(2,1)S(1)}, u32[]{:S(2)}, u32[]{:S(2)}) collective-permute-start(bf16[8,128,128]{2,1,0:T(8,128)(2,1)S(1)} %get-tuple-element.22), channel_id=1, source_target_pairs={{0,4},{4,8},{8,12},{12,16},{16,20},{20,24},{24,28},{1,5},{5,9},{9,... | collective-permute-start | bytes 786440 | tf_op jit(solution)/shard_map/ppermute | solution.py:16
  4.8 8.6 %collective-permute-start.1 = (bf16[8,128,128]{2,1,0:T(8,128)(2,1)S(1)}, bf16[8,128,128]{2,1,0:T(8,128)(2,1)S(1)}, u32[]{:S(2)}, u32[]{:S(2)}) collective-permute-start(bf16[8,128,128]{2,1,0:T(8,128)(2,1)S(1)} %get-tuple-element.21), channel_id=1, source_target_pairs={{4,0},{8,4},{12,8},{16,12},{20,16},{24,20},{28,24},{5,1},{9,5},{13... | collective-permute-start | bytes 786440 | tf_op jit(solution)/shard_map/ppermute | solution.py:19
  9.2 8.8 %copy-start.7 = (f32[256]{0:T(256)S(1)}, f32[256]{0:T(256)}, u32[]{:S(2)}) copy-start(f32[256]{0:T(256)} %param.17) | copy-start | bytes 3076
  13.5 6.2 %collective-permute-start.2 = (bf16[80,8,128]{2,1,0:T(8,128)(2,1)S(1)}, bf16[80,8,128]{2,1,0:T(8,128)(2,1)S(1)}, u32[]{:S(2)}, u32[]{:S(2)}) collective-permute-start(bf16[80,8,128]{2,1,0:T(8,128)(2,1)S(1)} %get-tuple-element.11), channel_id=1, source_target_pairs={{0,1},{1,2},{2,3},{4,5},{5,6},{6,7},{8,9},{9,10},{10,11},{12,13},{... | collective-permute-start | bytes 491528 | tf_op jit(solution)/shard_map/ppermute | solution.py:16
  16.7 7.0 %collective-permute-start.3 = (bf16[80,8,128]{2,1,0:T(8,128)(2,1)S(1)}, bf16[80,8,128]{2,1,0:T(8,128)(2,1)S(1)}, u32[]{:S(2)}, u32[]{:S(2)}) collective-permute-start(bf16[80,8,128]{2,1,0:T(8,128)(2,1)S(1)} %get-tuple-element.12), channel_id=1, source_target_pairs={{1,0},{2,1},{3,2},{5,4},{6,5},{7,6},{9,8},{10,9},{11,10},{13,12},{... | collective-permute-start | bytes 491528 | tf_op jit(solution)/shard_map/ppermute | solution.py:19
  138.1 4.8 %copy-start.1 = (f32[66,136,128]{2,1,0:T(8,128)S(1)}, f32[66,136,128]{2,1,0:T(8,128)}, u32[]{:S(2)}) copy-start(f32[66,136,128]{2,1,0:T(8,128)} %shard_map.100) | copy-start | bytes 13787140
  167.7 0.8 copy-start.5
  168.6 6.0 %copy-start.4 = (f32[15,15,256]{2,1,0:T(8,128)S(1)}, f32[15,15,256]{2,1,0:T(8,128)}, u32[]{:S(2)}) copy-start(f32[15,15,256]{2,1,0:T(8,128)} %param.16) | copy-start | bytes 691204
  168.6 6.0 %copy-start.6 = (f32[256]{0:T(256)S(1)}, f32[256]{0:T(256)}, u32[]{:S(2)}) copy-start(f32[256]{0:T(256)} %multiply_multiply_fusion.2) | copy-start | bytes 3076
  168.6 17.2 %copy-start.8 = (pred[34]{0:T(512)(128)(4,1)S(1)}, pred[34]{0:T(512)(128)(4,1)}, u32[]{:S(2)}) copy-start(pred[34]{0:T(512)(128)(4,1)} %or_and_fusion.3) | copy-start | bytes 106
  169.1 7.5 %collective-permute-start.4 = (bf16[8,64,256]{2,1,0:T(8,128)(2,1)S(1)}, bf16[8,64,256]{2,1,0:T(8,128)(2,1)S(1)}, u32[]{:S(2)}, u32[]{:S(2)}) collective-permute-start(bf16[8,64,256]{2,1,0:T(8,128)(2,1)S(1)} %get-tuple-element.27), channel_id=1, source_target_pairs={{0,4},{4,8},{8,12},{12,16},{16,20},{20,24},{24,28},{1,5},{5,9},{9,... | collective-permute-start | bytes 786440 | tf_op jit(solution)/shard_map/ppermute | solution.py:16
  172.6 8.6 %collective-permute-start.5 = (bf16[8,64,256]{2,1,0:T(8,128)(2,1)S(1)}, bf16[8,64,256]{2,1,0:T(8,128)(2,1)S(1)}, u32[]{:S(2)}, u32[]{:S(2)}) collective-permute-start(bf16[8,64,256]{2,1,0:T(8,128)(2,1)S(1)} %get-tuple-element.28), channel_id=1, source_target_pairs={{4,0},{8,4},{12,8},{16,12},{20,16},{24,20},{28,24},{5,1},{9,5},{13... | collective-permute-start | bytes 786440 | tf_op jit(solution)/shard_map/ppermute | solution.py:19
  181.3 6.3 %collective-permute-start.6 = (bf16[48,8,256]{2,1,0:T(8,128)(2,1)S(1)}, bf16[48,8,256]{2,1,0:T(8,128)(2,1)S(1)}, u32[]{:S(2)}, u32[]{:S(2)}) collective-permute-start(bf16[48,8,256]{2,1,0:T(8,128)(2,1)S(1)} %get-tuple-element.23), channel_id=1, source_target_pairs={{0,1},{1,2},{2,3},{4,5},{5,6},{6,7},{8,9},{9,10},{10,11},{12,13},{... | collective-permute-start | bytes 589832 | tf_op jit(solution)/shard_map/ppermute | solution.py:16
  184.5 7.2 %collective-permute-start.7 = (bf16[48,8,256]{2,1,0:T(8,128)(2,1)S(1)}, bf16[48,8,256]{2,1,0:T(8,128)(2,1)S(1)}, u32[]{:S(2)}, u32[]{:S(2)}) collective-permute-start(bf16[48,8,256]{2,1,0:T(8,128)(2,1)S(1)} %get-tuple-element.24), channel_id=1, source_target_pairs={{1,0},{2,1},{3,2},{5,4},{6,5},{7,6},{9,8},{10,9},{11,10},{13,12},{... | collective-permute-start | bytes 589832 | tf_op jit(solution)/shard_map/ppermute | solution.py:19
  191.8 2.7 copy-start.3
  263.2 5.3 %copy-start.2 = (f32[36,72,256]{2,1,0:T(8,128)S(1)}, f32[36,72,256]{2,1,0:T(8,128)}, u32[]{:S(2)}) copy-start(f32[36,72,256]{2,1,0:T(8,128)} %shard_map.101) | copy-start | bytes 7962628

commit v4 on v2

--- a/solution.py
+++ b/solution.py
@@ -8,17 +8,42 @@
 from jax.sharding import PartitionSpec as P
 
 
-def padded_2(block, sides, width):
-    for axis, dim in sides:
-        count = lax.axis_size(axis)
-        forward = [(i, i + 1) for i in range(count - 1)]
-        backward = [(target, source) for source, target in forward]
-        low = lax.ppermute(
-            lax.slice_in_dim(block, block.shape[dim] - width, None, axis=dim), axis, forward
-        )
-        high = lax.ppermute(lax.slice_in_dim(block, 0, width, axis=dim), axis, backward)
-        block = jnp.concatenate([low, block, high], axis=dim)
+def _piece(block, d, dim, width):
+    if d < 0:
+        return lax.slice_in_dim(block, block.shape[dim] - width, None, axis=dim)
+    if d > 0:
+        return lax.slice_in_dim(block, 0, width, axis=dim)
     return block
+
+
+def padded_2(block, width):
+    nr = lax.axis_size("row")
+    nc = lax.axis_size("col")
+    got = {}
+    for dr in (-1, 0, 1):
+        for dc in (-1, 0, 1):
+            if dr == 0 and dc == 0:
+                continue
+            piece = _piece(_piece(block, dr, 0, width), dc, 1, width)
+            if dc == 0:
+                pairs = [(r, r - dr) for r in range(nr) if 0 <= r - dr < nr]
+                got[dr, dc] = lax.ppermute(piece, "row", pairs)
+            elif dr == 0:
+                pairs = [(c, c - dc) for c in range(nc) if 0 <= c - dc < nc]
+                got[dr, dc] = lax.ppermute(piece, "col", pairs)
+            else:
+                pairs = [
+                    (r * nc + c, (r - dr) * nc + (c - dc))
+                    for r in range(nr)
+                    for c in range(nc)
+                    if 0 <= r - dr < nr and 0 <= c - dc < nc
+                ]
+                got[dr, dc] = lax.ppermute(piece, ("row", "col"), pairs)
+    got[0, 0] = block
+    bands = [
+        jnp.concatenate([got[dr, -1], got[dr, 0], got[dr, 1]], axis=1) for dr in (-1, 0, 1)
+    ]
+    return jnp.concatenate(bands, axis=0)
 
 
 def masked_kernel(raw, sigma):
@@ -128,14 +153,14 @@
     out_second,
 ):
     reach = 7
-    extended = padded_2(image, (("row", 0), ("col", 1)), reach)
+    extended = padded_2(image, reach)
     first = local_section(extended, raw_first, sigma_first, in_first, out_first)
-    first_cycle = padded_2(first, (("row", 0), ("col", 1)), 1)
+    first_cycle = padded_2(first, 1)
     first_pooled = blur_down(first_cycle)
     widened = jnp.dot(first_pooled, widen, preferred_element_type=jnp.float32).astype(jnp.bfloat16)
-    widened_ext = padded_2(widened, (("row", 0), ("col", 1)), reach)
+    widened_ext = padded_2(widened, reach)
     second = local_section(widened_ext, raw_second, sigma_second, in_second, out_second)
-    second_cycle = padded_2(second, (("row", 0), ("col", 1)), 1)
+    second_cycle = padded_2(second, 1)
     return blur_down(second_cycle)
 
 

time: 279 us -> 340 us (1.22)
  starting transfers between devices: 38.1 us -> 93.1 us
  waiting for transfers between devices: 35.2 us -> 26.2 us
  other arithmetic: 24.6 us -> 32.9 us
  local copies, waits for them, and re-layouts: 10.5 us -> 14.4 us
    ppermute x16 -> x32, starting transfers between devices: 38.1 us -> 93.1 us  [the longest x16 52.3 us: padded_2(): got[dr, dc] = lax.ppermute(piece, ('row', 'col'), pairs)]
    ppermute x16 -> x32, waiting for transfers between devices: 35.2 us -> 26.2 us  [the longest x16 20.8 us: padded_2(): got[dr, dc] = lax.ppermute(piece, ('row', 'col'), pairs)]
    slice x5 -> x12, local copies, waits for them, and re-layouts: 2.03 us -> 8.01 us  [_piece(): return lax.slice_in_dim(block, block.shape[dim] - width, None, axis=dim)]
    convert_element_type x2, other arithmetic: 6.08 us -> 10.9 us  [depthwise(): extended.astype(jnp.float32)]
    convert_element_type x2, other arithmetic: 2.6 us -> 6.19 us  [blur_down(): padded = padded.astype(jnp.float32)]
  transfers between devices with their start and end apart: 16 -> 32, of which waited for: 12 -> 8; matrix products, arithmetic and copies ran while one was open for 1% -> 1% of each run, Pallas kernels for 0% -> 0%
where the time goes in v4:
time: 340 us; the launch traced here: 337 us
  Pallas kernels  155 us (46%)
  starting transfers between devices  93.1 us (27%)
  other arithmetic  32.9 us (10%)
  waiting for transfers between devices  26.2 us (8%)
  matrix products  15.4 us (5%)
  local copies, waits for them, and re-layouts  14.4 us (4%)
    pallas_call x2, Pallas kernels, depthwise(): pl.pallas_call(body, out_shape=jax.ShapeDtypeStruct((rows, cols, chans),...  155 us
    ppermute x16, starting transfers between devices, padded_2(): got[dr, dc] = lax.ppermute(piece, ('row', 'col'), pairs)  52.3 us
    ppermute x8, starting transfers between devices, padded_2(): got[dr, dc] = lax.ppermute(piece, 'row', pairs)  21.2 us
    ppermute x16, waiting for transfers between devices, padded_2(): got[dr, dc] = lax.ppermute(piece, ('row', 'col'), pairs)  20.8 us
    ppermute x8, starting transfers between devices, padded_2(): got[dr, dc] = lax.ppermute(piece, 'col', pairs)  19.6 us
    dot_general x2, matrix products, local_section(): mixed = jnp.dot(hidden, w_out, preferred_element_type=jnp.float32)  14.9 us
    convert_element_type x2, other arithmetic, depthwise(): extended.astype(jnp.float32)  10.9 us
    slice x12, local copies, waits for them, and re-layouts, _piece(): return lax.slice_in_dim(block, block.shape[dim] - width, None, axis=dim)  8.01 us
  transfers between devices with their start and end apart: 32, of which 8 were waited for; matrix products, arithmetic and copies ran while one was open for 1% of the time, Pallas kernels for 0%

profile of v4, /device:TPU:3, one launch (start us, length us, event | category | flops | bytes accessed | tf_op | source)
XLA Modules:
  0.0 337.4 jit_solution(759941866373736751)
XLA Ops:
  0.0 0.8 fusion.81
  0.8 4.7 %collective-permute-start = (bf16[7,7,128]{2,1,0:T(8,128)(2,1)S(1)}, bf16[7,7,128]{2,1,0:T(8,128)(2,1)S(1)}, u32[]{:S(2)}, u32[]{:S(2)}) collective-permute-start(bf16[7,7,128]{2,1,0:T(8,128)(2,1)S(1)} %get-tuple-element.27), channel_id=1, source_target_pairs={{0,5},{1,6},{2,7},{4,9},{5,10},{6,11},{8,13},{9,14},{10,15},{12,17... | collective-permute-start | bytes 37640 | tf_op jit(solution)/shard_map/ppermute | solution.py:41
  5.5 1.3 collective-permute-start.2
  6.8 4.3 %collective-permute-start.5 = (bf16[7,7,128]{2,1,0:T(8,128)(2,1)S(1)}, bf16[7,7,128]{2,1,0:T(8,128)(2,1)S(1)}, u32[]{:S(2)}, u32[]{:S(2)}) collective-permute-start(bf16[7,7,128]{2,1,0:T(8,128)(2,1)S(1)} %get-tuple-element.28), channel_id=1, source_target_pairs={{4,1},{5,2},{6,3},{8,5},{9,6},{10,7},{12,9},{13,10},{14,11},{16,13... | collective-permute-start | bytes 37640 | tf_op jit(solution)/shard_map/ppermute | solution.py:41
  11.1 1.3 collective-permute-start.7
  12.4 1.1 fusion.82
  13.5 3.8 %collective-permute-start.1 = (bf16[7,128,128]{2,1,0:T(8,128)(2,1)S(1)}, bf16[7,128,128]{2,1,0:T(8,128)(2,1)S(1)}, u32[]{:S(2)}, u32[]{:S(2)}) collective-permute-start(bf16[7,128,128]{2,1,0:T(8,128)(2,1)S(1)} %get-tuple-element.31), channel_id=1, source_target_pairs={{0,4},{4,8},{8,12},{12,16},{16,20},{20,24},{24,28},{1,5},{5,9},{9,... | collective-permute-start | bytes 688136 | tf_op jit(solution)/shard_map/ppermute | solution.py:30
  17.3 1.0 fusion.83
  19.1 1.9 collective-permute-start.6
  21.0 4.4 %collective-permute-start.3 = (bf16[64,7,128]{2,1,0:T(8,128)(2,1)S(1)}, bf16[64,7,128]{2,1,0:T(8,128)(2,1)S(1)}, u32[]{:S(2)}, u32[]{:S(2)}) collective-permute-start(bf16[64,7,128]{2,1,0:T(8,128)(2,1)S(1)} %get-tuple-element.33), channel_id=1, source_target_pairs={{0,1},{1,2},{2,3},{4,5},{5,6},{6,7},{8,9},{9,10},{10,11},{12,13},{... | collective-permute-start | bytes 344072 | tf_op jit(solution)/shard_map/ppermute | solution.py:33
  25.5 1.3 collective-permute-start.4
  26.8 1.0 fusion.62
  27.8 0.8 collective-permute-done.3
  28.6 3.9 %collective-permute-done.4 = bf16[64,7,128]{2,1,0:T(8,128)(2,1)S(1)} collective-permute-done((bf16[64,7,128]{2,1,0:T(8,128)(2,1)S(1)}, bf16[64,7,128]{2,1,0:T(8,128)(2,1)S(1)}, u32[]{:S(2)}, u32[]{:S(2)}) %collective-permute-start.4) | collective-permute-done | bytes 114720 | tf_op jit(solution)/shard_map/ppermute | solution.py:33
  32.5 8.6 %maximum_convert_fusion.x_ref = f32[78,142,128]{2,1,0:T(8,128)} fusion(bf16[7,7,128]{2,1,0:T(8,128)(2,1)S(1)} %collective-permute-done.7, bf16[7,128,128]{2,1,0:T(8,128)(2,1)S(1)} %collective-permute-done.6, bf16[7,7,128]{2,1,0:T(8,128)(2,1)S(1)} %collective-permute-done.5, bf16[64,7,128]{2,1,0:T(8,128)(2,1)S(1)} %collective-permute-done.4, ...), kind=kLoop, calls=%fused_computation.23 | loop fusion | flops 25519104 | bytes 8506368 | tf_op jit(solution)/shard_map/convert_element_type | solution.py:112
  41.1 1.0 broadcast_in_dim.4.k_ref
  42.1 100.6 %shard_map.100 = f32[64,128,128]{2,1,0:T(8,128)} custom-call(f32[78,142,128]{2,1,0:T(8,128)} %maximum_convert_fusion.x_ref, f32[15,15,8,128]{3,2,1,0:T(8,128)} %broadcast_in_dim.4.k_ref), custom_call_target="tpu_custom_call" | custom-call | flops 471859200 | bytes 9865216 | tf_op jit(solution)/shard_map/pallas_call | solution.py:101
  142.6 3.3 reduce_sum.36
  146.0 4.1 %multiply_reduce_fusion = f32[64,128]{1,0:T(8,128)S(1)} fusion(f32[64,128,128]{2,1,0:T(8,128)} %shard_map.100, f32[64,128]{1,0:T(8,128)S(1)} %broadcast_multiply_fusion), kind=kLoop, calls=%fused_computation.20 | loop fusion | flops 3137536 | bytes 4259840 | tf_op jit(solution)/shard_map/reduce_sum | solution.py:120
  150.2 9.6 %add_convert_fusion = bf16[64,128,128]{2,1,0:T(8,128)(2,1)} fusion(bf16[64,128,128]{2,1,0:T(8,128)(2,1)S(1)} %copy-done.3, f32[64,128,128]{2,1,0:T(8,128)} %shard_map.100, f32[64,128]{1,0:T(8,128)S(1)} %add_rsqrt_fusion, f32[64,128]{1,0:T(8,128)S(1)} %broadcast_multiply_fusion, bf16[512,128]{1,0:T(8,128)(2,1)S(1)} %copy-done.8, ...), kind=kOutput, calls=%fused_computation.18 | convolution fusion | flops 2191523840 | bytes 8716288 | tf_op jit(solution)/shard_map/dot_general | solution.py:125
  160.4 1.0 fusion.80
  161.5 0.8 fusion.79
  162.2 1.3 collective-permute-start.10
  163.5 4.5 %collective-permute-start.13 = (bf16[1,1,128]{2,1,0:T(2,128)(2,1)S(1)}, bf16[1,1,128]{2,1,0:T(2,128)(2,1)S(1)}, u32[]{:S(2)}, u32[]{:S(2)}) collective-permute-start(bf16[1,1,128]{2,1,0:T(2,128)(2,1)S(1)} %get-tuple-element.21), channel_id=1, source_target_pairs={{4,1},{5,2},{6,3},{8,5},{9,6},{10,7},{12,9},{13,10},{14,11},{16,13... | collective-permute-start | bytes 776 | tf_op jit(solution)/shard_map/ppermute | solution.py:41
  168.1 1.3 collective-permute-start.15
  169.4 7.9 %collective-permute-start.8 = (bf16[1,1,128]{2,1,0:T(2,128)(2,1)S(1)}, bf16[1,1,128]{2,1,0:T(2,128)(2,1)S(1)}, u32[]{:S(2)}, u32[]{:S(2)}) collective-permute-start(bf16[1,1,128]{2,1,0:T(2,128)(2,1)S(1)} %get-tuple-element.19), channel_id=1, source_target_pairs={{0,5},{1,6},{2,7},{4,9},{5,10},{6,11},{8,13},{9,14},{10,15},{12,17... | collective-permute-start | bytes 776 | tf_op jit(solution)/shard_map/ppermute | solution.py:41
  177.2 3.2 collective-permute-start.11
  180.4 1.3 collective-permute-start.12
  181.8 1.9 collective-permute-start.14
  183.7 4.7 %collective-permute-start.9 = (bf16[1,128,128]{2,1,0:T(8,128)(2,1)S(1)}, bf16[1,128,128]{2,1,0:T(8,128)(2,1)S(1)}, u32[]{:S(2)}, u32[]{:S(2)}) collective-permute-start(bf16[1,128,128]{2,1,0:T(8,128)(2,1)S(1)} %get-tuple-element.23), channel_id=1, source_target_pairs={{0,4},{4,8},{8,12},{12,16},{16,20},{20,24},{24,28},{1,5},{5,9},{9,... | collective-permute-start | bytes 98312 | tf_op jit(solution)/shard_map/ppermute | solution.py:30
  188.5 0.8 collective-permute-done.9
  189.3 4.4 %maximum_convert_fusion.1 = f32[66,130,128]{2,1,0:T(8,128)S(1)} fusion(bf16[1,1,128]{2,1,0:T(2,128)(2,1)S(1)} %collective-permute-done.15, bf16[1,128,128]{2,1,0:T(8,128)(2,1)S(1)} %collective-permute-done.14, bf16[1,1,128]{2,1,0:T(2,128)(2,1)S(1)} %collective-permute-done.13, bf16[64,1,128]{2,1,0:T(2,128)(2,1)S(1)} %collective-permute-done.12, ...), kind=kLoop, calls=%fused_computation.25 | loop fusion | flops 19768320 | bytes 6589440 | tf_op jit(solution)/shard_map/convert_element_type | solution.py:132
  194.9 1.6 fusion.22
  198.4 6.9 %collective-permute-start.16 = (bf16[7,7,256]{2,1,0:T(8,128)(2,1)S(1)}, bf16[7,7,256]{2,1,0:T(8,128)(2,1)S(1)}, u32[]{:S(2)}, u32[]{:S(2)}) collective-permute-start(bf16[7,7,256]{2,1,0:T(8,128)(2,1)S(1)} %get-tuple-element.45), channel_id=1, source_target_pairs={{0,5},{1,6},{2,7},{4,9},{5,10},{6,11},{8,13},{9,14},{10,15},{12,17... | collective-permute-start | bytes 75272 | tf_op jit(solution)/shard_map/ppermute | solution.py:41
  205.3 1.3 collective-permute-start.18
  206.6 4.3 %collective-permute-start.21 = (bf16[7,7,256]{2,1,0:T(8,128)(2,1)S(1)}, bf16[7,7,256]{2,1,0:T(8,128)(2,1)S(1)}, u32[]{:S(2)}, u32[]{:S(2)}) collective-permute-start(bf16[7,7,256]{2,1,0:T(8,128)(2,1)S(1)} %get-tuple-element.47), channel_id=1, source_target_pairs={{4,1},{5,2},{6,3},{8,5},{9,6},{10,7},{12,9},{13,10},{14,11},{16,13... | collective-permute-start | bytes 75272 | tf_op jit(solution)/shard_map/ppermute | solution.py:41
  210.9 2.7 collective-permute-start.17
  213.7 1.9 collective-permute-start.22
  215.6 3.2 collective-permute-start.19
  218.8 1.3 collective-permute-start.20
  220.1 1.3 collective-permute-start.23
  221.5 7.0 %collective-permute-done.23 = bf16[7,7,256]{2,1,0:T(8,128)(2,1)S(1)} collective-permute-done((bf16[7,7,256]{2,1,0:T(8,128)(2,1)S(1)}, bf16[7,7,256]{2,1,0:T(8,128)(2,1)S(1)}, u32[]{:S(2)}, u32[]{:S(2)}) %collective-permute-start.23) | collective-permute-done | bytes 25120 | tf_op jit(solution)/shard_map/ppermute | solution.py:41
  228.6 2.3 maximum_convert_fusion.2.x_ref
  230.9 1.4 broadcast_in_dim.5.k_ref
  232.3 54.2 %shard_map.101 = f32[32,64,256]{2,1,0:T(8,128)} custom-call(f32[46,78,256]{2,1,0:T(8,128)} %maximum_convert_fusion.2.x_ref, f32[15,15,8,256]{3,2,1,0:T(8,128)} %broadcast_in_dim.5.k_ref), custom_call_target="tpu_custom_call" | custom-call | flops 235929600 | bytes 5771264 | tf_op jit(solution)/shard_map/pallas_call | solution.py:101
  286.5 2.1 reduce_sum.38
  289.4 5.4 %add_convert_fusion.1 = bf16[32,64,256]{2,1,0:T(8,128)(2,1)} fusion(bf16[32,64,256]{2,1,0:T(8,128)(2,1)} %copy-done.2, f32[32,64,256]{2,1,0:T(8,128)S(1)} %copy-done.1, f32[32,64]{1,0:T(8,128)S(1)} %add_rsqrt_fusion.1, f32[32,64]{1,0:T(8,128)S(1)} %broadcast_multiply_fusion.1, bf16[1024,256]{1,0:T(8,128)(2,1)S(1)} %copy-done, ...), kind=kOutput, calls=%fused_computation.33 | convolution fusion | flops 2169503744 | bytes 5259264 | tf_op jit(solution)/shard_map/dot_general | solution.py:125
  294.8 0.8 fusion.86
  295.5 1.0 fusion.87
  296.6 2.2 collective-permute-start.25
  298.8 3.6 %collective-permute-start.27 = (bf16[32,1,256]{2,1,0:T(2,128)(2,1)S(1)}, bf16[32,1,256]{2,1,0:T(2,128)(2,1)S(1)}, u32[]{:S(2)}, u32[]{:S(2)}) collective-permute-start(bf16[32,1,256]{2,1,0:T(2,128)(2,1)S(1)} %get-tuple-element.43), channel_id=1, source_target_pairs={{0,1},{1,2},{2,3},{4,5},{5,6},{6,7},{8,9},{9,10},{10,11},{12,13},{... | collective-permute-start | bytes 49160 | tf_op jit(solution)/shard_map/ppermute | solution.py:33
  302.4 1.3 collective-permute-start.28
  303.7 1.9 collective-permute-start.30
  306.3 6.3 %collective-permute-start.24 = (bf16[1,1,256]{2,1,0:T(2,128)(2,1)S(1)}, bf16[1,1,256]{2,1,0:T(2,128)(2,1)S(1)}, u32[]{:S(2)}, u32[]{:S(2)}) collective-permute-start(bf16[1,1,256]{2,1,0:T(2,128)(2,1)S(1)} %get-tuple-element.37), channel_id=1, source_target_pairs={{0,5},{1,6},{2,7},{4,9},{5,10},{6,11},{8,13},{9,14},{10,15},{12,17... | collective-permute-start | bytes 1544 | tf_op jit(solution)/shard_map/ppermute | solution.py:41
  312.7 0.7 collective-permute-done.24
  313.4 1.3 collective-permute-start.26
  314.7 3.6 %collective-permute-done.26 = bf16[1,1,256]{2,1,0:T(2,128)(2,1)S(1)} collective-permute-done((bf16[1,1,256]{2,1,0:T(2,128)(2,1)S(1)}, bf16[1,1,256]{2,1,0:T(2,128)(2,1)S(1)}, u32[]{:S(2)}, u32[]{:S(2)}) %collective-permute-start.26) | collective-permute-done | bytes 544 | tf_op jit(solution)/shard_map/ppermute | solution.py:41
  318.3 3.2 collective-permute-start.29
  321.4 0.7 collective-permute-done.29
  322.2 1.3 collective-permute-start.31
  323.4 8.7 %collective-permute-done.31 = bf16[1,1,256]{2,1,0:T(2,128)(2,1)S(1)} collective-permute-done((bf16[1,1,256]{2,1,0:T(2,128)(2,1)S(1)}, bf16[1,1,256]{2,1,0:T(2,128)(2,1)S(1)}, u32[]{:S(2)}, u32[]{:S(2)}) %collective-permute-start.31) | collective-permute-done | bytes 544 | tf_op jit(solution)/shard_map/ppermute | solution.py:41
  332.2 1.8 maximum_convert_fusion.3
  334.7 1.4 fusion.32
  336.7 0.8 copy.20
  (69 shorter events, 7.5 us)
Async XLA Ops:
  0.0 289.4 %copy-start = (bf16[1024,256]{1,0:T(8,128)(2,1)S(1)}, bf16[1024,256]{1,0:T(8,128)(2,1)}, u32[]{:S(2)}) copy-start(bf16[1024,256]{1,0:T(8,128)(2,1)} %param.19) | copy-start | bytes 1572868
  0.8 18.3 %collective-permute-start = (bf16[7,7,128]{2,1,0:T(8,128)(2,1)S(1)}, bf16[7,7,128]{2,1,0:T(8,128)(2,1)S(1)}, u32[]{:S(2)}, u32[]{:S(2)}) collective-permute-start(bf16[7,7,128]{2,1,0:T(8,128)(2,1)S(1)} %get-tuple-element.27), channel_id=1, source_target_pairs={{0,5},{1,6},{2,7},{4,9},{5,10},{6,11},{8,13},{9,14},{10,15},{12,17... | collective-permute-start | bytes 37640 | tf_op jit(solution)/shard_map/ppermute | solution.py:41
  5.5 15.5 %collective-permute-start.2 = (bf16[7,7,128]{2,1,0:T(8,128)(2,1)S(1)}, bf16[7,7,128]{2,1,0:T(8,128)(2,1)S(1)}, u32[]{:S(2)}, u32[]{:S(2)}) collective-permute-start(bf16[7,7,128]{2,1,0:T(8,128)(2,1)S(1)} %get-tuple-element.29), channel_id=1, source_target_pairs={{1,4},{2,5},{3,6},{5,8},{6,9},{7,10},{9,12},{10,13},{11,14},{13,16... | collective-permute-start | bytes 37640 | tf_op jit(solution)/shard_map/ppermute | solution.py:41
  6.8 18.6 %collective-permute-start.5 = (bf16[7,7,128]{2,1,0:T(8,128)(2,1)S(1)}, bf16[7,7,128]{2,1,0:T(8,128)(2,1)S(1)}, u32[]{:S(2)}, u32[]{:S(2)}) collective-permute-start(bf16[7,7,128]{2,1,0:T(8,128)(2,1)S(1)} %get-tuple-element.28), channel_id=1, source_target_pairs={{4,1},{5,2},{6,3},{8,5},{9,6},{10,7},{12,9},{13,10},{14,11},{16,13... | collective-permute-start | bytes 37640 | tf_op jit(solution)/shard_map/ppermute | solution.py:41
  11.1 16.7 %collective-permute-start.7 = (bf16[7,7,128]{2,1,0:T(8,128)(2,1)S(1)}, bf16[7,7,128]{2,1,0:T(8,128)(2,1)S(1)}, u32[]{:S(2)}, u32[]{:S(2)}) collective-permute-start(bf16[7,7,128]{2,1,0:T(8,128)(2,1)S(1)} %get-tuple-element.30), channel_id=1, source_target_pairs={{5,0},{6,1},{7,2},{9,4},{10,5},{11,6},{13,8},{14,9},{15,10},{17,12... | collective-permute-start | bytes 37640 | tf_op jit(solution)/shard_map/ppermute | solution.py:41
  13.5 19.0 %collective-permute-start.1 = (bf16[7,128,128]{2,1,0:T(8,128)(2,1)S(1)}, bf16[7,128,128]{2,1,0:T(8,128)(2,1)S(1)}, u32[]{:S(2)}, u32[]{:S(2)}) collective-permute-start(bf16[7,128,128]{2,1,0:T(8,128)(2,1)S(1)} %get-tuple-element.31), channel_id=1, source_target_pairs={{0,4},{4,8},{8,12},{12,16},{16,20},{20,24},{24,28},{1,5},{5,9},{9,... | collective-permute-start | bytes 688136 | tf_op jit(solution)/shard_map/ppermute | solution.py:30
  19.1 13.4 %collective-permute-start.6 = (bf16[7,128,128]{2,1,0:T(8,128)(2,1)S(1)}, bf16[7,128,128]{2,1,0:T(8,128)(2,1)S(1)}, u32[]{:S(2)}, u32[]{:S(2)}) collective-permute-start(bf16[7,128,128]{2,1,0:T(8,128)(2,1)S(1)} %get-tuple-element.32), channel_id=1, source_target_pairs={{4,0},{8,4},{12,8},{16,12},{20,16},{24,20},{28,24},{5,1},{9,5},{13... | collective-permute-start | bytes 688136 | tf_op jit(solution)/shard_map/ppermute | solution.py:30
  21.0 7.5 %collective-permute-start.3 = (bf16[64,7,128]{2,1,0:T(8,128)(2,1)S(1)}, bf16[64,7,128]{2,1,0:T(8,128)(2,1)S(1)}, u32[]{:S(2)}, u32[]{:S(2)}) collective-permute-start(bf16[64,7,128]{2,1,0:T(8,128)(2,1)S(1)} %get-tuple-element.33), channel_id=1, source_target_pairs={{0,1},{1,2},{2,3},{4,5},{5,6},{6,7},{8,9},{9,10},{10,11},{12,13},{... | collective-permute-start | bytes 344072 | tf_op jit(solution)/shard_map/ppermute | solution.py:33
  25.5 7.0 %collective-permute-start.4 = (bf16[64,7,128]{2,1,0:T(8,128)(2,1)S(1)}, bf16[64,7,128]{2,1,0:T(8,128)(2,1)S(1)}, u32[]{:S(2)}, u32[]{:S(2)}) collective-permute-start(bf16[64,7,128]{2,1,0:T(8,128)(2,1)S(1)} %get-tuple-element.34), channel_id=1, source_target_pairs={{1,0},{2,1},{3,2},{5,4},{6,5},{7,6},{9,8},{10,9},{11,10},{13,12},{... | collective-permute-start | bytes 344072 | tf_op jit(solution)/shard_map/ppermute | solution.py:33
  146.0 4.2 %copy-start.3 = (bf16[64,128,128]{2,1,0:T(8,128)(2,1)S(1)}, bf16[64,128,128]{2,1,0:T(8,128)(2,1)}, u32[]{:S(2)}) copy-start(bf16[64,128,128]{2,1,0:T(8,128)(2,1)} %param.10) | copy-start | bytes 6291460
  146.0 4.2 %copy-start.8 = (bf16[512,128]{1,0:T(8,128)(2,1)S(1)}, bf16[512,128]{1,0:T(8,128)(2,1)}, u32[]{:S(2)}) copy-start(bf16[512,128]{1,0:T(8,128)(2,1)} %param.14) | copy-start | bytes 393220
  146.0 4.2 %copy-start.9 = (bf16[128,512]{1,0:T(8,128)(2,1)S(1)}, bf16[128,512]{1,0:T(8,128)(2,1)}, u32[]{:S(2)}) copy-start(bf16[128,512]{1,0:T(8,128)(2,1)} %param.13) | copy-start | bytes 393220
  150.2 38.2 %copy-start.6 = (f32[256]{0:T(256)S(1)}, f32[256]{0:T(256)}, u32[]{:S(2)}) copy-start(f32[256]{0:T(256)} %param.17) | copy-start | bytes 3076
  162.2 18.2 %collective-permute-start.10 = (bf16[1,1,128]{2,1,0:T(2,128)(2,1)S(1)}, bf16[1,1,128]{2,1,0:T(2,128)(2,1)S(1)}, u32[]{:S(2)}, u32[]{:S(2)}) collective-permute-start(bf16[1,1,128]{2,1,0:T(2,128)(2,1)S(1)} %get-tuple-element.22), channel_id=1, source_target_pairs={{1,4},{2,5},{3,6},{5,8},{6,9},{7,10},{9,12},{10,13},{11,14},{13,16... | collective-permute-start | bytes 776 | tf_op jit(solution)/shard_map/ppermute | solution.py:41
  163.5 18.2 %collective-permute-start.13 = (bf16[1,1,128]{2,1,0:T(2,128)(2,1)S(1)}, bf16[1,1,128]{2,1,0:T(2,128)(2,1)S(1)}, u32[]{:S(2)}, u32[]{:S(2)}) collective-permute-start(bf16[1,1,128]{2,1,0:T(2,128)(2,1)S(1)} %get-tuple-element.21), channel_id=1, source_target_pairs={{4,1},{5,2},{6,3},{8,5},{9,6},{10,7},{12,9},{13,10},{14,11},{16,13... | collective-permute-start | bytes 776 | tf_op jit(solution)/shard_map/ppermute | solution.py:41
  168.1 15.6 %collective-permute-start.15 = (bf16[1,1,128]{2,1,0:T(2,128)(2,1)S(1)}, bf16[1,1,128]{2,1,0:T(2,128)(2,1)S(1)}, u32[]{:S(2)}, u32[]{:S(2)}) collective-permute-start(bf16[1,1,128]{2,1,0:T(2,128)(2,1)S(1)} %get-tuple-element.20), channel_id=1, source_target_pairs={{5,0},{6,1},{7,2},{9,4},{10,5},{11,6},{13,8},{14,9},{15,10},{17,12... | collective-permute-start | bytes 776 | tf_op jit(solution)/shard_map/ppermute | solution.py:41
  169.4 19.1 %collective-permute-start.8 = (bf16[1,1,128]{2,1,0:T(2,128)(2,1)S(1)}, bf16[1,1,128]{2,1,0:T(2,128)(2,1)S(1)}, u32[]{:S(2)}, u32[]{:S(2)}) collective-permute-start(bf16[1,1,128]{2,1,0:T(2,128)(2,1)S(1)} %get-tuple-element.19), channel_id=1, source_target_pairs={{0,5},{1,6},{2,7},{4,9},{5,10},{6,11},{8,13},{9,14},{10,15},{12,17... | collective-permute-start | bytes 776 | tf_op jit(solution)/shard_map/ppermute | solution.py:41
  177.2 11.2 %collective-permute-start.11 = (bf16[64,1,128]{2,1,0:T(2,128)(2,1)S(1)}, bf16[64,1,128]{2,1,0:T(2,128)(2,1)S(1)}, u32[]{:S(2)}, u32[]{:S(2)}) collective-permute-start(bf16[64,1,128]{2,1,0:T(2,128)(2,1)S(1)} %get-tuple-element.25), channel_id=1, source_target_pairs={{0,1},{1,2},{2,3},{4,5},{5,6},{6,7},{8,9},{9,10},{10,11},{12,13},{... | collective-permute-start | bytes 49160 | tf_op jit(solution)/shard_map/ppermute | solution.py:33
  180.4 8.0 %collective-permute-start.12 = (bf16[64,1,128]{2,1,0:T(2,128)(2,1)S(1)}, bf16[64,1,128]{2,1,0:T(2,128)(2,1)S(1)}, u32[]{:S(2)}, u32[]{:S(2)}) collective-permute-start(bf16[64,1,128]{2,1,0:T(2,128)(2,1)S(1)} %get-tuple-element.26), channel_id=1, source_target_pairs={{1,0},{2,1},{3,2},{5,4},{6,5},{7,6},{9,8},{10,9},{11,10},{13,12},{... | collective-permute-start | bytes 49160 | tf_op jit(solution)/shard_map/ppermute | solution.py:33
  181.8 6.7 %collective-permute-start.14 = (bf16[1,128,128]{2,1,0:T(8,128)(2,1)S(1)}, bf16[1,128,128]{2,1,0:T(8,128)(2,1)S(1)}, u32[]{:S(2)}, u32[]{:S(2)}) collective-permute-start(bf16[1,128,128]{2,1,0:T(8,128)(2,1)S(1)} %get-tuple-element.24), channel_id=1, source_target_pairs={{4,0},{8,4},{12,8},{16,12},{20,16},{24,20},{28,24},{5,1},{9,5},{13... | collective-permute-start | bytes 98312 | tf_op jit(solution)/shard_map/ppermute | solution.py:30
  183.7 5.6 %collective-permute-start.9 = (bf16[1,128,128]{2,1,0:T(8,128)(2,1)S(1)}, bf16[1,128,128]{2,1,0:T(8,128)(2,1)S(1)}, u32[]{:S(2)}, u32[]{:S(2)}) collective-permute-start(bf16[1,128,128]{2,1,0:T(8,128)(2,1)S(1)} %get-tuple-element.23), channel_id=1, source_target_pairs={{0,4},{4,8},{8,12},{12,16},{16,20},{20,24},{24,28},{1,5},{5,9},{9,... | collective-permute-start | bytes 98312 | tf_op jit(solution)/shard_map/ppermute | solution.py:30
  197.0 0.8 copy-start.5
  197.9 23.6 %copy-start.4 = (f32[15,15,256]{2,1,0:T(8,128)S(1)}, f32[15,15,256]{2,1,0:T(8,128)}, u32[]{:S(2)}) copy-start(f32[15,15,256]{2,1,0:T(8,128)} %param.16) | copy-start | bytes 691204
  198.3 32.6 %copy-start.2 = (bf16[32,64,256]{2,1,0:T(8,128)(2,1)}, bf16[32,64,256]{2,1,0:T(8,128)(2,1)S(1)}, u32[]{:S(2)}) copy-start(bf16[32,64,256]{2,1,0:T(8,128)(2,1)S(1)} %convolution_convert_fusion) | copy-start | bytes 3145732
  198.4 17.2 %collective-permute-start.16 = (bf16[7,7,256]{2,1,0:T(8,128)(2,1)S(1)}, bf16[7,7,256]{2,1,0:T(8,128)(2,1)S(1)}, u32[]{:S(2)}, u32[]{:S(2)}) collective-permute-start(bf16[7,7,256]{2,1,0:T(8,128)(2,1)S(1)} %get-tuple-element.45), channel_id=1, source_target_pairs={{0,5},{1,6},{2,7},{4,9},{5,10},{6,11},{8,13},{9,14},{10,15},{12,17... | collective-permute-start | bytes 75272 | tf_op jit(solution)/shard_map/ppermute | solution.py:41
  205.3 13.5 %collective-permute-start.18 = (bf16[7,7,256]{2,1,0:T(8,128)(2,1)S(1)}, bf16[7,7,256]{2,1,0:T(8,128)(2,1)S(1)}, u32[]{:S(2)}, u32[]{:S(2)}) collective-permute-start(bf16[7,7,256]{2,1,0:T(8,128)(2,1)S(1)} %get-tuple-element.48), channel_id=1, source_target_pairs={{1,4},{2,5},{3,6},{5,8},{6,9},{7,10},{9,12},{10,13},{11,14},{13,16... | collective-permute-start | bytes 75272 | tf_op jit(solution)/shard_map/ppermute | solution.py:41
  206.6 13.5 %collective-permute-start.21 = (bf16[7,7,256]{2,1,0:T(8,128)(2,1)S(1)}, bf16[7,7,256]{2,1,0:T(8,128)(2,1)S(1)}, u32[]{:S(2)}, u32[]{:S(2)}) collective-permute-start(bf16[7,7,256]{2,1,0:T(8,128)(2,1)S(1)} %get-tuple-element.47), channel_id=1, source_target_pairs={{4,1},{5,2},{6,3},{8,5},{9,6},{10,7},{12,9},{13,10},{14,11},{16,13... | collective-permute-start | bytes 75272 | tf_op jit(solution)/shard_map/ppermute | solution.py:41
  210.9 17.7 %collective-permute-start.17 = (bf16[7,64,256]{2,1,0:T(8,128)(2,1)S(1)}, bf16[7,64,256]{2,1,0:T(8,128)(2,1)S(1)}, u32[]{:S(2)}, u32[]{:S(2)}) collective-permute-start(bf16[7,64,256]{2,1,0:T(8,128)(2,1)S(1)} %get-tuple-element.49), channel_id=1, source_target_pairs={{0,4},{4,8},{8,12},{12,16},{16,20},{20,24},{24,28},{1,5},{5,9},{9,... | collective-permute-start | bytes 688136 | tf_op jit(solution)/shard_map/ppermute | solution.py:30
  213.7 14.9 %collective-permute-start.22 = (bf16[7,64,256]{2,1,0:T(8,128)(2,1)S(1)}, bf16[7,64,256]{2,1,0:T(8,128)(2,1)S(1)}, u32[]{:S(2)}, u32[]{:S(2)}) collective-permute-start(bf16[7,64,256]{2,1,0:T(8,128)(2,1)S(1)} %get-tuple-element.50), channel_id=1, source_target_pairs={{4,0},{8,4},{12,8},{16,12},{20,16},{24,20},{28,24},{5,1},{9,5},{13... | collective-permute-start | bytes 688136 | tf_op jit(solution)/shard_map/ppermute | solution.py:30
  215.6 13.0 %collective-permute-start.19 = (bf16[32,7,256]{2,1,0:T(8,128)(2,1)S(1)}, bf16[32,7,256]{2,1,0:T(8,128)(2,1)S(1)}, u32[]{:S(2)}, u32[]{:S(2)}) collective-permute-start(bf16[32,7,256]{2,1,0:T(8,128)(2,1)S(1)} %get-tuple-element.51), channel_id=1, source_target_pairs={{0,1},{1,2},{2,3},{4,5},{5,6},{6,7},{8,9},{9,10},{10,11},{12,13},{... | collective-permute-start | bytes 344072 | tf_op jit(solution)/shard_map/ppermute | solution.py:33
  218.8 9.8 %collective-permute-start.20 = (bf16[32,7,256]{2,1,0:T(8,128)(2,1)S(1)}, bf16[32,7,256]{2,1,0:T(8,128)(2,1)S(1)}, u32[]{:S(2)}, u32[]{:S(2)}) collective-permute-start(bf16[32,7,256]{2,1,0:T(8,128)(2,1)S(1)} %get-tuple-element.52), channel_id=1, source_target_pairs={{1,0},{2,1},{3,2},{5,4},{6,5},{7,6},{9,8},{10,9},{11,10},{13,12},{... | collective-permute-start | bytes 344072 | tf_op jit(solution)/shard_map/ppermute | solution.py:33
  220.1 8.4 %collective-permute-start.23 = (bf16[7,7,256]{2,1,0:T(8,128)(2,1)S(1)}, bf16[7,7,256]{2,1,0:T(8,128)(2,1)S(1)}, u32[]{:S(2)}, u32[]{:S(2)}) collective-permute-start(bf16[7,7,256]{2,1,0:T(8,128)(2,1)S(1)} %get-tuple-element.46), channel_id=1, source_target_pairs={{5,0},{6,1},{7,2},{9,4},{10,5},{11,6},{13,8},{14,9},{15,10},{17,12... | collective-permute-start | bytes 75272 | tf_op jit(solution)/shard_map/ppermute | solution.py:41
  286.5 2.2 copy-start.1
  286.5 2.9 copy-start.7
  296.6 35.6 %collective-permute-start.25 = (bf16[1,64,256]{2,1,0:T(8,128)(2,1)S(1)}, bf16[1,64,256]{2,1,0:T(8,128)(2,1)S(1)}, u32[]{:S(2)}, u32[]{:S(2)}) collective-permute-start(bf16[1,64,256]{2,1,0:T(8,128)(2,1)S(1)} %get-tuple-element.41), channel_id=1, source_target_pairs={{0,4},{4,8},{8,12},{12,16},{16,20},{20,24},{24,28},{1,5},{5,9},{9,... | collective-permute-start | bytes 98312 | tf_op jit(solution)/shard_map/ppermute | solution.py:30
  298.8 33.4 %collective-permute-start.27 = (bf16[32,1,256]{2,1,0:T(2,128)(2,1)S(1)}, bf16[32,1,256]{2,1,0:T(2,128)(2,1)S(1)}, u32[]{:S(2)}, u32[]{:S(2)}) collective-permute-start(bf16[32,1,256]{2,1,0:T(2,128)(2,1)S(1)} %get-tuple-element.43), channel_id=1, source_target_pairs={{0,1},{1,2},{2,3},{4,5},{5,6},{6,7},{8,9},{9,10},{10,11},{12,13},{... | collective-permute-start | bytes 49160 | tf_op jit(solution)/shard_map/ppermute | solution.py:33
  302.4 29.7 %collective-permute-start.28 = (bf16[32,1,256]{2,1,0:T(2,128)(2,1)S(1)}, bf16[32,1,256]{2,1,0:T(2,128)(2,1)S(1)}, u32[]{:S(2)}, u32[]{:S(2)}) collective-permute-start(bf16[32,1,256]{2,1,0:T(2,128)(2,1)S(1)} %get-tuple-element.44), channel_id=1, source_target_pairs={{1,0},{2,1},{3,2},{5,4},{6,5},{7,6},{9,8},{10,9},{11,10},{13,12},{... | collective-permute-start | bytes 49160 | tf_op jit(solution)/shard_map/ppermute | solution.py:33
  303.7 28.5 %collective-permute-start.30 = (bf16[1,64,256]{2,1,0:T(8,128)(2,1)S(1)}, bf16[1,64,256]{2,1,0:T(8,128)(2,1)S(1)}, u32[]{:S(2)}, u32[]{:S(2)}) collective-permute-start(bf16[1,64,256]{2,1,0:T(8,128)(2,1)S(1)} %get-tuple-element.42), channel_id=1, source_target_pairs={{4,0},{8,4},{12,8},{16,12},{20,16},{24,20},{28,24},{5,1},{9,5},{13... | collective-permute-start | bytes 98312 | tf_op jit(solution)/shard_map/ppermute | solution.py:30
  306.3 7.0 %collective-permute-start.24 = (bf16[1,1,256]{2,1,0:T(2,128)(2,1)S(1)}, bf16[1,1,256]{2,1,0:T(2,128)(2,1)S(1)}, u32[]{:S(2)}, u32[]{:S(2)}) collective-permute-start(bf16[1,1,256]{2,1,0:T(2,128)(2,1)S(1)} %get-tuple-element.37), channel_id=1, source_target_pairs={{0,5},{1,6},{2,7},{4,9},{5,10},{6,11},{8,13},{9,14},{10,15},{12,17... | collective-permute-start | bytes 1544 | tf_op jit(solution)/shard_map/ppermute | solution.py:41
  313.4 4.9 %collective-permute-start.26 = (bf16[1,1,256]{2,1,0:T(2,128)(2,1)S(1)}, bf16[1,1,256]{2,1,0:T(2,128)(2,1)S(1)}, u32[]{:S(2)}, u32[]{:S(2)}) collective-permute-start(bf16[1,1,256]{2,1,0:T(2,128)(2,1)S(1)} %get-tuple-element.40), channel_id=1, source_target_pairs={{1,4},{2,5},{3,6},{5,8},{6,9},{7,10},{9,12},{10,13},{11,14},{13,16... | collective-permute-start | bytes 1544 | tf_op jit(solution)/shard_map/ppermute | solution.py:41
  318.3 3.9 %collective-permute-start.29 = (bf16[1,1,256]{2,1,0:T(2,128)(2,1)S(1)}, bf16[1,1,256]{2,1,0:T(2,128)(2,1)S(1)}, u32[]{:S(2)}, u32[]{:S(2)}) collective-permute-start(bf16[1,1,256]{2,1,0:T(2,128)(2,1)S(1)} %get-tuple-element.39), channel_id=1, source_target_pairs={{4,1},{5,2},{6,3},{8,5},{9,6},{10,7},{12,9},{13,10},{14,11},{16,13... | collective-permute-start | bytes 1544 | tf_op jit(solution)/shard_map/ppermute | solution.py:41
  322.2 10.0 %collective-permute-start.31 = (bf16[1,1,256]{2,1,0:T(2,128)(2,1)S(1)}, bf16[1,1,256]{2,1,0:T(2,128)(2,1)S(1)}, u32[]{:S(2)}, u32[]{:S(2)}) collective-permute-start(bf16[1,1,256]{2,1,0:T(2,128)(2,1)S(1)} %get-tuple-element.38), channel_id=1, source_target_pairs={{5,0},{6,1},{7,2},{9,4},{10,5},{11,6},{13,8},{14,9},{15,10},{17,12... | collective-permute-start | bytes 1544 | tf_op jit(solution)/shard_map/ppermute | solution.py:41

commit v5 on v2

--- a/solution.py
+++ b/solution.py
@@ -130,13 +130,25 @@
     reach = 7
     extended = padded_2(image, (("row", 0), ("col", 1)), reach)
     first = local_section(extended, raw_first, sigma_first, in_first, out_first)
-    first_cycle = padded_2(first, (("row", 0), ("col", 1)), 1)
-    first_pooled = blur_down(first_cycle)
-    widened = jnp.dot(first_pooled, widen, preferred_element_type=jnp.float32).astype(jnp.bfloat16)
-    widened_ext = padded_2(widened, (("row", 0), ("col", 1)), reach)
+    first_cycle = padded_2(first, (("row", 0), ("col", 1)), 2 * reach + 1)
+    first_pooled = zero_outside(blur_down(first_cycle), reach)
+    widened_ext = jnp.dot(first_pooled, widen, preferred_element_type=jnp.float32).astype(
+        jnp.bfloat16
+    )
     second = local_section(widened_ext, raw_second, sigma_second, in_second, out_second)
     second_cycle = padded_2(second, (("row", 0), ("col", 1)), 1)
     return blur_down(second_cycle)
+
+
+def zero_outside(block, width):
+    keep = None
+    for axis, dim in (("row", 0), ("col", 1)):
+        index = lax.axis_index(axis)
+        last = lax.axis_size(axis) - 1
+        pos = lax.broadcasted_iota(jnp.int32, block.shape[:2], dim)
+        ok = ((pos >= width) | (index != 0)) & ((pos < block.shape[dim] - width) | (index != last))
+        keep = ok if keep is None else keep & ok
+    return jnp.where(keep[:, :, None], block, jnp.zeros_like(block))
 
 
 def solution(mesh):

time: 279 us -> 318 us (1.14)
  local copies, waits for them, and re-layouts: 10.5 us -> 32.9 us
  other arithmetic: 24.6 us -> 45.3 us
  starting transfers between devices: 38.1 us -> 30.5 us
    div x2, other arithmetic: 2.95 us -> 15.4 us  [blur_down(): (upper[:, 0] + 3.0 * upper[:, 1] + 3.0 * lower[:, 0] + lower[:, 1]) / 8.0]
    ppermute x8 -> x6, waiting for transfers between devices: 30.4 us -> 18.7 us  [padded_2(): lax.ppermute(lax.slice_in_dim(block, 0, width, axis=dim), axis, backward)]
    slice x2, local copies, waits for them, and re-layouts: 0.97 us -> 12.3 us  [blur_down(): upper = padded[0:rows].reshape(rows // 2, 2, cols + 2, -1)]
    slice x2, local copies, waits for them, and re-layouts: 0.77 us -> 11.1 us  [blur_down(): upper[:, 0] + 3.0 * upper[:, 1] + 3.0 * lower[:, 0] + lower[:, 1]]
    ppermute x8 -> x6, waiting for transfers between devices: 4.72 us -> 14.6 us  [padded_2(): lax.ppermute(lax.slice_in_dim(block, block.shape[dim] - width, None, axis...]
    convert_element_type x2, other arithmetic: 2.6 us -> 9.16 us  [blur_down(): padded = padded.astype(jnp.float32)]
    ppermute x8 -> x6, starting transfers between devices: 25 us -> 19.1 us  [padded_2(): lax.ppermute(lax.slice_in_dim(block, block.shape[dim] - width, None, axis...]
    ppermute x8 -> x6, starting transfers between devices: 13 us -> 11.3 us  [padded_2(): lax.ppermute(lax.slice_in_dim(block, 0, width, axis=dim), axis, backward)]
  transfers between devices with their start and end apart: 16 -> 12, of which waited for: 12 -> 10; matrix products, arithmetic and copies ran while one was open for 1% -> 1% of each run, Pallas kernels for 0% -> 0%
where the time goes in v5:
time: 318 us; the launch traced here: 314 us
  Pallas kernels  155 us (49%)
  other arithmetic  45.3 us (14%)
  waiting for transfers between devices  33.3 us (10%)
  local copies, waits for them, and re-layouts  32.9 us (10%)
  starting transfers between devices  30.5 us (10%)
  matrix products  17.3 us (5%)
    pallas_call x2, Pallas kernels, depthwise(): pl.pallas_call(body, out_shape=jax.ShapeDtypeStruct((rows, cols, chans),...  155 us
    ppermute x6, starting transfers between devices, padded_2(): lax.ppermute(lax.slice_in_dim(block, block.shape[dim] - width, None, axis...  19.1 us
    ppermute x6, waiting for transfers between devices, padded_2(): lax.ppermute(lax.slice_in_dim(block, 0, width, axis=dim), axis, backward)  18.7 us
    div x2, other arithmetic, blur_down(): (upper[:, 0] + 3.0 * upper[:, 1] + 3.0 * lower[:, 0] + lower[:, 1]) / 8.0  15.4 us
    ppermute x6, waiting for transfers between devices, padded_2(): lax.ppermute(lax.slice_in_dim(block, block.shape[dim] - width, None, axis...  14.6 us
    dot_general x2, matrix products, local_section(): mixed = jnp.dot(hidden, w_out, preferred_element_type=jnp.float32)  14.3 us
    slice x2, local copies, waits for them, and re-layouts, blur_down(): upper = padded[0:rows].reshape(rows // 2, 2, cols + 2, -1)  12.3 us
    ppermute x6, starting transfers between devices, padded_2(): lax.ppermute(lax.slice_in_dim(block, 0, width, axis=dim), axis, backward)  11.3 us
  transfers between devices with their start and end apart: 12, of which 10 were waited for; matrix products, arithmetic and copies ran while one was open for 1% of the time, Pallas kernels for 0%

profile of v5, /device:TPU:3, one launch (start us, length us, event | category | flops | bytes accessed | tf_op | source)
XLA Modules:
  0.0 314.4 jit_solution(14218761693319614971)
XLA Ops:
  0.0 1.1 fusion.79
  1.2 3.7 %collective-permute-start = (bf16[7,128,128]{2,1,0:T(8,128)(2,1)S(1)}, bf16[7,128,128]{2,1,0:T(8,128)(2,1)S(1)}, u32[]{:S(2)}, u32[]{:S(2)}) collective-permute-start(bf16[7,128,128]{2,1,0:T(8,128)(2,1)S(1)} %get-tuple-element.26), channel_id=1, source_target_pairs={{0,4},{4,8},{8,12},{12,16},{16,20},{20,24},{24,28},{1,5},{5,9},{9,... | collective-permute-start | bytes 688136 | tf_op jit(solution)/shard_map/ppermute | solution.py:16
  4.8 1.9 collective-permute-start.1
  6.8 0.7 multiply_multiply_fusion.3
  7.4 0.1 add_negate_fusion
  7.5 0.3 collective-permute-done
  7.8 2.0 constant_dynamic-update-slice_fusion.1
  9.8 3.3 %collective-permute-done.1 = bf16[7,128,128]{2,1,0:T(8,128)(2,1)S(1)} collective-permute-done((bf16[7,128,128]{2,1,0:T(8,128)(2,1)S(1)}, bf16[7,128,128]{2,1,0:T(8,128)(2,1)S(1)}, u32[]{:S(2)}, u32[]{:S(2)}) %collective-permute-start.1) | collective-permute-done | bytes 229408 | tf_op jit(solution)/shard_map/ppermute | solution.py:19
  13.1 0.1 fusion.74
  13.2 3.2 %collective-permute-start.2 = (bf16[78,7,128]{2,1,0:T(8,128)(2,1)S(1)}, bf16[78,7,128]{2,1,0:T(8,128)(2,1)S(1)}, u32[]{:S(2)}, u32[]{:S(2)}) collective-permute-start(bf16[78,7,128]{2,1,0:T(8,128)(2,1)S(1)} %get-tuple-element.15), channel_id=1, source_target_pairs={{0,1},{1,2},{2,3},{4,5},{5,6},{6,7},{8,9},{9,10},{10,11},{12,13},{... | collective-permute-start | bytes 419336 | tf_op jit(solution)/shard_map/ppermute | solution.py:16
  16.4 1.3 collective-permute-start.3
  17.7 0.1 fusion.61
  17.8 1.0 collective-permute-done.2
  18.9 4.1 %collective-permute-done.3 = bf16[78,7,128]{2,1,0:T(8,128)(2,1)S(1)} collective-permute-done((bf16[78,7,128]{2,1,0:T(8,128)(2,1)S(1)}, bf16[78,7,128]{2,1,0:T(8,128)(2,1)S(1)}, u32[]{:S(2)}, u32[]{:S(2)}) %collective-permute-start.3) | collective-permute-done | bytes 139808 | tf_op jit(solution)/shard_map/ppermute | solution.py:19
  23.0 3.6 %maximum_convert_fusion.1.x_ref = f32[78,142,128]{2,1,0:T(8,128)} fusion(bf16[78,7,128]{2,1,0:T(8,128)(2,1)S(1)} %collective-permute-done.3, bf16[78,128,128]{2,1,0:T(8,128)(2,1)S(1)} %constant_dynamic-update-slice_fusion, bf16[78,7,128]{2,1,0:T(8,128)(2,1)S(1)} %collective-permute-done.2), kind=kLoop, calls=%fused_computation.31 | loop fusion | flops 8506368 | bytes 8506368 | tf_op jit(solution)/shard_map/convert_element_type | solution.py:87
  26.6 1.0 broadcast_in_dim.12.k_ref
  27.6 100.6 %shard_map.100 = f32[64,128,128]{2,1,0:T(8,128)} custom-call(f32[78,142,128]{2,1,0:T(8,128)} %maximum_convert_fusion.1.x_ref, f32[15,15,8,128]{3,2,1,0:T(8,128)} %broadcast_in_dim.12.k_ref), custom_call_target="tpu_custom_call" | custom-call | flops 471859200 | bytes 9865216 | tf_op jit(solution)/shard_map/pallas_call | solution.py:76
  128.1 3.4 %reduce_sum.36 = f32[64,128]{1,0:T(8,128)S(1)} reduce(f32[64,128,128]{2,1,0:T(8,128)} %shard_map.100, f32[]{:T(128)} %constant.31.clone.1), dimensions={2}, to_apply=%region_0.0 | reduce | flops 1040384 | bytes 4227076 | tf_op jit(solution)/shard_map/reduce_sum | solution.py:94
  131.5 3.9 %multiply_reduce_fusion = f32[64,128]{1,0:T(8,128)S(1)} fusion(f32[64,128,128]{2,1,0:T(8,128)} %shard_map.100, f32[64,128]{1,0:T(8,128)S(1)} %broadcast_multiply_fusion), kind=kLoop, calls=%fused_computation.20 | loop fusion | flops 3137536 | bytes 4259840 | tf_op jit(solution)/shard_map/reduce_sum | solution.py:95
  135.5 8.8 %add_convert_fusion = bf16[64,128,128]{2,1,0:T(8,128)(2,1)S(1)} fusion(bf16[64,128,128]{2,1,0:T(8,128)(2,1)} %param.10, f32[64,128,128]{2,1,0:T(8,128)} %shard_map.100, f32[64,128]{1,0:T(8,128)S(1)} %add_rsqrt_fusion, f32[64,128]{1,0:T(8,128)S(1)} %broadcast_multiply_fusion, bf16[512,128]{1,0:T(8,128)(2,1)S(1)} %copy-done.6, bf16[128,512]{1,0:T(8,128)(2,1)S(1)} %copy-done.7), kind=kOutput, calls=%fused_computation.18 | convolution fusion | flops 2191523840 | bytes 8716288 | tf_op jit(solution)/shard_map/dot_general | solution.py:100
  144.4 0.0 copy-start.4
  144.4 1.0 fusion.78
  145.4 3.9 %collective-permute-start.4 = (bf16[15,128,128]{2,1,0:T(8,128)(2,1)}, bf16[15,128,128]{2,1,0:T(8,128)(2,1)S(1)}, u32[]{:S(2)}, u32[]{:S(2)}) collective-permute-start(bf16[15,128,128]{2,1,0:T(8,128)(2,1)} %get-tuple-element.23), channel_id=1, source_target_pairs={{0,4},{4,8},{8,12},{12,16},{16,20},{20,24},{24,28},{1,5},{5,9},{9,... | collective-permute-start | bytes 1474568 | tf_op jit(solution)/shard_map/ppermute | solution.py:16
  149.4 1.9 collective-permute-start.5
  151.3 0.1 broadcast_and_fusion
  151.4 7.9 %collective-permute-done.4 = bf16[15,128,128]{2,1,0:T(8,128)(2,1)S(1)} collective-permute-done((bf16[15,128,128]{2,1,0:T(8,128)(2,1)}, bf16[15,128,128]{2,1,0:T(8,128)(2,1)S(1)}, u32[]{:S(2)}, u32[]{:S(2)}) %collective-permute-start.4) | collective-permute-done | bytes 491552 | tf_op jit(solution)/shard_map/ppermute | solution.py:16
  159.3 1.4 collective-permute-done.5
  160.7 1.0 pad_maximum_fusion.2
  161.8 3.2 %collective-permute-start.6 = (bf16[94,15,128]{2,1,0:T(8,128)(2,1)S(1)}, bf16[94,15,128]{2,1,0:T(8,128)(2,1)S(1)}, u32[]{:S(2)}, u32[]{:S(2)}) collective-permute-start(bf16[94,15,128]{2,1,0:T(8,128)(2,1)S(1)} %get-tuple-element.13), channel_id=1, source_target_pairs={{0,1},{1,2},{2,3},{4,5},{5,6},{6,7},{8,9},{9,10},{10,11},{12,13},{... | collective-permute-start | bytes 1082888 | tf_op jit(solution)/shard_map/ppermute | solution.py:16
  165.0 1.5 collective-permute-start.7
  166.5 1.1 fusion.59
  167.6 5.4 %collective-permute-done.6 = bf16[94,15,128]{2,1,0:T(8,128)(2,1)S(1)} collective-permute-done((bf16[94,15,128]{2,1,0:T(8,128)(2,1)S(1)}, bf16[94,15,128]{2,1,0:T(8,128)(2,1)S(1)}, u32[]{:S(2)}, u32[]{:S(2)}) %collective-permute-start.6) | collective-permute-done | bytes 360992 | tf_op jit(solution)/shard_map/ppermute | solution.py:16
  172.9 3.8 %collective-permute-done.7 = bf16[94,15,128]{2,1,0:T(8,128)(2,1)S(1)} collective-permute-done((bf16[94,15,128]{2,1,0:T(8,128)(2,1)S(1)}, bf16[94,15,128]{2,1,0:T(8,128)(2,1)S(1)}, u32[]{:S(2)}, u32[]{:S(2)}) %collective-permute-start.7) | collective-permute-done | bytes 360992 | tf_op jit(solution)/shard_map/ppermute | solution.py:19
  176.7 7.4 %maximum_convert_fusion = f32[94,158,128]{2,1,0:T(8,128)} fusion(bf16[94,15,128]{2,1,0:T(8,128)(2,1)S(1)} %collective-permute-done.7, bf16[15,128,128]{2,1,0:T(8,128)(2,1)} %collective-permute-done.5, bf16[64,128,128]{2,1,0:T(8,128)(2,1)S(1)} %add_convert_fusion, bf16[15,128,128]{2,1,0:T(8,128)(2,1)S(1)} %collective-permute-done.4, ...), kind=kLoop, calls=%fused_computation.29 | loop fusion | flops 19010560 | bytes 11406336 | tf_op jit(solution)/shard_map/convert_element_type | solution.py:107
  184.1 12.0 %fusion.70 = (f32[92,158,128]{2,1,0:T(8,128)}, f32[92,158,128]{2,1,0:T(8,128)}) fusion(f32[94,158,128]{2,1,0:T(8,128)} %maximum_convert_fusion), kind=kLoop, calls=%fused_computation.107 | loop fusion | bytes 29769728 | tf_op jit(solution)/shard_map/slice | solution.py:108
  196.1 10.9 %fusion.71 = (f32[46,1,158,128]{3,2,1,0:T(8,128)}, f32[46,1,158,128]{3,2,1,0:T(8,128)}, f32[46,1,158,128]{3,2,1,0:T(8,128)}, f32[46,1,158,128]{3,2,1,0:T(8,128)}) fusion(f32[46,2,158,128]{3,2,1,0:T(8,128)} %bitcast.35, f32[46,2,158,128]{3,2,1,0:T(8,128)} %bitcast.36), kind=kLoop, calls=%fused_computation.108 | loop fusion | bytes 29769728 | tf_op jit(solution)/shard_map/slice | solution.py:110
  207.0 14.0 %fusion.19 = f32[46,158,128]{2,0,1:T(8,128)S(1)} fusion(f32[46,1,158,128]{3,2,1,0:T(8,128)} %get-tuple-element.35, f32[46,1,158,128]{3,2,1,0:T(8,128)} %get-tuple-element.36, f32[46,1,158,128]{3,2,1,0:T(8,128)} %get-tuple-element.8, f32[46,1,158,128]{3,2,1,0:T(8,128)} %get-tuple-element.7), kind=kLoop, calls=%fused_computation.24 | loop fusion | flops 5581824 | bytes 18606080 | tf_op jit(solution)/shard_map/div | solution.py:110
  221.0 0.7 fusion.73
  221.8 0.0 copy-start.3
  221.8 1.1 bitcast_select_fusion
  222.9 3.0 fusion.82
  226.0 1.4 broadcast_in_dim.14.k_ref
  227.4 54.2 %shard_map.101 = f32[32,64,256]{2,1,0:T(8,128)} custom-call(f32[46,78,256]{2,1,0:T(8,128)} %get-tuple-element.33.x_ref, f32[15,15,8,256]{3,2,1,0:T(8,128)} %broadcast_in_dim.14.k_ref), custom_call_target="tpu_custom_call" | custom-call | flops 235929600 | bytes 5771264 | tf_op jit(solution)/shard_map/pallas_call | solution.py:76
  281.6 2.1 reduce_sum.38
  283.7 2.2 multiply_reduce_fusion.1
  286.0 5.4 %add_convert_fusion.1 = bf16[32,64,256]{2,1,0:T(8,128)(2,1)} fusion(f32[32,64,256]{2,1,0:T(8,128)S(1)} %copy-done.1, bf16[46,78,256]{2,1,0:T(8,128)(2,1)} %get-tuple-element.34, f32[32,64]{1,0:T(8,128)S(1)} %add_rsqrt_fusion.1, f32[32,64]{1,0:T(8,128)S(1)} %broadcast_multiply_fusion.1, bf16[1024,256]{1,0:T(8,128)(2,1)S(1)} %copy-done, ...), kind=kOutput, calls=%fused_computation.33 | convolution fusion | flops 2169503744 | bytes 5259264 | tf_op jit(solution)/shard_map/dot_general | solution.py:100
  291.4 0.8 fusion.81
  292.2 1.9 collective-permute-start.8
  294.1 3.4 %collective-permute-start.9 = (bf16[1,64,256]{2,1,0:T(8,128)(2,1)S(1)}, bf16[1,64,256]{2,1,0:T(8,128)(2,1)S(1)}, u32[]{:S(2)}, u32[]{:S(2)}) collective-permute-start(bf16[1,64,256]{2,1,0:T(8,128)(2,1)S(1)} %get-tuple-element.32), channel_id=1, source_target_pairs={{4,0},{8,4},{12,8},{16,12},{20,16},{24,20},{28,24},{5,1},{9,5},{13... | collective-permute-start | bytes 98312 | tf_op jit(solution)/shard_map/ppermute | solution.py:19
  297.5 0.0 collective-permute-done.8
  297.5 2.7 collective-permute-done.9
  300.3 1.0 pad_maximum_fusion.5
  301.3 3.2 %collective-permute-start.10 = (bf16[34,1,256]{2,1,0:T(2,128)(2,1)S(1)}, bf16[34,1,256]{2,1,0:T(2,128)(2,1)S(1)}, u32[]{:S(2)}, u32[]{:S(2)}) collective-permute-start(bf16[34,1,256]{2,1,0:T(2,128)(2,1)S(1)} %get-tuple-element.27), channel_id=1, source_target_pairs={{0,1},{1,2},{2,3},{4,5},{5,6},{6,7},{8,9},{9,10},{10,11},{12,13},{... | collective-permute-start | bytes 52232 | tf_op jit(solution)/shard_map/ppermute | solution.py:16
  304.5 1.3 collective-permute-start.11
  305.8 0.0 collective-permute-done.10
  305.8 3.4 %collective-permute-done.11 = bf16[34,1,256]{2,1,0:T(2,128)(2,1)S(1)} collective-permute-done((bf16[34,1,256]{2,1,0:T(2,128)(2,1)S(1)}, bf16[34,1,256]{2,1,0:T(2,128)(2,1)S(1)}, u32[]{:S(2)}, u32[]{:S(2)}) %collective-permute-start.11) | collective-permute-done | bytes 17440 | tf_op jit(solution)/shard_map/ppermute | solution.py:19
  309.2 1.8 maximum_convert_fusion.2
  310.9 0.4 fusion.75
  311.3 0.2 fusion.76
  311.5 0.2 fusion.77
  311.7 1.4 fusion.36
  313.1 0.3 fusion.80
  313.4 0.2 fusion.51
  313.6 0.8 copy.20
  (24 shorter events, 0.1 us)
Async XLA Ops:
  0.0 285.9 %copy-start = (bf16[1024,256]{1,0:T(8,128)(2,1)S(1)}, bf16[1024,256]{1,0:T(8,128)(2,1)}, u32[]{:S(2)}) copy-start(bf16[1024,256]{1,0:T(8,128)(2,1)} %param.19) | copy-start | bytes 1572868
  0.0 17.7 %copy-start.2 = (f32[15,15,128]{2,1,0:T(8,128)S(1)}, f32[15,15,128]{2,1,0:T(8,128)}, u32[]{:S(2)}) copy-start(f32[15,15,128]{2,1,0:T(8,128)} %param.11) | copy-start | bytes 345604
  1.2 6.6 %collective-permute-start = (bf16[7,128,128]{2,1,0:T(8,128)(2,1)S(1)}, bf16[7,128,128]{2,1,0:T(8,128)(2,1)S(1)}, u32[]{:S(2)}, u32[]{:S(2)}) collective-permute-start(bf16[7,128,128]{2,1,0:T(8,128)(2,1)S(1)} %get-tuple-element.26), channel_id=1, source_target_pairs={{0,4},{4,8},{8,12},{12,16},{16,20},{20,24},{24,28},{1,5},{5,9},{9,... | collective-permute-start | bytes 688136 | tf_op jit(solution)/shard_map/ppermute | solution.py:16
  4.8 8.2 %collective-permute-start.1 = (bf16[7,128,128]{2,1,0:T(8,128)(2,1)S(1)}, bf16[7,128,128]{2,1,0:T(8,128)(2,1)S(1)}, u32[]{:S(2)}, u32[]{:S(2)}) collective-permute-start(bf16[7,128,128]{2,1,0:T(8,128)(2,1)S(1)} %get-tuple-element.25), channel_id=1, source_target_pairs={{4,0},{8,4},{12,8},{16,12},{20,16},{24,20},{28,24},{5,1},{9,5},{13... | collective-permute-start | bytes 688136 | tf_op jit(solution)/shard_map/ppermute | solution.py:19
  13.2 5.7 %collective-permute-start.2 = (bf16[78,7,128]{2,1,0:T(8,128)(2,1)S(1)}, bf16[78,7,128]{2,1,0:T(8,128)(2,1)S(1)}, u32[]{:S(2)}, u32[]{:S(2)}) collective-permute-start(bf16[78,7,128]{2,1,0:T(8,128)(2,1)S(1)} %get-tuple-element.15), channel_id=1, source_target_pairs={{0,1},{1,2},{2,3},{4,5},{5,6},{6,7},{8,9},{9,10},{10,11},{12,13},{... | collective-permute-start | bytes 419336 | tf_op jit(solution)/shard_map/ppermute | solution.py:16
  16.4 6.6 %collective-permute-start.3 = (bf16[78,7,128]{2,1,0:T(8,128)(2,1)S(1)}, bf16[78,7,128]{2,1,0:T(8,128)(2,1)S(1)}, u32[]{:S(2)}, u32[]{:S(2)}) collective-permute-start(bf16[78,7,128]{2,1,0:T(8,128)(2,1)S(1)} %get-tuple-element.16), channel_id=1, source_target_pairs={{1,0},{2,1},{3,2},{5,4},{6,5},{7,6},{9,8},{10,9},{11,10},{13,12},{... | collective-permute-start | bytes 419336 | tf_op jit(solution)/shard_map/ppermute | solution.py:19
  128.1 7.4 %copy-start.6 = (bf16[512,128]{1,0:T(8,128)(2,1)S(1)}, bf16[512,128]{1,0:T(8,128)(2,1)}, u32[]{:S(2)}) copy-start(bf16[512,128]{1,0:T(8,128)(2,1)} %param.14) | copy-start | bytes 393220
  128.1 7.4 %copy-start.7 = (bf16[128,512]{1,0:T(8,128)(2,1)S(1)}, bf16[128,512]{1,0:T(8,128)(2,1)}, u32[]{:S(2)}) copy-start(bf16[128,512]{1,0:T(8,128)(2,1)} %param.13) | copy-start | bytes 393220
  144.4 22.1 %copy-start.4 = (f32[256]{0:T(256)S(1)}, f32[256]{0:T(256)}, u32[]{:S(2)}) copy-start(f32[256]{0:T(256)} %param.17) | copy-start | bytes 3076
  145.4 13.9 %collective-permute-start.4 = (bf16[15,128,128]{2,1,0:T(8,128)(2,1)}, bf16[15,128,128]{2,1,0:T(8,128)(2,1)S(1)}, u32[]{:S(2)}, u32[]{:S(2)}) collective-permute-start(bf16[15,128,128]{2,1,0:T(8,128)(2,1)} %get-tuple-element.23), channel_id=1, source_target_pairs={{0,4},{4,8},{8,12},{12,16},{16,20},{20,24},{24,28},{1,5},{5,9},{9,... | collective-permute-start | bytes 1474568 | tf_op jit(solution)/shard_map/ppermute | solution.py:16
  149.4 11.4 %collective-permute-start.5 = (bf16[15,128,128]{2,1,0:T(8,128)(2,1)}, bf16[15,128,128]{2,1,0:T(8,128)(2,1)}, u32[]{:S(2)}, u32[]{:S(2)}) collective-permute-start(bf16[15,128,128]{2,1,0:T(8,128)(2,1)} %get-tuple-element.24), channel_id=1, source_target_pairs={{4,0},{8,4},{12,8},{16,12},{20,16},{24,20},{28,24},{5,1},{9,5},{13... | collective-permute-start | bytes 1474568 | tf_op jit(solution)/shard_map/ppermute | solution.py:19
  161.8 11.1 %collective-permute-start.6 = (bf16[94,15,128]{2,1,0:T(8,128)(2,1)S(1)}, bf16[94,15,128]{2,1,0:T(8,128)(2,1)S(1)}, u32[]{:S(2)}, u32[]{:S(2)}) collective-permute-start(bf16[94,15,128]{2,1,0:T(8,128)(2,1)S(1)} %get-tuple-element.13), channel_id=1, source_target_pairs={{0,1},{1,2},{2,3},{4,5},{5,6},{6,7},{8,9},{9,10},{10,11},{12,13},{... | collective-permute-start | bytes 1082888 | tf_op jit(solution)/shard_map/ppermute | solution.py:16
  165.0 11.7 %collective-permute-start.7 = (bf16[94,15,128]{2,1,0:T(8,128)(2,1)S(1)}, bf16[94,15,128]{2,1,0:T(8,128)(2,1)S(1)}, u32[]{:S(2)}, u32[]{:S(2)}) collective-permute-start(bf16[94,15,128]{2,1,0:T(8,128)(2,1)S(1)} %get-tuple-element.14), channel_id=1, source_target_pairs={{1,0},{2,1},{3,2},{5,4},{6,5},{7,6},{9,8},{10,9},{11,10},{13,12},{... | collective-permute-start | bytes 1082888 | tf_op jit(solution)/shard_map/ppermute | solution.py:19
  221.8 1.1 copy-start.3
  281.6 4.4 %copy-start.1 = (f32[32,64,256]{2,1,0:T(8,128)S(1)}, f32[32,64,256]{2,1,0:T(8,128)}, u32[]{:S(2)}) copy-start(f32[32,64,256]{2,1,0:T(8,128)} %shard_map.101) | copy-start | bytes 6291460
  281.6 4.4 %copy-start.5 = (bf16[256,1024]{1,0:T(8,128)(2,1)S(1)}, bf16[256,1024]{1,0:T(8,128)(2,1)}, u32[]{:S(2)}) copy-start(bf16[256,1024]{1,0:T(8,128)(2,1)} %param.18) | copy-start | bytes 1572868
  292.2 5.4 %collective-permute-start.8 = (bf16[1,64,256]{2,1,0:T(8,128)(2,1)S(1)}, bf16[1,64,256]{2,1,0:T(8,128)(2,1)S(1)}, u32[]{:S(2)}, u32[]{:S(2)}) collective-permute-start(bf16[1,64,256]{2,1,0:T(8,128)(2,1)S(1)} %get-tuple-element.31), channel_id=1, source_target_pairs={{0,4},{4,8},{8,12},{12,16},{16,20},{20,24},{24,28},{1,5},{5,9},{9,... | collective-permute-start | bytes 98312 | tf_op jit(solution)/shard_map/ppermute | solution.py:16
  294.1 6.1 %collective-permute-start.9 = (bf16[1,64,256]{2,1,0:T(8,128)(2,1)S(1)}, bf16[1,64,256]{2,1,0:T(8,128)(2,1)S(1)}, u32[]{:S(2)}, u32[]{:S(2)}) collective-permute-start(bf16[1,64,256]{2,1,0:T(8,128)(2,1)S(1)} %get-tuple-element.32), channel_id=1, source_target_pairs={{4,0},{8,4},{12,8},{16,12},{20,16},{24,20},{28,24},{5,1},{9,5},{13... | collective-permute-start | bytes 98312 | tf_op jit(solution)/shard_map/ppermute | solution.py:19
  301.3 4.5 %collective-permute-start.10 = (bf16[34,1,256]{2,1,0:T(2,128)(2,1)S(1)}, bf16[34,1,256]{2,1,0:T(2,128)(2,1)S(1)}, u32[]{:S(2)}, u32[]{:S(2)}) collective-permute-start(bf16[34,1,256]{2,1,0:T(2,128)(2,1)S(1)} %get-tuple-element.27), channel_id=1, source_target_pairs={{0,1},{1,2},{2,3},{4,5},{5,6},{6,7},{8,9},{9,10},{10,11},{12,13},{... | collective-permute-start | bytes 52232 | tf_op jit(solution)/shard_map/ppermute | solution.py:16
  304.5 4.7 %collective-permute-start.11 = (bf16[34,1,256]{2,1,0:T(2,128)(2,1)S(1)}, bf16[34,1,256]{2,1,0:T(2,128)(2,1)S(1)}, u32[]{:S(2)}, u32[]{:S(2)}) collective-permute-start(bf16[34,1,256]{2,1,0:T(2,128)(2,1)S(1)} %get-tuple-element.28), channel_id=1, source_target_pairs={{1,0},{2,1},{3,2},{5,4},{6,5},{7,6},{9,8},{10,9},{11,10},{13,12},{... | collective-permute-start | bytes 52232 | tf_op jit(solution)/shard_map/ppermute | solution.py:19

commit v6 on v5

--- a/solution.py
+++ b/solution.py
@@ -130,11 +130,11 @@
     reach = 7
     extended = padded_2(image, (("row", 0), ("col", 1)), reach)
     first = local_section(extended, raw_first, sigma_first, in_first, out_first)
-    first_cycle = padded_2(first, (("row", 0), ("col", 1)), 2 * reach + 1)
-    first_pooled = zero_outside(blur_down(first_cycle), reach)
+    first_cycle = padded_2(first, (("row", 0), ("col", 1)), 2 * reach + 3)
+    first_pooled = zero_outside(blur_down(first_cycle), reach + 1)
     widened_ext = jnp.dot(first_pooled, widen, preferred_element_type=jnp.float32).astype(
         jnp.bfloat16
-    )
+    )[1:-1, 1:-1]
     second = local_section(widened_ext, raw_second, sigma_second, in_second, out_second)
     second_cycle = padded_2(second, (("row", 0), ("col", 1)), 1)
     return blur_down(second_cycle)

time: 318 us -> 297 us (0.934)
  local copies, waits for them, and re-layouts: 32.9 us -> 20.8 us
  other arithmetic: 45.3 us -> 35.8 us
    div x2, other arithmetic: 15.4 us -> 5.32 us  [blur_down(): (upper[:, 0] + 3.0 * upper[:, 1] + 3.0 * lower[:, 0] + lower[:, 1]) / 8.0]
    slice x2, local copies, waits for them, and re-layouts: 12.3 us -> 4.12 us  [blur_down(): upper = padded[0:rows].reshape(rows // 2, 2, cols + 2, -1)]
    slice x2, local copies, waits for them, and re-layouts: 11.1 us -> 5.47 us  [blur_down(): upper[:, 0] + 3.0 * upper[:, 1] + 3.0 * lower[:, 0] + lower[:, 1]]
    ppermute x6, waiting for transfers between devices: 14.6 us -> 17.9 us  [padded_2(): lax.ppermute(lax.slice_in_dim(block, block.shape[dim] - width, None, axis...]
where the time goes in v6:
time: 297 us; the launch traced here: 293 us
  Pallas kernels  155 us (52%)
  other arithmetic  35.8 us (12%)
  waiting for transfers between devices  35.8 us (12%)
  starting transfers between devices  30.9 us (10%)
  local copies, waits for them, and re-layouts  20.8 us (7%)
  matrix products  15 us (5%)
    pallas_call x2, Pallas kernels, depthwise(): pl.pallas_call(body, out_shape=jax.ShapeDtypeStruct((rows, cols, chans),...  155 us
    ppermute x6, starting transfers between devices, padded_2(): lax.ppermute(lax.slice_in_dim(block, block.shape[dim] - width, None, axis...  19.2 us
    ppermute x6, waiting for transfers between devices, padded_2(): lax.ppermute(lax.slice_in_dim(block, block.shape[dim] - width, None, axis...  17.9 us
    ppermute x6, waiting for transfers between devices, padded_2(): lax.ppermute(lax.slice_in_dim(block, 0, width, axis=dim), axis, backward)  17.9 us
    dot_general x2, matrix products, local_section(): mixed = jnp.dot(hidden, w_out, preferred_element_type=jnp.float32)  14.4 us
    ppermute x6, starting transfers between devices, padded_2(): lax.ppermute(lax.slice_in_dim(block, 0, width, axis=dim), axis, backward)  11.7 us
    convert_element_type x2, other arithmetic, blur_down(): padded = padded.astype(jnp.float32)  10 us
  transfers between devices with their start and end apart: 12, of which 10 were waited for; matrix products, arithmetic and copies ran while one was open for 1% of the time, Pallas kernels for 0%

profile of v6, /device:TPU:3, one launch (start us, length us, event | category | flops | bytes accessed | tf_op | source)
XLA Modules:
  0.0 293.5 jit_solution(14208760254828846156)
XLA Ops:
  0.0 1.1 fusion.79
  1.1 3.7 %collective-permute-start = (bf16[7,128,128]{2,1,0:T(8,128)(2,1)S(1)}, bf16[7,128,128]{2,1,0:T(8,128)(2,1)S(1)}, u32[]{:S(2)}, u32[]{:S(2)}) collective-permute-start(bf16[7,128,128]{2,1,0:T(8,128)(2,1)S(1)} %get-tuple-element.26), channel_id=1, source_target_pairs={{0,4},{4,8},{8,12},{12,16},{16,20},{20,24},{24,28},{1,5},{5,9},{9,... | collective-permute-start | bytes 688136 | tf_op jit(solution)/shard_map/ppermute | solution.py:16
  4.8 1.9 collective-permute-start.1
  6.8 0.7 multiply_multiply_fusion.3
  7.4 0.1 add_negate_fusion
  7.5 0.3 collective-permute-done
  7.8 2.0 constant_dynamic-update-slice_fusion.1
  9.8 3.3 %collective-permute-done.1 = bf16[7,128,128]{2,1,0:T(8,128)(2,1)S(1)} collective-permute-done((bf16[7,128,128]{2,1,0:T(8,128)(2,1)S(1)}, bf16[7,128,128]{2,1,0:T(8,128)(2,1)S(1)}, u32[]{:S(2)}, u32[]{:S(2)}) %collective-permute-start.1) | collective-permute-done | bytes 229408 | tf_op jit(solution)/shard_map/ppermute | solution.py:19
  13.2 3.2 %collective-permute-start.2 = (bf16[78,7,128]{2,1,0:T(8,128)(2,1)S(1)}, bf16[78,7,128]{2,1,0:T(8,128)(2,1)S(1)}, u32[]{:S(2)}, u32[]{:S(2)}) collective-permute-start(bf16[78,7,128]{2,1,0:T(8,128)(2,1)S(1)} %get-tuple-element.15), channel_id=1, source_target_pairs={{0,1},{1,2},{2,3},{4,5},{5,6},{6,7},{8,9},{9,10},{10,11},{12,13},{... | collective-permute-start | bytes 419336 | tf_op jit(solution)/shard_map/ppermute | solution.py:16
  16.4 1.3 collective-permute-start.3
  17.7 0.1 fusion.61
  17.8 1.0 collective-permute-done.2
  18.9 4.1 %collective-permute-done.3 = bf16[78,7,128]{2,1,0:T(8,128)(2,1)S(1)} collective-permute-done((bf16[78,7,128]{2,1,0:T(8,128)(2,1)S(1)}, bf16[78,7,128]{2,1,0:T(8,128)(2,1)S(1)}, u32[]{:S(2)}, u32[]{:S(2)}) %collective-permute-start.3) | collective-permute-done | bytes 139808 | tf_op jit(solution)/shard_map/ppermute | solution.py:19
  23.0 3.6 %maximum_convert_fusion.1.x_ref = f32[78,142,128]{2,1,0:T(8,128)} fusion(bf16[78,7,128]{2,1,0:T(8,128)(2,1)S(1)} %collective-permute-done.3, bf16[78,128,128]{2,1,0:T(8,128)(2,1)S(1)} %constant_dynamic-update-slice_fusion, bf16[78,7,128]{2,1,0:T(8,128)(2,1)S(1)} %collective-permute-done.2), kind=kLoop, calls=%fused_computation.31 | loop fusion | flops 8506368 | bytes 8506368 | tf_op jit(solution)/shard_map/convert_element_type | solution.py:87
  26.6 1.0 broadcast_in_dim.12.k_ref
  27.6 100.5 %shard_map.100 = f32[64,128,128]{2,1,0:T(8,128)} custom-call(f32[78,142,128]{2,1,0:T(8,128)} %maximum_convert_fusion.1.x_ref, f32[15,15,8,128]{3,2,1,0:T(8,128)} %broadcast_in_dim.12.k_ref), custom_call_target="tpu_custom_call" | custom-call | flops 471859200 | bytes 9865216 | tf_op jit(solution)/shard_map/pallas_call | solution.py:76
  128.1 3.3 %reduce_sum.36 = f32[64,128]{1,0:T(8,128)S(1)} reduce(f32[64,128,128]{2,1,0:T(8,128)} %shard_map.100, f32[]{:T(128)} %constant.33.clone.1), dimensions={2}, to_apply=%region_0.0 | reduce | flops 1040384 | bytes 4227076 | tf_op jit(solution)/shard_map/reduce_sum | solution.py:94
  131.5 4.0 %multiply_reduce_fusion = f32[64,128]{1,0:T(8,128)S(1)} fusion(f32[64,128,128]{2,1,0:T(8,128)} %shard_map.100, f32[64,128]{1,0:T(8,128)S(1)} %broadcast_multiply_fusion), kind=kLoop, calls=%fused_computation.21 | loop fusion | flops 3137536 | bytes 4259840 | tf_op jit(solution)/shard_map/reduce_sum | solution.py:95
  135.6 8.8 %add_convert_fusion = bf16[64,128,128]{2,1,0:T(8,128)(2,1)S(1)} fusion(bf16[64,128,128]{2,1,0:T(8,128)(2,1)} %param.10, f32[64,128,128]{2,1,0:T(8,128)} %shard_map.100, f32[64,128]{1,0:T(8,128)S(1)} %add_rsqrt_fusion, f32[64,128]{1,0:T(8,128)S(1)} %broadcast_multiply_fusion, bf16[512,128]{1,0:T(8,128)(2,1)S(1)} %copy-done.8, bf16[128,512]{1,0:T(8,128)(2,1)S(1)} %copy-done.9), kind=kOutput, calls=%fused_computation.19 | convolution fusion | flops 2191523840 | bytes 8716288 | tf_op jit(solution)/shard_map/dot_general | solution.py:100
  144.4 1.1 fusion.78
  145.5 3.9 %collective-permute-start.4 = (bf16[17,128,128]{2,1,0:T(8,128)(2,1)}, bf16[17,128,128]{2,1,0:T(8,128)(2,1)S(1)}, u32[]{:S(2)}, u32[]{:S(2)}) collective-permute-start(bf16[17,128,128]{2,1,0:T(8,128)(2,1)} %get-tuple-element.23), channel_id=1, source_target_pairs={{0,4},{4,8},{8,12},{12,16},{16,20},{20,24},{24,28},{1,5},{5,9},{9,... | collective-permute-start | bytes 1671176 | tf_op jit(solution)/shard_map/ppermute | solution.py:16
  149.4 1.9 collective-permute-start.5
  151.4 0.1 broadcast_and_fusion
  151.5 9.3 %collective-permute-done.4 = bf16[17,128,128]{2,1,0:T(8,128)(2,1)S(1)} collective-permute-done((bf16[17,128,128]{2,1,0:T(8,128)(2,1)}, bf16[17,128,128]{2,1,0:T(8,128)(2,1)S(1)}, u32[]{:S(2)}, u32[]{:S(2)}) %collective-permute-start.4) | collective-permute-done | bytes 557088 | tf_op jit(solution)/shard_map/ppermute | solution.py:16
  160.8 1.0 collective-permute-done.5
  161.9 1.2 pad_maximum_fusion.2
  163.2 3.2 %collective-permute-start.6 = (bf16[98,17,128]{2,0,1:T(8,128)(2,1)S(1)}, bf16[98,17,128]{2,0,1:T(8,128)(2,1)S(1)}, u32[]{:S(2)}, u32[]{:S(2)}) collective-permute-start(bf16[98,17,128]{2,0,1:T(8,128)(2,1)S(1)} %copy.21), channel_id=1, source_target_pairs={{0,1},{1,2},{2,3},{4,5},{5,6},{6,7},{8,9},{9,10},{10,11},{12,13},{... | collective-permute-start | bytes 1279496 | tf_op jit(solution)/shard_map/ppermute | solution.py:16
  166.5 1.5 collective-permute-start.7
  168.0 0.1 fusion.59
  168.1 7.3 %collective-permute-done.6 = bf16[98,17,128]{2,0,1:T(8,128)(2,1)S(1)} collective-permute-done((bf16[98,17,128]{2,0,1:T(8,128)(2,1)S(1)}, bf16[98,17,128]{2,0,1:T(8,128)(2,1)S(1)}, u32[]{:S(2)}, u32[]{:S(2)}) %collective-permute-start.6) | collective-permute-done | bytes 426528 | tf_op jit(solution)/shard_map/ppermute | solution.py:16
  175.4 0.1 copy.23
  175.5 3.8 %collective-permute-done.7 = bf16[98,17,128]{2,0,1:T(8,128)(2,1)S(1)} collective-permute-done((bf16[98,17,128]{2,0,1:T(8,128)(2,1)S(1)}, bf16[98,17,128]{2,0,1:T(8,128)(2,1)S(1)}, u32[]{:S(2)}, u32[]{:S(2)}) %collective-permute-start.7) | collective-permute-done | bytes 426528 | tf_op jit(solution)/shard_map/ppermute | solution.py:19
  179.3 0.1 copy.24
  179.4 8.3 %maximum_convert_fusion = f32[98,162,128]{2,1,0:T(8,128)S(1)} fusion(bf16[98,17,128]{2,1,0:T(8,128)(2,1)S(1)} %copy.24, bf16[17,128,128]{2,1,0:T(8,128)(2,1)} %collective-permute-done.5, bf16[64,128,128]{2,1,0:T(8,128)(2,1)S(1)} %add_convert_fusion, bf16[17,128,128]{2,1,0:T(8,128)(2,1)S(1)} %collective-permute-done.4, bf16[98,17,128]{2,1,0:T(8,128)(2,1)S(1)} %copy.23), kind=kLoop, calls=%fused_computation.18 | loop fusion | flops 20321280 | bytes 12192768 | tf_op jit(solution)/shard_map/convert_element_type | solution.py:107
  187.7 3.7 %fusion.70 = (f32[96,162,128]{2,1,0:T(8,128)S(1)}, f32[96,162,128]{2,1,0:T(8,128)}) fusion(f32[98,162,128]{2,1,0:T(8,128)S(1)} %maximum_convert_fusion), kind=kLoop, calls=%fused_computation.108 | loop fusion | bytes 31850496 | tf_op jit(solution)/shard_map/slice | solution.py:108
  191.4 5.3 %fusion.71 = (f32[48,1,162,128]{3,2,1,0:T(8,128)S(1)}, f32[48,1,162,128]{3,2,1,0:T(8,128)S(1)}, f32[48,1,162,128]{3,2,1,0:T(8,128)S(1)}, f32[48,1,162,128]{3,2,1,0:T(8,128)}) fusion(f32[48,2,162,128]{3,2,1,0:T(8,128)S(1)} %bitcast.33, f32[48,2,162,128]{3,2,1,0:T(8,128)} %bitcast.34), kind=kLoop, calls=%fused_computation.109 | loop fusion | bytes 31850496 | tf_op jit(solution)/shard_map/slice | solution.py:110
  196.7 3.9 %fusion.19 = f32[48,162,128]{2,0,1:T(8,128)S(1)} fusion(f32[48,1,162,128]{3,2,1,0:T(8,128)S(1)} %get-tuple-element.33, f32[48,1,162,128]{3,2,1,0:T(8,128)} %get-tuple-element.34, f32[48,1,162,128]{3,2,1,0:T(8,128)S(1)} %get-tuple-element.8, f32[48,1,162,128]{3,2,1,0:T(8,128)S(1)} %get-tuple-element.7), kind=kLoop, calls=%fused_computation.25 | loop fusion | flops 5971968 | bytes 19906560 | tf_op jit(solution)/shard_map/div | solution.py:110
  200.6 0.6 fusion.73
  201.3 0.8 bitcast_select_fusion
  202.1 0.7 convolution_convert_fusion
  202.8 1.3 copy-done.2
  204.1 2.3 slice_convert_fusion.x_ref
  206.4 1.4 broadcast_in_dim.14.k_ref
  207.9 54.2 %shard_map.101 = f32[32,64,256]{2,1,0:T(8,128)} custom-call(f32[46,78,256]{2,1,0:T(8,128)} %slice_convert_fusion.x_ref, f32[15,15,8,256]{3,2,1,0:T(8,128)} %broadcast_in_dim.14.k_ref), custom_call_target="tpu_custom_call" | custom-call | flops 235929600 | bytes 5771264 | tf_op jit(solution)/shard_map/pallas_call | solution.py:76
  262.1 2.1 reduce_sum.38
  264.2 0.1 copy-done.1
  264.3 0.6 multiply_reduce_fusion.1
  265.0 5.6 %add_convert_fusion.1 = bf16[32,64,256]{2,1,0:T(8,128)(2,1)} fusion(f32[32,64,256]{2,1,0:T(8,128)S(1)} %copy-done.1, bf16[48,80,256]{2,1,0:T(8,128)(2,1)} %copy-done.2, f32[32,64]{1,0:T(8,128)S(1)} %add_rsqrt_fusion.1, f32[32,64]{1,0:T(8,128)S(1)} %broadcast_multiply_fusion.1, bf16[1024,256]{1,0:T(8,128)(2,1)S(1)} %copy-done, ...), kind=kOutput, calls=%fused_computation.33 | convolution fusion | flops 2169503744 | bytes 5259264 | tf_op jit(solution)/shard_map/dot_general | solution.py:100
  270.5 0.8 fusion.81
  271.3 1.9 collective-permute-start.8
  273.2 3.8 %collective-permute-start.9 = (bf16[1,64,256]{2,1,0:T(8,128)(2,1)S(1)}, bf16[1,64,256]{2,1,0:T(8,128)(2,1)S(1)}, u32[]{:S(2)}, u32[]{:S(2)}) collective-permute-start(bf16[1,64,256]{2,1,0:T(8,128)(2,1)S(1)} %get-tuple-element.32), channel_id=1, source_target_pairs={{4,0},{8,4},{12,8},{16,12},{20,16},{24,20},{28,24},{5,1},{9,5},{13... | collective-permute-start | bytes 98312 | tf_op jit(solution)/shard_map/ppermute | solution.py:19
  277.0 2.3 collective-permute-done.9
  279.3 1.0 pad_maximum_fusion.5
  280.4 3.2 %collective-permute-start.10 = (bf16[34,1,256]{2,1,0:T(2,128)(2,1)S(1)}, bf16[34,1,256]{2,1,0:T(2,128)(2,1)S(1)}, u32[]{:S(2)}, u32[]{:S(2)}) collective-permute-start(bf16[34,1,256]{2,1,0:T(2,128)(2,1)S(1)} %get-tuple-element.27), channel_id=1, source_target_pairs={{0,1},{1,2},{2,3},{4,5},{5,6},{6,7},{8,9},{9,10},{10,11},{12,13},{... | collective-permute-start | bytes 52232 | tf_op jit(solution)/shard_map/ppermute | solution.py:16
  283.6 1.3 collective-permute-start.11
  284.9 3.4 %collective-permute-done.11 = bf16[34,1,256]{2,1,0:T(2,128)(2,1)S(1)} collective-permute-done((bf16[34,1,256]{2,1,0:T(2,128)(2,1)S(1)}, bf16[34,1,256]{2,1,0:T(2,128)(2,1)S(1)}, u32[]{:S(2)}, u32[]{:S(2)}) %collective-permute-start.11) | collective-permute-done | bytes 17440 | tf_op jit(solution)/shard_map/ppermute | solution.py:19
  288.3 1.8 maximum_convert_fusion.2
  290.0 0.4 fusion.75
  290.4 0.2 fusion.76
  290.6 0.2 fusion.77
  290.8 1.4 fusion.36
  292.2 0.3 fusion.80
  292.5 0.2 fusion.51
  292.7 0.8 copy.34
  (33 shorter events, 0.4 us)
Async XLA Ops:
  0.0 264.9 %copy-start = (bf16[1024,256]{1,0:T(8,128)(2,1)S(1)}, bf16[1024,256]{1,0:T(8,128)(2,1)}, u32[]{:S(2)}) copy-start(bf16[1024,256]{1,0:T(8,128)(2,1)} %param.19) | copy-start | bytes 1572868
  1.1 6.6 %collective-permute-start = (bf16[7,128,128]{2,1,0:T(8,128)(2,1)S(1)}, bf16[7,128,128]{2,1,0:T(8,128)(2,1)S(1)}, u32[]{:S(2)}, u32[]{:S(2)}) collective-permute-start(bf16[7,128,128]{2,1,0:T(8,128)(2,1)S(1)} %get-tuple-element.26), channel_id=1, source_target_pairs={{0,4},{4,8},{8,12},{12,16},{16,20},{20,24},{24,28},{1,5},{5,9},{9,... | collective-permute-start | bytes 688136 | tf_op jit(solution)/shard_map/ppermute | solution.py:16
  4.8 8.2 %collective-permute-start.1 = (bf16[7,128,128]{2,1,0:T(8,128)(2,1)S(1)}, bf16[7,128,128]{2,1,0:T(8,128)(2,1)S(1)}, u32[]{:S(2)}, u32[]{:S(2)}) collective-permute-start(bf16[7,128,128]{2,1,0:T(8,128)(2,1)S(1)} %get-tuple-element.25), channel_id=1, source_target_pairs={{4,0},{8,4},{12,8},{16,12},{20,16},{24,20},{28,24},{5,1},{9,5},{13... | collective-permute-start | bytes 688136 | tf_op jit(solution)/shard_map/ppermute | solution.py:19
  7.5 10.2 %copy-start.4 = (f32[15,15,128]{2,1,0:T(8,128)S(1)}, f32[15,15,128]{2,1,0:T(8,128)}, u32[]{:S(2)}) copy-start(f32[15,15,128]{2,1,0:T(8,128)} %param.11) | copy-start | bytes 345604
  13.2 5.7 %collective-permute-start.2 = (bf16[78,7,128]{2,1,0:T(8,128)(2,1)S(1)}, bf16[78,7,128]{2,1,0:T(8,128)(2,1)S(1)}, u32[]{:S(2)}, u32[]{:S(2)}) collective-permute-start(bf16[78,7,128]{2,1,0:T(8,128)(2,1)S(1)} %get-tuple-element.15), channel_id=1, source_target_pairs={{0,1},{1,2},{2,3},{4,5},{5,6},{6,7},{8,9},{9,10},{10,11},{12,13},{... | collective-permute-start | bytes 419336 | tf_op jit(solution)/shard_map/ppermute | solution.py:16
  16.4 6.6 %collective-permute-start.3 = (bf16[78,7,128]{2,1,0:T(8,128)(2,1)S(1)}, bf16[78,7,128]{2,1,0:T(8,128)(2,1)S(1)}, u32[]{:S(2)}, u32[]{:S(2)}) collective-permute-start(bf16[78,7,128]{2,1,0:T(8,128)(2,1)S(1)} %get-tuple-element.16), channel_id=1, source_target_pairs={{1,0},{2,1},{3,2},{5,4},{6,5},{7,6},{9,8},{10,9},{11,10},{13,12},{... | collective-permute-start | bytes 419336 | tf_op jit(solution)/shard_map/ppermute | solution.py:19
  131.5 4.1 %copy-start.8 = (bf16[512,128]{1,0:T(8,128)(2,1)S(1)}, bf16[512,128]{1,0:T(8,128)(2,1)}, u32[]{:S(2)}) copy-start(bf16[512,128]{1,0:T(8,128)(2,1)} %param.14) | copy-start | bytes 393220
  131.5 4.1 %copy-start.9 = (bf16[128,512]{1,0:T(8,128)(2,1)S(1)}, bf16[128,512]{1,0:T(8,128)(2,1)}, u32[]{:S(2)}) copy-start(bf16[128,512]{1,0:T(8,128)(2,1)} %param.13) | copy-start | bytes 393220
  145.5 15.3 %collective-permute-start.4 = (bf16[17,128,128]{2,1,0:T(8,128)(2,1)}, bf16[17,128,128]{2,1,0:T(8,128)(2,1)S(1)}, u32[]{:S(2)}, u32[]{:S(2)}) collective-permute-start(bf16[17,128,128]{2,1,0:T(8,128)(2,1)} %get-tuple-element.23), channel_id=1, source_target_pairs={{0,4},{4,8},{8,12},{12,16},{16,20},{20,24},{24,28},{1,5},{5,9},{9,... | collective-permute-start | bytes 1671176 | tf_op jit(solution)/shard_map/ppermute | solution.py:16
  149.4 12.4 %collective-permute-start.5 = (bf16[17,128,128]{2,1,0:T(8,128)(2,1)}, bf16[17,128,128]{2,1,0:T(8,128)(2,1)}, u32[]{:S(2)}, u32[]{:S(2)}) collective-permute-start(bf16[17,128,128]{2,1,0:T(8,128)(2,1)} %get-tuple-element.24), channel_id=1, source_target_pairs={{4,0},{8,4},{12,8},{16,12},{20,16},{24,20},{28,24},{5,1},{9,5},{13... | collective-permute-start | bytes 1671176 | tf_op jit(solution)/shard_map/ppermute | solution.py:19
  151.5 16.5 %copy-start.6 = (f32[256]{0:T(256)S(1)}, f32[256]{0:T(256)}, u32[]{:S(2)}) copy-start(f32[256]{0:T(256)} %param.17) | copy-start | bytes 3076
  151.5 16.5 %copy-start.3 = (f32[15,15,256]{2,1,0:T(8,128)S(1)}, f32[15,15,256]{2,1,0:T(8,128)}, u32[]{:S(2)}) copy-start(f32[15,15,256]{2,1,0:T(8,128)} %param.16) | copy-start | bytes 691204
  163.2 12.2 %collective-permute-start.6 = (bf16[98,17,128]{2,0,1:T(8,128)(2,1)S(1)}, bf16[98,17,128]{2,0,1:T(8,128)(2,1)S(1)}, u32[]{:S(2)}, u32[]{:S(2)}) collective-permute-start(bf16[98,17,128]{2,0,1:T(8,128)(2,1)S(1)} %copy.21), channel_id=1, source_target_pairs={{0,1},{1,2},{2,3},{4,5},{5,6},{6,7},{8,9},{9,10},{10,11},{12,13},{... | collective-permute-start | bytes 1279496 | tf_op jit(solution)/shard_map/ppermute | solution.py:16
  166.5 12.8 %collective-permute-start.7 = (bf16[98,17,128]{2,0,1:T(8,128)(2,1)S(1)}, bf16[98,17,128]{2,0,1:T(8,128)(2,1)S(1)}, u32[]{:S(2)}, u32[]{:S(2)}) collective-permute-start(bf16[98,17,128]{2,0,1:T(8,128)(2,1)S(1)} %copy.22), channel_id=1, source_target_pairs={{1,0},{2,1},{3,2},{5,4},{6,5},{7,6},{9,8},{10,9},{11,10},{13,12},{... | collective-permute-start | bytes 1279496 | tf_op jit(solution)/shard_map/ppermute | solution.py:19
  201.3 0.8 copy-start.5
  202.8 1.3 copy-start.2
  262.0 2.2 copy-start.1
  262.0 2.9 copy-start.7
  271.3 5.7 %collective-permute-start.8 = (bf16[1,64,256]{2,1,0:T(8,128)(2,1)S(1)}, bf16[1,64,256]{2,1,0:T(8,128)(2,1)S(1)}, u32[]{:S(2)}, u32[]{:S(2)}) collective-permute-start(bf16[1,64,256]{2,1,0:T(8,128)(2,1)S(1)} %get-tuple-element.31), channel_id=1, source_target_pairs={{0,4},{4,8},{8,12},{12,16},{16,20},{20,24},{24,28},{1,5},{5,9},{9,... | collective-permute-start | bytes 98312 | tf_op jit(solution)/shard_map/ppermute | solution.py:16
  273.2 6.1 %collective-permute-start.9 = (bf16[1,64,256]{2,1,0:T(8,128)(2,1)S(1)}, bf16[1,64,256]{2,1,0:T(8,128)(2,1)S(1)}, u32[]{:S(2)}, u32[]{:S(2)}) collective-permute-start(bf16[1,64,256]{2,1,0:T(8,128)(2,1)S(1)} %get-tuple-element.32), channel_id=1, source_target_pairs={{4,0},{8,4},{12,8},{16,12},{20,16},{24,20},{28,24},{5,1},{9,5},{13... | collective-permute-start | bytes 98312 | tf_op jit(solution)/shard_map/ppermute | solution.py:19
  280.4 4.5 %collective-permute-start.10 = (bf16[34,1,256]{2,1,0:T(2,128)(2,1)S(1)}, bf16[34,1,256]{2,1,0:T(2,128)(2,1)S(1)}, u32[]{:S(2)}, u32[]{:S(2)}) collective-permute-start(bf16[34,1,256]{2,1,0:T(2,128)(2,1)S(1)} %get-tuple-element.27), channel_id=1, source_target_pairs={{0,1},{1,2},{2,3},{4,5},{5,6},{6,7},{8,9},{9,10},{10,11},{12,13},{... | collective-permute-start | bytes 52232 | tf_op jit(solution)/shard_map/ppermute | solution.py:16
  283.6 4.7 %collective-permute-start.11 = (bf16[34,1,256]{2,1,0:T(2,128)(2,1)S(1)}, bf16[34,1,256]{2,1,0:T(2,128)(2,1)S(1)}, u32[]{:S(2)}, u32[]{:S(2)}) collective-permute-start(bf16[34,1,256]{2,1,0:T(2,128)(2,1)S(1)} %get-tuple-element.28), channel_id=1, source_target_pairs={{1,0},{2,1},{3,2},{5,4},{6,5},{7,6},{9,8},{10,9},{11,10},{13,12},{... | collective-permute-start | bytes 52232 | tf_op jit(solution)/shard_map/ppermute | solution.py:19

commit v7 on v1

--- a/solution.py
+++ b/solution.py
@@ -32,30 +32,49 @@
     nlb = chans // 128
     njb = cols // 8
     nrb = rows // rb
-    for b in range(taps):
-        def shift(r, c):
-            xs_ref[r] = x_ref[r, pl.ds(b, cols), :]
-            return c
+    first = True
+    for s in range(8):
+        if s == 0:
+            src = x_ref
+        else:
+            width = cols + 8 if s + 8 < taps else cols
 
-        lax.fori_loop(0, rows + taps - 1, shift, 0)
-        for lb in range(nlb):
-            lanes = pl.ds(lb * 128, 128)
-            ks = [k_ref[a, b, :, lanes] for a in range(taps)]
-
-            def body(i, c):
-                r0 = pl.multiple_of((i // njb) * rb, rb)
-                j0 = pl.multiple_of((i % njb) * 8, 8)
-                xs = xs_ref[pl.ds(r0, rb + taps - 1), pl.ds(j0, 8), lanes]
-                if b == 0:
-                    acc = jnp.zeros((rb, 8, 128), jnp.float32)
-                else:
-                    acc = o_ref[pl.ds(r0, rb), pl.ds(j0, 8), lanes]
-                for a in range(taps):
-                    acc = acc + xs[a : a + rb] * ks[a][None]
-                o_ref[pl.ds(r0, rb), pl.ds(j0, 8), lanes] = acc
+            def shift(r, c):
+                xs_ref[r, pl.ds(0, width), :] = x_ref[r, pl.ds(s, width), :]
                 return c
 
-            lax.fori_loop(0, nrb * njb, body, 0)
+            lax.fori_loop(0, rows + taps - 1, shift, 0)
+            src = xs_ref
+        for q in range(2):
+            b = 8 * q + s
+            if b >= taps:
+                continue
+            for lb in range(nlb):
+                lanes = pl.ds(lb * 128, 128)
+                ks = [k_ref[a, b, :, lanes] for a in range(taps)]
+
+                def body(i, c, src=src, q=q, ks=ks, lanes=lanes, first=first):
+                    r0 = pl.multiple_of((i // njb) * rb, rb)
+                    j0 = pl.multiple_of((i % njb) * 8, 8)
+                    xs = src[pl.ds(r0, rb + taps - 1), pl.ds(j0 + 8 * q, 8), lanes]
+                    if first:
+                        acc = jnp.zeros((rb, 8, 128), jnp.float32)
+                    else:
+                        acc = o_ref[pl.ds(r0, rb), pl.ds(j0, 8), lanes]
+                    terms = [xs[a : a + rb] * ks[a][None] for a in range(taps)]
+                    for g in range(0, taps, 5):
+                        group = terms[g : g + 5]
+                        while len(group) > 1:
+                            group = [
+                                group[i] + group[i + 1] if i + 1 < len(group) else group[i]
+                                for i in range(0, len(group), 2)
+                            ]
+                        acc = acc + group[0]
+                    o_ref[pl.ds(r0, rb), pl.ds(j0, 8), lanes] = acc
+                    return c
+
+                lax.fori_loop(0, nrb * njb, body, 0, unroll=2)
+            first = False
 
 
 def depthwise(extended, kernel):
@@ -71,7 +90,7 @@
         out_shape=jax.ShapeDtypeStruct((rows, cols, chans), jnp.float32),
         in_specs=[vmem, vmem],
         out_specs=vmem,
-        scratch_shapes=[pltpu.VMEM((extended.shape[0], cols, chans), jnp.float32)],
+        scratch_shapes=[pltpu.VMEM((extended.shape[0], cols + 8, chans), jnp.float32)],
         cost_estimate=pl.CostEstimate(
             flops=2 * rows * cols * chans * taps * taps,
             transcendentals=0,

time: 289 us -> 272 us (0.941)
  Pallas kernels: 164 us -> 148 us
    pallas_call x2, Pallas kernels: 164 us -> 148 us  [depthwise(): pl.pallas_call(body, out_shape=jax.ShapeDtypeStruct((rows, cols, chans),...]
where the time goes in v7:
time: 272 us; the launch traced here: 271 us
  Pallas kernels  148 us (54%)
  starting transfers between devices  38.1 us (14%)
  waiting for transfers between devices  35.2 us (13%)
  other arithmetic  24.6 us (9%)
  matrix products  14.7 us (5%)
  local copies, waits for them, and re-layouts  10.5 us (4%)
    pallas_call x2, Pallas kernels, depthwise(): pl.pallas_call(body, out_shape=jax.ShapeDtypeStruct((rows, cols, chans),...  148 us
    ppermute x8, waiting for transfers between devices, padded_2(): lax.ppermute(lax.slice_in_dim(block, 0, width, axis=dim), axis, backward)  30.4 us
    ppermute x8, starting transfers between devices, padded_2(): lax.ppermute(lax.slice_in_dim(block, block.shape[dim] - width, None, axis...  25 us
    dot_general x2, matrix products, local_section(): mixed = jnp.dot(hidden, w_out, preferred_element_type=jnp.float32)  14.3 us
    ppermute x8, starting transfers between devices, padded_2(): lax.ppermute(lax.slice_in_dim(block, 0, width, axis=dim), axis, backward)  13 us
    convert_element_type x2, other arithmetic, depthwise(): extended.astype(jnp.float32)  6.08 us
  transfers between devices with their start and end apart: 16, of which 12 were waited for; matrix products, arithmetic and copies ran while one was open for 1% of the time, Pallas kernels for 0%

profile of v7, /device:TPU:3, one launch (start us, length us, event | category | flops | bytes accessed | tf_op | source)
XLA Modules:
  0.0 271.1 jit_solution(6535101769261548248)
XLA Ops:
  0.0 1.1 fusion.80
  1.1 3.7 %collective-permute-start = (bf16[7,128,128]{2,1,0:T(8,128)(2,1)S(1)}, bf16[7,128,128]{2,1,0:T(8,128)(2,1)S(1)}, u32[]{:S(2)}, u32[]{:S(2)}) collective-permute-start(bf16[7,128,128]{2,1,0:T(8,128)(2,1)S(1)} %get-tuple-element.26), channel_id=1, source_target_pairs={{0,4},{4,8},{8,12},{12,16},{16,20},{20,24},{24,28},{1,5},{5,9},{9,... | collective-permute-start | bytes 688136 | tf_op jit(solution)/shard_map/ppermute | solution.py:16
  4.8 1.9 collective-permute-start.1
  6.8 0.7 multiply_multiply_fusion.3
  7.5 0.3 collective-permute-done
  7.8 2.0 constant_dynamic-update-slice_fusion.1
  9.8 3.2 %collective-permute-done.1 = bf16[7,128,128]{2,1,0:T(8,128)(2,1)S(1)} collective-permute-done((bf16[7,128,128]{2,1,0:T(8,128)(2,1)S(1)}, bf16[7,128,128]{2,1,0:T(8,128)(2,1)S(1)}, u32[]{:S(2)}, u32[]{:S(2)}) %collective-permute-start.1) | collective-permute-done | bytes 229408 | tf_op jit(solution)/shard_map/ppermute | solution.py:19
  13.2 3.2 %collective-permute-start.2 = (bf16[78,7,128]{2,1,0:T(8,128)(2,1)S(1)}, bf16[78,7,128]{2,1,0:T(8,128)(2,1)S(1)}, u32[]{:S(2)}, u32[]{:S(2)}) collective-permute-start(bf16[78,7,128]{2,1,0:T(8,128)(2,1)S(1)} %get-tuple-element.11), channel_id=1, source_target_pairs={{0,1},{1,2},{2,3},{4,5},{5,6},{6,7},{8,9},{9,10},{10,11},{12,13},{... | collective-permute-start | bytes 419336 | tf_op jit(solution)/shard_map/ppermute | solution.py:16
  16.4 1.3 collective-permute-start.3
  17.7 0.1 fusion.62
  17.8 1.1 collective-permute-done.2
  18.9 4.1 %collective-permute-done.3 = bf16[78,7,128]{2,1,0:T(8,128)(2,1)S(1)} collective-permute-done((bf16[78,7,128]{2,1,0:T(8,128)(2,1)S(1)}, bf16[78,7,128]{2,1,0:T(8,128)(2,1)S(1)}, u32[]{:S(2)}, u32[]{:S(2)}) %collective-permute-start.3) | collective-permute-done | bytes 139808 | tf_op jit(solution)/shard_map/ppermute | solution.py:19
  23.0 3.6 %maximum_convert_fusion.x_ref = f32[78,142,128]{2,1,0:T(8,128)} fusion(bf16[78,7,128]{2,1,0:T(8,128)(2,1)S(1)} %collective-permute-done.3, bf16[78,128,128]{2,1,0:T(8,128)(2,1)S(1)} %constant_dynamic-update-slice_fusion, bf16[78,7,128]{2,1,0:T(8,128)(2,1)S(1)} %collective-permute-done.2), kind=kLoop, calls=%fused_computation.23 | loop fusion | flops 8506368 | bytes 8506368 | tf_op jit(solution)/shard_map/convert_element_type | solution.py:99
  26.6 1.0 broadcast_in_dim.4.k_ref
  27.6 96.6 %shard_map.100 = f32[64,128,128]{2,1,0:T(8,128)} custom-call(f32[78,142,128]{2,1,0:T(8,128)} %maximum_convert_fusion.x_ref, f32[15,15,8,128]{3,2,1,0:T(8,128)} %broadcast_in_dim.4.k_ref), custom_call_target="tpu_custom_call" | custom-call | flops 471859200 | bytes 9865216 | tf_op jit(solution)/shard_map/pallas_call | solution.py:88
  124.3 3.3 %reduce_sum.36 = f32[64,128]{1,0:T(8,128)S(1)} reduce(f32[64,128,128]{2,1,0:T(8,128)} %shard_map.100, f32[]{:T(128)} %constant.14.clone.1), dimensions={2}, to_apply=%region_0.0 | reduce | flops 1040384 | bytes 4227076 | tf_op jit(solution)/shard_map/reduce_sum | solution.py:106
  127.6 4.0 %multiply_reduce_fusion = f32[64,128]{1,0:T(8,128)S(1)} fusion(f32[64,128,128]{2,1,0:T(8,128)} %shard_map.100, f32[64,128]{1,0:T(8,128)S(1)} %broadcast_multiply_fusion), kind=kLoop, calls=%fused_computation.20 | loop fusion | flops 3137536 | bytes 4259840 | tf_op jit(solution)/shard_map/reduce_sum | solution.py:107
  131.7 8.9 %add_convert_fusion = bf16[64,128,128]{2,1,0:T(8,128)(2,1)S(1)} fusion(bf16[64,128,128]{2,1,0:T(8,128)(2,1)} %param.10, f32[64,128,128]{2,1,0:T(8,128)} %shard_map.100, f32[64,128]{1,0:T(8,128)S(1)} %add_rsqrt_fusion, f32[64,128]{1,0:T(8,128)S(1)} %broadcast_multiply_fusion, bf16[512,128]{1,0:T(8,128)(2,1)S(1)} %copy-done.8, bf16[128,512]{1,0:T(8,128)(2,1)S(1)} %copy-done.9), kind=kOutput, calls=%fused_computation.18 | convolution fusion | flops 2191523840 | bytes 8716288 | tf_op jit(solution)/shard_map/dot_general | solution.py:112
  140.6 3.9 %collective-permute-start.4 = (bf16[1,128,128]{2,1,0:T(8,128)(2,1)S(1)}, bf16[1,128,128]{2,1,0:T(8,128)(2,1)S(1)}, u32[]{:S(2)}, u32[]{:S(2)}) collective-permute-start(bf16[1,128,128]{2,1,0:T(8,128)(2,1)S(1)} %get-tuple-element.23), channel_id=1, source_target_pairs={{0,4},{4,8},{8,12},{12,16},{16,20},{20,24},{24,28},{1,5},{5,9},{9,... | collective-permute-start | bytes 98312 | tf_op jit(solution)/shard_map/ppermute | solution.py:16
  144.5 1.9 collective-permute-start.5
  146.5 4.2 %collective-permute-done.5 = bf16[1,128,128]{2,1,0:T(8,128)(2,1)S(1)} collective-permute-done((bf16[1,128,128]{2,1,0:T(8,128)(2,1)S(1)}, bf16[1,128,128]{2,1,0:T(8,128)(2,1)S(1)}, u32[]{:S(2)}, u32[]{:S(2)}) %collective-permute-start.5) | collective-permute-done | bytes 32800 | tf_op jit(solution)/shard_map/ppermute | solution.py:19
  150.7 3.2 %collective-permute-start.6 = (bf16[66,1,128]{2,1,0:T(2,128)(2,1)S(1)}, bf16[66,1,128]{2,1,0:T(2,128)(2,1)S(1)}, u32[]{:S(2)}, u32[]{:S(2)}) collective-permute-start(bf16[66,1,128]{2,1,0:T(2,128)(2,1)S(1)} %get-tuple-element.19), channel_id=1, source_target_pairs={{0,1},{1,2},{2,3},{4,5},{5,6},{6,7},{8,9},{9,10},{10,11},{12,13},{... | collective-permute-start | bytes 50696 | tf_op jit(solution)/shard_map/ppermute | solution.py:16
  153.9 1.5 collective-permute-start.7
  155.4 3.2 %collective-permute-done.7 = bf16[66,1,128]{2,1,0:T(2,128)(2,1)S(1)} collective-permute-done((bf16[66,1,128]{2,1,0:T(2,128)(2,1)S(1)}, bf16[66,1,128]{2,1,0:T(2,128)(2,1)S(1)}, u32[]{:S(2)}, u32[]{:S(2)}) %collective-permute-start.7) | collective-permute-done | bytes 16928 | tf_op jit(solution)/shard_map/ppermute | solution.py:19
  158.6 0.8 maximum_convert_fusion.1
  159.5 0.6 fusion.71
  160.0 0.6 fusion.72
  160.6 1.6 fusion.22
  162.2 0.6 fusion.78
  162.8 0.5 fusion.51
  163.3 0.3 copy-done.5
  163.6 0.4 convolution_convert_fusion
  164.1 3.3 %collective-permute-start.8 = (bf16[7,64,256]{2,1,0:T(8,128)(2,1)S(1)}, bf16[7,64,256]{2,1,0:T(8,128)(2,1)S(1)}, u32[]{:S(2)}, u32[]{:S(2)}) collective-permute-start(bf16[7,64,256]{2,1,0:T(8,128)(2,1)S(1)} %get-tuple-element.35), channel_id=1, source_target_pairs={{0,4},{4,8},{8,12},{12,16},{16,20},{20,24},{24,28},{1,5},{5,9},{9,... | collective-permute-start | bytes 688136 | tf_op jit(solution)/shard_map/ppermute | solution.py:16
  167.5 1.9 collective-permute-start.9
  169.4 2.2 collective-permute-done.8
  171.7 4.0 %collective-permute-done.9 = bf16[7,64,256]{2,1,0:T(8,128)(2,1)S(1)} collective-permute-done((bf16[7,64,256]{2,1,0:T(8,128)(2,1)S(1)}, bf16[7,64,256]{2,1,0:T(8,128)(2,1)S(1)}, u32[]{:S(2)}, u32[]{:S(2)}) %collective-permute-start.9) | collective-permute-done | bytes 229408 | tf_op jit(solution)/shard_map/ppermute | solution.py:19
  175.8 3.2 %collective-permute-start.10 = (bf16[46,7,256]{2,1,0:T(8,128)(2,1)S(1)}, bf16[46,7,256]{2,1,0:T(8,128)(2,1)S(1)}, u32[]{:S(2)}, u32[]{:S(2)}) collective-permute-start(bf16[46,7,256]{2,1,0:T(8,128)(2,1)S(1)} %get-tuple-element.27), channel_id=1, source_target_pairs={{0,1},{1,2},{2,3},{4,5},{5,6},{6,7},{8,9},{9,10},{10,11},{12,13},{... | collective-permute-start | bytes 494600 | tf_op jit(solution)/shard_map/ppermute | solution.py:16
  179.0 1.3 collective-permute-start.11
  180.3 0.1 fusion.60
  180.4 1.1 collective-permute-done.10
  181.5 4.1 %collective-permute-done.11 = bf16[46,7,256]{2,1,0:T(8,128)(2,1)S(1)} collective-permute-done((bf16[46,7,256]{2,1,0:T(8,128)(2,1)S(1)}, bf16[46,7,256]{2,1,0:T(8,128)(2,1)S(1)}, u32[]{:S(2)}, u32[]{:S(2)}) %collective-permute-start.11) | collective-permute-done | bytes 164896 | tf_op jit(solution)/shard_map/ppermute | solution.py:19
  185.6 2.5 maximum_convert_fusion.2.x_ref
  188.1 1.4 broadcast_in_dim.5.k_ref
  189.5 51.0 %shard_map.101 = f32[32,64,256]{2,1,0:T(8,128)} custom-call(f32[46,78,256]{2,1,0:T(8,128)} %maximum_convert_fusion.2.x_ref, f32[15,15,8,256]{3,2,1,0:T(8,128)} %broadcast_in_dim.5.k_ref), custom_call_target="tpu_custom_call" | custom-call | flops 235929600 | bytes 5771264 | tf_op jit(solution)/shard_map/pallas_call | solution.py:88
  240.4 2.1 reduce_sum.38
  242.5 0.1 copy-done.1
  242.7 0.6 multiply_reduce_fusion.1
  243.3 5.4 %add_convert_fusion.1 = bf16[32,64,256]{2,1,0:T(8,128)(2,1)} fusion(bf16[32,64,256]{2,1,0:T(8,128)(2,1)} %copy-done.2, f32[32,64,256]{2,1,0:T(8,128)S(1)} %copy-done.1, f32[32,64]{1,0:T(8,128)S(1)} %add_rsqrt_fusion.1, f32[32,64]{1,0:T(8,128)S(1)} %broadcast_multiply_fusion.1, bf16[1024,256]{1,0:T(8,128)(2,1)S(1)} %copy-done, ...), kind=kOutput, calls=%fused_computation.33 | convolution fusion | flops 2169503744 | bytes 5259264 | tf_op jit(solution)/shard_map/dot_general | solution.py:112
  248.7 0.8 fusion.82
  249.5 2.9 %collective-permute-start.12 = (bf16[1,64,256]{2,1,0:T(8,128)(2,1)S(1)}, bf16[1,64,256]{2,1,0:T(8,128)(2,1)S(1)}, u32[]{:S(2)}, u32[]{:S(2)}) collective-permute-start(bf16[1,64,256]{2,1,0:T(8,128)(2,1)S(1)} %get-tuple-element.33), channel_id=1, source_target_pairs={{0,4},{4,8},{8,12},{12,16},{16,20},{20,24},{24,28},{1,5},{5,9},{9,... | collective-permute-start | bytes 98312 | tf_op jit(solution)/shard_map/ppermute | solution.py:16
  252.3 1.9 collective-permute-start.13
  254.3 4.2 %collective-permute-done.13 = bf16[1,64,256]{2,1,0:T(8,128)(2,1)S(1)} collective-permute-done((bf16[1,64,256]{2,1,0:T(8,128)(2,1)S(1)}, bf16[1,64,256]{2,1,0:T(8,128)(2,1)S(1)}, u32[]{:S(2)}, u32[]{:S(2)}) %collective-permute-start.13) | collective-permute-done | bytes 32800 | tf_op jit(solution)/shard_map/ppermute | solution.py:19
  258.5 1.0 pad_maximum_fusion.5
  259.5 1.6 collective-permute-start.14
  261.1 1.3 collective-permute-start.15
  262.4 3.4 %collective-permute-done.15 = bf16[34,1,256]{2,1,0:T(2,128)(2,1)S(1)} collective-permute-done((bf16[34,1,256]{2,1,0:T(2,128)(2,1)S(1)}, bf16[34,1,256]{2,1,0:T(2,128)(2,1)S(1)}, u32[]{:S(2)}, u32[]{:S(2)}) %collective-permute-start.15) | collective-permute-done | bytes 17440 | tf_op jit(solution)/shard_map/ppermute | solution.py:19
  265.8 1.8 maximum_convert_fusion.3
  267.6 0.4 fusion.75
  268.0 0.2 fusion.76
  268.2 0.2 fusion.77
  268.4 1.4 fusion.32
  269.8 0.3 fusion.81
  270.1 0.2 fusion.52
  270.3 0.8 copy.20
  (36 shorter events, 0.4 us)
Async XLA Ops:
  0.0 243.3 %copy-start = (bf16[1024,256]{1,0:T(8,128)(2,1)S(1)}, bf16[1024,256]{1,0:T(8,128)(2,1)}, u32[]{:S(2)}) copy-start(bf16[1024,256]{1,0:T(8,128)(2,1)} %param.19) | copy-start | bytes 1572868
  1.1 6.6 %collective-permute-start = (bf16[7,128,128]{2,1,0:T(8,128)(2,1)S(1)}, bf16[7,128,128]{2,1,0:T(8,128)(2,1)S(1)}, u32[]{:S(2)}, u32[]{:S(2)}) collective-permute-start(bf16[7,128,128]{2,1,0:T(8,128)(2,1)S(1)} %get-tuple-element.26), channel_id=1, source_target_pairs={{0,4},{4,8},{8,12},{12,16},{16,20},{20,24},{24,28},{1,5},{5,9},{9,... | collective-permute-start | bytes 688136 | tf_op jit(solution)/shard_map/ppermute | solution.py:16
  4.8 8.2 %collective-permute-start.1 = (bf16[7,128,128]{2,1,0:T(8,128)(2,1)S(1)}, bf16[7,128,128]{2,1,0:T(8,128)(2,1)S(1)}, u32[]{:S(2)}, u32[]{:S(2)}) collective-permute-start(bf16[7,128,128]{2,1,0:T(8,128)(2,1)S(1)} %get-tuple-element.25), channel_id=1, source_target_pairs={{4,0},{8,4},{12,8},{16,12},{20,16},{24,20},{28,24},{5,1},{9,5},{13... | collective-permute-start | bytes 688136 | tf_op jit(solution)/shard_map/ppermute | solution.py:19
  7.8 9.9 %copy-start.4 = (f32[15,15,128]{2,1,0:T(8,128)S(1)}, f32[15,15,128]{2,1,0:T(8,128)}, u32[]{:S(2)}) copy-start(f32[15,15,128]{2,1,0:T(8,128)} %param.11) | copy-start | bytes 345604
  13.2 5.7 %collective-permute-start.2 = (bf16[78,7,128]{2,1,0:T(8,128)(2,1)S(1)}, bf16[78,7,128]{2,1,0:T(8,128)(2,1)S(1)}, u32[]{:S(2)}, u32[]{:S(2)}) collective-permute-start(bf16[78,7,128]{2,1,0:T(8,128)(2,1)S(1)} %get-tuple-element.11), channel_id=1, source_target_pairs={{0,1},{1,2},{2,3},{4,5},{5,6},{6,7},{8,9},{9,10},{10,11},{12,13},{... | collective-permute-start | bytes 419336 | tf_op jit(solution)/shard_map/ppermute | solution.py:16
  16.4 6.6 %collective-permute-start.3 = (bf16[78,7,128]{2,1,0:T(8,128)(2,1)S(1)}, bf16[78,7,128]{2,1,0:T(8,128)(2,1)S(1)}, u32[]{:S(2)}, u32[]{:S(2)}) collective-permute-start(bf16[78,7,128]{2,1,0:T(8,128)(2,1)S(1)} %get-tuple-element.12), channel_id=1, source_target_pairs={{1,0},{2,1},{3,2},{5,4},{6,5},{7,6},{9,8},{10,9},{11,10},{13,12},{... | collective-permute-start | bytes 419336 | tf_op jit(solution)/shard_map/ppermute | solution.py:19
  127.6 4.1 %copy-start.8 = (bf16[512,128]{1,0:T(8,128)(2,1)S(1)}, bf16[512,128]{1,0:T(8,128)(2,1)}, u32[]{:S(2)}) copy-start(bf16[512,128]{1,0:T(8,128)(2,1)} %param.14) | copy-start | bytes 393220
  127.6 4.1 %copy-start.9 = (bf16[128,512]{1,0:T(8,128)(2,1)S(1)}, bf16[128,512]{1,0:T(8,128)(2,1)}, u32[]{:S(2)}) copy-start(bf16[128,512]{1,0:T(8,128)(2,1)} %param.13) | copy-start | bytes 393220
  140.6 5.8 %collective-permute-start.4 = (bf16[1,128,128]{2,1,0:T(8,128)(2,1)S(1)}, bf16[1,128,128]{2,1,0:T(8,128)(2,1)S(1)}, u32[]{:S(2)}, u32[]{:S(2)}) collective-permute-start(bf16[1,128,128]{2,1,0:T(8,128)(2,1)S(1)} %get-tuple-element.23), channel_id=1, source_target_pairs={{0,4},{4,8},{8,12},{12,16},{16,20},{20,24},{24,28},{1,5},{5,9},{9,... | collective-permute-start | bytes 98312 | tf_op jit(solution)/shard_map/ppermute | solution.py:16
  144.5 6.1 %collective-permute-start.5 = (bf16[1,128,128]{2,1,0:T(8,128)(2,1)S(1)}, bf16[1,128,128]{2,1,0:T(8,128)(2,1)S(1)}, u32[]{:S(2)}, u32[]{:S(2)}) collective-permute-start(bf16[1,128,128]{2,1,0:T(8,128)(2,1)S(1)} %get-tuple-element.24), channel_id=1, source_target_pairs={{4,0},{8,4},{12,8},{16,12},{20,16},{24,20},{28,24},{5,1},{9,5},{13... | collective-permute-start | bytes 98312 | tf_op jit(solution)/shard_map/ppermute | solution.py:19
  150.7 4.7 %collective-permute-start.6 = (bf16[66,1,128]{2,1,0:T(2,128)(2,1)S(1)}, bf16[66,1,128]{2,1,0:T(2,128)(2,1)S(1)}, u32[]{:S(2)}, u32[]{:S(2)}) collective-permute-start(bf16[66,1,128]{2,1,0:T(2,128)(2,1)S(1)} %get-tuple-element.19), channel_id=1, source_target_pairs={{0,1},{1,2},{2,3},{4,5},{5,6},{6,7},{8,9},{9,10},{10,11},{12,13},{... | collective-permute-start | bytes 50696 | tf_op jit(solution)/shard_map/ppermute | solution.py:16
  153.9 4.7 %collective-permute-start.7 = (bf16[66,1,128]{2,1,0:T(2,128)(2,1)S(1)}, bf16[66,1,128]{2,1,0:T(2,128)(2,1)S(1)}, u32[]{:S(2)}, u32[]{:S(2)}) collective-permute-start(bf16[66,1,128]{2,1,0:T(2,128)(2,1)S(1)} %get-tuple-element.20), channel_id=1, source_target_pairs={{1,0},{2,1},{3,2},{5,4},{6,5},{7,6},{9,8},{10,9},{11,10},{13,12},{... | collective-permute-start | bytes 50696 | tf_op jit(solution)/shard_map/ppermute | solution.py:19
  162.8 0.8 copy-start.5
  162.8 6.6 %copy-start.6 = (f32[256]{0:T(256)S(1)}, f32[256]{0:T(256)}, u32[]{:S(2)}) copy-start(f32[256]{0:T(256)} %param.17) | copy-start | bytes 3076
  163.6 16.6 %copy-start.3 = (f32[15,15,256]{2,1,0:T(8,128)S(1)}, f32[15,15,256]{2,1,0:T(8,128)}, u32[]{:S(2)}) copy-start(f32[15,15,256]{2,1,0:T(8,128)} %param.16) | copy-start | bytes 691204
  164.1 24.0 %copy-start.2 = (bf16[32,64,256]{2,1,0:T(8,128)(2,1)}, bf16[32,64,256]{2,1,0:T(8,128)(2,1)S(1)}, u32[]{:S(2)}) copy-start(bf16[32,64,256]{2,1,0:T(8,128)(2,1)S(1)} %convolution_convert_fusion) | copy-start | bytes 3145732
  164.1 7.5 %collective-permute-start.8 = (bf16[7,64,256]{2,1,0:T(8,128)(2,1)S(1)}, bf16[7,64,256]{2,1,0:T(8,128)(2,1)S(1)}, u32[]{:S(2)}, u32[]{:S(2)}) collective-permute-start(bf16[7,64,256]{2,1,0:T(8,128)(2,1)S(1)} %get-tuple-element.35), channel_id=1, source_target_pairs={{0,4},{4,8},{8,12},{12,16},{16,20},{20,24},{24,28},{1,5},{5,9},{9,... | collective-permute-start | bytes 688136 | tf_op jit(solution)/shard_map/ppermute | solution.py:16
  167.5 8.2 %collective-permute-start.9 = (bf16[7,64,256]{2,1,0:T(8,128)(2,1)S(1)}, bf16[7,64,256]{2,1,0:T(8,128)(2,1)S(1)}, u32[]{:S(2)}, u32[]{:S(2)}) collective-permute-start(bf16[7,64,256]{2,1,0:T(8,128)(2,1)S(1)} %get-tuple-element.36), channel_id=1, source_target_pairs={{4,0},{8,4},{12,8},{16,12},{20,16},{24,20},{28,24},{5,1},{9,5},{13... | collective-permute-start | bytes 688136 | tf_op jit(solution)/shard_map/ppermute | solution.py:19
  175.8 5.7 %collective-permute-start.10 = (bf16[46,7,256]{2,1,0:T(8,128)(2,1)S(1)}, bf16[46,7,256]{2,1,0:T(8,128)(2,1)S(1)}, u32[]{:S(2)}, u32[]{:S(2)}) collective-permute-start(bf16[46,7,256]{2,1,0:T(8,128)(2,1)S(1)} %get-tuple-element.27), channel_id=1, source_target_pairs={{0,1},{1,2},{2,3},{4,5},{5,6},{6,7},{8,9},{9,10},{10,11},{12,13},{... | collective-permute-start | bytes 494600 | tf_op jit(solution)/shard_map/ppermute | solution.py:16
  179.0 6.6 %collective-permute-start.11 = (bf16[46,7,256]{2,1,0:T(8,128)(2,1)S(1)}, bf16[46,7,256]{2,1,0:T(8,128)(2,1)S(1)}, u32[]{:S(2)}, u32[]{:S(2)}) collective-permute-start(bf16[46,7,256]{2,1,0:T(8,128)(2,1)S(1)} %get-tuple-element.28), channel_id=1, source_target_pairs={{1,0},{2,1},{3,2},{5,4},{6,5},{7,6},{9,8},{10,9},{11,10},{13,12},{... | collective-permute-start | bytes 494600 | tf_op jit(solution)/shard_map/ppermute | solution.py:19
  240.4 2.2 copy-start.1
  240.4 2.9 %copy-start.7 = (bf16[256,1024]{1,0:T(8,128)(2,1)S(1)}, bf16[256,1024]{1,0:T(8,128)(2,1)}, u32[]{:S(2)}) copy-start(bf16[256,1024]{1,0:T(8,128)(2,1)} %param.18) | copy-start | bytes 1572868
  249.5 4.8 %collective-permute-start.12 = (bf16[1,64,256]{2,1,0:T(8,128)(2,1)S(1)}, bf16[1,64,256]{2,1,0:T(8,128)(2,1)S(1)}, u32[]{:S(2)}, u32[]{:S(2)}) collective-permute-start(bf16[1,64,256]{2,1,0:T(8,128)(2,1)S(1)} %get-tuple-element.33), channel_id=1, source_target_pairs={{0,4},{4,8},{8,12},{12,16},{16,20},{20,24},{24,28},{1,5},{5,9},{9,... | collective-permute-start | bytes 98312 | tf_op jit(solution)/shard_map/ppermute | solution.py:16
  252.3 6.1 %collective-permute-start.13 = (bf16[1,64,256]{2,1,0:T(8,128)(2,1)S(1)}, bf16[1,64,256]{2,1,0:T(8,128)(2,1)S(1)}, u32[]{:S(2)}, u32[]{:S(2)}) collective-permute-start(bf16[1,64,256]{2,1,0:T(8,128)(2,1)S(1)} %get-tuple-element.34), channel_id=1, source_target_pairs={{4,0},{8,4},{12,8},{16,12},{20,16},{24,20},{28,24},{5,1},{9,5},{13... | collective-permute-start | bytes 98312 | tf_op jit(solution)/shard_map/ppermute | solution.py:19
  259.5 2.9 %collective-permute-start.14 = (bf16[34,1,256]{2,1,0:T(2,128)(2,1)S(1)}, bf16[34,1,256]{2,1,0:T(2,128)(2,1)S(1)}, u32[]{:S(2)}, u32[]{:S(2)}) collective-permute-start(bf16[34,1,256]{2,1,0:T(2,128)(2,1)S(1)} %get-tuple-element.29), channel_id=1, source_target_pairs={{0,1},{1,2},{2,3},{4,5},{5,6},{6,7},{8,9},{9,10},{10,11},{12,13},{... | collective-permute-start | bytes 52232 | tf_op jit(solution)/shard_map/ppermute | solution.py:16
  261.1 4.7 %collective-permute-start.15 = (bf16[34,1,256]{2,1,0:T(2,128)(2,1)S(1)}, bf16[34,1,256]{2,1,0:T(2,128)(2,1)S(1)}, u32[]{:S(2)}, u32[]{:S(2)}) collective-permute-start(bf16[34,1,256]{2,1,0:T(2,128)(2,1)S(1)} %get-tuple-element.30), channel_id=1, source_target_pairs={{1,0},{2,1},{3,2},{5,4},{6,5},{7,6},{9,8},{10,9},{11,10},{13,12},{... | collective-permute-start | bytes 52232 | tf_op jit(solution)/shard_map/ppermute | solution.py:19

commit v8 on v7

--- a/solution.py
+++ b/solution.py
@@ -28,7 +28,7 @@
     return (raw * mask).astype(jnp.bfloat16)
 
 
-def _dw_body(x_ref, k_ref, o_ref, xs_ref, *, taps, rows, cols, chans, rb):
+def _dw_body(x_ref, k_ref, w_in_ref, w_out_ref, y_ref, o_ref, xs_ref, *, taps, rows, cols, chans, rb):
     nlb = chans // 128
     njb = cols // 8
     nrb = rows // rb
@@ -76,41 +76,50 @@
                 lax.fori_loop(0, nrb * njb, body, 0, unroll=2)
             first = False
 
+    er = 2
+    half = (taps - 1) // 2
 
-def depthwise(extended, kernel):
+    def epilogue(i, c):
+        r0 = pl.multiple_of(i * er, er)
+        d = o_ref[pl.ds(r0, er)].reshape(er * cols, chans)
+        mean = jnp.mean(d, axis=-1, keepdims=True)
+        var = jnp.mean((d - mean) ** 2, axis=-1, keepdims=True)
+        normed = ((d - mean) * lax.rsqrt(var + 1e-06)).astype(jnp.bfloat16)
+        hidden = jnp.dot(normed, w_in_ref[...], preferred_element_type=jnp.float32)
+        hidden = jax.nn.gelu(hidden).astype(jnp.bfloat16)
+        mixed = jnp.dot(hidden, w_out_ref[...], preferred_element_type=jnp.float32)
+        field = x_ref[pl.ds(r0 + half, er), pl.ds(half, cols), :].reshape(er * cols, chans)
+        y_ref[pl.ds(r0, er)] = (field + mixed).astype(y_ref.dtype).reshape(er, cols, chans)
+        return c
+
+    lax.fori_loop(0, rows // er, epilogue, 0)
+
+
+def local_section(extended, raw, sigma, w_in, w_out):
+    kernel = masked_kernel(raw, sigma)
     taps = kernel.shape[0]
     rows = extended.shape[0] - taps + 1
     cols = extended.shape[1] - taps + 1
     chans = extended.shape[2]
+    hid = w_in.shape[1]
     kb = jnp.broadcast_to(kernel.astype(jnp.float32)[:, :, None, :], (taps, taps, 8, chans))
     body = functools.partial(_dw_body, taps=taps, rows=rows, cols=cols, chans=chans, rb=8)
     vmem = pl.BlockSpec(memory_space=pltpu.VMEM)
     return pl.pallas_call(
         body,
-        out_shape=jax.ShapeDtypeStruct((rows, cols, chans), jnp.float32),
-        in_specs=[vmem, vmem],
+        out_shape=jax.ShapeDtypeStruct((rows, cols, chans), jnp.bfloat16),
+        in_specs=[vmem, vmem, vmem, vmem],
         out_specs=vmem,
-        scratch_shapes=[pltpu.VMEM((extended.shape[0], cols + 8, chans), jnp.float32)],
+        scratch_shapes=[
+            pltpu.VMEM((rows, cols, chans), jnp.float32),
+            pltpu.VMEM((extended.shape[0], cols + 8, chans), jnp.float32),
+        ],
         cost_estimate=pl.CostEstimate(
-            flops=2 * rows * cols * chans * taps * taps,
-            transcendentals=0,
-            bytes_accessed=extended.size * 4 + rows * cols * chans * 4,
+            flops=2 * rows * cols * chans * (taps * taps + 2 * hid),
+            transcendentals=rows * cols * hid,
+            bytes_accessed=extended.size * 4 + rows * cols * chans * 2,
         ),
-    )(extended.astype(jnp.float32), kb)
-
-
-def local_section(extended, raw, sigma, w_in, w_out):
-    kernel = masked_kernel(raw, sigma)
-    conv_out = depthwise(extended, kernel)
-    field = extended[7 : extended.shape[0] - 7, 7 : extended.shape[1] - 7]
-    mean = jnp.mean(conv_out, axis=-1, keepdims=True)
-    var = jnp.mean((conv_out - mean) ** 2, axis=-1, keepdims=True)
-    normed = ((conv_out - mean) * lax.rsqrt(var + 1e-06)).astype(jnp.bfloat16)
-    hidden = jax.nn.gelu(jnp.dot(normed, w_in, preferred_element_type=jnp.float32)).astype(
-        jnp.bfloat16
-    )
-    mixed = jnp.dot(hidden, w_out, preferred_element_type=jnp.float32)
-    return (field.astype(jnp.float32) + mixed).astype(jnp.bfloat16)
+    )(extended.astype(jnp.float32), kb, w_in, w_out)
 
 
 def blur_down(padded):

time: 272 us -> 276 us (1.015)
  Pallas kernels: 148 us -> 175 us
  matrix products: 14.7 us -> 0.43 us
  other arithmetic: 24.6 us -> 15.5 us
    pallas_call x2, Pallas kernels: 148 us -> 175 us  [local_section(): pl.pallas_call(body, out_shape=jax.ShapeDtypeStruct((rows, cols, chans),...]
    dot_general x2 -> x0, matrix products: 14.3 us -> none  [local_section(): mixed = jnp.dot(hidden, w_out, preferred_element_type=jnp.float32)]
    reduce_sum x4 -> x0, other arithmetic: 10.1 us -> none  [the longest x2 5.42 us: local_section(): mean = jnp.mean(conv_out, axis=-1, keepdims=True)]
where the time goes in v8:
time: 276 us
  Pallas kernels  175 us (63%)
  starting transfers between devices  38 us (14%)
  waiting for transfers between devices  35.2 us (13%)
  other arithmetic  15.5 us (6%)
  local copies, waits for them, and re-layouts  11 us (4%)
    pallas_call x2, Pallas kernels, local_section(): pl.pallas_call(body, out_shape=jax.ShapeDtypeStruct((rows, cols, chans),...  175 us
    ppermute x8, waiting for transfers between devices, padded_2(): lax.ppermute(lax.slice_in_dim(block, 0, width, axis=dim), axis, backward)  30.6 us
    ppermute x8, starting transfers between devices, padded_2(): lax.ppermute(lax.slice_in_dim(block, block.shape[dim] - width, None, axis...  25 us
    ppermute x8, starting transfers between devices, padded_2(): lax.ppermute(lax.slice_in_dim(block, 0, width, axis=dim), axis, backward)  13 us
    convert_element_type x2, other arithmetic, local_section(): extended.astype(jnp.float32)  6.08 us
  transfers between devices with their start and end apart: 16, of which 12 were waited for; matrix products, arithmetic and copies ran while one was open for 1% of the time, Pallas kernels for 0%

profile of v8, /device:TPU:3, one launch (start us, length us, event | category | flops | bytes accessed | tf_op | source)
XLA Modules:
  0.0 275.8 jit_solution(9886459938136917564)
XLA Ops:
  0.0 1.1 fusion.35
  1.1 3.7 %collective-permute-start = (bf16[7,128,128]{2,1,0:T(8,128)(2,1)S(1)}, bf16[7,128,128]{2,1,0:T(8,128)(2,1)S(1)}, u32[]{:S(2)}, u32[]{:S(2)}) collective-permute-start(bf16[7,128,128]{2,1,0:T(8,128)(2,1)S(1)} %get-tuple-element.26), channel_id=1, source_target_pairs={{0,4},{4,8},{8,12},{12,16},{16,20},{20,24},{24,28},{1,5},{5,9},{9,... | collective-permute-start | bytes 688136 | tf_op jit(solution)/shard_map/ppermute | solution.py:16
  4.8 1.9 collective-permute-start.1
  6.7 0.7 multiply_multiply_fusion.1
  7.4 0.1 add_negate_fusion
  7.5 0.3 collective-permute-done
  7.8 0.0 copy-start.3
  7.8 2.0 constant_dynamic-update-slice_fusion.1
  9.8 3.2 %collective-permute-done.1 = bf16[7,128,128]{2,1,0:T(8,128)(2,1)S(1)} collective-permute-done((bf16[7,128,128]{2,1,0:T(8,128)(2,1)S(1)}, bf16[7,128,128]{2,1,0:T(8,128)(2,1)S(1)}, u32[]{:S(2)}, u32[]{:S(2)}) %collective-permute-start.1) | collective-permute-done | bytes 229408 | tf_op jit(solution)/shard_map/ppermute | solution.py:19
  13.1 0.1 fusion.29
  13.2 3.2 %collective-permute-start.2 = (bf16[78,7,128]{2,1,0:T(8,128)(2,1)S(1)}, bf16[78,7,128]{2,1,0:T(8,128)(2,1)S(1)}, u32[]{:S(2)}, u32[]{:S(2)}) collective-permute-start(bf16[78,7,128]{2,1,0:T(8,128)(2,1)S(1)} %get-tuple-element.11), channel_id=1, source_target_pairs={{0,1},{1,2},{2,3},{4,5},{5,6},{6,7},{8,9},{9,10},{10,11},{12,13},{... | collective-permute-start | bytes 419336 | tf_op jit(solution)/shard_map/ppermute | solution.py:16
  16.4 1.3 collective-permute-start.3
  17.7 0.1 fusion.25
  17.8 1.1 collective-permute-done.2
  18.9 4.1 %collective-permute-done.3 = bf16[78,7,128]{2,1,0:T(8,128)(2,1)S(1)} collective-permute-done((bf16[78,7,128]{2,1,0:T(8,128)(2,1)S(1)}, bf16[78,7,128]{2,1,0:T(8,128)(2,1)S(1)}, u32[]{:S(2)}, u32[]{:S(2)}) %collective-permute-start.3) | collective-permute-done | bytes 139808 | tf_op jit(solution)/shard_map/ppermute | solution.py:19
  23.0 3.6 %maximum_convert_fusion.x_ref = f32[78,142,128]{2,1,0:T(8,128)} fusion(bf16[78,7,128]{2,1,0:T(8,128)(2,1)S(1)} %collective-permute-done.3, bf16[78,128,128]{2,1,0:T(8,128)(2,1)S(1)} %constant_dynamic-update-slice_fusion, bf16[78,7,128]{2,1,0:T(8,128)(2,1)S(1)} %collective-permute-done.2), kind=kLoop, calls=%fused_computation | loop fusion | flops 8506368 | bytes 8506368 | tf_op jit(solution)/shard_map/convert_element_type | solution.py:122
  26.6 1.0 broadcast_in_dim.4.k_ref
  27.6 115.1 %shard_map.100 = bf16[64,128,128]{2,1,0:T(8,128)(2,1)} custom-call(f32[78,142,128]{2,1,0:T(8,128)} %maximum_convert_fusion.x_ref, f32[15,15,8,128]{3,2,1,0:T(8,128)} %broadcast_in_dim.4.k_ref, bf16[128,512]{1,0:T(8,128)(2,1)} %w_in_ref.2, bf16[512,128]{1,0:T(8,128)(2,1)} %w_out_ref.2), custom_call_target="tpu_custom_call" | custom-call | flops 2619342848 | bytes 7768064 | tf_op jit(solution)/shard_map/pallas_call | solution.py:108
  142.8 0.9 fusion.34
  143.7 3.9 %collective-permute-start.4 = (bf16[1,128,128]{2,1,0:T(8,128)(2,1)S(1)}, bf16[1,128,128]{2,1,0:T(8,128)(2,1)S(1)}, u32[]{:S(2)}, u32[]{:S(2)}) collective-permute-start(bf16[1,128,128]{2,1,0:T(8,128)(2,1)S(1)} %get-tuple-element.23), channel_id=1, source_target_pairs={{0,4},{4,8},{8,12},{12,16},{16,20},{20,24},{24,28},{1,5},{5,9},{9,... | collective-permute-start | bytes 98312 | tf_op jit(solution)/shard_map/ppermute | solution.py:16
  147.6 1.9 collective-permute-start.5
  149.5 4.2 %collective-permute-done.5 = bf16[1,128,128]{2,1,0:T(8,128)(2,1)S(1)} collective-permute-done((bf16[1,128,128]{2,1,0:T(8,128)(2,1)S(1)}, bf16[1,128,128]{2,1,0:T(8,128)(2,1)S(1)}, u32[]{:S(2)}, u32[]{:S(2)}) %collective-permute-start.5) | collective-permute-done | bytes 32800 | tf_op jit(solution)/shard_map/ppermute | solution.py:19
  153.7 1.0 pad_maximum_fusion.8
  154.8 3.2 %collective-permute-start.6 = (bf16[66,1,128]{2,1,0:T(2,128)(2,1)S(1)}, bf16[66,1,128]{2,1,0:T(2,128)(2,1)S(1)}, u32[]{:S(2)}, u32[]{:S(2)}) collective-permute-start(bf16[66,1,128]{2,1,0:T(2,128)(2,1)S(1)} %get-tuple-element.19), channel_id=1, source_target_pairs={{0,1},{1,2},{2,3},{4,5},{5,6},{6,7},{8,9},{9,10},{10,11},{12,13},{... | collective-permute-start | bytes 50696 | tf_op jit(solution)/shard_map/ppermute | solution.py:16
  158.0 1.3 collective-permute-start.7
  159.3 3.4 %collective-permute-done.7 = bf16[66,1,128]{2,1,0:T(2,128)(2,1)S(1)} collective-permute-done((bf16[66,1,128]{2,1,0:T(2,128)(2,1)S(1)}, bf16[66,1,128]{2,1,0:T(2,128)(2,1)S(1)}, u32[]{:S(2)}, u32[]{:S(2)}) %collective-permute-start.7) | collective-permute-done | bytes 16928 | tf_op jit(solution)/shard_map/ppermute | solution.py:19
  162.6 0.9 maximum_convert_fusion.1
  163.5 0.6 fusion.26
  164.1 0.6 fusion.27
  164.7 1.6 fusion.1
  166.2 0.6 fusion.33
  166.8 0.5 fusion.17
  167.4 0.0 copy-start.4
  167.4 0.0 copy-start.2
  167.4 0.4 convolution_convert_fusion
  167.9 3.3 %collective-permute-start.8 = (bf16[7,64,256]{2,1,0:T(8,128)(2,1)S(1)}, bf16[7,64,256]{2,1,0:T(8,128)(2,1)S(1)}, u32[]{:S(2)}, u32[]{:S(2)}) collective-permute-start(bf16[7,64,256]{2,1,0:T(8,128)(2,1)S(1)} %get-tuple-element.35), channel_id=1, source_target_pairs={{0,4},{4,8},{8,12},{12,16},{16,20},{20,24},{24,28},{1,5},{5,9},{9,... | collective-permute-start | bytes 688136 | tf_op jit(solution)/shard_map/ppermute | solution.py:16
  171.2 1.9 collective-permute-start.9
  173.2 2.2 collective-permute-done.8
  175.4 4.0 %collective-permute-done.9 = bf16[7,64,256]{2,1,0:T(8,128)(2,1)S(1)} collective-permute-done((bf16[7,64,256]{2,1,0:T(8,128)(2,1)S(1)}, bf16[7,64,256]{2,1,0:T(8,128)(2,1)S(1)}, u32[]{:S(2)}, u32[]{:S(2)}) %collective-permute-start.9) | collective-permute-done | bytes 229408 | tf_op jit(solution)/shard_map/ppermute | solution.py:19
  179.4 0.1 pad_maximum_fusion.2
  179.5 3.2 %collective-permute-start.10 = (bf16[46,7,256]{2,1,0:T(8,128)(2,1)S(1)}, bf16[46,7,256]{2,1,0:T(8,128)(2,1)S(1)}, u32[]{:S(2)}, u32[]{:S(2)}) collective-permute-start(bf16[46,7,256]{2,1,0:T(8,128)(2,1)S(1)} %get-tuple-element.27), channel_id=1, source_target_pairs={{0,1},{1,2},{2,3},{4,5},{5,6},{6,7},{8,9},{9,10},{10,11},{12,13},{... | collective-permute-start | bytes 494600 | tf_op jit(solution)/shard_map/ppermute | solution.py:16
  182.7 1.5 collective-permute-start.11
  184.2 0.1 fusion.23
  184.3 0.9 collective-permute-done.10
  185.2 4.1 %collective-permute-done.11 = bf16[46,7,256]{2,1,0:T(8,128)(2,1)S(1)} collective-permute-done((bf16[46,7,256]{2,1,0:T(8,128)(2,1)S(1)}, bf16[46,7,256]{2,1,0:T(8,128)(2,1)S(1)}, u32[]{:S(2)}, u32[]{:S(2)}) %collective-permute-start.11) | collective-permute-done | bytes 164896 | tf_op jit(solution)/shard_map/ppermute | solution.py:19
  189.4 2.5 maximum_convert_fusion.2.x_ref
  191.8 1.4 broadcast_in_dim.5.k_ref
  193.2 60.1 %shard_map.101 = bf16[32,64,256]{2,1,0:T(8,128)(2,1)} custom-call(f32[46,78,256]{2,1,0:T(8,128)} %maximum_convert_fusion.2.x_ref, f32[15,15,8,256]{3,2,1,0:T(8,128)} %broadcast_in_dim.5.k_ref, bf16[256,1024]{1,0:T(8,128)(2,1)} %w_in_ref.3, bf16[1024,256]{1,0:T(8,128)(2,1)} %w_out_ref.3), custom_call_target="tpu_custom_call" | custom-call | flops 2383413248 | bytes 4722688 | tf_op jit(solution)/shard_map/pallas_call | solution.py:108
  253.4 0.8 fusion.37
  254.1 2.9 %collective-permute-start.12 = (bf16[1,64,256]{2,1,0:T(8,128)(2,1)S(1)}, bf16[1,64,256]{2,1,0:T(8,128)(2,1)S(1)}, u32[]{:S(2)}, u32[]{:S(2)}) collective-permute-start(bf16[1,64,256]{2,1,0:T(8,128)(2,1)S(1)} %get-tuple-element.33), channel_id=1, source_target_pairs={{0,4},{4,8},{8,12},{12,16},{16,20},{20,24},{24,28},{1,5},{5,9},{9,... | collective-permute-start | bytes 98312 | tf_op jit(solution)/shard_map/ppermute | solution.py:16
  257.0 1.9 collective-permute-start.13
  258.9 4.2 %collective-permute-done.13 = bf16[1,64,256]{2,1,0:T(8,128)(2,1)S(1)} collective-permute-done((bf16[1,64,256]{2,1,0:T(8,128)(2,1)S(1)}, bf16[1,64,256]{2,1,0:T(8,128)(2,1)S(1)}, u32[]{:S(2)}, u32[]{:S(2)}) %collective-permute-start.13) | collective-permute-done | bytes 32800 | tf_op jit(solution)/shard_map/ppermute | solution.py:19
  263.1 1.0 pad_maximum_fusion.5
  264.2 1.6 collective-permute-start.14
  265.8 1.3 collective-permute-start.15
  267.1 3.4 %collective-permute-done.15 = bf16[34,1,256]{2,1,0:T(2,128)(2,1)S(1)} collective-permute-done((bf16[34,1,256]{2,1,0:T(2,128)(2,1)S(1)}, bf16[34,1,256]{2,1,0:T(2,128)(2,1)S(1)}, u32[]{:S(2)}, u32[]{:S(2)}) %collective-permute-start.15) | collective-permute-done | bytes 17440 | tf_op jit(solution)/shard_map/ppermute | solution.py:19
  270.5 1.8 maximum_convert_fusion.3
  272.2 0.4 fusion.30
  272.6 0.2 fusion.31
  272.9 0.2 fusion.32
  273.1 1.4 fusion.5
  274.5 0.3 fusion.36
  274.7 0.2 fusion.18
  275.0 0.8 copy.20
  (16 shorter events, 0.1 us)
Async XLA Ops:
  0.0 167.3 %copy-start = (bf16[128,256]{1,0:T(8,128)(2,1)S(1)}, bf16[128,256]{1,0:T(8,128)(2,1)}, u32[]{:S(2)}) copy-start(bf16[128,256]{1,0:T(8,128)(2,1)} %param.15) | copy-start | bytes 196612
  1.1 6.6 %collective-permute-start = (bf16[7,128,128]{2,1,0:T(8,128)(2,1)S(1)}, bf16[7,128,128]{2,1,0:T(8,128)(2,1)S(1)}, u32[]{:S(2)}, u32[]{:S(2)}) collective-permute-start(bf16[7,128,128]{2,1,0:T(8,128)(2,1)S(1)} %get-tuple-element.26), channel_id=1, source_target_pairs={{0,4},{4,8},{8,12},{12,16},{16,20},{20,24},{24,28},{1,5},{5,9},{9,... | collective-permute-start | bytes 688136 | tf_op jit(solution)/shard_map/ppermute | solution.py:16
  4.8 8.2 %collective-permute-start.1 = (bf16[7,128,128]{2,1,0:T(8,128)(2,1)S(1)}, bf16[7,128,128]{2,1,0:T(8,128)(2,1)S(1)}, u32[]{:S(2)}, u32[]{:S(2)}) collective-permute-start(bf16[7,128,128]{2,1,0:T(8,128)(2,1)S(1)} %get-tuple-element.25), channel_id=1, source_target_pairs={{4,0},{8,4},{12,8},{16,12},{20,16},{24,20},{28,24},{5,1},{9,5},{13... | collective-permute-start | bytes 688136 | tf_op jit(solution)/shard_map/ppermute | solution.py:19
  7.8 9.9 %copy-start.3 = (f32[15,15,128]{2,1,0:T(8,128)S(1)}, f32[15,15,128]{2,1,0:T(8,128)}, u32[]{:S(2)}) copy-start(f32[15,15,128]{2,1,0:T(8,128)} %param.11) | copy-start | bytes 345604
  13.2 5.7 %collective-permute-start.2 = (bf16[78,7,128]{2,1,0:T(8,128)(2,1)S(1)}, bf16[78,7,128]{2,1,0:T(8,128)(2,1)S(1)}, u32[]{:S(2)}, u32[]{:S(2)}) collective-permute-start(bf16[78,7,128]{2,1,0:T(8,128)(2,1)S(1)} %get-tuple-element.11), channel_id=1, source_target_pairs={{0,1},{1,2},{2,3},{4,5},{5,6},{6,7},{8,9},{9,10},{10,11},{12,13},{... | collective-permute-start | bytes 419336 | tf_op jit(solution)/shard_map/ppermute | solution.py:16
  16.4 6.6 %collective-permute-start.3 = (bf16[78,7,128]{2,1,0:T(8,128)(2,1)S(1)}, bf16[78,7,128]{2,1,0:T(8,128)(2,1)S(1)}, u32[]{:S(2)}, u32[]{:S(2)}) collective-permute-start(bf16[78,7,128]{2,1,0:T(8,128)(2,1)S(1)} %get-tuple-element.12), channel_id=1, source_target_pairs={{1,0},{2,1},{3,2},{5,4},{6,5},{7,6},{9,8},{10,9},{11,10},{13,12},{... | collective-permute-start | bytes 419336 | tf_op jit(solution)/shard_map/ppermute | solution.py:19
  142.8 19.9 %copy-start.1 = (bf16[64,128,128]{2,1,0:T(8,128)(2,1)S(1)}, bf16[64,128,128]{2,1,0:T(8,128)(2,1)}, u32[]{:S(2)}) copy-start(bf16[64,128,128]{2,1,0:T(8,128)(2,1)} %shard_map.100) | copy-start | bytes 6291460
  143.7 5.8 %collective-permute-start.4 = (bf16[1,128,128]{2,1,0:T(8,128)(2,1)S(1)}, bf16[1,128,128]{2,1,0:T(8,128)(2,1)S(1)}, u32[]{:S(2)}, u32[]{:S(2)}) collective-permute-start(bf16[1,128,128]{2,1,0:T(8,128)(2,1)S(1)} %get-tuple-element.23), channel_id=1, source_target_pairs={{0,4},{4,8},{8,12},{12,16},{16,20},{20,24},{24,28},{1,5},{5,9},{9,... | collective-permute-start | bytes 98312 | tf_op jit(solution)/shard_map/ppermute | solution.py:16
  147.6 6.1 %collective-permute-start.5 = (bf16[1,128,128]{2,1,0:T(8,128)(2,1)S(1)}, bf16[1,128,128]{2,1,0:T(8,128)(2,1)S(1)}, u32[]{:S(2)}, u32[]{:S(2)}) collective-permute-start(bf16[1,128,128]{2,1,0:T(8,128)(2,1)S(1)} %get-tuple-element.24), channel_id=1, source_target_pairs={{4,0},{8,4},{12,8},{16,12},{20,16},{24,20},{28,24},{5,1},{9,5},{13... | collective-permute-start | bytes 98312 | tf_op jit(solution)/shard_map/ppermute | solution.py:19
  154.8 4.5 %collective-permute-start.6 = (bf16[66,1,128]{2,1,0:T(2,128)(2,1)S(1)}, bf16[66,1,128]{2,1,0:T(2,128)(2,1)S(1)}, u32[]{:S(2)}, u32[]{:S(2)}) collective-permute-start(bf16[66,1,128]{2,1,0:T(2,128)(2,1)S(1)} %get-tuple-element.19), channel_id=1, source_target_pairs={{0,1},{1,2},{2,3},{4,5},{5,6},{6,7},{8,9},{9,10},{10,11},{12,13},{... | collective-permute-start | bytes 50696 | tf_op jit(solution)/shard_map/ppermute | solution.py:16
  158.0 4.7 %collective-permute-start.7 = (bf16[66,1,128]{2,1,0:T(2,128)(2,1)S(1)}, bf16[66,1,128]{2,1,0:T(2,128)(2,1)S(1)}, u32[]{:S(2)}, u32[]{:S(2)}) collective-permute-start(bf16[66,1,128]{2,1,0:T(2,128)(2,1)S(1)} %get-tuple-element.20), channel_id=1, source_target_pairs={{1,0},{2,1},{3,2},{5,4},{6,5},{7,6},{9,8},{10,9},{11,10},{13,12},{... | collective-permute-start | bytes 50696 | tf_op jit(solution)/shard_map/ppermute | solution.py:19
  167.4 5.8 %copy-start.4 = (f32[256]{0:T(256)S(1)}, f32[256]{0:T(256)}, u32[]{:S(2)}) copy-start(f32[256]{0:T(256)} %param.17) | copy-start | bytes 3076
  167.4 16.8 %copy-start.2 = (f32[15,15,256]{2,1,0:T(8,128)S(1)}, f32[15,15,256]{2,1,0:T(8,128)}, u32[]{:S(2)}) copy-start(f32[15,15,256]{2,1,0:T(8,128)} %param.16) | copy-start | bytes 691204
  167.9 7.5 %collective-permute-start.8 = (bf16[7,64,256]{2,1,0:T(8,128)(2,1)S(1)}, bf16[7,64,256]{2,1,0:T(8,128)(2,1)S(1)}, u32[]{:S(2)}, u32[]{:S(2)}) collective-permute-start(bf16[7,64,256]{2,1,0:T(8,128)(2,1)S(1)} %get-tuple-element.35), channel_id=1, source_target_pairs={{0,4},{4,8},{8,12},{12,16},{16,20},{20,24},{24,28},{1,5},{5,9},{9,... | collective-permute-start | bytes 688136 | tf_op jit(solution)/shard_map/ppermute | solution.py:16
  171.2 8.2 %collective-permute-start.9 = (bf16[7,64,256]{2,1,0:T(8,128)(2,1)S(1)}, bf16[7,64,256]{2,1,0:T(8,128)(2,1)S(1)}, u32[]{:S(2)}, u32[]{:S(2)}) collective-permute-start(bf16[7,64,256]{2,1,0:T(8,128)(2,1)S(1)} %get-tuple-element.36), channel_id=1, source_target_pairs={{4,0},{8,4},{12,8},{16,12},{20,16},{24,20},{28,24},{5,1},{9,5},{13... | collective-permute-start | bytes 688136 | tf_op jit(solution)/shard_map/ppermute | solution.py:19
  179.5 5.8 %collective-permute-start.10 = (bf16[46,7,256]{2,1,0:T(8,128)(2,1)S(1)}, bf16[46,7,256]{2,1,0:T(8,128)(2,1)S(1)}, u32[]{:S(2)}, u32[]{:S(2)}) collective-permute-start(bf16[46,7,256]{2,1,0:T(8,128)(2,1)S(1)} %get-tuple-element.27), channel_id=1, source_target_pairs={{0,1},{1,2},{2,3},{4,5},{5,6},{6,7},{8,9},{9,10},{10,11},{12,13},{... | collective-permute-start | bytes 494600 | tf_op jit(solution)/shard_map/ppermute | solution.py:16
  182.7 6.6 %collective-permute-start.11 = (bf16[46,7,256]{2,1,0:T(8,128)(2,1)S(1)}, bf16[46,7,256]{2,1,0:T(8,128)(2,1)S(1)}, u32[]{:S(2)}, u32[]{:S(2)}) collective-permute-start(bf16[46,7,256]{2,1,0:T(8,128)(2,1)S(1)} %get-tuple-element.28), channel_id=1, source_target_pairs={{1,0},{2,1},{3,2},{5,4},{6,5},{7,6},{9,8},{10,9},{11,10},{13,12},{... | collective-permute-start | bytes 494600 | tf_op jit(solution)/shard_map/ppermute | solution.py:19
  254.1 4.8 %collective-permute-start.12 = (bf16[1,64,256]{2,1,0:T(8,128)(2,1)S(1)}, bf16[1,64,256]{2,1,0:T(8,128)(2,1)S(1)}, u32[]{:S(2)}, u32[]{:S(2)}) collective-permute-start(bf16[1,64,256]{2,1,0:T(8,128)(2,1)S(1)} %get-tuple-element.33), channel_id=1, source_target_pairs={{0,4},{4,8},{8,12},{12,16},{16,20},{20,24},{24,28},{1,5},{5,9},{9,... | collective-permute-start | bytes 98312 | tf_op jit(solution)/shard_map/ppermute | solution.py:16
  257.0 6.1 %collective-permute-start.13 = (bf16[1,64,256]{2,1,0:T(8,128)(2,1)S(1)}, bf16[1,64,256]{2,1,0:T(8,128)(2,1)S(1)}, u32[]{:S(2)}, u32[]{:S(2)}) collective-permute-start(bf16[1,64,256]{2,1,0:T(8,128)(2,1)S(1)} %get-tuple-element.34), channel_id=1, source_target_pairs={{4,0},{8,4},{12,8},{16,12},{20,16},{24,20},{28,24},{5,1},{9,5},{13... | collective-permute-start | bytes 98312 | tf_op jit(solution)/shard_map/ppermute | solution.py:19
  264.2 2.9 %collective-permute-start.14 = (bf16[34,1,256]{2,1,0:T(2,128)(2,1)S(1)}, bf16[34,1,256]{2,1,0:T(2,128)(2,1)S(1)}, u32[]{:S(2)}, u32[]{:S(2)}) collective-permute-start(bf16[34,1,256]{2,1,0:T(2,128)(2,1)S(1)} %get-tuple-element.29), channel_id=1, source_target_pairs={{0,1},{1,2},{2,3},{4,5},{5,6},{6,7},{8,9},{9,10},{10,11},{12,13},{... | collective-permute-start | bytes 52232 | tf_op jit(solution)/shard_map/ppermute | solution.py:16
  265.8 4.7 %collective-permute-start.15 = (bf16[34,1,256]{2,1,0:T(2,128)(2,1)S(1)}, bf16[34,1,256]{2,1,0:T(2,128)(2,1)S(1)}, u32[]{:S(2)}, u32[]{:S(2)}) collective-permute-start(bf16[34,1,256]{2,1,0:T(2,128)(2,1)S(1)} %get-tuple-element.30), channel_id=1, source_target_pairs={{1,0},{2,1},{3,2},{5,4},{6,5},{7,6},{9,8},{10,9},{11,10},{13,12},{... | collective-permute-start | bytes 52232 | tf_op jit(solution)/shard_map/ppermute | solution.py:19

commit v9 on v7

--- a/solution.py
+++ b/solution.py
@@ -28,19 +28,25 @@
     return (raw * mask).astype(jnp.bfloat16)
 
 
-def _dw_body(x_ref, k_ref, o_ref, xs_ref, *, taps, rows, cols, chans, rb):
+def _dw_body(x_ref, k_ref, o_ref, xf_ref, xs_ref, *, taps, rows, cols, chans, rb):
     nlb = chans // 128
     njb = cols // 8
     nrb = rows // rb
+
+    def widen_row(r, c):
+        xf_ref[r] = x_ref[r].astype(jnp.float32)
+        return c
+
+    lax.fori_loop(0, rows + taps - 1, widen_row, 0)
     first = True
     for s in range(8):
         if s == 0:
-            src = x_ref
+            src = xf_ref
         else:
             width = cols + 8 if s + 8 < taps else cols
 
             def shift(r, c):
-                xs_ref[r, pl.ds(0, width), :] = x_ref[r, pl.ds(s, width), :]
+                xs_ref[r, pl.ds(0, width), :] = xf_ref[r, pl.ds(s, width), :]
                 return c
 
             lax.fori_loop(0, rows + taps - 1, shift, 0)
@@ -51,7 +57,7 @@
                 continue
             for lb in range(nlb):
                 lanes = pl.ds(lb * 128, 128)
-                ks = [k_ref[a, b, :, lanes] for a in range(taps)]
+                ks = [jnp.broadcast_to(k_ref[a, pl.ds(b, 1), lanes], (8, 128)) for a in range(taps)]
 
                 def body(i, c, src=src, q=q, ks=ks, lanes=lanes, first=first):
                     r0 = pl.multiple_of((i // njb) * rb, rb)
@@ -82,7 +88,6 @@
     rows = extended.shape[0] - taps + 1
     cols = extended.shape[1] - taps + 1
     chans = extended.shape[2]
-    kb = jnp.broadcast_to(kernel.astype(jnp.float32)[:, :, None, :], (taps, taps, 8, chans))
     body = functools.partial(_dw_body, taps=taps, rows=rows, cols=cols, chans=chans, rb=8)
     vmem = pl.BlockSpec(memory_space=pltpu.VMEM)
     return pl.pallas_call(
@@ -90,13 +95,16 @@
         out_shape=jax.ShapeDtypeStruct((rows, cols, chans), jnp.float32),
         in_specs=[vmem, vmem],
         out_specs=vmem,
-        scratch_shapes=[pltpu.VMEM((extended.shape[0], cols + 8, chans), jnp.float32)],
+        scratch_shapes=[
+            pltpu.VMEM(extended.shape, jnp.float32),
+            pltpu.VMEM((extended.shape[0], cols + 8, chans), jnp.float32),
+        ],
         cost_estimate=pl.CostEstimate(
             flops=2 * rows * cols * chans * taps * taps,
             transcendentals=0,
-            bytes_accessed=extended.size * 4 + rows * cols * chans * 4,
+            bytes_accessed=extended.size * 2 + rows * cols * chans * 4,
         ),
-    )(extended.astype(jnp.float32), kb)
+    )(extended, kernel.astype(jnp.float32))
 
 
 def local_section(extended, raw, sigma, w_in, w_out):

time: 272 us -> 270 us (level)
    concatenate x0 -> x2, other arithmetic: none -> 5.37 us  [padded_2(): block = jnp.concatenate([low, block, high], axis=dim)]
    convert_element_type x4 -> x2, other arithmetic: 6.29 us -> 1.56 us  [depthwise(): kernel.astype(jnp.float32)]
  transfers between devices with their start and end apart: 16 -> 16, of which waited for: 12 -> 12; matrix products, arithmetic and copies ran while one was open for 1% -> 2% of each run, Pallas kernels for 0% -> 0%
where the time goes in v9:
time: 270 us; the launch traced here: 269 us
  Pallas kernels  149 us (55%)
  starting transfers between devices  38.1 us (14%)
  waiting for transfers between devices  33.8 us (13%)
  other arithmetic  25.2 us (9%)
  matrix products  14.7 us (5%)
  local copies, waits for them, and re-layouts  8.13 us (3%)
    pallas_call x2, Pallas kernels, depthwise(): pl.pallas_call(body, out_shape=jax.ShapeDtypeStruct((rows, cols, chans),...  149 us
    ppermute x8, waiting for transfers between devices, padded_2(): lax.ppermute(lax.slice_in_dim(block, 0, width, axis=dim), axis, backward)  30.4 us
    ppermute x8, starting transfers between devices, padded_2(): lax.ppermute(lax.slice_in_dim(block, block.shape[dim] - width, None, axis...  25 us
    dot_general x2, matrix products, local_section(): mixed = jnp.dot(hidden, w_out, preferred_element_type=jnp.float32)  14.3 us
    ppermute x8, starting transfers between devices, padded_2(): lax.ppermute(lax.slice_in_dim(block, 0, width, axis=dim), axis, backward)  13 us
    reduce_sum x2, other arithmetic, local_section(): mean = jnp.mean(conv_out, axis=-1, keepdims=True)  5.42 us
  transfers between devices with their start and end apart: 16, of which 12 were waited for; matrix products, arithmetic and copies ran while one was open for 2% of the time, Pallas kernels for 0%

profile of v9, /device:TPU:3, one launch (start us, length us, event | category | flops | bytes accessed | tf_op | source)
XLA Modules:
  0.0 269.2 jit_solution(13233100596452201155)
XLA Ops:
  0.0 1.1 fusion.80
  1.1 3.7 %collective-permute-start = (bf16[7,128,128]{2,1,0:T(8,128)(2,1)S(1)}, bf16[7,128,128]{2,1,0:T(8,128)(2,1)S(1)}, u32[]{:S(2)}, u32[]{:S(2)}) collective-permute-start(bf16[7,128,128]{2,1,0:T(8,128)(2,1)S(1)} %get-tuple-element.26), channel_id=1, source_target_pairs={{0,4},{4,8},{8,12},{12,16},{16,20},{20,24},{24,28},{1,5},{5,9},{9,... | collective-permute-start | bytes 688136 | tf_op jit(solution)/shard_map/ppermute | solution.py:16
  4.8 1.9 collective-permute-start.1
  6.8 0.7 multiply_multiply_fusion.3
  7.4 0.1 add_negate_fusion
  7.5 0.3 collective-permute-done
  7.8 2.0 constant_dynamic-update-slice_fusion.1
  9.8 3.2 %collective-permute-done.1 = bf16[7,128,128]{2,1,0:T(8,128)(2,1)S(1)} collective-permute-done((bf16[7,128,128]{2,1,0:T(8,128)(2,1)S(1)}, bf16[7,128,128]{2,1,0:T(8,128)(2,1)S(1)}, u32[]{:S(2)}, u32[]{:S(2)}) %collective-permute-start.1) | collective-permute-done | bytes 229408 | tf_op jit(solution)/shard_map/ppermute | solution.py:19
  13.1 0.1 fusion.74
  13.2 3.2 %collective-permute-start.2 = (bf16[78,7,128]{2,1,0:T(8,128)(2,1)S(1)}, bf16[78,7,128]{2,1,0:T(8,128)(2,1)S(1)}, u32[]{:S(2)}, u32[]{:S(2)}) collective-permute-start(bf16[78,7,128]{2,1,0:T(8,128)(2,1)S(1)} %get-tuple-element.11), channel_id=1, source_target_pairs={{0,1},{1,2},{2,3},{4,5},{5,6},{6,7},{8,9},{9,10},{10,11},{12,13},{... | collective-permute-start | bytes 419336 | tf_op jit(solution)/shard_map/ppermute | solution.py:16
  16.4 1.3 collective-permute-start.3
  17.7 0.8 fusion.62.k_ref
  18.5 0.4 collective-permute-done.2
  18.9 4.1 %collective-permute-done.3 = bf16[78,7,128]{2,1,0:T(8,128)(2,1)S(1)} collective-permute-done((bf16[78,7,128]{2,1,0:T(8,128)(2,1)S(1)}, bf16[78,7,128]{2,1,0:T(8,128)(2,1)S(1)}, u32[]{:S(2)}, u32[]{:S(2)}) %collective-permute-start.3) | collective-permute-done | bytes 139808 | tf_op jit(solution)/shard_map/ppermute | solution.py:19
  23.0 3.0 %pad_maximum_fusion.x_ref = bf16[78,142,128]{2,1,0:T(8,128)(2,1)} fusion(bf16[78,7,128]{2,1,0:T(8,128)(2,1)S(1)} %collective-permute-done.3, bf16[78,128,128]{2,1,0:T(8,128)(2,1)S(1)} %constant_dynamic-update-slice_fusion, bf16[78,7,128]{2,1,0:T(8,128)(2,1)S(1)} %collective-permute-done.2), kind=kLoop, calls=%fused_computation.23 | loop fusion | flops 8506368 | bytes 5670912 | tf_op jit(solution)/shard_map/concatenate | solution.py:20
  26.0 98.5 %shard_map.100 = f32[64,128,128]{2,1,0:T(8,128)} custom-call(bf16[78,142,128]{2,1,0:T(8,128)(2,1)} %pad_maximum_fusion.x_ref, f32[15,15,128]{2,1,0:T(8,128)} %fusion.62.k_ref), custom_call_target="tpu_custom_call" | custom-call | flops 471859200 | bytes 7029760 | tf_op jit(solution)/shard_map/pallas_call | solution.py:93
  124.5 3.3 %reduce_sum.36 = f32[64,128]{1,0:T(8,128)S(1)} reduce(f32[64,128,128]{2,1,0:T(8,128)} %shard_map.100, f32[]{:T(128)} %constant.14.clone.1), dimensions={2}, to_apply=%region_0.0 | reduce | flops 1040384 | bytes 4227076 | tf_op jit(solution)/shard_map/reduce_sum | solution.py:114
  127.9 4.0 %multiply_reduce_fusion = f32[64,128]{1,0:T(8,128)S(1)} fusion(f32[64,128,128]{2,1,0:T(8,128)} %shard_map.100, f32[64,128]{1,0:T(8,128)S(1)} %broadcast_multiply_fusion), kind=kLoop, calls=%fused_computation.20 | loop fusion | flops 3137536 | bytes 4259840 | tf_op jit(solution)/shard_map/reduce_sum | solution.py:115
  131.9 8.9 %add_convert_fusion = bf16[64,128,128]{2,1,0:T(8,128)(2,1)S(1)} fusion(bf16[64,128,128]{2,1,0:T(8,128)(2,1)} %param.10, f32[64,128,128]{2,1,0:T(8,128)} %shard_map.100, f32[64,128]{1,0:T(8,128)S(1)} %add_rsqrt_fusion, f32[64,128]{1,0:T(8,128)S(1)} %broadcast_multiply_fusion, bf16[512,128]{1,0:T(8,128)(2,1)S(1)} %copy-done.8, bf16[128,512]{1,0:T(8,128)(2,1)S(1)} %copy-done.9), kind=kOutput, calls=%fused_computation.18 | convolution fusion | flops 2191523840 | bytes 8716288 | tf_op jit(solution)/shard_map/dot_general | solution.py:120
  140.9 3.9 %collective-permute-start.4 = (bf16[1,128,128]{2,1,0:T(8,128)(2,1)S(1)}, bf16[1,128,128]{2,1,0:T(8,128)(2,1)S(1)}, u32[]{:S(2)}, u32[]{:S(2)}) collective-permute-start(bf16[1,128,128]{2,1,0:T(8,128)(2,1)S(1)} %get-tuple-element.23), channel_id=1, source_target_pairs={{0,4},{4,8},{8,12},{12,16},{16,20},{20,24},{24,28},{1,5},{5,9},{9,... | collective-permute-start | bytes 98312 | tf_op jit(solution)/shard_map/ppermute | solution.py:16
  144.8 1.9 collective-permute-start.5
  146.7 4.2 %collective-permute-done.5 = bf16[1,128,128]{2,1,0:T(8,128)(2,1)S(1)} collective-permute-done((bf16[1,128,128]{2,1,0:T(8,128)(2,1)S(1)}, bf16[1,128,128]{2,1,0:T(8,128)(2,1)S(1)}, u32[]{:S(2)}, u32[]{:S(2)}) %collective-permute-start.5) | collective-permute-done | bytes 32800 | tf_op jit(solution)/shard_map/ppermute | solution.py:19
  150.9 3.2 %collective-permute-start.6 = (bf16[66,1,128]{2,1,0:T(2,128)(2,1)S(1)}, bf16[66,1,128]{2,1,0:T(2,128)(2,1)S(1)}, u32[]{:S(2)}, u32[]{:S(2)}) collective-permute-start(bf16[66,1,128]{2,1,0:T(2,128)(2,1)S(1)} %get-tuple-element.19), channel_id=1, source_target_pairs={{0,1},{1,2},{2,3},{4,5},{5,6},{6,7},{8,9},{9,10},{10,11},{12,13},{... | collective-permute-start | bytes 50696 | tf_op jit(solution)/shard_map/ppermute | solution.py:16
  154.2 1.5 collective-permute-start.7
  155.7 3.2 %collective-permute-done.7 = bf16[66,1,128]{2,1,0:T(2,128)(2,1)S(1)} collective-permute-done((bf16[66,1,128]{2,1,0:T(2,128)(2,1)S(1)}, bf16[66,1,128]{2,1,0:T(2,128)(2,1)S(1)}, u32[]{:S(2)}, u32[]{:S(2)}) %collective-permute-start.7) | collective-permute-done | bytes 16928 | tf_op jit(solution)/shard_map/ppermute | solution.py:19
  158.8 0.8 maximum_convert_fusion
  159.7 0.6 fusion.71
  160.3 0.6 fusion.72
  160.9 1.6 fusion.22
  162.4 0.6 fusion.78
  163.0 0.5 fusion.51
  163.5 0.3 copy-done.5
  163.9 0.4 convolution_convert_fusion
  164.4 3.3 %collective-permute-start.8 = (bf16[7,64,256]{2,1,0:T(8,128)(2,1)S(1)}, bf16[7,64,256]{2,1,0:T(8,128)(2,1)S(1)}, u32[]{:S(2)}, u32[]{:S(2)}) collective-permute-start(bf16[7,64,256]{2,1,0:T(8,128)(2,1)S(1)} %get-tuple-element.35), channel_id=1, source_target_pairs={{0,4},{4,8},{8,12},{12,16},{16,20},{20,24},{24,28},{1,5},{5,9},{9,... | collective-permute-start | bytes 688136 | tf_op jit(solution)/shard_map/ppermute | solution.py:16
  167.7 1.9 collective-permute-start.9
  169.7 2.2 collective-permute-done.8
  171.9 4.0 %collective-permute-done.9 = bf16[7,64,256]{2,1,0:T(8,128)(2,1)S(1)} collective-permute-done((bf16[7,64,256]{2,1,0:T(8,128)(2,1)S(1)}, bf16[7,64,256]{2,1,0:T(8,128)(2,1)S(1)}, u32[]{:S(2)}, u32[]{:S(2)}) %collective-permute-start.9) | collective-permute-done | bytes 229408 | tf_op jit(solution)/shard_map/ppermute | solution.py:19
  176.0 3.2 %collective-permute-start.10 = (bf16[46,7,256]{2,1,0:T(8,128)(2,1)S(1)}, bf16[46,7,256]{2,1,0:T(8,128)(2,1)S(1)}, u32[]{:S(2)}, u32[]{:S(2)}) collective-permute-start(bf16[46,7,256]{2,1,0:T(8,128)(2,1)S(1)} %get-tuple-element.27), channel_id=1, source_target_pairs={{0,1},{1,2},{2,3},{4,5},{5,6},{6,7},{8,9},{9,10},{10,11},{12,13},{... | collective-permute-start | bytes 494600 | tf_op jit(solution)/shard_map/ppermute | solution.py:16
  179.2 1.3 collective-permute-start.11
  180.5 0.8 fusion.60.k_ref
  181.3 0.4 collective-permute-done.10
  181.7 4.1 %collective-permute-done.11 = bf16[46,7,256]{2,1,0:T(8,128)(2,1)S(1)} collective-permute-done((bf16[46,7,256]{2,1,0:T(8,128)(2,1)S(1)}, bf16[46,7,256]{2,1,0:T(8,128)(2,1)S(1)}, u32[]{:S(2)}, u32[]{:S(2)}) %collective-permute-start.11) | collective-permute-done | bytes 164896 | tf_op jit(solution)/shard_map/ppermute | solution.py:19
  185.9 2.4 pad_maximum_fusion.1.x_ref
  188.2 50.3 %shard_map.101 = f32[32,64,256]{2,1,0:T(8,128)} custom-call(bf16[46,78,256]{2,1,0:T(8,128)(2,1)} %pad_maximum_fusion.1.x_ref, f32[15,15,256]{2,1,0:T(8,128)} %fusion.60.k_ref), custom_call_target="tpu_custom_call" | custom-call | flops 235929600 | bytes 3934208 | tf_op jit(solution)/shard_map/pallas_call | solution.py:93
  238.5 2.1 reduce_sum.38
  240.6 0.1 copy-done.1
  240.8 0.6 multiply_reduce_fusion.1
  241.4 5.4 %add_convert_fusion.1 = bf16[32,64,256]{2,1,0:T(8,128)(2,1)} fusion(bf16[32,64,256]{2,1,0:T(8,128)(2,1)} %copy-done.2, f32[32,64,256]{2,1,0:T(8,128)S(1)} %copy-done.1, f32[32,64]{1,0:T(8,128)S(1)} %add_rsqrt_fusion.1, f32[32,64]{1,0:T(8,128)S(1)} %broadcast_multiply_fusion.1, bf16[1024,256]{1,0:T(8,128)(2,1)S(1)} %copy-done, ...), kind=kOutput, calls=%fused_computation.33 | convolution fusion | flops 2169503744 | bytes 5259264 | tf_op jit(solution)/shard_map/dot_general | solution.py:120
  246.8 0.8 fusion.82
  247.6 2.9 %collective-permute-start.12 = (bf16[1,64,256]{2,1,0:T(8,128)(2,1)S(1)}, bf16[1,64,256]{2,1,0:T(8,128)(2,1)S(1)}, u32[]{:S(2)}, u32[]{:S(2)}) collective-permute-start(bf16[1,64,256]{2,1,0:T(8,128)(2,1)S(1)} %get-tuple-element.33), channel_id=1, source_target_pairs={{0,4},{4,8},{8,12},{12,16},{16,20},{20,24},{24,28},{1,5},{5,9},{9,... | collective-permute-start | bytes 98312 | tf_op jit(solution)/shard_map/ppermute | solution.py:16
  250.4 1.9 collective-permute-start.13
  252.4 4.2 %collective-permute-done.13 = bf16[1,64,256]{2,1,0:T(8,128)(2,1)S(1)} collective-permute-done((bf16[1,64,256]{2,1,0:T(8,128)(2,1)S(1)}, bf16[1,64,256]{2,1,0:T(8,128)(2,1)S(1)}, u32[]{:S(2)}, u32[]{:S(2)}) %collective-permute-start.13) | collective-permute-done | bytes 32800 | tf_op jit(solution)/shard_map/ppermute | solution.py:19
  256.6 1.0 pad_maximum_fusion.7
  257.6 1.6 collective-permute-start.14
  259.3 1.3 collective-permute-start.15
  260.6 3.4 %collective-permute-done.15 = bf16[34,1,256]{2,1,0:T(2,128)(2,1)S(1)} collective-permute-done((bf16[34,1,256]{2,1,0:T(2,128)(2,1)S(1)}, bf16[34,1,256]{2,1,0:T(2,128)(2,1)S(1)}, u32[]{:S(2)}, u32[]{:S(2)}) %collective-permute-start.15) | collective-permute-done | bytes 17440 | tf_op jit(solution)/shard_map/ppermute | solution.py:19
  263.9 1.8 maximum_convert_fusion.1
  265.7 0.4 fusion.75
  266.1 0.2 fusion.76
  266.3 0.2 fusion.77
  266.5 1.4 fusion.32
  267.9 0.3 fusion.81
  268.2 0.2 fusion.52
  268.4 0.8 copy.20
  (34 shorter events, 0.3 us)
Async XLA Ops:
  0.0 241.4 %copy-start = (bf16[1024,256]{1,0:T(8,128)(2,1)S(1)}, bf16[1024,256]{1,0:T(8,128)(2,1)}, u32[]{:S(2)}) copy-start(bf16[1024,256]{1,0:T(8,128)(2,1)} %param.19) | copy-start | bytes 1572868
  1.1 6.6 %collective-permute-start = (bf16[7,128,128]{2,1,0:T(8,128)(2,1)S(1)}, bf16[7,128,128]{2,1,0:T(8,128)(2,1)S(1)}, u32[]{:S(2)}, u32[]{:S(2)}) collective-permute-start(bf16[7,128,128]{2,1,0:T(8,128)(2,1)S(1)} %get-tuple-element.26), channel_id=1, source_target_pairs={{0,4},{4,8},{8,12},{12,16},{16,20},{20,24},{24,28},{1,5},{5,9},{9,... | collective-permute-start | bytes 688136 | tf_op jit(solution)/shard_map/ppermute | solution.py:16
  4.8 8.2 %collective-permute-start.1 = (bf16[7,128,128]{2,1,0:T(8,128)(2,1)S(1)}, bf16[7,128,128]{2,1,0:T(8,128)(2,1)S(1)}, u32[]{:S(2)}, u32[]{:S(2)}) collective-permute-start(bf16[7,128,128]{2,1,0:T(8,128)(2,1)S(1)} %get-tuple-element.25), channel_id=1, source_target_pairs={{4,0},{8,4},{12,8},{16,12},{20,16},{24,20},{28,24},{5,1},{9,5},{13... | collective-permute-start | bytes 688136 | tf_op jit(solution)/shard_map/ppermute | solution.py:19
  7.8 9.9 %copy-start.4 = (f32[15,15,128]{2,1,0:T(8,128)S(1)}, f32[15,15,128]{2,1,0:T(8,128)}, u32[]{:S(2)}) copy-start(f32[15,15,128]{2,1,0:T(8,128)} %param.11) | copy-start | bytes 345604
  13.2 5.7 %collective-permute-start.2 = (bf16[78,7,128]{2,1,0:T(8,128)(2,1)S(1)}, bf16[78,7,128]{2,1,0:T(8,128)(2,1)S(1)}, u32[]{:S(2)}, u32[]{:S(2)}) collective-permute-start(bf16[78,7,128]{2,1,0:T(8,128)(2,1)S(1)} %get-tuple-element.11), channel_id=1, source_target_pairs={{0,1},{1,2},{2,3},{4,5},{5,6},{6,7},{8,9},{9,10},{10,11},{12,13},{... | collective-permute-start | bytes 419336 | tf_op jit(solution)/shard_map/ppermute | solution.py:16
  16.4 6.6 %collective-permute-start.3 = (bf16[78,7,128]{2,1,0:T(8,128)(2,1)S(1)}, bf16[78,7,128]{2,1,0:T(8,128)(2,1)S(1)}, u32[]{:S(2)}, u32[]{:S(2)}) collective-permute-start(bf16[78,7,128]{2,1,0:T(8,128)(2,1)S(1)} %get-tuple-element.12), channel_id=1, source_target_pairs={{1,0},{2,1},{3,2},{5,4},{6,5},{7,6},{9,8},{10,9},{11,10},{13,12},{... | collective-permute-start | bytes 419336 | tf_op jit(solution)/shard_map/ppermute | solution.py:19
  127.8 4.1 %copy-start.8 = (bf16[512,128]{1,0:T(8,128)(2,1)S(1)}, bf16[512,128]{1,0:T(8,128)(2,1)}, u32[]{:S(2)}) copy-start(bf16[512,128]{1,0:T(8,128)(2,1)} %param.14) | copy-start | bytes 393220
  127.8 4.1 %copy-start.9 = (bf16[128,512]{1,0:T(8,128)(2,1)S(1)}, bf16[128,512]{1,0:T(8,128)(2,1)}, u32[]{:S(2)}) copy-start(bf16[128,512]{1,0:T(8,128)(2,1)} %param.13) | copy-start | bytes 393220
  140.9 5.8 %collective-permute-start.4 = (bf16[1,128,128]{2,1,0:T(8,128)(2,1)S(1)}, bf16[1,128,128]{2,1,0:T(8,128)(2,1)S(1)}, u32[]{:S(2)}, u32[]{:S(2)}) collective-permute-start(bf16[1,128,128]{2,1,0:T(8,128)(2,1)S(1)} %get-tuple-element.23), channel_id=1, source_target_pairs={{0,4},{4,8},{8,12},{12,16},{16,20},{20,24},{24,28},{1,5},{5,9},{9,... | collective-permute-start | bytes 98312 | tf_op jit(solution)/shard_map/ppermute | solution.py:16
  144.8 6.1 %collective-permute-start.5 = (bf16[1,128,128]{2,1,0:T(8,128)(2,1)S(1)}, bf16[1,128,128]{2,1,0:T(8,128)(2,1)S(1)}, u32[]{:S(2)}, u32[]{:S(2)}) collective-permute-start(bf16[1,128,128]{2,1,0:T(8,128)(2,1)S(1)} %get-tuple-element.24), channel_id=1, source_target_pairs={{4,0},{8,4},{12,8},{16,12},{20,16},{24,20},{28,24},{5,1},{9,5},{13... | collective-permute-start | bytes 98312 | tf_op jit(solution)/shard_map/ppermute | solution.py:19
  150.9 4.7 %collective-permute-start.6 = (bf16[66,1,128]{2,1,0:T(2,128)(2,1)S(1)}, bf16[66,1,128]{2,1,0:T(2,128)(2,1)S(1)}, u32[]{:S(2)}, u32[]{:S(2)}) collective-permute-start(bf16[66,1,128]{2,1,0:T(2,128)(2,1)S(1)} %get-tuple-element.19), channel_id=1, source_target_pairs={{0,1},{1,2},{2,3},{4,5},{5,6},{6,7},{8,9},{9,10},{10,11},{12,13},{... | collective-permute-start | bytes 50696 | tf_op jit(solution)/shard_map/ppermute | solution.py:16
  154.2 4.7 %collective-permute-start.7 = (bf16[66,1,128]{2,1,0:T(2,128)(2,1)S(1)}, bf16[66,1,128]{2,1,0:T(2,128)(2,1)S(1)}, u32[]{:S(2)}, u32[]{:S(2)}) collective-permute-start(bf16[66,1,128]{2,1,0:T(2,128)(2,1)S(1)} %get-tuple-element.20), channel_id=1, source_target_pairs={{1,0},{2,1},{3,2},{5,4},{6,5},{7,6},{9,8},{10,9},{11,10},{13,12},{... | collective-permute-start | bytes 50696 | tf_op jit(solution)/shard_map/ppermute | solution.py:19
  163.0 0.8 copy-start.5
  163.9 5.8 %copy-start.6 = (f32[256]{0:T(256)S(1)}, f32[256]{0:T(256)}, u32[]{:S(2)}) copy-start(f32[256]{0:T(256)} %param.17) | copy-start | bytes 3076
  163.9 16.6 %copy-start.3 = (f32[15,15,256]{2,1,0:T(8,128)S(1)}, f32[15,15,256]{2,1,0:T(8,128)}, u32[]{:S(2)}) copy-start(f32[15,15,256]{2,1,0:T(8,128)} %param.16) | copy-start | bytes 691204
  164.3 21.6 %copy-start.2 = (bf16[32,64,256]{2,1,0:T(8,128)(2,1)}, bf16[32,64,256]{2,1,0:T(8,128)(2,1)S(1)}, u32[]{:S(2)}) copy-start(bf16[32,64,256]{2,1,0:T(8,128)(2,1)S(1)} %convolution_convert_fusion) | copy-start | bytes 3145732
  164.4 7.5 %collective-permute-start.8 = (bf16[7,64,256]{2,1,0:T(8,128)(2,1)S(1)}, bf16[7,64,256]{2,1,0:T(8,128)(2,1)S(1)}, u32[]{:S(2)}, u32[]{:S(2)}) collective-permute-start(bf16[7,64,256]{2,1,0:T(8,128)(2,1)S(1)} %get-tuple-element.35), channel_id=1, source_target_pairs={{0,4},{4,8},{8,12},{12,16},{16,20},{20,24},{24,28},{1,5},{5,9},{9,... | collective-permute-start | bytes 688136 | tf_op jit(solution)/shard_map/ppermute | solution.py:16
  167.7 8.2 %collective-permute-start.9 = (bf16[7,64,256]{2,1,0:T(8,128)(2,1)S(1)}, bf16[7,64,256]{2,1,0:T(8,128)(2,1)S(1)}, u32[]{:S(2)}, u32[]{:S(2)}) collective-permute-start(bf16[7,64,256]{2,1,0:T(8,128)(2,1)S(1)} %get-tuple-element.36), channel_id=1, source_target_pairs={{4,0},{8,4},{12,8},{16,12},{20,16},{24,20},{28,24},{5,1},{9,5},{13... | collective-permute-start | bytes 688136 | tf_op jit(solution)/shard_map/ppermute | solution.py:19
  176.0 5.7 %collective-permute-start.10 = (bf16[46,7,256]{2,1,0:T(8,128)(2,1)S(1)}, bf16[46,7,256]{2,1,0:T(8,128)(2,1)S(1)}, u32[]{:S(2)}, u32[]{:S(2)}) collective-permute-start(bf16[46,7,256]{2,1,0:T(8,128)(2,1)S(1)} %get-tuple-element.27), channel_id=1, source_target_pairs={{0,1},{1,2},{2,3},{4,5},{5,6},{6,7},{8,9},{9,10},{10,11},{12,13},{... | collective-permute-start | bytes 494600 | tf_op jit(solution)/shard_map/ppermute | solution.py:16
  179.2 6.6 %collective-permute-start.11 = (bf16[46,7,256]{2,1,0:T(8,128)(2,1)S(1)}, bf16[46,7,256]{2,1,0:T(8,128)(2,1)S(1)}, u32[]{:S(2)}, u32[]{:S(2)}) collective-permute-start(bf16[46,7,256]{2,1,0:T(8,128)(2,1)S(1)} %get-tuple-element.28), channel_id=1, source_target_pairs={{1,0},{2,1},{3,2},{5,4},{6,5},{7,6},{9,8},{10,9},{11,10},{13,12},{... | collective-permute-start | bytes 494600 | tf_op jit(solution)/shard_map/ppermute | solution.py:19
  238.5 2.2 copy-start.1
  238.5 2.9 %copy-start.7 = (bf16[256,1024]{1,0:T(8,128)(2,1)S(1)}, bf16[256,1024]{1,0:T(8,128)(2,1)}, u32[]{:S(2)}) copy-start(bf16[256,1024]{1,0:T(8,128)(2,1)} %param.18) | copy-start | bytes 1572868
  247.6 4.8 %collective-permute-start.12 = (bf16[1,64,256]{2,1,0:T(8,128)(2,1)S(1)}, bf16[1,64,256]{2,1,0:T(8,128)(2,1)S(1)}, u32[]{:S(2)}, u32[]{:S(2)}) collective-permute-start(bf16[1,64,256]{2,1,0:T(8,128)(2,1)S(1)} %get-tuple-element.33), channel_id=1, source_target_pairs={{0,4},{4,8},{8,12},{12,16},{16,20},{20,24},{24,28},{1,5},{5,9},{9,... | collective-permute-start | bytes 98312 | tf_op jit(solution)/shard_map/ppermute | solution.py:16
  250.4 6.1 %collective-permute-start.13 = (bf16[1,64,256]{2,1,0:T(8,128)(2,1)S(1)}, bf16[1,64,256]{2,1,0:T(8,128)(2,1)S(1)}, u32[]{:S(2)}, u32[]{:S(2)}) collective-permute-start(bf16[1,64,256]{2,1,0:T(8,128)(2,1)S(1)} %get-tuple-element.34), channel_id=1, source_target_pairs={{4,0},{8,4},{12,8},{16,12},{20,16},{24,20},{28,24},{5,1},{9,5},{13... | collective-permute-start | bytes 98312 | tf_op jit(solution)/shard_map/ppermute | solution.py:19
  257.6 2.9 %collective-permute-start.14 = (bf16[34,1,256]{2,1,0:T(2,128)(2,1)S(1)}, bf16[34,1,256]{2,1,0:T(2,128)(2,1)S(1)}, u32[]{:S(2)}, u32[]{:S(2)}) collective-permute-start(bf16[34,1,256]{2,1,0:T(2,128)(2,1)S(1)} %get-tuple-element.29), channel_id=1, source_target_pairs={{0,1},{1,2},{2,3},{4,5},{5,6},{6,7},{8,9},{9,10},{10,11},{12,13},{... | collective-permute-start | bytes 52232 | tf_op jit(solution)/shard_map/ppermute | solution.py:16
  259.3 4.7 %collective-permute-start.15 = (bf16[34,1,256]{2,1,0:T(2,128)(2,1)S(1)}, bf16[34,1,256]{2,1,0:T(2,128)(2,1)S(1)}, u32[]{:S(2)}, u32[]{:S(2)}) collective-permute-start(bf16[34,1,256]{2,1,0:T(2,128)(2,1)S(1)} %get-tuple-element.30), channel_id=1, source_target_pairs={{1,0},{2,1},{3,2},{5,4},{6,5},{7,6},{9,8},{10,9},{11,10},{13,12},{... | collective-permute-start | bytes 52232 | tf_op jit(solution)/shard_map/ppermute | solution.py:19

commit v10 on v0

--- a/solution.py
+++ b/solution.py
@@ -1,6 +1,10 @@
+import functools
+
 import jax
 import jax.numpy as jnp
 from jax import lax
+from jax.experimental import pallas as pl
+from jax.experimental.pallas import tpu as pltpu
 from jax.sharding import PartitionSpec as P
 
 
@@ -24,19 +28,125 @@
     return (raw * mask).astype(jnp.bfloat16)
 
 
-def local_section(extended, raw, sigma, w_in, w_out):
-    channels = extended.shape[2]
+def _dw_body(x_all, k_ref, o_all, xf_ref, xs_ref, *, taps, base, rows, cols, chans, rb):
+    nlb = chans // 128
+    njb = cols // 8
+    nrb = rows // rb
+
+    def one_strip(n, carry):
+        x_ref = x_all.at[n]
+        o_ref = o_all.at[n]
+
+        def widen_row(r, c):
+            xf_ref[r] = x_ref[base + r].astype(jnp.float32)
+            return c
+
+        lax.fori_loop(0, rows + taps - 1, widen_row, 0)
+        first = True
+        for s in range(8):
+            if s == 0:
+                src = xf_ref
+            else:
+                width = cols + 8 if s + 8 < taps else cols
+
+                def shift(r, c, s=s, width=width):
+                    xs_ref[r, pl.ds(0, width), :] = xf_ref[r, pl.ds(s, width), :]
+                    return c
+
+                lax.fori_loop(0, rows + taps - 1, shift, 0)
+                src = xs_ref
+            for q in range(2):
+                b = 8 * q + s
+                if b >= taps:
+                    continue
+                for lb in range(nlb):
+                    lanes = pl.ds(lb * 128, 128)
+                    ks = [
+                        jnp.broadcast_to(k_ref[a, pl.ds(b, 1), lanes], (8, 128))
+                        for a in range(taps)
+                    ]
+
+                    def body(i, c, src=src, q=q, ks=ks, lanes=lanes, first=first):
+                        r0 = pl.multiple_of((i // njb) * rb, rb)
+                        j0 = pl.multiple_of((i % njb) * 8, 8)
+                        xs = src[pl.ds(r0, rb + taps - 1), pl.ds(j0 + 8 * q, 8), lanes]
+                        if first:
+                            acc = jnp.zeros((rb, 8, 128), jnp.float32)
+                        else:
+                            acc = o_ref[pl.ds(r0, rb), pl.ds(j0, 8), lanes]
+                        terms = [xs[a : a + rb] * ks[a][None] for a in range(taps)]
+                        for g in range(0, taps, 5):
+                            group = terms[g : g + 5]
+                            while len(group) > 1:
+                                group = [
+                                    group[i] + group[i + 1] if i + 1 < len(group) else group[i]
+                                    for i in range(0, len(group), 2)
+                                ]
+                            acc = acc + group[0]
+                        o_ref[pl.ds(r0, rb), pl.ds(j0, 8), lanes] = acc
+                        return c
+
+                    lax.fori_loop(0, nrb * njb, body, 0, unroll=2)
+                first = False
+        return carry
+
+    lax.fori_loop(0, x_all.shape[0], one_strip, 0)
+
+
+def depthwise(strips, kernel, base, rows):
+    taps = kernel.shape[0]
+    count = strips.shape[0]
+    cols = strips.shape[2] - taps + 1
+    chans = strips.shape[3]
+    body = functools.partial(
+        _dw_body, taps=taps, base=base, rows=rows, cols=cols, chans=chans, rb=8
+    )
+    vmem = pl.BlockSpec(memory_space=pltpu.VMEM)
+    return pl.pallas_call(
+        body,
+        out_shape=jax.ShapeDtypeStruct((count, rows, cols, chans), jnp.float32),
+        in_specs=[vmem, vmem],
+        out_specs=vmem,
+        scratch_shapes=[
+            pltpu.VMEM((rows + taps - 1,) + strips.shape[2:], jnp.float32),
+            pltpu.VMEM((rows + taps - 1, cols + 8, chans), jnp.float32),
+        ],
+        cost_estimate=pl.CostEstimate(
+            flops=2 * count * rows * cols * chans * taps * taps,
+            transcendentals=0,
+            bytes_accessed=strips.size * 2 + count * rows * cols * chans * 4,
+        ),
+    )(strips, kernel.astype(jnp.float32))
+
+
+def exchange(block, axis, dim, width):
+    count = lax.axis_size(axis)
+    forward = [(i, i + 1) for i in range(count - 1)]
+    backward = [(target, source) for source, target in forward]
+    low = lax.ppermute(
+        lax.slice_in_dim(block, block.shape[dim] - width, None, axis=dim), axis, forward
+    )
+    high = lax.ppermute(lax.slice_in_dim(block, 0, width, axis=dim), axis, backward)
+    return jnp.concatenate([low, block, high], axis=dim)
+
+
+def section_conv(block, kernel):
+    reach = (kernel.shape[0] - 1) // 2
+    rows = block.shape[0]
+    band = 8
+    wide = exchange(block, "col", 1, reach)
+    middle = depthwise(wide[None], kernel, band - reach, rows - 2 * band)
+    full = exchange(wide, "row", 0, reach)
+    ends = jnp.stack(
+        [full[: band + 2 * reach], full[rows - band :]], axis=0
+    )
+    edge = depthwise(ends, kernel, 0, band)
+    return jnp.concatenate([edge[0], middle[0], edge[1]], axis=0)
+
+
+def local_section(field, raw, sigma, w_in, w_out):
     kernel = masked_kernel(raw, sigma)
-    conv_out = lax.conv_general_dilated(
-        extended[None],
-        kernel[:, :, None, :],
-        (1, 1),
-        "VALID",
-        dimension_numbers=("NHWC", "HWIO", "NHWC"),
-        feature_group_count=channels,
-        preferred_element_type=jnp.float32,
-    )[0]
-    field = extended[7 : extended.shape[0] - 7, 7 : extended.shape[1] - 7]
+    conv_out = section_conv(field, kernel)
     mean = jnp.mean(conv_out, axis=-1, keepdims=True)
     var = jnp.mean((conv_out - mean) ** 2, axis=-1, keepdims=True)
     normed = ((conv_out - mean) * lax.rsqrt(var + 1e-06)).astype(jnp.bfloat16)
@@ -73,14 +183,11 @@
     in_second,
     out_second,
 ):
-    reach = 7
-    extended = padded_2(image, (("row", 0), ("col", 1)), reach)
-    first = local_section(extended, raw_first, sigma_first, in_first, out_first)
+    first = local_section(image, raw_first, sigma_first, in_first, out_first)
     first_cycle = padded_2(first, (("row", 0), ("col", 1)), 1)
     first_pooled = blur_down(first_cycle)
     widened = jnp.dot(first_pooled, widen, preferred_element_type=jnp.float32).astype(jnp.bfloat16)
-    widened_ext = padded_2(widened, (("row", 0), ("col", 1)), reach)
-    second = local_section(widened_ext, raw_second, sigma_second, in_second, out_second)
+    second = local_section(widened, raw_second, sigma_second, in_second, out_second)
     second_cycle = padded_2(second, (("row", 0), ("col", 1)), 1)
     return blur_down(second_cycle)
 

time: 534 us -> 277 us (0.52)
  matrix products: 423 us -> 15.3 us
  Pallas kernels: 0 us -> 156 us
  waiting for transfers between devices: 34.8 us -> 23.5 us
  other arithmetic: 18.8 us -> 27.4 us
    conv_general_dilated x2 -> x0, matrix products: 409 us -> none  [local_section(): lax.conv_general_dilated(extended[None], kernel[:, :, None, :], (1, 1), '...]
    pallas_call x0 -> x4, Pallas kernels: none -> 156 us  [depthwise(): pl.pallas_call(body, out_shape=jax.ShapeDtypeStruct((count, rows, cols, c...]
    ppermute x0 -> x8, starting transfers between devices: none -> 22.2 us  [the longest x4 15.6 us: exchange(): lax.ppermute(lax.slice_in_dim(block, block.shape[dim] - width, None, axis...]
    ppermute x8 -> x4, waiting for transfers between devices: 30.1 us -> 14.7 us  [padded_2(): lax.ppermute(lax.slice_in_dim(block, 0, width, axis=dim), axis, backward)]
    ppermute x8 -> x4, starting transfers between devices: 25 us -> 13.9 us  [padded_2(): lax.ppermute(lax.slice_in_dim(block, block.shape[dim] - width, None, axis...]
    ppermute x0 -> x8, waiting for transfers between devices: none -> 8.77 us  [the longest x4 7.84 us: exchange(): lax.ppermute(lax.slice_in_dim(block, 0, width, axis=dim), axis, backward)]
    ppermute x8 -> x4, starting transfers between devices: 13.4 us -> 6.83 us  [padded_2(): lax.ppermute(lax.slice_in_dim(block, 0, width, axis=dim), axis, backward)]
  transfers between devices with their start and end apart: 16 -> 16, of which waited for: 12 -> 8; matrix products, arithmetic and copies ran while one was open for 1% -> 1% of each run, Pallas kernels for 0% -> 36%
where the time goes in v10:
time: 277 us
  Pallas kernels  156 us (56%)
  starting transfers between devices  42.9 us (15%)
  other arithmetic  27.4 us (10%)
  waiting for transfers between devices  23.5 us (8%)
  matrix products  15.3 us (6%)
  local copies, waits for them, and re-layouts  10.6 us (4%)
    pallas_call x4, Pallas kernels, depthwise(): pl.pallas_call(body, out_shape=jax.ShapeDtypeStruct((count, rows, cols, c...  156 us
    ppermute x4, starting transfers between devices, exchange(): lax.ppermute(lax.slice_in_dim(block, block.shape[dim] - width, None, axis...  15.6 us
    dot_general x2, matrix products, local_section(): mixed = jnp.dot(hidden, w_out, preferred_element_type=jnp.float32)  14.9 us
    ppermute x4, waiting for transfers between devices, padded_2(): lax.ppermute(lax.slice_in_dim(block, 0, width, axis=dim), axis, backward)  14.7 us
    ppermute x4, starting transfers between devices, padded_2(): lax.ppermute(lax.slice_in_dim(block, block.shape[dim] - width, None, axis...  13.9 us
    ppermute x4, waiting for transfers between devices, exchange(): lax.ppermute(lax.slice_in_dim(block, 0, width, axis=dim), axis, backward)  7.84 us
    ppermute x4, starting transfers between devices, padded_2(): lax.ppermute(lax.slice_in_dim(block, 0, width, axis=dim), axis, backward)  6.83 us
    ppermute x4, starting transfers between devices, exchange(): lax.ppermute(lax.slice_in_dim(block, 0, width, axis=dim), axis, backward)  6.56 us
  transfers between devices with their start and end apart: 16, of which 8 were waited for; matrix products, arithmetic and copies ran while one was open for 1% of the time, Pallas kernels for 36%

profile of v10, /device:TPU:3, one launch (start us, length us, event | category | flops | bytes accessed | tf_op | source)
XLA Modules:
  0.0 276.5 jit_solution(3613938807892337143)
XLA Ops:
  0.0 1.1 fusion.92
  1.1 3.2 %collective-permute-start = (bf16[64,7,128]{2,1,0:T(8,128)(2,1)S(1)}, bf16[64,7,128]{2,1,0:T(8,128)(2,1)S(1)}, u32[]{:S(2)}, u32[]{:S(2)}) collective-permute-start(bf16[64,7,128]{2,1,0:T(8,128)(2,1)S(1)} %get-tuple-element.29), channel_id=1, source_target_pairs={{0,1},{1,2},{2,3},{4,5},{5,6},{6,7},{8,9},{9,10},{10,11},{12,13},{... | collective-permute-start | bytes 344072 | tf_op jit(solution)/shard_map/ppermute | solution.py:126
  4.3 1.3 collective-permute-start.1
  5.7 0.7 multiply_multiply_fusion.3
  6.4 3.6 %collective-permute-done.1 = bf16[64,7,128]{2,1,0:T(8,128)(2,1)S(1)} collective-permute-done((bf16[64,7,128]{2,1,0:T(8,128)(2,1)S(1)}, bf16[64,7,128]{2,1,0:T(8,128)(2,1)S(1)}, u32[]{:S(2)}, u32[]{:S(2)}) %collective-permute-start.1) | collective-permute-done | bytes 114720 | tf_op jit(solution)/shard_map/ppermute | solution.py:129
  10.0 4.1 %fusion.82 = (bf16[1,64,142,128]{3,2,1,0:T(8,128)(2,1)}, bf16[64,142,128]{2,1,0:T(8,128)(2,1)S(1)}) fusion(bf16[64,7,128]{2,1,0:T(8,128)(2,1)S(1)} %collective-permute-done.1, bf16[64,128,128]{2,1,0:T(8,128)(2,1)} %param.10, bf16[64,7,128]{2,1,0:T(8,128)(2,1)S(1)} %collective-permute-done), kind=kLoop, calls=%fused_computation.131 | loop fusion | flops 6979584 | bytes 6979584 | tf_op jit(solution)/shard_map/broadcast_in_dim | solution.py:138
  14.1 0.8 fusion.89
  14.9 5.1 %collective-permute-start.2 = (bf16[7,142,128]{2,1,0:T(8,128)(2,1)}, bf16[7,142,128]{2,1,0:T(8,128)(2,1)S(1)}, u32[]{:S(2)}, u32[]{:S(2)}) collective-permute-start(bf16[7,142,128]{2,1,0:T(8,128)(2,1)} %get-tuple-element.21), channel_id=1, source_target_pairs={{0,4},{4,8},{8,12},{12,16},{16,20},{20,24},{24,28},{1,5},{5,9},{9,... | collective-permute-start | bytes 763400 | tf_op jit(solution)/shard_map/ppermute | solution.py:126
  20.0 1.9 collective-permute-start.3
  21.9 0.8 fusion.68.k_ref
  22.7 74.1 %shard_map.101 = f32[1,48,128,128]{3,2,1,0:T(8,128)} custom-call(bf16[1,64,142,128]{3,2,1,0:T(8,128)(2,1)} %get-tuple-element.17.x_all, f32[15,15,128]{2,1,0:T(8,128)} %fusion.68.k_ref), custom_call_target="tpu_custom_call" | custom-call | flops 353894400 | bytes 5472256 | tf_op jit(solution)/shard_map/pallas_call | solution.py:105
  96.8 0.4 fusion.48
  97.2 1.3 pad_maximum_fusion.6.x_all
  98.5 27.6 %shard_map.100 = f32[2,8,128,128]{3,2,1,0:T(8,128)} custom-call(bf16[2,22,142,128]{3,2,1,0:T(8,128)(2,1)} %pad_maximum_fusion.6.x_all, f32[15,15,128]{2,1,0:T(8,128)} %fusion.68.k_ref), custom_call_target="tpu_custom_call" | custom-call | flops 117964800 | bytes 2648064 | tf_op jit(solution)/shard_map/pallas_call | solution.py:105
  126.1 1.3 slice_bitcast_fusion.3
  127.4 3.3 %fusion.29 = f32[64,128]{1,0:T(8,128)S(1)} fusion(f32[8,128,128]{2,1,0:T(8,128)S(1)} %get-tuple-element.48, f32[48,128,128]{2,1,0:T(8,128)} %bitcast.55, f32[8,128,128]{2,1,0:T(8,128)S(1)} %get-tuple-element.47), kind=kLoop, calls=%fused_computation.41 | loop fusion | flops 3137536 | bytes 4227072 | tf_op jit(solution)/shard_map/reduce_sum | solution.py:150
  130.7 2.6 multiply_reduce_fusion
  133.4 9.4 %add_convert_fusion = bf16[64,128,128]{2,1,0:T(8,128)(2,1)} fusion(bf16[64,128,128]{2,1,0:T(8,128)(2,1)S(1)} %copy-done.2, f32[64,128]{1,0:T(8,128)S(1)} %add_rsqrt_fusion, f32[64,128]{1,0:T(8,128)S(1)} %broadcast_multiply_fusion, f32[8,128,128]{2,1,0:T(8,128)} %copy-done.6, f32[48,128,128]{2,1,0:T(8,128)} %bitcast.56, ...), kind=kOutput, calls=%fused_computation.19 | convolution fusion | flops 2193620992 | bytes 8716288 | tf_op jit(solution)/shard_map/dot_general | solution.py:156
  142.8 0.9 fusion.91
  143.7 4.5 %collective-permute-start.4 = (bf16[1,128,128]{2,1,0:T(8,128)(2,1)S(1)}, bf16[1,128,128]{2,1,0:T(8,128)(2,1)S(1)}, u32[]{:S(2)}, u32[]{:S(2)}) collective-permute-start(bf16[1,128,128]{2,1,0:T(8,128)(2,1)S(1)} %get-tuple-element.27), channel_id=1, source_target_pairs={{0,4},{4,8},{8,12},{12,16},{16,20},{20,24},{24,28},{1,5},{5,9},{9,... | collective-permute-start | bytes 98312 | tf_op jit(solution)/shard_map/ppermute | solution.py:16
  148.3 1.9 collective-permute-start.5
  150.2 4.2 %collective-permute-done.5 = bf16[1,128,128]{2,1,0:T(8,128)(2,1)S(1)} collective-permute-done((bf16[1,128,128]{2,1,0:T(8,128)(2,1)S(1)}, bf16[1,128,128]{2,1,0:T(8,128)(2,1)S(1)}, u32[]{:S(2)}, u32[]{:S(2)}) %collective-permute-start.5) | collective-permute-done | bytes 32800 | tf_op jit(solution)/shard_map/ppermute | solution.py:19
  154.4 1.0 pad_maximum_fusion.27
  155.4 3.2 %collective-permute-start.6 = (bf16[66,1,128]{2,1,0:T(2,128)(2,1)S(1)}, bf16[66,1,128]{2,1,0:T(2,128)(2,1)S(1)}, u32[]{:S(2)}, u32[]{:S(2)}) collective-permute-start(bf16[66,1,128]{2,1,0:T(2,128)(2,1)S(1)} %get-tuple-element.23), channel_id=1, source_target_pairs={{0,1},{1,2},{2,3},{4,5},{5,6},{6,7},{8,9},{9,10},{10,11},{12,13},{... | collective-permute-start | bytes 50696 | tf_op jit(solution)/shard_map/ppermute | solution.py:16
  158.6 1.5 collective-permute-start.7
  160.1 3.2 %collective-permute-done.7 = bf16[66,1,128]{2,1,0:T(2,128)(2,1)S(1)} collective-permute-done((bf16[66,1,128]{2,1,0:T(2,128)(2,1)S(1)}, bf16[66,1,128]{2,1,0:T(2,128)(2,1)S(1)}, u32[]{:S(2)}, u32[]{:S(2)}) %collective-permute-start.7) | collective-permute-done | bytes 16928 | tf_op jit(solution)/shard_map/ppermute | solution.py:19
  163.3 0.9 maximum_convert_fusion
  164.2 0.6 fusion.83
  164.7 0.6 fusion.84
  165.3 1.6 fusion.22
  166.9 0.6 fusion.90
  167.5 0.5 fusion.57
  168.0 0.3 copy-done.9
  168.3 0.4 convolution_convert_fusion
  168.8 3.2 %collective-permute-start.8 = (bf16[32,7,256]{2,1,0:T(8,128)(2,1)S(1)}, bf16[32,7,256]{2,1,0:T(8,128)(2,1)S(1)}, u32[]{:S(2)}, u32[]{:S(2)}) collective-permute-start(bf16[32,7,256]{2,1,0:T(8,128)(2,1)S(1)} %get-tuple-element.45), channel_id=1, source_target_pairs={{0,1},{1,2},{2,3},{4,5},{5,6},{6,7},{8,9},{9,10},{10,11},{12,13},{... | collective-permute-start | bytes 344072 | tf_op jit(solution)/shard_map/ppermute | solution.py:126
  172.1 1.4 collective-permute-start.9
  173.5 0.8 collective-permute-done.8
  174.3 4.3 %collective-permute-done.9 = bf16[32,7,256]{2,1,0:T(8,128)(2,1)S(1)} collective-permute-done((bf16[32,7,256]{2,1,0:T(8,128)(2,1)S(1)}, bf16[32,7,256]{2,1,0:T(8,128)(2,1)S(1)}, u32[]{:S(2)}, u32[]{:S(2)}) %collective-permute-start.9) | collective-permute-done | bytes 114720 | tf_op jit(solution)/shard_map/ppermute | solution.py:129
  178.6 1.8 fusion.81
  180.4 4.1 %collective-permute-start.10 = (bf16[7,78,256]{2,1,0:T(8,128)(2,1)S(1)}, bf16[7,78,256]{2,1,0:T(8,128)(2,1)S(1)}, u32[]{:S(2)}, u32[]{:S(2)}) collective-permute-start(bf16[7,78,256]{2,1,0:T(8,128)(2,1)S(1)} %get-tuple-element.35), channel_id=1, source_target_pairs={{0,4},{4,8},{8,12},{12,16},{16,20},{20,24},{24,28},{1,5},{5,9},{9,... | collective-permute-start | bytes 838664 | tf_op jit(solution)/shard_map/ppermute | solution.py:126
  184.5 1.9 collective-permute-start.11
  186.5 0.8 fusion.66.k_ref
  187.3 26.6 %shard_map.103 = f32[1,16,64,256]{3,2,1,0:T(8,128)} custom-call(bf16[1,32,78,256]{3,2,1,0:T(8,128)(2,1)} %get-tuple-element.31.x_all, f32[15,15,256]{2,1,0:T(8,128)} %fusion.66.k_ref), custom_call_target="tpu_custom_call" | custom-call | flops 117964800 | bytes 2326528 | tf_op jit(solution)/shard_map/pallas_call | solution.py:105
  213.9 0.7 fusion.45
  214.7 1.4 pad_maximum_fusion.3.x_all
  216.1 28.1 %shard_map.102 = f32[2,8,64,256]{3,2,1,0:T(8,128)} custom-call(bf16[2,22,78,256]{3,2,1,0:T(8,128)(2,1)} %pad_maximum_fusion.3.x_all, f32[15,15,256]{2,1,0:T(8,128)} %fusion.66.k_ref), custom_call_target="tpu_custom_call" | custom-call | flops 117964800 | bytes 2805760 | tf_op jit(solution)/shard_map/pallas_call | solution.py:105
  244.2 1.3 slice_bitcast_fusion.1
  245.5 0.3 fusion.46
  245.8 0.4 copy-done.5
  246.3 0.6 multiply_reduce_fusion.1
  246.9 5.5 %add_convert_fusion.1 = bf16[32,64,256]{2,1,0:T(8,128)(2,1)} fusion(bf16[32,64,256]{2,1,0:T(8,128)(2,1)S(1)} %convolution_convert_fusion, f32[32,64]{1,0:T(8,128)S(1)} %add_rsqrt_fusion.1, f32[32,64]{1,0:T(8,128)S(1)} %broadcast_multiply_fusion.1, f32[8,64,256]{2,1,0:T(8,128)} %copy-done.5, f32[16,64,256]{2,1,0:T(8,128)S(1)} %bitcast.62, ...), kind=kOutput, calls=%fused_computation.35 | convolution fusion | flops 2170552320 | bytes 5259264 | tf_op jit(solution)/shard_map/dot_general | solution.py:156
  252.4 0.8 fusion.95
  253.2 4.5 %collective-permute-start.12 = (bf16[1,64,256]{2,1,0:T(8,128)(2,1)S(1)}, bf16[1,64,256]{2,1,0:T(8,128)(2,1)S(1)}, u32[]{:S(2)}, u32[]{:S(2)}) collective-permute-start(bf16[1,64,256]{2,1,0:T(8,128)(2,1)S(1)} %get-tuple-element.41), channel_id=1, source_target_pairs={{0,4},{4,8},{8,12},{12,16},{16,20},{20,24},{24,28},{1,5},{5,9},{9,... | collective-permute-start | bytes 98312 | tf_op jit(solution)/shard_map/ppermute | solution.py:16
  257.7 1.9 collective-permute-start.13
  259.7 4.2 %collective-permute-done.13 = bf16[1,64,256]{2,1,0:T(8,128)(2,1)S(1)} collective-permute-done((bf16[1,64,256]{2,1,0:T(8,128)(2,1)S(1)}, bf16[1,64,256]{2,1,0:T(8,128)(2,1)S(1)}, u32[]{:S(2)}, u32[]{:S(2)}) %collective-permute-start.13) | collective-permute-done | bytes 32800 | tf_op jit(solution)/shard_map/ppermute | solution.py:19
  263.9 1.0 pad_maximum_fusion.24
  264.9 1.6 collective-permute-start.14
  266.6 1.5 collective-permute-start.15
  268.1 3.1 %collective-permute-done.15 = bf16[34,1,256]{2,1,0:T(2,128)(2,1)S(1)} collective-permute-done((bf16[34,1,256]{2,1,0:T(2,128)(2,1)S(1)}, bf16[34,1,256]{2,1,0:T(2,128)(2,1)S(1)}, u32[]{:S(2)}, u32[]{:S(2)}) %collective-permute-start.15) | collective-permute-done | bytes 17440 | tf_op jit(solution)/shard_map/ppermute | solution.py:19
  271.2 1.8 maximum_convert_fusion.1
  273.0 0.4 fusion.86
  273.8 1.4 fusion.33
  275.2 0.3 fusion.94
  275.7 0.8 copy.20
  (45 shorter events, 1.0 us)
Async XLA Ops:
  0.0 246.9 %copy-start = (bf16[1024,256]{1,0:T(8,128)(2,1)S(1)}, bf16[1024,256]{1,0:T(8,128)(2,1)}, u32[]{:S(2)}) copy-start(bf16[1024,256]{1,0:T(8,128)(2,1)} %param.19) | copy-start | bytes 1572868
  1.1 5.4 %collective-permute-start = (bf16[64,7,128]{2,1,0:T(8,128)(2,1)S(1)}, bf16[64,7,128]{2,1,0:T(8,128)(2,1)S(1)}, u32[]{:S(2)}, u32[]{:S(2)}) collective-permute-start(bf16[64,7,128]{2,1,0:T(8,128)(2,1)S(1)} %get-tuple-element.29), channel_id=1, source_target_pairs={{0,1},{1,2},{2,3},{4,5},{5,6},{6,7},{8,9},{9,10},{10,11},{12,13},{... | collective-permute-start | bytes 344072 | tf_op jit(solution)/shard_map/ppermute | solution.py:126
  4.3 5.7 %collective-permute-start.1 = (bf16[64,7,128]{2,1,0:T(8,128)(2,1)S(1)}, bf16[64,7,128]{2,1,0:T(8,128)(2,1)S(1)}, u32[]{:S(2)}, u32[]{:S(2)}) collective-permute-start(bf16[64,7,128]{2,1,0:T(8,128)(2,1)S(1)} %get-tuple-element.30), channel_id=1, source_target_pairs={{1,0},{2,1},{3,2},{5,4},{6,5},{7,6},{9,8},{10,9},{11,10},{13,12},{... | collective-permute-start | bytes 344072 | tf_op jit(solution)/shard_map/ppermute | solution.py:129
  6.3 15.6 %copy-start.8 = (f32[15,15,128]{2,1,0:T(8,128)S(1)}, f32[15,15,128]{2,1,0:T(8,128)}, u32[]{:S(2)}) copy-start(f32[15,15,128]{2,1,0:T(8,128)} %param.11) | copy-start | bytes 345604
  14.9 81.9 %collective-permute-start.2 = (bf16[7,142,128]{2,1,0:T(8,128)(2,1)}, bf16[7,142,128]{2,1,0:T(8,128)(2,1)S(1)}, u32[]{:S(2)}, u32[]{:S(2)}) collective-permute-start(bf16[7,142,128]{2,1,0:T(8,128)(2,1)} %get-tuple-element.21), channel_id=1, source_target_pairs={{0,4},{4,8},{8,12},{12,16},{16,20},{20,24},{24,28},{1,5},{5,9},{9,... | collective-permute-start | bytes 763400 | tf_op jit(solution)/shard_map/ppermute | solution.py:126
  20.0 76.8 %collective-permute-start.3 = (bf16[7,142,128]{2,1,0:T(8,128)(2,1)}, bf16[7,142,128]{2,1,0:T(8,128)(2,1)S(1)}, u32[]{:S(2)}, u32[]{:S(2)}) collective-permute-start(bf16[7,142,128]{2,1,0:T(8,128)(2,1)} %get-tuple-element.22), channel_id=1, source_target_pairs={{4,0},{8,4},{12,8},{16,12},{20,16},{24,20},{28,24},{5,1},{9,5},{13... | collective-permute-start | bytes 763400 | tf_op jit(solution)/shard_map/ppermute | solution.py:129
  22.7 74.1 %copy-start.2 = (bf16[64,128,128]{2,1,0:T(8,128)(2,1)S(1)}, bf16[64,128,128]{2,1,0:T(8,128)(2,1)}, u32[]{:S(2)}) copy-start(bf16[64,128,128]{2,1,0:T(8,128)(2,1)} %param.10) | copy-start | bytes 6291460
  127.4 6.0 %copy-start.6 = (f32[8,128,128]{2,1,0:T(8,128)}, f32[8,128,128]{2,1,0:T(8,128)S(1)}, u32[]{:S(2)}) copy-start(f32[8,128,128]{2,1,0:T(8,128)S(1)} %get-tuple-element.48) | copy-start | bytes 1572868
  127.4 3.3 %copy-start.1 = (f32[1,48,128,128]{3,2,1,0:T(8,128)S(1)}, f32[1,48,128,128]{3,2,1,0:T(8,128)}, u32[]{:S(2)}) copy-start(f32[1,48,128,128]{3,2,1,0:T(8,128)} %shard_map.101) | copy-start | bytes 9437188
  130.7 2.7 copy-start.11
  130.7 2.7 copy-start.12
  142.8 20.5 %copy-start.4 = (bf16[64,128,128]{2,1,0:T(8,128)(2,1)S(1)}, bf16[64,128,128]{2,1,0:T(8,128)(2,1)}, u32[]{:S(2)}) copy-start(bf16[64,128,128]{2,1,0:T(8,128)(2,1)} %add_convert_fusion) | copy-start | bytes 6291460
  143.7 6.5 %collective-permute-start.4 = (bf16[1,128,128]{2,1,0:T(8,128)(2,1)S(1)}, bf16[1,128,128]{2,1,0:T(8,128)(2,1)S(1)}, u32[]{:S(2)}, u32[]{:S(2)}) collective-permute-start(bf16[1,128,128]{2,1,0:T(8,128)(2,1)S(1)} %get-tuple-element.27), channel_id=1, source_target_pairs={{0,4},{4,8},{8,12},{12,16},{16,20},{20,24},{24,28},{1,5},{5,9},{9,... | collective-permute-start | bytes 98312 | tf_op jit(solution)/shard_map/ppermute | solution.py:16
  148.3 6.1 %collective-permute-start.5 = (bf16[1,128,128]{2,1,0:T(8,128)(2,1)S(1)}, bf16[1,128,128]{2,1,0:T(8,128)(2,1)S(1)}, u32[]{:S(2)}, u32[]{:S(2)}) collective-permute-start(bf16[1,128,128]{2,1,0:T(8,128)(2,1)S(1)} %get-tuple-element.28), channel_id=1, source_target_pairs={{4,0},{8,4},{12,8},{16,12},{20,16},{24,20},{28,24},{5,1},{9,5},{13... | collective-permute-start | bytes 98312 | tf_op jit(solution)/shard_map/ppermute | solution.py:19
  155.4 4.7 %collective-permute-start.6 = (bf16[66,1,128]{2,1,0:T(2,128)(2,1)S(1)}, bf16[66,1,128]{2,1,0:T(2,128)(2,1)S(1)}, u32[]{:S(2)}, u32[]{:S(2)}) collective-permute-start(bf16[66,1,128]{2,1,0:T(2,128)(2,1)S(1)} %get-tuple-element.23), channel_id=1, source_target_pairs={{0,1},{1,2},{2,3},{4,5},{5,6},{6,7},{8,9},{9,10},{10,11},{12,13},{... | collective-permute-start | bytes 50696 | tf_op jit(solution)/shard_map/ppermute | solution.py:16
  158.6 4.7 %collective-permute-start.7 = (bf16[66,1,128]{2,1,0:T(2,128)(2,1)S(1)}, bf16[66,1,128]{2,1,0:T(2,128)(2,1)S(1)}, u32[]{:S(2)}, u32[]{:S(2)}) collective-permute-start(bf16[66,1,128]{2,1,0:T(2,128)(2,1)S(1)} %get-tuple-element.24), channel_id=1, source_target_pairs={{1,0},{2,1},{3,2},{5,4},{6,5},{7,6},{9,8},{10,9},{11,10},{13,12},{... | collective-permute-start | bytes 50696 | tf_op jit(solution)/shard_map/ppermute | solution.py:19
  167.5 0.8 copy-start.9
  168.8 5.5 %collective-permute-start.8 = (bf16[32,7,256]{2,1,0:T(8,128)(2,1)S(1)}, bf16[32,7,256]{2,1,0:T(8,128)(2,1)S(1)}, u32[]{:S(2)}, u32[]{:S(2)}) collective-permute-start(bf16[32,7,256]{2,1,0:T(8,128)(2,1)S(1)} %get-tuple-element.45), channel_id=1, source_target_pairs={{0,1},{1,2},{2,3},{4,5},{5,6},{6,7},{8,9},{9,10},{10,11},{12,13},{... | collective-permute-start | bytes 344072 | tf_op jit(solution)/shard_map/ppermute | solution.py:126
  172.0 14.4 %copy-start.10 = (f32[256]{0:T(256)S(1)}, f32[256]{0:T(256)}, u32[]{:S(2)}) copy-start(f32[256]{0:T(256)} %param.17) | copy-start | bytes 3076
  172.0 14.4 %copy-start.7 = (f32[15,15,256]{2,1,0:T(8,128)S(1)}, f32[15,15,256]{2,1,0:T(8,128)}, u32[]{:S(2)}) copy-start(f32[15,15,256]{2,1,0:T(8,128)} %param.16) | copy-start | bytes 691204
  172.1 6.5 %collective-permute-start.9 = (bf16[32,7,256]{2,1,0:T(8,128)(2,1)S(1)}, bf16[32,7,256]{2,1,0:T(8,128)(2,1)S(1)}, u32[]{:S(2)}, u32[]{:S(2)}) collective-permute-start(bf16[32,7,256]{2,1,0:T(8,128)(2,1)S(1)} %get-tuple-element.46), channel_id=1, source_target_pairs={{1,0},{2,1},{3,2},{5,4},{6,5},{7,6},{9,8},{10,9},{11,10},{13,12},{... | collective-permute-start | bytes 344072 | tf_op jit(solution)/shard_map/ppermute | solution.py:129
  180.4 33.5 %collective-permute-start.10 = (bf16[7,78,256]{2,1,0:T(8,128)(2,1)S(1)}, bf16[7,78,256]{2,1,0:T(8,128)(2,1)S(1)}, u32[]{:S(2)}, u32[]{:S(2)}) collective-permute-start(bf16[7,78,256]{2,1,0:T(8,128)(2,1)S(1)} %get-tuple-element.35), channel_id=1, source_target_pairs={{0,4},{4,8},{8,12},{12,16},{16,20},{20,24},{24,28},{1,5},{5,9},{9,... | collective-permute-start | bytes 838664 | tf_op jit(solution)/shard_map/ppermute | solution.py:126
  184.5 29.4 %collective-permute-start.11 = (bf16[7,78,256]{2,1,0:T(8,128)(2,1)S(1)}, bf16[7,78,256]{2,1,0:T(8,128)(2,1)S(1)}, u32[]{:S(2)}, u32[]{:S(2)}) collective-permute-start(bf16[7,78,256]{2,1,0:T(8,128)(2,1)S(1)} %get-tuple-element.36), channel_id=1, source_target_pairs={{4,0},{8,4},{12,8},{16,12},{20,16},{24,20},{28,24},{5,1},{9,5},{13... | collective-permute-start | bytes 838664 | tf_op jit(solution)/shard_map/ppermute | solution.py:129
  216.1 29.4 %copy-start.3 = (f32[1,16,64,256]{3,2,1,0:T(8,128)S(1)}, f32[1,16,64,256]{3,2,1,0:T(8,128)}, u32[]{:S(2)}) copy-start(f32[1,16,64,256]{3,2,1,0:T(8,128)} %shard_map.103) | copy-start | bytes 3145732
  245.5 0.8 copy-start.5
  253.2 6.5 %collective-permute-start.12 = (bf16[1,64,256]{2,1,0:T(8,128)(2,1)S(1)}, bf16[1,64,256]{2,1,0:T(8,128)(2,1)S(1)}, u32[]{:S(2)}, u32[]{:S(2)}) collective-permute-start(bf16[1,64,256]{2,1,0:T(8,128)(2,1)S(1)} %get-tuple-element.41), channel_id=1, source_target_pairs={{0,4},{4,8},{8,12},{12,16},{16,20},{20,24},{24,28},{1,5},{5,9},{9,... | collective-permute-start | bytes 98312 | tf_op jit(solution)/shard_map/ppermute | solution.py:16
  257.7 6.1 %collective-permute-start.13 = (bf16[1,64,256]{2,1,0:T(8,128)(2,1)S(1)}, bf16[1,64,256]{2,1,0:T(8,128)(2,1)S(1)}, u32[]{:S(2)}, u32[]{:S(2)}) collective-permute-start(bf16[1,64,256]{2,1,0:T(8,128)(2,1)S(1)} %get-tuple-element.42), channel_id=1, source_target_pairs={{4,0},{8,4},{12,8},{16,12},{20,16},{24,20},{28,24},{5,1},{9,5},{13... | collective-permute-start | bytes 98312 | tf_op jit(solution)/shard_map/ppermute | solution.py:19
  264.9 3.2 %collective-permute-start.14 = (bf16[34,1,256]{2,1,0:T(2,128)(2,1)S(1)}, bf16[34,1,256]{2,1,0:T(2,128)(2,1)S(1)}, u32[]{:S(2)}, u32[]{:S(2)}) collective-permute-start(bf16[34,1,256]{2,1,0:T(2,128)(2,1)S(1)} %get-tuple-element.37), channel_id=1, source_target_pairs={{0,1},{1,2},{2,3},{4,5},{5,6},{6,7},{8,9},{9,10},{10,11},{12,13},{... | collective-permute-start | bytes 52232 | tf_op jit(solution)/shard_map/ppermute | solution.py:16
  266.6 4.7 %collective-permute-start.15 = (bf16[34,1,256]{2,1,0:T(2,128)(2,1)S(1)}, bf16[34,1,256]{2,1,0:T(2,128)(2,1)S(1)}, u32[]{:S(2)}, u32[]{:S(2)}) collective-permute-start(bf16[34,1,256]{2,1,0:T(2,128)(2,1)S(1)} %get-tuple-element.38), channel_id=1, source_target_pairs={{1,0},{2,1},{3,2},{5,4},{6,5},{7,6},{9,8},{10,9},{11,10},{13,12},{... | collective-permute-start | bytes 52232 | tf_op jit(solution)/shard_map/ppermute | solution.py:19

commit v11 on v10

--- a/solution.py
+++ b/solution.py
@@ -28,7 +28,7 @@
     return (raw * mask).astype(jnp.bfloat16)
 
 
-def _dw_body(x_all, k_ref, o_all, xf_ref, xs_ref, *, taps, base, rows, cols, chans, rb):
+def _dw_body(x_all, k_ref, o_all, xf_ref, xs_ref, *, taps, cbase, rows, cols, chans, rb):
     nlb = chans // 128
     njb = cols // 8
     nrb = rows // rb
@@ -38,19 +38,19 @@
         o_ref = o_all.at[n]
 
         def widen_row(r, c):
-            xf_ref[r] = x_ref[base + r].astype(jnp.float32)
+            xf_ref[r] = x_ref[r].astype(jnp.float32)
             return c
 
         lax.fori_loop(0, rows + taps - 1, widen_row, 0)
         first = True
         for s in range(8):
-            if s == 0:
+            if cbase + s == 0:
                 src = xf_ref
             else:
                 width = cols + 8 if s + 8 < taps else cols
 
                 def shift(r, c, s=s, width=width):
-                    xs_ref[r, pl.ds(0, width), :] = xf_ref[r, pl.ds(s, width), :]
+                    xs_ref[r, pl.ds(0, width), :] = xf_ref[r, pl.ds(cbase + s, width), :]
                     return c
 
                 lax.fori_loop(0, rows + taps - 1, shift, 0)
@@ -93,13 +93,13 @@
     lax.fori_loop(0, x_all.shape[0], one_strip, 0)
 
 
-def depthwise(strips, kernel, base, rows):
+def depthwise(strips, kernel, cbase, cols):
     taps = kernel.shape[0]
     count = strips.shape[0]
-    cols = strips.shape[2] - taps + 1
+    rows = strips.shape[1] - taps + 1
     chans = strips.shape[3]
     body = functools.partial(
-        _dw_body, taps=taps, base=base, rows=rows, cols=cols, chans=chans, rb=8
+        _dw_body, taps=taps, cbase=cbase, rows=rows, cols=cols, chans=chans, rb=8
     )
     vmem = pl.BlockSpec(memory_space=pltpu.VMEM)
     return pl.pallas_call(
@@ -108,7 +108,7 @@
         in_specs=[vmem, vmem],
         out_specs=vmem,
         scratch_shapes=[
-            pltpu.VMEM((rows + taps - 1,) + strips.shape[2:], jnp.float32),
+            pltpu.VMEM(strips.shape[1:], jnp.float32),
             pltpu.VMEM((rows + taps - 1, cols + 8, chans), jnp.float32),
         ],
         cost_estimate=pl.CostEstimate(
@@ -132,16 +132,14 @@
 
 def section_conv(block, kernel):
     reach = (kernel.shape[0] - 1) // 2
-    rows = block.shape[0]
+    cols = block.shape[1]
     band = 8
-    wide = exchange(block, "col", 1, reach)
-    middle = depthwise(wide[None], kernel, band - reach, rows - 2 * band)
-    full = exchange(wide, "row", 0, reach)
-    ends = jnp.stack(
-        [full[: band + 2 * reach], full[rows - band :]], axis=0
-    )
+    tall = exchange(block, "row", 0, reach)
+    middle = depthwise(tall[None], kernel, band - reach, cols - 2 * band)
+    full = exchange(tall, "col", 1, reach)
+    ends = jnp.stack([full[:, : band + 2 * reach], full[:, cols - band :]], axis=0)
     edge = depthwise(ends, kernel, 0, band)
-    return jnp.concatenate([edge[0], middle[0], edge[1]], axis=0)
+    return jnp.concatenate([edge[0], middle[0], edge[1]], axis=1)
 
 
 def local_section(field, raw, sigma, w_in, w_out):

time: 277 us -> 276 us (level)
  Pallas kernels: 156 us -> 162 us
  other arithmetic: 27.4 us -> 22.5 us
    pallas_call x4, Pallas kernels: 156 us -> 162 us  [depthwise(): pl.pallas_call(body, out_shape=jax.ShapeDtypeStruct((count, rows, cols, c...]
    broadcast_in_dim x2 -> x1, other arithmetic: 5.91 us -> 1.37 us  [section_conv(): middle = depthwise(tall[None], kernel, band - reach, cols - 2 * band)]
  transfers between devices with their start and end apart: 16 -> 16, of which waited for: 8 -> 8; matrix products, arithmetic and copies ran while one was open for 1% -> 2% of each run, Pallas kernels for 36% -> 47%
where the time goes in v11:
time: 276 us; the launch traced here: 275 us
  Pallas kernels  162 us (59%)
  starting transfers between devices  40.2 us (15%)
  waiting for transfers between devices  24.4 us (9%)
  other arithmetic  22.5 us (8%)
  matrix products  14.5 us (5%)
  local copies, waits for them, and re-layouts  10.5 us (4%)
    pallas_call x4, Pallas kernels, depthwise(): pl.pallas_call(body, out_shape=jax.ShapeDtypeStruct((count, rows, cols, c...  162 us
    ppermute x4, waiting for transfers between devices, padded_2(): lax.ppermute(lax.slice_in_dim(block, 0, width, axis=dim), axis, backward)  14.5 us
    dot_general x2, matrix products, local_section(): mixed = jnp.dot(hidden, w_out, preferred_element_type=jnp.float32)  14.1 us
    ppermute x4, starting transfers between devices, exchange(): lax.ppermute(lax.slice_in_dim(block, block.shape[dim] - width, None, axis...  13.7 us
    ppermute x4, starting transfers between devices, padded_2(): lax.ppermute(lax.slice_in_dim(block, block.shape[dim] - width, None, axis...  12.9 us
    ppermute x4, waiting for transfers between devices, exchange(): lax.ppermute(lax.slice_in_dim(block, 0, width, axis=dim), axis, backward)  7.31 us
    ppermute x4, starting transfers between devices, padded_2(): lax.ppermute(lax.slice_in_dim(block, 0, width, axis=dim), axis, backward)  7.28 us
    ppermute x4, starting transfers between devices, exchange(): lax.ppermute(lax.slice_in_dim(block, 0, width, axis=dim), axis, backward)  6.41 us
  transfers between devices with their start and end apart: 16, of which 8 were waited for; matrix products, arithmetic and copies ran while one was open for 2% of the time, Pallas kernels for 47%

profile of v11, /device:TPU:3, one launch (start us, length us, event | category | flops | bytes accessed | tf_op | source)
XLA Modules:
  0.0 274.8 jit_solution(1972278773792846823)
XLA Ops:
  0.0 1.1 fusion.91
  1.1 3.7 %collective-permute-start = (bf16[7,128,128]{2,1,0:T(8,128)(2,1)S(1)}, bf16[7,128,128]{2,1,0:T(8,128)(2,1)S(1)}, u32[]{:S(2)}, u32[]{:S(2)}) collective-permute-start(bf16[7,128,128]{2,1,0:T(8,128)(2,1)S(1)} %get-tuple-element.28), channel_id=1, source_target_pairs={{0,4},{4,8},{8,12},{12,16},{16,20},{20,24},{24,28},{1,5},{5,9},{9,... | collective-permute-start | bytes 688136 | tf_op jit(solution)/shard_map/ppermute | solution.py:126
  4.8 1.9 collective-permute-start.1
  6.8 0.7 multiply_multiply_fusion.3
  7.5 0.3 collective-permute-done
  7.8 2.0 constant_dynamic-update-slice_fusion.1
  9.8 3.2 %collective-permute-done.1 = bf16[7,128,128]{2,1,0:T(8,128)(2,1)S(1)} collective-permute-done((bf16[7,128,128]{2,1,0:T(8,128)(2,1)S(1)}, bf16[7,128,128]{2,1,0:T(8,128)(2,1)S(1)}, u32[]{:S(2)}, u32[]{:S(2)}) %collective-permute-start.1) | collective-permute-done | bytes 229408 | tf_op jit(solution)/shard_map/ppermute | solution.py:129
  13.2 3.9 %collective-permute-start.2 = (bf16[78,7,128]{2,1,0:T(8,128)(2,1)S(1)}, bf16[78,7,128]{2,1,0:T(8,128)(2,1)}, u32[]{:S(2)}, u32[]{:S(2)}) collective-permute-start(bf16[78,7,128]{2,1,0:T(8,128)(2,1)S(1)} %get-tuple-element.13), channel_id=1, source_target_pairs={{0,1},{1,2},{2,3},{4,5},{5,6},{6,7},{8,9},{9,10},{10,11},{12,13},{... | collective-permute-start | bytes 419336 | tf_op jit(solution)/shard_map/ppermute | solution.py:126
  17.1 1.3 collective-permute-start.3
  18.4 0.8 fusion.68.k_ref
  19.1 87.5 %shard_map.101 = f32[1,64,112,128]{3,2,1,0:T(8,128)} custom-call(bf16[1,78,128,128]{3,2,1,0:T(8,128)(2,1)} %bitcast.62, f32[15,15,128]{2,1,0:T(8,128)} %fusion.68.k_ref), custom_call_target="tpu_custom_call" | custom-call | flops 412876800 | bytes 6225920 | tf_op jit(solution)/shard_map/pallas_call | solution.py:105
  106.6 1.6 fusion.57
  108.2 1.1 pad_maximum_fusion.6.x_all
  109.3 18.7 %shard_map.100 = f32[2,64,8,128]{3,2,1,0:T(8,128)} custom-call(bf16[2,78,22,128]{3,2,1,0:T(8,128)(2,1)} %pad_maximum_fusion.6.x_all, f32[15,15,128]{2,1,0:T(8,128)} %fusion.68.k_ref), custom_call_target="tpu_custom_call" | custom-call | flops 58982400 | bytes 1402880 | tf_op jit(solution)/shard_map/pallas_call | solution.py:105
  128.0 1.1 slice_bitcast_fusion.3
  129.0 3.3 %fusion.29 = f32[64,128]{1,0:T(8,128)S(1)} fusion(f32[64,8,128]{2,1,0:T(8,128)S(1)} %get-tuple-element.46, f32[64,112,128]{2,1,0:T(8,128)} %bitcast.54, f32[64,8,128]{2,1,0:T(8,128)S(1)} %get-tuple-element.45), kind=kLoop, calls=%fused_computation.39 | loop fusion | flops 3137536 | bytes 4227072 | tf_op jit(solution)/shard_map/reduce_sum | solution.py:148
  132.4 2.6 multiply_reduce_fusion
  135.1 8.6 %add_convert_fusion = bf16[64,128,128]{2,1,0:T(8,128)(2,1)S(1)} fusion(bf16[64,128,128]{2,1,0:T(8,128)(2,1)} %param.10, f32[64,128]{1,0:T(8,128)S(1)} %add_rsqrt_fusion, f32[64,128]{1,0:T(8,128)S(1)} %broadcast_multiply_fusion, f32[64,8,128]{2,1,0:T(8,128)S(1)} %get-tuple-element.46, f32[64,112,128]{2,1,0:T(8,128)} %bitcast.55, ...), kind=kOutput, calls=%fused_computation.19 | convolution fusion | flops 2193620992 | bytes 8716288 | tf_op jit(solution)/shard_map/dot_general | solution.py:154
  143.8 2.3 collective-permute-start.4
  146.1 2.0 collective-permute-start.5
  148.1 4.1 %collective-permute-done.5 = bf16[1,128,128]{2,1,0:T(8,128)(2,1)S(1)} collective-permute-done((bf16[1,128,128]{2,1,0:T(8,128)(2,1)S(1)}, bf16[1,128,128]{2,1,0:T(8,128)(2,1)S(1)}, u32[]{:S(2)}, u32[]{:S(2)}) %collective-permute-start.5) | collective-permute-done | bytes 32800 | tf_op jit(solution)/shard_map/ppermute | solution.py:19
  152.3 4.3 %collective-permute-start.6 = (bf16[66,1,128]{2,1,0:T(2,128)(2,1)S(1)}, bf16[66,1,128]{2,1,0:T(2,128)(2,1)S(1)}, u32[]{:S(2)}, u32[]{:S(2)}) collective-permute-start(bf16[66,1,128]{2,1,0:T(2,128)(2,1)S(1)} %get-tuple-element.21), channel_id=1, source_target_pairs={{0,1},{1,2},{2,3},{4,5},{5,6},{6,7},{8,9},{9,10},{10,11},{12,13},{... | collective-permute-start | bytes 50696 | tf_op jit(solution)/shard_map/ppermute | solution.py:16
  156.6 1.5 collective-permute-start.7
  158.1 3.2 %collective-permute-done.7 = bf16[66,1,128]{2,1,0:T(2,128)(2,1)S(1)} collective-permute-done((bf16[66,1,128]{2,1,0:T(2,128)(2,1)S(1)}, bf16[66,1,128]{2,1,0:T(2,128)(2,1)S(1)}, u32[]{:S(2)}, u32[]{:S(2)}) %collective-permute-start.7) | collective-permute-done | bytes 16928 | tf_op jit(solution)/shard_map/ppermute | solution.py:19
  161.2 0.8 maximum_convert_fusion
  162.1 0.6 fusion.82
  162.7 0.6 fusion.83
  163.3 1.6 fusion.22
  164.8 0.6 fusion.89
  165.4 0.5 fusion.55
  166.0 0.3 copy-done.7
  166.3 0.4 convolution_convert_fusion
  166.8 3.3 %collective-permute-start.8 = (bf16[7,64,256]{2,1,0:T(8,128)(2,1)S(1)}, bf16[7,64,256]{2,1,0:T(8,128)(2,1)S(1)}, u32[]{:S(2)}, u32[]{:S(2)}) collective-permute-start(bf16[7,64,256]{2,1,0:T(8,128)(2,1)S(1)} %get-tuple-element.41), channel_id=1, source_target_pairs={{0,4},{4,8},{8,12},{12,16},{16,20},{20,24},{24,28},{1,5},{5,9},{9,... | collective-permute-start | bytes 688136 | tf_op jit(solution)/shard_map/ppermute | solution.py:126
  170.1 1.9 collective-permute-start.9
  172.1 2.2 collective-permute-done.8
  174.3 4.1 %collective-permute-done.9 = bf16[7,64,256]{2,1,0:T(8,128)(2,1)S(1)} collective-permute-done((bf16[7,64,256]{2,1,0:T(8,128)(2,1)S(1)}, bf16[7,64,256]{2,1,0:T(8,128)(2,1)S(1)}, u32[]{:S(2)}, u32[]{:S(2)}) %collective-permute-start.9) | collective-permute-done | bytes 229408 | tf_op jit(solution)/shard_map/ppermute | solution.py:129
  178.3 1.4 fusion.81
  179.8 2.8 %collective-permute-start.10 = (bf16[46,7,256]{2,1,0:T(8,128)(2,1)S(1)}, bf16[46,7,256]{2,1,0:T(8,128)(2,1)S(1)}, u32[]{:S(2)}, u32[]{:S(2)}) collective-permute-start(bf16[46,7,256]{2,1,0:T(8,128)(2,1)S(1)} %get-tuple-element.33), channel_id=1, source_target_pairs={{0,1},{1,2},{2,3},{4,5},{5,6},{6,7},{8,9},{9,10},{10,11},{12,13},{... | collective-permute-start | bytes 494600 | tf_op jit(solution)/shard_map/ppermute | solution.py:126
  182.5 1.3 collective-permute-start.11
  183.9 0.8 fusion.66.k_ref
  184.7 40.4 %shard_map.103 = f32[1,32,48,256]{3,2,1,0:T(8,128)} custom-call(bf16[1,46,64,256]{3,2,1,0:T(8,128)(2,1)} %get-tuple-element.29.x_all, f32[15,15,256]{2,1,0:T(8,128)} %fusion.66.k_ref), custom_call_target="tpu_custom_call" | custom-call | flops 176947200 | bytes 3080192 | tf_op jit(solution)/shard_map/pallas_call | solution.py:105
  225.1 0.6 fusion.46
  225.6 1.1 pad_maximum_fusion.5.x_all
  226.8 15.7 %shard_map.102 = f32[2,32,8,256]{3,2,1,0:T(8,128)} custom-call(bf16[2,46,22,256]{3,2,1,0:T(8,128)(2,1)} %pad_maximum_fusion.5.x_all, f32[15,15,256]{2,1,0:T(8,128)} %fusion.66.k_ref), custom_call_target="tpu_custom_call" | custom-call | flops 58982400 | bytes 1560576 | tf_op jit(solution)/shard_map/pallas_call | solution.py:105
  242.5 1.1 slice_bitcast_fusion.1
  243.6 0.4 fusion.44
  244.0 0.3 copy-done.4
  244.3 0.6 multiply_reduce_fusion.1
  244.9 5.4 %add_convert_fusion.1 = bf16[32,64,256]{2,1,0:T(8,128)(2,1)} fusion(bf16[32,64,256]{2,1,0:T(8,128)(2,1)S(1)} %convolution_convert_fusion, f32[32,64]{1,0:T(8,128)S(1)} %add_rsqrt_fusion.1, f32[32,64]{1,0:T(8,128)S(1)} %broadcast_multiply_fusion.1, f32[32,8,256]{2,1,0:T(8,128)} %copy-done.4, f32[32,48,256]{2,1,0:T(8,128)S(1)} %bitcast.61, ...), kind=kOutput, calls=%fused_computation.34 | convolution fusion | flops 2170552320 | bytes 5259264 | tf_op jit(solution)/shard_map/dot_general | solution.py:154
  250.4 0.8 fusion.94
  251.1 2.0 collective-permute-start.12
  253.2 2.3 collective-permute-start.13
  255.5 3.8 %collective-permute-done.13 = bf16[1,64,256]{2,1,0:T(8,128)(2,1)S(1)} collective-permute-done((bf16[1,64,256]{2,1,0:T(8,128)(2,1)S(1)}, bf16[1,64,256]{2,1,0:T(8,128)(2,1)S(1)}, u32[]{:S(2)}, u32[]{:S(2)}) %collective-permute-start.13) | collective-permute-done | bytes 32800 | tf_op jit(solution)/shard_map/ppermute | solution.py:19
  259.3 1.0 pad_maximum_fusion.19
  260.3 4.3 %collective-permute-start.14 = (bf16[34,1,256]{2,1,0:T(2,128)(2,1)S(1)}, bf16[34,1,256]{2,1,0:T(2,128)(2,1)S(1)}, u32[]{:S(2)}, u32[]{:S(2)}) collective-permute-start(bf16[34,1,256]{2,1,0:T(2,128)(2,1)S(1)} %get-tuple-element.35), channel_id=1, source_target_pairs={{0,1},{1,2},{2,3},{4,5},{5,6},{6,7},{8,9},{9,10},{10,11},{12,13},{... | collective-permute-start | bytes 52232 | tf_op jit(solution)/shard_map/ppermute | solution.py:16
  264.6 1.5 collective-permute-start.15
  266.1 3.4 %collective-permute-done.15 = bf16[34,1,256]{2,1,0:T(2,128)(2,1)S(1)} collective-permute-done((bf16[34,1,256]{2,1,0:T(2,128)(2,1)S(1)}, bf16[34,1,256]{2,1,0:T(2,128)(2,1)S(1)}, u32[]{:S(2)}, u32[]{:S(2)}) %collective-permute-start.15) | collective-permute-done | bytes 17440 | tf_op jit(solution)/shard_map/ppermute | solution.py:19
  269.6 1.8 maximum_convert_fusion.1
  271.3 0.4 fusion.86
  271.7 0.2 fusion.87
  272.1 1.4 fusion.33
  273.5 0.3 fusion.93
  273.8 0.2 fusion.58
  274.1 0.8 copy.20
  (43 shorter events, 0.7 us)
Async XLA Ops:
  0.0 244.9 %copy-start = (bf16[1024,256]{1,0:T(8,128)(2,1)S(1)}, bf16[1024,256]{1,0:T(8,128)(2,1)}, u32[]{:S(2)}) copy-start(bf16[1024,256]{1,0:T(8,128)(2,1)} %param.19) | copy-start | bytes 1572868
  1.1 6.6 %collective-permute-start = (bf16[7,128,128]{2,1,0:T(8,128)(2,1)S(1)}, bf16[7,128,128]{2,1,0:T(8,128)(2,1)S(1)}, u32[]{:S(2)}, u32[]{:S(2)}) collective-permute-start(bf16[7,128,128]{2,1,0:T(8,128)(2,1)S(1)} %get-tuple-element.28), channel_id=1, source_target_pairs={{0,4},{4,8},{8,12},{12,16},{16,20},{20,24},{24,28},{1,5},{5,9},{9,... | collective-permute-start | bytes 688136 | tf_op jit(solution)/shard_map/ppermute | solution.py:126
  4.8 8.2 %collective-permute-start.1 = (bf16[7,128,128]{2,1,0:T(8,128)(2,1)S(1)}, bf16[7,128,128]{2,1,0:T(8,128)(2,1)S(1)}, u32[]{:S(2)}, u32[]{:S(2)}) collective-permute-start(bf16[7,128,128]{2,1,0:T(8,128)(2,1)S(1)} %get-tuple-element.27), channel_id=1, source_target_pairs={{4,0},{8,4},{12,8},{16,12},{20,16},{24,20},{28,24},{5,1},{9,5},{13... | collective-permute-start | bytes 688136 | tf_op jit(solution)/shard_map/ppermute | solution.py:129
  7.8 10.6 %copy-start.6 = (f32[15,15,128]{2,1,0:T(8,128)S(1)}, f32[15,15,128]{2,1,0:T(8,128)}, u32[]{:S(2)}) copy-start(f32[15,15,128]{2,1,0:T(8,128)} %param.11) | copy-start | bytes 345604
  13.1 6.0 %copy-start.3 = (bf16[78,128,128]{2,1,0:T(8,128)(2,1)}, bf16[78,128,128]{2,1,0:T(8,128)(2,1)S(1)}, u32[]{:S(2)}) copy-start(bf16[78,128,128]{2,1,0:T(8,128)(2,1)S(1)} %constant_dynamic-update-slice_fusion) | copy-start | bytes 7667716
  13.2 93.4 %collective-permute-start.2 = (bf16[78,7,128]{2,1,0:T(8,128)(2,1)S(1)}, bf16[78,7,128]{2,1,0:T(8,128)(2,1)}, u32[]{:S(2)}, u32[]{:S(2)}) collective-permute-start(bf16[78,7,128]{2,1,0:T(8,128)(2,1)S(1)} %get-tuple-element.13), channel_id=1, source_target_pairs={{0,1},{1,2},{2,3},{4,5},{5,6},{6,7},{8,9},{9,10},{10,11},{12,13},{... | collective-permute-start | bytes 419336 | tf_op jit(solution)/shard_map/ppermute | solution.py:126
  17.1 89.5 %collective-permute-start.3 = (bf16[78,7,128]{2,1,0:T(8,128)(2,1)S(1)}, bf16[78,7,128]{2,1,0:T(8,128)(2,1)}, u32[]{:S(2)}, u32[]{:S(2)}) collective-permute-start(bf16[78,7,128]{2,1,0:T(8,128)(2,1)S(1)} %get-tuple-element.14), channel_id=1, source_target_pairs={{1,0},{2,1},{3,2},{5,4},{6,5},{7,6},{9,8},{10,9},{11,10},{13,12},{... | collective-permute-start | bytes 419336 | tf_op jit(solution)/shard_map/ppermute | solution.py:129
  129.0 3.4 %copy-start.1 = (f32[1,64,112,128]{3,2,1,0:T(8,128)S(1)}, f32[1,64,112,128]{3,2,1,0:T(8,128)}, u32[]{:S(2)}) copy-start(f32[1,64,112,128]{3,2,1,0:T(8,128)} %shard_map.101) | copy-start | bytes 11010052
  132.4 2.7 copy-start.9
  132.4 2.7 copy-start.10
  143.8 4.3 %collective-permute-start.4 = (bf16[1,128,128]{2,1,0:T(8,128)(2,1)S(1)}, bf16[1,128,128]{2,1,0:T(8,128)(2,1)S(1)}, u32[]{:S(2)}, u32[]{:S(2)}) collective-permute-start(bf16[1,128,128]{2,1,0:T(8,128)(2,1)S(1)} %get-tuple-element.25), channel_id=1, source_target_pairs={{0,4},{4,8},{8,12},{12,16},{16,20},{20,24},{24,28},{1,5},{5,9},{9,... | collective-permute-start | bytes 98312 | tf_op jit(solution)/shard_map/ppermute | solution.py:16
  146.1 6.1 %collective-permute-start.5 = (bf16[1,128,128]{2,1,0:T(8,128)(2,1)S(1)}, bf16[1,128,128]{2,1,0:T(8,128)(2,1)S(1)}, u32[]{:S(2)}, u32[]{:S(2)}) collective-permute-start(bf16[1,128,128]{2,1,0:T(8,128)(2,1)S(1)} %get-tuple-element.26), channel_id=1, source_target_pairs={{4,0},{8,4},{12,8},{16,12},{20,16},{24,20},{28,24},{5,1},{9,5},{13... | collective-permute-start | bytes 98312 | tf_op jit(solution)/shard_map/ppermute | solution.py:19
  152.3 5.8 %collective-permute-start.6 = (bf16[66,1,128]{2,1,0:T(2,128)(2,1)S(1)}, bf16[66,1,128]{2,1,0:T(2,128)(2,1)S(1)}, u32[]{:S(2)}, u32[]{:S(2)}) collective-permute-start(bf16[66,1,128]{2,1,0:T(2,128)(2,1)S(1)} %get-tuple-element.21), channel_id=1, source_target_pairs={{0,1},{1,2},{2,3},{4,5},{5,6},{6,7},{8,9},{9,10},{10,11},{12,13},{... | collective-permute-start | bytes 50696 | tf_op jit(solution)/shard_map/ppermute | solution.py:16
  156.6 4.7 %collective-permute-start.7 = (bf16[66,1,128]{2,1,0:T(2,128)(2,1)S(1)}, bf16[66,1,128]{2,1,0:T(2,128)(2,1)S(1)}, u32[]{:S(2)}, u32[]{:S(2)}) collective-permute-start(bf16[66,1,128]{2,1,0:T(2,128)(2,1)S(1)} %get-tuple-element.22), channel_id=1, source_target_pairs={{1,0},{2,1},{3,2},{5,4},{6,5},{7,6},{9,8},{10,9},{11,10},{13,12},{... | collective-permute-start | bytes 50696 | tf_op jit(solution)/shard_map/ppermute | solution.py:19
  165.4 0.8 copy-start.7
  166.3 5.8 %copy-start.8 = (f32[256]{0:T(256)S(1)}, f32[256]{0:T(256)}, u32[]{:S(2)}) copy-start(f32[256]{0:T(256)} %param.17) | copy-start | bytes 3076
  166.8 7.5 %collective-permute-start.8 = (bf16[7,64,256]{2,1,0:T(8,128)(2,1)S(1)}, bf16[7,64,256]{2,1,0:T(8,128)(2,1)S(1)}, u32[]{:S(2)}, u32[]{:S(2)}) collective-permute-start(bf16[7,64,256]{2,1,0:T(8,128)(2,1)S(1)} %get-tuple-element.41), channel_id=1, source_target_pairs={{0,4},{4,8},{8,12},{12,16},{16,20},{20,24},{24,28},{1,5},{5,9},{9,... | collective-permute-start | bytes 688136 | tf_op jit(solution)/shard_map/ppermute | solution.py:126
  170.1 8.2 %collective-permute-start.9 = (bf16[7,64,256]{2,1,0:T(8,128)(2,1)S(1)}, bf16[7,64,256]{2,1,0:T(8,128)(2,1)S(1)}, u32[]{:S(2)}, u32[]{:S(2)}) collective-permute-start(bf16[7,64,256]{2,1,0:T(8,128)(2,1)S(1)} %get-tuple-element.42), channel_id=1, source_target_pairs={{4,0},{8,4},{12,8},{16,12},{20,16},{24,20},{28,24},{5,1},{9,5},{13... | collective-permute-start | bytes 688136 | tf_op jit(solution)/shard_map/ppermute | solution.py:129
  172.1 11.8 %copy-start.5 = (f32[15,15,256]{2,1,0:T(8,128)S(1)}, f32[15,15,256]{2,1,0:T(8,128)}, u32[]{:S(2)}) copy-start(f32[15,15,256]{2,1,0:T(8,128)} %param.16) | copy-start | bytes 691204
  179.8 45.3 %collective-permute-start.10 = (bf16[46,7,256]{2,1,0:T(8,128)(2,1)S(1)}, bf16[46,7,256]{2,1,0:T(8,128)(2,1)S(1)}, u32[]{:S(2)}, u32[]{:S(2)}) collective-permute-start(bf16[46,7,256]{2,1,0:T(8,128)(2,1)S(1)} %get-tuple-element.33), channel_id=1, source_target_pairs={{0,1},{1,2},{2,3},{4,5},{5,6},{6,7},{8,9},{9,10},{10,11},{12,13},{... | collective-permute-start | bytes 494600 | tf_op jit(solution)/shard_map/ppermute | solution.py:126
  182.5 42.5 %collective-permute-start.11 = (bf16[46,7,256]{2,1,0:T(8,128)(2,1)S(1)}, bf16[46,7,256]{2,1,0:T(8,128)(2,1)S(1)}, u32[]{:S(2)}, u32[]{:S(2)}) collective-permute-start(bf16[46,7,256]{2,1,0:T(8,128)(2,1)S(1)} %get-tuple-element.34), channel_id=1, source_target_pairs={{1,0},{2,1},{3,2},{5,4},{6,5},{7,6},{9,8},{10,9},{11,10},{13,12},{... | collective-permute-start | bytes 494600 | tf_op jit(solution)/shard_map/ppermute | solution.py:129
  225.6 17.9 %copy-start.2 = (f32[1,32,48,256]{3,2,1,0:T(8,128)S(1)}, f32[1,32,48,256]{3,2,1,0:T(8,128)}, u32[]{:S(2)}) copy-start(f32[1,32,48,256]{3,2,1,0:T(8,128)} %shard_map.103) | copy-start | bytes 4718596
  243.6 0.7 copy-start.4
  251.1 4.3 %collective-permute-start.12 = (bf16[1,64,256]{2,1,0:T(8,128)(2,1)S(1)}, bf16[1,64,256]{2,1,0:T(8,128)(2,1)S(1)}, u32[]{:S(2)}, u32[]{:S(2)}) collective-permute-start(bf16[1,64,256]{2,1,0:T(8,128)(2,1)S(1)} %get-tuple-element.39), channel_id=1, source_target_pairs={{0,4},{4,8},{8,12},{12,16},{16,20},{20,24},{24,28},{1,5},{5,9},{9,... | collective-permute-start | bytes 98312 | tf_op jit(solution)/shard_map/ppermute | solution.py:16
  253.2 6.1 %collective-permute-start.13 = (bf16[1,64,256]{2,1,0:T(8,128)(2,1)S(1)}, bf16[1,64,256]{2,1,0:T(8,128)(2,1)S(1)}, u32[]{:S(2)}, u32[]{:S(2)}) collective-permute-start(bf16[1,64,256]{2,1,0:T(8,128)(2,1)S(1)} %get-tuple-element.40), channel_id=1, source_target_pairs={{4,0},{8,4},{12,8},{16,12},{20,16},{24,20},{28,24},{5,1},{9,5},{13... | collective-permute-start | bytes 98312 | tf_op jit(solution)/shard_map/ppermute | solution.py:19
  260.3 5.8 %collective-permute-start.14 = (bf16[34,1,256]{2,1,0:T(2,128)(2,1)S(1)}, bf16[34,1,256]{2,1,0:T(2,128)(2,1)S(1)}, u32[]{:S(2)}, u32[]{:S(2)}) collective-permute-start(bf16[34,1,256]{2,1,0:T(2,128)(2,1)S(1)} %get-tuple-element.35), channel_id=1, source_target_pairs={{0,1},{1,2},{2,3},{4,5},{5,6},{6,7},{8,9},{9,10},{10,11},{12,13},{... | collective-permute-start | bytes 52232 | tf_op jit(solution)/shard_map/ppermute | solution.py:16
  264.6 5.0 %collective-permute-start.15 = (bf16[34,1,256]{2,1,0:T(2,128)(2,1)S(1)}, bf16[34,1,256]{2,1,0:T(2,128)(2,1)S(1)}, u32[]{:S(2)}, u32[]{:S(2)}) collective-permute-start(bf16[34,1,256]{2,1,0:T(2,128)(2,1)S(1)} %get-tuple-element.36), channel_id=1, source_target_pairs={{1,0},{2,1},{3,2},{5,4},{6,5},{7,6},{9,8},{10,9},{11,10},{13,12},{... | collective-permute-start | bytes 52232 | tf_op jit(solution)/shard_map/ppermute | solution.py:19

commit v12 on v11

--- a/solution.py
+++ b/solution.py
@@ -32,6 +32,7 @@
     nlb = chans // 128
     njb = cols // 8
     nrb = rows // rb
+    spread = max(1, min(8, 16 // (njb * nlb)))
 
     def one_strip(n, carry):
         x_ref = x_all.at[n]
@@ -41,7 +42,7 @@
             xf_ref[r] = x_ref[r].astype(jnp.float32)
             return c
 
-        lax.fori_loop(0, rows + taps - 1, widen_row, 0)
+        lax.fori_loop(0, rows + taps - 1, widen_row, 0, unroll=spread)
         first = True
         for s in range(8):
             if cbase + s == 0:
@@ -53,7 +54,7 @@
                     xs_ref[r, pl.ds(0, width), :] = xf_ref[r, pl.ds(cbase + s, width), :]
                     return c
 
-                lax.fori_loop(0, rows + taps - 1, shift, 0)
+                lax.fori_loop(0, rows + taps - 1, shift, 0, unroll=spread)
                 src = xs_ref
             for q in range(2):
                 b = 8 * q + s

time: 276 us -> 267 us (0.967)
  Pallas kernels: 162 us -> 153 us
    pallas_call x4, Pallas kernels: 162 us -> 153 us  [depthwise(): pl.pallas_call(body, out_shape=jax.ShapeDtypeStruct((count, rows, cols, c...]
  transfers between devices with their start and end apart: 16 -> 16, of which waited for: 8 -> 8; matrix products, arithmetic and copies ran while one was open for 2% -> 2% of each run, Pallas kernels for 47% -> 48%
where the time goes in v12:
time: 267 us; the launch traced here: 266 us
  Pallas kernels  153 us (57%)
  starting transfers between devices  40.2 us (15%)
  waiting for transfers between devices  24.4 us (9%)
  other arithmetic  22.5 us (8%)
  matrix products  14.5 us (5%)
  local copies, waits for them, and re-layouts  10.5 us (4%)
    pallas_call x4, Pallas kernels, depthwise(): pl.pallas_call(body, out_shape=jax.ShapeDtypeStruct((count, rows, cols, c...  153 us
    ppermute x4, waiting for transfers between devices, padded_2(): lax.ppermute(lax.slice_in_dim(block, 0, width, axis=dim), axis, backward)  14.5 us
    dot_general x2, matrix products, local_section(): mixed = jnp.dot(hidden, w_out, preferred_element_type=jnp.float32)  14.1 us
    ppermute x4, starting transfers between devices, exchange(): lax.ppermute(lax.slice_in_dim(block, block.shape[dim] - width, None, axis...  13.7 us
    ppermute x4, starting transfers between devices, padded_2(): lax.ppermute(lax.slice_in_dim(block, block.shape[dim] - width, None, axis...  12.9 us
    ppermute x4, waiting for transfers between devices, exchange(): lax.ppermute(lax.slice_in_dim(block, 0, width, axis=dim), axis, backward)  7.3 us
    ppermute x4, starting transfers between devices, padded_2(): lax.ppermute(lax.slice_in_dim(block, 0, width, axis=dim), axis, backward)  7.27 us
    ppermute x4, starting transfers between devices, exchange(): lax.ppermute(lax.slice_in_dim(block, 0, width, axis=dim), axis, backward)  6.41 us
  transfers between devices with their start and end apart: 16, of which 8 were waited for; matrix products, arithmetic and copies ran while one was open for 2% of the time, Pallas kernels for 48%

profile of v12, /device:TPU:3, one launch (start us, length us, event | category | flops | bytes accessed | tf_op | source)
XLA Modules:
  0.0 265.5 jit_solution(13429687004047754025)
XLA Ops:
  0.0 1.1 fusion.91
  1.1 3.7 %collective-permute-start = (bf16[7,128,128]{2,1,0:T(8,128)(2,1)S(1)}, bf16[7,128,128]{2,1,0:T(8,128)(2,1)S(1)}, u32[]{:S(2)}, u32[]{:S(2)}) collective-permute-start(bf16[7,128,128]{2,1,0:T(8,128)(2,1)S(1)} %get-tuple-element.28), channel_id=1, source_target_pairs={{0,4},{4,8},{8,12},{12,16},{16,20},{20,24},{24,28},{1,5},{5,9},{9,... | collective-permute-start | bytes 688136 | tf_op jit(solution)/shard_map/ppermute | solution.py:127
  4.8 1.9 collective-permute-start.1
  6.8 0.7 multiply_multiply_fusion.3
  7.5 0.3 collective-permute-done
  7.8 2.0 constant_dynamic-update-slice_fusion.1
  9.8 3.2 %collective-permute-done.1 = bf16[7,128,128]{2,1,0:T(8,128)(2,1)S(1)} collective-permute-done((bf16[7,128,128]{2,1,0:T(8,128)(2,1)S(1)}, bf16[7,128,128]{2,1,0:T(8,128)(2,1)S(1)}, u32[]{:S(2)}, u32[]{:S(2)}) %collective-permute-start.1) | collective-permute-done | bytes 229408 | tf_op jit(solution)/shard_map/ppermute | solution.py:130
  13.2 3.9 %collective-permute-start.2 = (bf16[78,7,128]{2,1,0:T(8,128)(2,1)S(1)}, bf16[78,7,128]{2,1,0:T(8,128)(2,1)}, u32[]{:S(2)}, u32[]{:S(2)}) collective-permute-start(bf16[78,7,128]{2,1,0:T(8,128)(2,1)S(1)} %get-tuple-element.13), channel_id=1, source_target_pairs={{0,1},{1,2},{2,3},{4,5},{5,6},{6,7},{8,9},{9,10},{10,11},{12,13},{... | collective-permute-start | bytes 419336 | tf_op jit(solution)/shard_map/ppermute | solution.py:127
  17.1 1.3 collective-permute-start.3
  18.4 0.8 fusion.68.k_ref
  19.1 87.5 %shard_map.101 = f32[1,64,112,128]{3,2,1,0:T(8,128)} custom-call(bf16[1,78,128,128]{3,2,1,0:T(8,128)(2,1)} %bitcast.62, f32[15,15,128]{2,1,0:T(8,128)} %fusion.68.k_ref), custom_call_target="tpu_custom_call" | custom-call | flops 412876800 | bytes 6225920 | tf_op jit(solution)/shard_map/pallas_call | solution.py:106
  106.6 1.6 fusion.57
  108.2 1.1 pad_maximum_fusion.6.x_all
  109.3 12.3 %shard_map.100 = f32[2,64,8,128]{3,2,1,0:T(8,128)} custom-call(bf16[2,78,22,128]{3,2,1,0:T(8,128)(2,1)} %pad_maximum_fusion.6.x_all, f32[15,15,128]{2,1,0:T(8,128)} %fusion.68.k_ref), custom_call_target="tpu_custom_call" | custom-call | flops 58982400 | bytes 1402880 | tf_op jit(solution)/shard_map/pallas_call | solution.py:106
  121.6 1.1 slice_bitcast_fusion.3
  122.7 3.3 %fusion.29 = f32[64,128]{1,0:T(8,128)S(1)} fusion(f32[64,8,128]{2,1,0:T(8,128)S(1)} %get-tuple-element.46, f32[64,112,128]{2,1,0:T(8,128)} %bitcast.54, f32[64,8,128]{2,1,0:T(8,128)S(1)} %get-tuple-element.45), kind=kLoop, calls=%fused_computation.39 | loop fusion | flops 3137536 | bytes 4227072 | tf_op jit(solution)/shard_map/reduce_sum | solution.py:149
  126.0 2.6 multiply_reduce_fusion
  128.7 8.6 %add_convert_fusion = bf16[64,128,128]{2,1,0:T(8,128)(2,1)S(1)} fusion(bf16[64,128,128]{2,1,0:T(8,128)(2,1)} %param.10, f32[64,128]{1,0:T(8,128)S(1)} %add_rsqrt_fusion, f32[64,128]{1,0:T(8,128)S(1)} %broadcast_multiply_fusion, f32[64,8,128]{2,1,0:T(8,128)S(1)} %get-tuple-element.46, f32[64,112,128]{2,1,0:T(8,128)} %bitcast.55, ...), kind=kOutput, calls=%fused_computation.19 | convolution fusion | flops 2193620992 | bytes 8716288 | tf_op jit(solution)/shard_map/dot_general | solution.py:155
  137.4 2.3 collective-permute-start.4
  139.7 2.0 collective-permute-start.5
  141.7 4.1 %collective-permute-done.5 = bf16[1,128,128]{2,1,0:T(8,128)(2,1)S(1)} collective-permute-done((bf16[1,128,128]{2,1,0:T(8,128)(2,1)S(1)}, bf16[1,128,128]{2,1,0:T(8,128)(2,1)S(1)}, u32[]{:S(2)}, u32[]{:S(2)}) %collective-permute-start.5) | collective-permute-done | bytes 32800 | tf_op jit(solution)/shard_map/ppermute | solution.py:19
  145.9 4.3 %collective-permute-start.6 = (bf16[66,1,128]{2,1,0:T(2,128)(2,1)S(1)}, bf16[66,1,128]{2,1,0:T(2,128)(2,1)S(1)}, u32[]{:S(2)}, u32[]{:S(2)}) collective-permute-start(bf16[66,1,128]{2,1,0:T(2,128)(2,1)S(1)} %get-tuple-element.21), channel_id=1, source_target_pairs={{0,1},{1,2},{2,3},{4,5},{5,6},{6,7},{8,9},{9,10},{10,11},{12,13},{... | collective-permute-start | bytes 50696 | tf_op jit(solution)/shard_map/ppermute | solution.py:16
  150.2 1.5 collective-permute-start.7
  151.7 3.2 %collective-permute-done.7 = bf16[66,1,128]{2,1,0:T(2,128)(2,1)S(1)} collective-permute-done((bf16[66,1,128]{2,1,0:T(2,128)(2,1)S(1)}, bf16[66,1,128]{2,1,0:T(2,128)(2,1)S(1)}, u32[]{:S(2)}, u32[]{:S(2)}) %collective-permute-start.7) | collective-permute-done | bytes 16928 | tf_op jit(solution)/shard_map/ppermute | solution.py:19
  154.8 0.8 maximum_convert_fusion
  155.7 0.6 fusion.82
  156.3 0.6 fusion.83
  156.9 1.6 fusion.22
  158.4 0.6 fusion.89
  159.0 0.5 fusion.55
  159.6 0.3 copy-done.7
  159.9 0.4 convolution_convert_fusion
  160.3 3.3 %collective-permute-start.8 = (bf16[7,64,256]{2,1,0:T(8,128)(2,1)S(1)}, bf16[7,64,256]{2,1,0:T(8,128)(2,1)S(1)}, u32[]{:S(2)}, u32[]{:S(2)}) collective-permute-start(bf16[7,64,256]{2,1,0:T(8,128)(2,1)S(1)} %get-tuple-element.41), channel_id=1, source_target_pairs={{0,4},{4,8},{8,12},{12,16},{16,20},{20,24},{24,28},{1,5},{5,9},{9,... | collective-permute-start | bytes 688136 | tf_op jit(solution)/shard_map/ppermute | solution.py:127
  163.7 1.9 collective-permute-start.9
  165.7 2.2 collective-permute-done.8
  167.9 4.0 %collective-permute-done.9 = bf16[7,64,256]{2,1,0:T(8,128)(2,1)S(1)} collective-permute-done((bf16[7,64,256]{2,1,0:T(8,128)(2,1)S(1)}, bf16[7,64,256]{2,1,0:T(8,128)(2,1)S(1)}, u32[]{:S(2)}, u32[]{:S(2)}) %collective-permute-start.9) | collective-permute-done | bytes 229408 | tf_op jit(solution)/shard_map/ppermute | solution.py:130
  171.9 1.4 fusion.81
  173.4 2.8 %collective-permute-start.10 = (bf16[46,7,256]{2,1,0:T(8,128)(2,1)S(1)}, bf16[46,7,256]{2,1,0:T(8,128)(2,1)S(1)}, u32[]{:S(2)}, u32[]{:S(2)}) collective-permute-start(bf16[46,7,256]{2,1,0:T(8,128)(2,1)S(1)} %get-tuple-element.33), channel_id=1, source_target_pairs={{0,1},{1,2},{2,3},{4,5},{5,6},{6,7},{8,9},{9,10},{10,11},{12,13},{... | collective-permute-start | bytes 494600 | tf_op jit(solution)/shard_map/ppermute | solution.py:127
  176.1 1.3 collective-permute-start.11
  177.4 0.8 fusion.66.k_ref
  178.2 40.4 %shard_map.103 = f32[1,32,48,256]{3,2,1,0:T(8,128)} custom-call(bf16[1,46,64,256]{3,2,1,0:T(8,128)(2,1)} %get-tuple-element.29.x_all, f32[15,15,256]{2,1,0:T(8,128)} %fusion.66.k_ref), custom_call_target="tpu_custom_call" | custom-call | flops 176947200 | bytes 3080192 | tf_op jit(solution)/shard_map/pallas_call | solution.py:106
  218.7 0.6 fusion.46
  219.2 1.1 pad_maximum_fusion.5.x_all
  220.4 12.8 %shard_map.102 = f32[2,32,8,256]{3,2,1,0:T(8,128)} custom-call(bf16[2,46,22,256]{3,2,1,0:T(8,128)(2,1)} %pad_maximum_fusion.5.x_all, f32[15,15,256]{2,1,0:T(8,128)} %fusion.66.k_ref), custom_call_target="tpu_custom_call" | custom-call | flops 58982400 | bytes 1560576 | tf_op jit(solution)/shard_map/pallas_call | solution.py:106
  233.2 1.1 slice_bitcast_fusion.1
  234.3 0.4 fusion.44
  234.7 0.3 copy-done.4
  235.0 0.6 multiply_reduce_fusion.1
  235.6 5.4 %add_convert_fusion.1 = bf16[32,64,256]{2,1,0:T(8,128)(2,1)} fusion(bf16[32,64,256]{2,1,0:T(8,128)(2,1)S(1)} %convolution_convert_fusion, f32[32,64]{1,0:T(8,128)S(1)} %add_rsqrt_fusion.1, f32[32,64]{1,0:T(8,128)S(1)} %broadcast_multiply_fusion.1, f32[32,8,256]{2,1,0:T(8,128)} %copy-done.4, f32[32,48,256]{2,1,0:T(8,128)S(1)} %bitcast.61, ...), kind=kOutput, calls=%fused_computation.34 | convolution fusion | flops 2170552320 | bytes 5259264 | tf_op jit(solution)/shard_map/dot_general | solution.py:155
  241.1 0.8 fusion.94
  241.8 2.0 collective-permute-start.12
  243.9 2.3 collective-permute-start.13
  246.2 3.8 %collective-permute-done.13 = bf16[1,64,256]{2,1,0:T(8,128)(2,1)S(1)} collective-permute-done((bf16[1,64,256]{2,1,0:T(8,128)(2,1)S(1)}, bf16[1,64,256]{2,1,0:T(8,128)(2,1)S(1)}, u32[]{:S(2)}, u32[]{:S(2)}) %collective-permute-start.13) | collective-permute-done | bytes 32800 | tf_op jit(solution)/shard_map/ppermute | solution.py:19
  250.0 1.0 pad_maximum_fusion.19
  251.0 4.3 %collective-permute-start.14 = (bf16[34,1,256]{2,1,0:T(2,128)(2,1)S(1)}, bf16[34,1,256]{2,1,0:T(2,128)(2,1)S(1)}, u32[]{:S(2)}, u32[]{:S(2)}) collective-permute-start(bf16[34,1,256]{2,1,0:T(2,128)(2,1)S(1)} %get-tuple-element.35), channel_id=1, source_target_pairs={{0,1},{1,2},{2,3},{4,5},{5,6},{6,7},{8,9},{9,10},{10,11},{12,13},{... | collective-permute-start | bytes 52232 | tf_op jit(solution)/shard_map/ppermute | solution.py:16
  255.3 1.5 collective-permute-start.15
  256.8 3.4 %collective-permute-done.15 = bf16[34,1,256]{2,1,0:T(2,128)(2,1)S(1)} collective-permute-done((bf16[34,1,256]{2,1,0:T(2,128)(2,1)S(1)}, bf16[34,1,256]{2,1,0:T(2,128)(2,1)S(1)}, u32[]{:S(2)}, u32[]{:S(2)}) %collective-permute-start.15) | collective-permute-done | bytes 17440 | tf_op jit(solution)/shard_map/ppermute | solution.py:19
  260.3 1.8 maximum_convert_fusion.1
  262.0 0.4 fusion.86
  262.4 0.2 fusion.87
  262.8 1.4 fusion.33
  264.2 0.3 fusion.93
  264.5 0.2 fusion.58
  264.7 0.8 copy.20
  (43 shorter events, 0.7 us)
Async XLA Ops:
  0.0 235.6 %copy-start = (bf16[1024,256]{1,0:T(8,128)(2,1)S(1)}, bf16[1024,256]{1,0:T(8,128)(2,1)}, u32[]{:S(2)}) copy-start(bf16[1024,256]{1,0:T(8,128)(2,1)} %param.19) | copy-start | bytes 1572868
  1.1 6.6 %collective-permute-start = (bf16[7,128,128]{2,1,0:T(8,128)(2,1)S(1)}, bf16[7,128,128]{2,1,0:T(8,128)(2,1)S(1)}, u32[]{:S(2)}, u32[]{:S(2)}) collective-permute-start(bf16[7,128,128]{2,1,0:T(8,128)(2,1)S(1)} %get-tuple-element.28), channel_id=1, source_target_pairs={{0,4},{4,8},{8,12},{12,16},{16,20},{20,24},{24,28},{1,5},{5,9},{9,... | collective-permute-start | bytes 688136 | tf_op jit(solution)/shard_map/ppermute | solution.py:127
  4.8 8.2 %collective-permute-start.1 = (bf16[7,128,128]{2,1,0:T(8,128)(2,1)S(1)}, bf16[7,128,128]{2,1,0:T(8,128)(2,1)S(1)}, u32[]{:S(2)}, u32[]{:S(2)}) collective-permute-start(bf16[7,128,128]{2,1,0:T(8,128)(2,1)S(1)} %get-tuple-element.27), channel_id=1, source_target_pairs={{4,0},{8,4},{12,8},{16,12},{20,16},{24,20},{28,24},{5,1},{9,5},{13... | collective-permute-start | bytes 688136 | tf_op jit(solution)/shard_map/ppermute | solution.py:130
  7.8 10.6 %copy-start.6 = (f32[15,15,128]{2,1,0:T(8,128)S(1)}, f32[15,15,128]{2,1,0:T(8,128)}, u32[]{:S(2)}) copy-start(f32[15,15,128]{2,1,0:T(8,128)} %param.11) | copy-start | bytes 345604
  13.1 6.0 %copy-start.3 = (bf16[78,128,128]{2,1,0:T(8,128)(2,1)}, bf16[78,128,128]{2,1,0:T(8,128)(2,1)S(1)}, u32[]{:S(2)}) copy-start(bf16[78,128,128]{2,1,0:T(8,128)(2,1)S(1)} %constant_dynamic-update-slice_fusion) | copy-start | bytes 7667716
  13.2 93.4 %collective-permute-start.2 = (bf16[78,7,128]{2,1,0:T(8,128)(2,1)S(1)}, bf16[78,7,128]{2,1,0:T(8,128)(2,1)}, u32[]{:S(2)}, u32[]{:S(2)}) collective-permute-start(bf16[78,7,128]{2,1,0:T(8,128)(2,1)S(1)} %get-tuple-element.13), channel_id=1, source_target_pairs={{0,1},{1,2},{2,3},{4,5},{5,6},{6,7},{8,9},{9,10},{10,11},{12,13},{... | collective-permute-start | bytes 419336 | tf_op jit(solution)/shard_map/ppermute | solution.py:127
  17.1 89.5 %collective-permute-start.3 = (bf16[78,7,128]{2,1,0:T(8,128)(2,1)S(1)}, bf16[78,7,128]{2,1,0:T(8,128)(2,1)}, u32[]{:S(2)}, u32[]{:S(2)}) collective-permute-start(bf16[78,7,128]{2,1,0:T(8,128)(2,1)S(1)} %get-tuple-element.14), channel_id=1, source_target_pairs={{1,0},{2,1},{3,2},{5,4},{6,5},{7,6},{9,8},{10,9},{11,10},{13,12},{... | collective-permute-start | bytes 419336 | tf_op jit(solution)/shard_map/ppermute | solution.py:130
  122.6 3.4 %copy-start.1 = (f32[1,64,112,128]{3,2,1,0:T(8,128)S(1)}, f32[1,64,112,128]{3,2,1,0:T(8,128)}, u32[]{:S(2)}) copy-start(f32[1,64,112,128]{3,2,1,0:T(8,128)} %shard_map.101) | copy-start | bytes 11010052
  126.0 2.7 %copy-start.9 = (bf16[512,128]{1,0:T(8,128)(2,1)S(1)}, bf16[512,128]{1,0:T(8,128)(2,1)}, u32[]{:S(2)}) copy-start(bf16[512,128]{1,0:T(8,128)(2,1)} %param.14) | copy-start | bytes 393220
  126.0 2.7 %copy-start.10 = (bf16[128,512]{1,0:T(8,128)(2,1)S(1)}, bf16[128,512]{1,0:T(8,128)(2,1)}, u32[]{:S(2)}) copy-start(bf16[128,512]{1,0:T(8,128)(2,1)} %param.13) | copy-start | bytes 393220
  137.4 4.3 %collective-permute-start.4 = (bf16[1,128,128]{2,1,0:T(8,128)(2,1)S(1)}, bf16[1,128,128]{2,1,0:T(8,128)(2,1)S(1)}, u32[]{:S(2)}, u32[]{:S(2)}) collective-permute-start(bf16[1,128,128]{2,1,0:T(8,128)(2,1)S(1)} %get-tuple-element.25), channel_id=1, source_target_pairs={{0,4},{4,8},{8,12},{12,16},{16,20},{20,24},{24,28},{1,5},{5,9},{9,... | collective-permute-start | bytes 98312 | tf_op jit(solution)/shard_map/ppermute | solution.py:16
  139.7 6.1 %collective-permute-start.5 = (bf16[1,128,128]{2,1,0:T(8,128)(2,1)S(1)}, bf16[1,128,128]{2,1,0:T(8,128)(2,1)S(1)}, u32[]{:S(2)}, u32[]{:S(2)}) collective-permute-start(bf16[1,128,128]{2,1,0:T(8,128)(2,1)S(1)} %get-tuple-element.26), channel_id=1, source_target_pairs={{4,0},{8,4},{12,8},{16,12},{20,16},{24,20},{28,24},{5,1},{9,5},{13... | collective-permute-start | bytes 98312 | tf_op jit(solution)/shard_map/ppermute | solution.py:19
  145.9 5.8 %collective-permute-start.6 = (bf16[66,1,128]{2,1,0:T(2,128)(2,1)S(1)}, bf16[66,1,128]{2,1,0:T(2,128)(2,1)S(1)}, u32[]{:S(2)}, u32[]{:S(2)}) collective-permute-start(bf16[66,1,128]{2,1,0:T(2,128)(2,1)S(1)} %get-tuple-element.21), channel_id=1, source_target_pairs={{0,1},{1,2},{2,3},{4,5},{5,6},{6,7},{8,9},{9,10},{10,11},{12,13},{... | collective-permute-start | bytes 50696 | tf_op jit(solution)/shard_map/ppermute | solution.py:16
  150.2 4.7 %collective-permute-start.7 = (bf16[66,1,128]{2,1,0:T(2,128)(2,1)S(1)}, bf16[66,1,128]{2,1,0:T(2,128)(2,1)S(1)}, u32[]{:S(2)}, u32[]{:S(2)}) collective-permute-start(bf16[66,1,128]{2,1,0:T(2,128)(2,1)S(1)} %get-tuple-element.22), channel_id=1, source_target_pairs={{1,0},{2,1},{3,2},{5,4},{6,5},{7,6},{9,8},{10,9},{11,10},{13,12},{... | collective-permute-start | bytes 50696 | tf_op jit(solution)/shard_map/ppermute | solution.py:19
  159.0 0.8 copy-start.7
  159.9 5.8 %copy-start.8 = (f32[256]{0:T(256)S(1)}, f32[256]{0:T(256)}, u32[]{:S(2)}) copy-start(f32[256]{0:T(256)} %param.17) | copy-start | bytes 3076
  160.3 7.5 %collective-permute-start.8 = (bf16[7,64,256]{2,1,0:T(8,128)(2,1)S(1)}, bf16[7,64,256]{2,1,0:T(8,128)(2,1)S(1)}, u32[]{:S(2)}, u32[]{:S(2)}) collective-permute-start(bf16[7,64,256]{2,1,0:T(8,128)(2,1)S(1)} %get-tuple-element.41), channel_id=1, source_target_pairs={{0,4},{4,8},{8,12},{12,16},{16,20},{20,24},{24,28},{1,5},{5,9},{9,... | collective-permute-start | bytes 688136 | tf_op jit(solution)/shard_map/ppermute | solution.py:127
  163.7 8.2 %collective-permute-start.9 = (bf16[7,64,256]{2,1,0:T(8,128)(2,1)S(1)}, bf16[7,64,256]{2,1,0:T(8,128)(2,1)S(1)}, u32[]{:S(2)}, u32[]{:S(2)}) collective-permute-start(bf16[7,64,256]{2,1,0:T(8,128)(2,1)S(1)} %get-tuple-element.42), channel_id=1, source_target_pairs={{4,0},{8,4},{12,8},{16,12},{20,16},{24,20},{28,24},{5,1},{9,5},{13... | collective-permute-start | bytes 688136 | tf_op jit(solution)/shard_map/ppermute | solution.py:130
  165.6 11.8 %copy-start.5 = (f32[15,15,256]{2,1,0:T(8,128)S(1)}, f32[15,15,256]{2,1,0:T(8,128)}, u32[]{:S(2)}) copy-start(f32[15,15,256]{2,1,0:T(8,128)} %param.16) | copy-start | bytes 691204
  173.4 45.3 %collective-permute-start.10 = (bf16[46,7,256]{2,1,0:T(8,128)(2,1)S(1)}, bf16[46,7,256]{2,1,0:T(8,128)(2,1)S(1)}, u32[]{:S(2)}, u32[]{:S(2)}) collective-permute-start(bf16[46,7,256]{2,1,0:T(8,128)(2,1)S(1)} %get-tuple-element.33), channel_id=1, source_target_pairs={{0,1},{1,2},{2,3},{4,5},{5,6},{6,7},{8,9},{9,10},{10,11},{12,13},{... | collective-permute-start | bytes 494600 | tf_op jit(solution)/shard_map/ppermute | solution.py:127
  176.1 42.5 %collective-permute-start.11 = (bf16[46,7,256]{2,1,0:T(8,128)(2,1)S(1)}, bf16[46,7,256]{2,1,0:T(8,128)(2,1)S(1)}, u32[]{:S(2)}, u32[]{:S(2)}) collective-permute-start(bf16[46,7,256]{2,1,0:T(8,128)(2,1)S(1)} %get-tuple-element.34), channel_id=1, source_target_pairs={{1,0},{2,1},{3,2},{5,4},{6,5},{7,6},{9,8},{10,9},{11,10},{13,12},{... | collective-permute-start | bytes 494600 | tf_op jit(solution)/shard_map/ppermute | solution.py:130
  219.2 15.0 %copy-start.2 = (f32[1,32,48,256]{3,2,1,0:T(8,128)S(1)}, f32[1,32,48,256]{3,2,1,0:T(8,128)}, u32[]{:S(2)}) copy-start(f32[1,32,48,256]{3,2,1,0:T(8,128)} %shard_map.103) | copy-start | bytes 4718596
  234.3 0.7 copy-start.4
  241.8 4.3 %collective-permute-start.12 = (bf16[1,64,256]{2,1,0:T(8,128)(2,1)S(1)}, bf16[1,64,256]{2,1,0:T(8,128)(2,1)S(1)}, u32[]{:S(2)}, u32[]{:S(2)}) collective-permute-start(bf16[1,64,256]{2,1,0:T(8,128)(2,1)S(1)} %get-tuple-element.39), channel_id=1, source_target_pairs={{0,4},{4,8},{8,12},{12,16},{16,20},{20,24},{24,28},{1,5},{5,9},{9,... | collective-permute-start | bytes 98312 | tf_op jit(solution)/shard_map/ppermute | solution.py:16
  243.9 6.1 %collective-permute-start.13 = (bf16[1,64,256]{2,1,0:T(8,128)(2,1)S(1)}, bf16[1,64,256]{2,1,0:T(8,128)(2,1)S(1)}, u32[]{:S(2)}, u32[]{:S(2)}) collective-permute-start(bf16[1,64,256]{2,1,0:T(8,128)(2,1)S(1)} %get-tuple-element.40), channel_id=1, source_target_pairs={{4,0},{8,4},{12,8},{16,12},{20,16},{24,20},{28,24},{5,1},{9,5},{13... | collective-permute-start | bytes 98312 | tf_op jit(solution)/shard_map/ppermute | solution.py:19
  251.0 5.8 %collective-permute-start.14 = (bf16[34,1,256]{2,1,0:T(2,128)(2,1)S(1)}, bf16[34,1,256]{2,1,0:T(2,128)(2,1)S(1)}, u32[]{:S(2)}, u32[]{:S(2)}) collective-permute-start(bf16[34,1,256]{2,1,0:T(2,128)(2,1)S(1)} %get-tuple-element.35), channel_id=1, source_target_pairs={{0,1},{1,2},{2,3},{4,5},{5,6},{6,7},{8,9},{9,10},{10,11},{12,13},{... | collective-permute-start | bytes 52232 | tf_op jit(solution)/shard_map/ppermute | solution.py:16
  255.3 5.0 %collective-permute-start.15 = (bf16[34,1,256]{2,1,0:T(2,128)(2,1)S(1)}, bf16[34,1,256]{2,1,0:T(2,128)(2,1)S(1)}, u32[]{:S(2)}, u32[]{:S(2)}) collective-permute-start(bf16[34,1,256]{2,1,0:T(2,128)(2,1)S(1)} %get-tuple-element.36), channel_id=1, source_target_pairs={{1,0},{2,1},{3,2},{5,4},{6,5},{7,6},{9,8},{10,9},{11,10},{13,12},{... | collective-permute-start | bytes 52232 | tf_op jit(solution)/shard_map/ppermute | solution.py:19

commit v13 on v12

--- a/solution.py
+++ b/solution.py
@@ -45,9 +45,10 @@
         lax.fori_loop(0, rows + taps - 1, widen_row, 0, unroll=spread)
         first = True
         for s in range(8):
-            if cbase + s == 0:
-                src = xf_ref
+            if (cbase + s) % 8 == 0:
+                src, off = xf_ref, cbase + s
             else:
+                off = 0
                 width = cols + 8 if s + 8 < taps else cols
 
                 def shift(r, c, s=s, width=width):
@@ -67,10 +68,10 @@
                         for a in range(taps)
                     ]
 
-                    def body(i, c, src=src, q=q, ks=ks, lanes=lanes, first=first):
+                    def body(i, c, src=src, off=off, q=q, ks=ks, lanes=lanes, first=first):
                         r0 = pl.multiple_of((i // njb) * rb, rb)
                         j0 = pl.multiple_of((i % njb) * 8, 8)
-                        xs = src[pl.ds(r0, rb + taps - 1), pl.ds(j0 + 8 * q, 8), lanes]
+                        xs = src[pl.ds(r0, rb + taps - 1), pl.ds(j0 + off + 8 * q, 8), lanes]
                         if first:
                             acc = jnp.zeros((rb, 8, 128), jnp.float32)
                         else:

time: 267 us -> 266 us (level)
  no operation moved by 1% of the time
where the time goes in v13:
time: 266 us; the launch traced here: 265 us
  Pallas kernels  152 us (57%)
  starting transfers between devices  40.2 us (15%)
  waiting for transfers between devices  24.4 us (9%)
  other arithmetic  22.5 us (8%)
  matrix products  14.5 us (5%)
  local copies, waits for them, and re-layouts  10.5 us (4%)
    pallas_call x4, Pallas kernels, depthwise(): pl.pallas_call(body, out_shape=jax.ShapeDtypeStruct((count, rows, cols, c...  152 us
    ppermute x4, waiting for transfers between devices, padded_2(): lax.ppermute(lax.slice_in_dim(block, 0, width, axis=dim), axis, backward)  14.5 us
    dot_general x2, matrix products, local_section(): mixed = jnp.dot(hidden, w_out, preferred_element_type=jnp.float32)  14.1 us
    ppermute x4, starting transfers between devices, exchange(): lax.ppermute(lax.slice_in_dim(block, block.shape[dim] - width, None, axis...  13.7 us
    ppermute x4, starting transfers between devices, padded_2(): lax.ppermute(lax.slice_in_dim(block, block.shape[dim] - width, None, axis...  12.9 us
    ppermute x4, waiting for transfers between devices, exchange(): lax.ppermute(lax.slice_in_dim(block, 0, width, axis=dim), axis, backward)  7.3 us
    ppermute x4, starting transfers between devices, padded_2(): lax.ppermute(lax.slice_in_dim(block, 0, width, axis=dim), axis, backward)  7.28 us
    ppermute x4, starting transfers between devices, exchange(): lax.ppermute(lax.slice_in_dim(block, 0, width, axis=dim), axis, backward)  6.41 us
  transfers between devices with their start and end apart: 16, of which 8 were waited for; matrix products, arithmetic and copies ran while one was open for 2% of the time, Pallas kernels for 48%

profile of v13, /device:TPU:3, one launch (start us, length us, event | category | flops | bytes accessed | tf_op | source)
XLA Modules:
  0.0 264.8 jit_solution(15010151432534591587)
XLA Ops:
  0.0 1.1 fusion.91
  1.1 3.7 %collective-permute-start = (bf16[7,128,128]{2,1,0:T(8,128)(2,1)S(1)}, bf16[7,128,128]{2,1,0:T(8,128)(2,1)S(1)}, u32[]{:S(2)}, u32[]{:S(2)}) collective-permute-start(bf16[7,128,128]{2,1,0:T(8,128)(2,1)S(1)} %get-tuple-element.28), channel_id=1, source_target_pairs={{0,4},{4,8},{8,12},{12,16},{16,20},{20,24},{24,28},{1,5},{5,9},{9,... | collective-permute-start | bytes 688136 | tf_op jit(solution)/shard_map/ppermute | solution.py:128
  4.8 1.9 collective-permute-start.1
  6.8 0.7 multiply_multiply_fusion.3
  7.5 0.3 collective-permute-done
  7.8 2.0 constant_dynamic-update-slice_fusion.1
  9.8 3.2 %collective-permute-done.1 = bf16[7,128,128]{2,1,0:T(8,128)(2,1)S(1)} collective-permute-done((bf16[7,128,128]{2,1,0:T(8,128)(2,1)S(1)}, bf16[7,128,128]{2,1,0:T(8,128)(2,1)S(1)}, u32[]{:S(2)}, u32[]{:S(2)}) %collective-permute-start.1) | collective-permute-done | bytes 229408 | tf_op jit(solution)/shard_map/ppermute | solution.py:131
  13.2 3.9 %collective-permute-start.2 = (bf16[78,7,128]{2,1,0:T(8,128)(2,1)S(1)}, bf16[78,7,128]{2,1,0:T(8,128)(2,1)}, u32[]{:S(2)}, u32[]{:S(2)}) collective-permute-start(bf16[78,7,128]{2,1,0:T(8,128)(2,1)S(1)} %get-tuple-element.13), channel_id=1, source_target_pairs={{0,1},{1,2},{2,3},{4,5},{5,6},{6,7},{8,9},{9,10},{10,11},{12,13},{... | collective-permute-start | bytes 419336 | tf_op jit(solution)/shard_map/ppermute | solution.py:128
  17.1 1.3 collective-permute-start.3
  18.4 0.8 fusion.68.k_ref
  19.1 87.0 %shard_map.101 = f32[1,64,112,128]{3,2,1,0:T(8,128)} custom-call(bf16[1,78,128,128]{3,2,1,0:T(8,128)(2,1)} %bitcast.62, f32[15,15,128]{2,1,0:T(8,128)} %fusion.68.k_ref), custom_call_target="tpu_custom_call" | custom-call | flops 412876800 | bytes 6225920 | tf_op jit(solution)/shard_map/pallas_call | solution.py:107
  106.1 1.6 fusion.57
  107.7 1.1 pad_maximum_fusion.6.x_all
  108.8 12.3 %shard_map.100 = f32[2,64,8,128]{3,2,1,0:T(8,128)} custom-call(bf16[2,78,22,128]{3,2,1,0:T(8,128)(2,1)} %pad_maximum_fusion.6.x_all, f32[15,15,128]{2,1,0:T(8,128)} %fusion.68.k_ref), custom_call_target="tpu_custom_call" | custom-call | flops 58982400 | bytes 1402880 | tf_op jit(solution)/shard_map/pallas_call | solution.py:107
  121.1 1.1 slice_bitcast_fusion.3
  122.2 3.3 %fusion.29 = f32[64,128]{1,0:T(8,128)S(1)} fusion(f32[64,8,128]{2,1,0:T(8,128)S(1)} %get-tuple-element.46, f32[64,112,128]{2,1,0:T(8,128)} %bitcast.54, f32[64,8,128]{2,1,0:T(8,128)S(1)} %get-tuple-element.45), kind=kLoop, calls=%fused_computation.39 | loop fusion | flops 3137536 | bytes 4227072 | tf_op jit(solution)/shard_map/reduce_sum | solution.py:150
  125.6 2.6 multiply_reduce_fusion
  128.2 8.6 %add_convert_fusion = bf16[64,128,128]{2,1,0:T(8,128)(2,1)S(1)} fusion(bf16[64,128,128]{2,1,0:T(8,128)(2,1)} %param.10, f32[64,128]{1,0:T(8,128)S(1)} %add_rsqrt_fusion, f32[64,128]{1,0:T(8,128)S(1)} %broadcast_multiply_fusion, f32[64,8,128]{2,1,0:T(8,128)S(1)} %get-tuple-element.46, f32[64,112,128]{2,1,0:T(8,128)} %bitcast.55, ...), kind=kOutput, calls=%fused_computation.19 | convolution fusion | flops 2193620992 | bytes 8716288 | tf_op jit(solution)/shard_map/dot_general | solution.py:156
  136.9 2.3 collective-permute-start.4
  139.2 2.0 collective-permute-start.5
  141.2 4.1 %collective-permute-done.5 = bf16[1,128,128]{2,1,0:T(8,128)(2,1)S(1)} collective-permute-done((bf16[1,128,128]{2,1,0:T(8,128)(2,1)S(1)}, bf16[1,128,128]{2,1,0:T(8,128)(2,1)S(1)}, u32[]{:S(2)}, u32[]{:S(2)}) %collective-permute-start.5) | collective-permute-done | bytes 32800 | tf_op jit(solution)/shard_map/ppermute | solution.py:19
  145.4 4.3 %collective-permute-start.6 = (bf16[66,1,128]{2,1,0:T(2,128)(2,1)S(1)}, bf16[66,1,128]{2,1,0:T(2,128)(2,1)S(1)}, u32[]{:S(2)}, u32[]{:S(2)}) collective-permute-start(bf16[66,1,128]{2,1,0:T(2,128)(2,1)S(1)} %get-tuple-element.21), channel_id=1, source_target_pairs={{0,1},{1,2},{2,3},{4,5},{5,6},{6,7},{8,9},{9,10},{10,11},{12,13},{... | collective-permute-start | bytes 50696 | tf_op jit(solution)/shard_map/ppermute | solution.py:16
  149.7 1.5 collective-permute-start.7
  151.2 3.2 %collective-permute-done.7 = bf16[66,1,128]{2,1,0:T(2,128)(2,1)S(1)} collective-permute-done((bf16[66,1,128]{2,1,0:T(2,128)(2,1)S(1)}, bf16[66,1,128]{2,1,0:T(2,128)(2,1)S(1)}, u32[]{:S(2)}, u32[]{:S(2)}) %collective-permute-start.7) | collective-permute-done | bytes 16928 | tf_op jit(solution)/shard_map/ppermute | solution.py:19
  154.4 0.8 maximum_convert_fusion
  155.2 0.6 fusion.82
  155.8 0.6 fusion.83
  156.4 1.6 fusion.22
  158.0 0.6 fusion.89
  158.6 0.5 fusion.55
  159.1 0.3 copy-done.7
  159.4 0.4 convolution_convert_fusion
  159.9 3.3 %collective-permute-start.8 = (bf16[7,64,256]{2,1,0:T(8,128)(2,1)S(1)}, bf16[7,64,256]{2,1,0:T(8,128)(2,1)S(1)}, u32[]{:S(2)}, u32[]{:S(2)}) collective-permute-start(bf16[7,64,256]{2,1,0:T(8,128)(2,1)S(1)} %get-tuple-element.41), channel_id=1, source_target_pairs={{0,4},{4,8},{8,12},{12,16},{16,20},{20,24},{24,28},{1,5},{5,9},{9,... | collective-permute-start | bytes 688136 | tf_op jit(solution)/shard_map/ppermute | solution.py:128
  163.2 1.9 collective-permute-start.9
  165.2 2.2 collective-permute-done.8
  167.4 4.0 %collective-permute-done.9 = bf16[7,64,256]{2,1,0:T(8,128)(2,1)S(1)} collective-permute-done((bf16[7,64,256]{2,1,0:T(8,128)(2,1)S(1)}, bf16[7,64,256]{2,1,0:T(8,128)(2,1)S(1)}, u32[]{:S(2)}, u32[]{:S(2)}) %collective-permute-start.9) | collective-permute-done | bytes 229408 | tf_op jit(solution)/shard_map/ppermute | solution.py:131
  171.5 1.4 fusion.81
  172.9 2.8 %collective-permute-start.10 = (bf16[46,7,256]{2,1,0:T(8,128)(2,1)S(1)}, bf16[46,7,256]{2,1,0:T(8,128)(2,1)S(1)}, u32[]{:S(2)}, u32[]{:S(2)}) collective-permute-start(bf16[46,7,256]{2,1,0:T(8,128)(2,1)S(1)} %get-tuple-element.33), channel_id=1, source_target_pairs={{0,1},{1,2},{2,3},{4,5},{5,6},{6,7},{8,9},{9,10},{10,11},{12,13},{... | collective-permute-start | bytes 494600 | tf_op jit(solution)/shard_map/ppermute | solution.py:128
  175.7 1.3 collective-permute-start.11
  177.0 0.8 fusion.66.k_ref
  177.8 40.1 %shard_map.103 = f32[1,32,48,256]{3,2,1,0:T(8,128)} custom-call(bf16[1,46,64,256]{3,2,1,0:T(8,128)(2,1)} %get-tuple-element.29.x_all, f32[15,15,256]{2,1,0:T(8,128)} %fusion.66.k_ref), custom_call_target="tpu_custom_call" | custom-call | flops 176947200 | bytes 3080192 | tf_op jit(solution)/shard_map/pallas_call | solution.py:107
  217.9 0.6 fusion.46
  218.5 1.1 pad_maximum_fusion.5.x_all
  219.6 12.8 %shard_map.102 = f32[2,32,8,256]{3,2,1,0:T(8,128)} custom-call(bf16[2,46,22,256]{3,2,1,0:T(8,128)(2,1)} %pad_maximum_fusion.5.x_all, f32[15,15,256]{2,1,0:T(8,128)} %fusion.66.k_ref), custom_call_target="tpu_custom_call" | custom-call | flops 58982400 | bytes 1560576 | tf_op jit(solution)/shard_map/pallas_call | solution.py:107
  232.5 1.1 slice_bitcast_fusion.1
  233.5 0.4 fusion.44
  233.9 0.3 copy-done.4
  234.2 0.6 multiply_reduce_fusion.1
  234.9 5.4 %add_convert_fusion.1 = bf16[32,64,256]{2,1,0:T(8,128)(2,1)} fusion(bf16[32,64,256]{2,1,0:T(8,128)(2,1)S(1)} %convolution_convert_fusion, f32[32,64]{1,0:T(8,128)S(1)} %add_rsqrt_fusion.1, f32[32,64]{1,0:T(8,128)S(1)} %broadcast_multiply_fusion.1, f32[32,8,256]{2,1,0:T(8,128)} %copy-done.4, f32[32,48,256]{2,1,0:T(8,128)S(1)} %bitcast.61, ...), kind=kOutput, calls=%fused_computation.34 | convolution fusion | flops 2170552320 | bytes 5259264 | tf_op jit(solution)/shard_map/dot_general | solution.py:156
  240.3 0.8 fusion.94
  241.1 2.0 collective-permute-start.12
  243.1 2.3 collective-permute-start.13
  245.4 3.8 %collective-permute-done.13 = bf16[1,64,256]{2,1,0:T(8,128)(2,1)S(1)} collective-permute-done((bf16[1,64,256]{2,1,0:T(8,128)(2,1)S(1)}, bf16[1,64,256]{2,1,0:T(8,128)(2,1)S(1)}, u32[]{:S(2)}, u32[]{:S(2)}) %collective-permute-start.13) | collective-permute-done | bytes 32800 | tf_op jit(solution)/shard_map/ppermute | solution.py:19
  249.3 1.0 pad_maximum_fusion.19
  250.3 4.3 %collective-permute-start.14 = (bf16[34,1,256]{2,1,0:T(2,128)(2,1)S(1)}, bf16[34,1,256]{2,1,0:T(2,128)(2,1)S(1)}, u32[]{:S(2)}, u32[]{:S(2)}) collective-permute-start(bf16[34,1,256]{2,1,0:T(2,128)(2,1)S(1)} %get-tuple-element.35), channel_id=1, source_target_pairs={{0,1},{1,2},{2,3},{4,5},{5,6},{6,7},{8,9},{9,10},{10,11},{12,13},{... | collective-permute-start | bytes 52232 | tf_op jit(solution)/shard_map/ppermute | solution.py:16
  254.6 1.5 collective-permute-start.15
  256.1 3.4 %collective-permute-done.15 = bf16[34,1,256]{2,1,0:T(2,128)(2,1)S(1)} collective-permute-done((bf16[34,1,256]{2,1,0:T(2,128)(2,1)S(1)}, bf16[34,1,256]{2,1,0:T(2,128)(2,1)S(1)}, u32[]{:S(2)}, u32[]{:S(2)}) %collective-permute-start.15) | collective-permute-done | bytes 17440 | tf_op jit(solution)/shard_map/ppermute | solution.py:19
  259.5 1.8 maximum_convert_fusion.1
  261.3 0.4 fusion.86
  261.7 0.2 fusion.87
  262.1 1.4 fusion.33
  263.5 0.3 fusion.93
  263.8 0.2 fusion.58
  264.0 0.8 copy.20
  (43 shorter events, 0.7 us)
Async XLA Ops:
  0.0 234.9 %copy-start = (bf16[1024,256]{1,0:T(8,128)(2,1)S(1)}, bf16[1024,256]{1,0:T(8,128)(2,1)}, u32[]{:S(2)}) copy-start(bf16[1024,256]{1,0:T(8,128)(2,1)} %param.19) | copy-start | bytes 1572868
  1.1 6.6 %collective-permute-start = (bf16[7,128,128]{2,1,0:T(8,128)(2,1)S(1)}, bf16[7,128,128]{2,1,0:T(8,128)(2,1)S(1)}, u32[]{:S(2)}, u32[]{:S(2)}) collective-permute-start(bf16[7,128,128]{2,1,0:T(8,128)(2,1)S(1)} %get-tuple-element.28), channel_id=1, source_target_pairs={{0,4},{4,8},{8,12},{12,16},{16,20},{20,24},{24,28},{1,5},{5,9},{9,... | collective-permute-start | bytes 688136 | tf_op jit(solution)/shard_map/ppermute | solution.py:128
  4.8 8.2 %collective-permute-start.1 = (bf16[7,128,128]{2,1,0:T(8,128)(2,1)S(1)}, bf16[7,128,128]{2,1,0:T(8,128)(2,1)S(1)}, u32[]{:S(2)}, u32[]{:S(2)}) collective-permute-start(bf16[7,128,128]{2,1,0:T(8,128)(2,1)S(1)} %get-tuple-element.27), channel_id=1, source_target_pairs={{4,0},{8,4},{12,8},{16,12},{20,16},{24,20},{28,24},{5,1},{9,5},{13... | collective-permute-start | bytes 688136 | tf_op jit(solution)/shard_map/ppermute | solution.py:131
  7.8 10.6 %copy-start.6 = (f32[15,15,128]{2,1,0:T(8,128)S(1)}, f32[15,15,128]{2,1,0:T(8,128)}, u32[]{:S(2)}) copy-start(f32[15,15,128]{2,1,0:T(8,128)} %param.11) | copy-start | bytes 345604
  13.1 6.0 %copy-start.3 = (bf16[78,128,128]{2,1,0:T(8,128)(2,1)}, bf16[78,128,128]{2,1,0:T(8,128)(2,1)S(1)}, u32[]{:S(2)}) copy-start(bf16[78,128,128]{2,1,0:T(8,128)(2,1)S(1)} %constant_dynamic-update-slice_fusion) | copy-start | bytes 7667716
  13.2 92.9 %collective-permute-start.2 = (bf16[78,7,128]{2,1,0:T(8,128)(2,1)S(1)}, bf16[78,7,128]{2,1,0:T(8,128)(2,1)}, u32[]{:S(2)}, u32[]{:S(2)}) collective-permute-start(bf16[78,7,128]{2,1,0:T(8,128)(2,1)S(1)} %get-tuple-element.13), channel_id=1, source_target_pairs={{0,1},{1,2},{2,3},{4,5},{5,6},{6,7},{8,9},{9,10},{10,11},{12,13},{... | collective-permute-start | bytes 419336 | tf_op jit(solution)/shard_map/ppermute | solution.py:128
  17.1 89.0 %collective-permute-start.3 = (bf16[78,7,128]{2,1,0:T(8,128)(2,1)S(1)}, bf16[78,7,128]{2,1,0:T(8,128)(2,1)}, u32[]{:S(2)}, u32[]{:S(2)}) collective-permute-start(bf16[78,7,128]{2,1,0:T(8,128)(2,1)S(1)} %get-tuple-element.14), channel_id=1, source_target_pairs={{1,0},{2,1},{3,2},{5,4},{6,5},{7,6},{9,8},{10,9},{11,10},{13,12},{... | collective-permute-start | bytes 419336 | tf_op jit(solution)/shard_map/ppermute | solution.py:131
  122.2 3.4 %copy-start.1 = (f32[1,64,112,128]{3,2,1,0:T(8,128)S(1)}, f32[1,64,112,128]{3,2,1,0:T(8,128)}, u32[]{:S(2)}) copy-start(f32[1,64,112,128]{3,2,1,0:T(8,128)} %shard_map.101) | copy-start | bytes 11010052
  125.5 2.7 %copy-start.9 = (bf16[512,128]{1,0:T(8,128)(2,1)S(1)}, bf16[512,128]{1,0:T(8,128)(2,1)}, u32[]{:S(2)}) copy-start(bf16[512,128]{1,0:T(8,128)(2,1)} %param.14) | copy-start | bytes 393220
  125.5 2.7 %copy-start.10 = (bf16[128,512]{1,0:T(8,128)(2,1)S(1)}, bf16[128,512]{1,0:T(8,128)(2,1)}, u32[]{:S(2)}) copy-start(bf16[128,512]{1,0:T(8,128)(2,1)} %param.13) | copy-start | bytes 393220
  136.9 4.3 %collective-permute-start.4 = (bf16[1,128,128]{2,1,0:T(8,128)(2,1)S(1)}, bf16[1,128,128]{2,1,0:T(8,128)(2,1)S(1)}, u32[]{:S(2)}, u32[]{:S(2)}) collective-permute-start(bf16[1,128,128]{2,1,0:T(8,128)(2,1)S(1)} %get-tuple-element.25), channel_id=1, source_target_pairs={{0,4},{4,8},{8,12},{12,16},{16,20},{20,24},{24,28},{1,5},{5,9},{9,... | collective-permute-start | bytes 98312 | tf_op jit(solution)/shard_map/ppermute | solution.py:16
  139.2 6.1 %collective-permute-start.5 = (bf16[1,128,128]{2,1,0:T(8,128)(2,1)S(1)}, bf16[1,128,128]{2,1,0:T(8,128)(2,1)S(1)}, u32[]{:S(2)}, u32[]{:S(2)}) collective-permute-start(bf16[1,128,128]{2,1,0:T(8,128)(2,1)S(1)} %get-tuple-element.26), channel_id=1, source_target_pairs={{4,0},{8,4},{12,8},{16,12},{20,16},{24,20},{28,24},{5,1},{9,5},{13... | collective-permute-start | bytes 98312 | tf_op jit(solution)/shard_map/ppermute | solution.py:19
  145.4 5.8 %collective-permute-start.6 = (bf16[66,1,128]{2,1,0:T(2,128)(2,1)S(1)}, bf16[66,1,128]{2,1,0:T(2,128)(2,1)S(1)}, u32[]{:S(2)}, u32[]{:S(2)}) collective-permute-start(bf16[66,1,128]{2,1,0:T(2,128)(2,1)S(1)} %get-tuple-element.21), channel_id=1, source_target_pairs={{0,1},{1,2},{2,3},{4,5},{5,6},{6,7},{8,9},{9,10},{10,11},{12,13},{... | collective-permute-start | bytes 50696 | tf_op jit(solution)/shard_map/ppermute | solution.py:16
  149.7 4.7 %collective-permute-start.7 = (bf16[66,1,128]{2,1,0:T(2,128)(2,1)S(1)}, bf16[66,1,128]{2,1,0:T(2,128)(2,1)S(1)}, u32[]{:S(2)}, u32[]{:S(2)}) collective-permute-start(bf16[66,1,128]{2,1,0:T(2,128)(2,1)S(1)} %get-tuple-element.22), channel_id=1, source_target_pairs={{1,0},{2,1},{3,2},{5,4},{6,5},{7,6},{9,8},{10,9},{11,10},{13,12},{... | collective-permute-start | bytes 50696 | tf_op jit(solution)/shard_map/ppermute | solution.py:19
  158.6 0.8 copy-start.7
  159.4 5.8 %copy-start.8 = (f32[256]{0:T(256)S(1)}, f32[256]{0:T(256)}, u32[]{:S(2)}) copy-start(f32[256]{0:T(256)} %param.17) | copy-start | bytes 3076
  159.9 7.5 %collective-permute-start.8 = (bf16[7,64,256]{2,1,0:T(8,128)(2,1)S(1)}, bf16[7,64,256]{2,1,0:T(8,128)(2,1)S(1)}, u32[]{:S(2)}, u32[]{:S(2)}) collective-permute-start(bf16[7,64,256]{2,1,0:T(8,128)(2,1)S(1)} %get-tuple-element.41), channel_id=1, source_target_pairs={{0,4},{4,8},{8,12},{12,16},{16,20},{20,24},{24,28},{1,5},{5,9},{9,... | collective-permute-start | bytes 688136 | tf_op jit(solution)/shard_map/ppermute | solution.py:128
  163.2 8.2 %collective-permute-start.9 = (bf16[7,64,256]{2,1,0:T(8,128)(2,1)S(1)}, bf16[7,64,256]{2,1,0:T(8,128)(2,1)S(1)}, u32[]{:S(2)}, u32[]{:S(2)}) collective-permute-start(bf16[7,64,256]{2,1,0:T(8,128)(2,1)S(1)} %get-tuple-element.42), channel_id=1, source_target_pairs={{4,0},{8,4},{12,8},{16,12},{20,16},{24,20},{28,24},{5,1},{9,5},{13... | collective-permute-start | bytes 688136 | tf_op jit(solution)/shard_map/ppermute | solution.py:131
  165.2 11.8 %copy-start.5 = (f32[15,15,256]{2,1,0:T(8,128)S(1)}, f32[15,15,256]{2,1,0:T(8,128)}, u32[]{:S(2)}) copy-start(f32[15,15,256]{2,1,0:T(8,128)} %param.16) | copy-start | bytes 691204
  172.9 45.0 %collective-permute-start.10 = (bf16[46,7,256]{2,1,0:T(8,128)(2,1)S(1)}, bf16[46,7,256]{2,1,0:T(8,128)(2,1)S(1)}, u32[]{:S(2)}, u32[]{:S(2)}) collective-permute-start(bf16[46,7,256]{2,1,0:T(8,128)(2,1)S(1)} %get-tuple-element.33), channel_id=1, source_target_pairs={{0,1},{1,2},{2,3},{4,5},{5,6},{6,7},{8,9},{9,10},{10,11},{12,13},{... | collective-permute-start | bytes 494600 | tf_op jit(solution)/shard_map/ppermute | solution.py:128
  175.7 42.3 %collective-permute-start.11 = (bf16[46,7,256]{2,1,0:T(8,128)(2,1)S(1)}, bf16[46,7,256]{2,1,0:T(8,128)(2,1)S(1)}, u32[]{:S(2)}, u32[]{:S(2)}) collective-permute-start(bf16[46,7,256]{2,1,0:T(8,128)(2,1)S(1)} %get-tuple-element.34), channel_id=1, source_target_pairs={{1,0},{2,1},{3,2},{5,4},{6,5},{7,6},{9,8},{10,9},{11,10},{13,12},{... | collective-permute-start | bytes 494600 | tf_op jit(solution)/shard_map/ppermute | solution.py:131
  218.5 15.0 %copy-start.2 = (f32[1,32,48,256]{3,2,1,0:T(8,128)S(1)}, f32[1,32,48,256]{3,2,1,0:T(8,128)}, u32[]{:S(2)}) copy-start(f32[1,32,48,256]{3,2,1,0:T(8,128)} %shard_map.103) | copy-start | bytes 4718596
  233.5 0.7 copy-start.4
  241.1 4.3 %collective-permute-start.12 = (bf16[1,64,256]{2,1,0:T(8,128)(2,1)S(1)}, bf16[1,64,256]{2,1,0:T(8,128)(2,1)S(1)}, u32[]{:S(2)}, u32[]{:S(2)}) collective-permute-start(bf16[1,64,256]{2,1,0:T(8,128)(2,1)S(1)} %get-tuple-element.39), channel_id=1, source_target_pairs={{0,4},{4,8},{8,12},{12,16},{16,20},{20,24},{24,28},{1,5},{5,9},{9,... | collective-permute-start | bytes 98312 | tf_op jit(solution)/shard_map/ppermute | solution.py:16
  243.1 6.1 %collective-permute-start.13 = (bf16[1,64,256]{2,1,0:T(8,128)(2,1)S(1)}, bf16[1,64,256]{2,1,0:T(8,128)(2,1)S(1)}, u32[]{:S(2)}, u32[]{:S(2)}) collective-permute-start(bf16[1,64,256]{2,1,0:T(8,128)(2,1)S(1)} %get-tuple-element.40), channel_id=1, source_target_pairs={{4,0},{8,4},{12,8},{16,12},{20,16},{24,20},{28,24},{5,1},{9,5},{13... | collective-permute-start | bytes 98312 | tf_op jit(solution)/shard_map/ppermute | solution.py:19
  250.3 5.8 %collective-permute-start.14 = (bf16[34,1,256]{2,1,0:T(2,128)(2,1)S(1)}, bf16[34,1,256]{2,1,0:T(2,128)(2,1)S(1)}, u32[]{:S(2)}, u32[]{:S(2)}) collective-permute-start(bf16[34,1,256]{2,1,0:T(2,128)(2,1)S(1)} %get-tuple-element.35), channel_id=1, source_target_pairs={{0,1},{1,2},{2,3},{4,5},{5,6},{6,7},{8,9},{9,10},{10,11},{12,13},{... | collective-permute-start | bytes 52232 | tf_op jit(solution)/shard_map/ppermute | solution.py:16
  254.6 5.0 %collective-permute-start.15 = (bf16[34,1,256]{2,1,0:T(2,128)(2,1)S(1)}, bf16[34,1,256]{2,1,0:T(2,128)(2,1)S(1)}, u32[]{:S(2)}, u32[]{:S(2)}) collective-permute-start(bf16[34,1,256]{2,1,0:T(2,128)(2,1)S(1)} %get-tuple-element.36), channel_id=1, source_target_pairs={{1,0},{2,1},{3,2},{5,4},{6,5},{7,6},{9,8},{10,9},{11,10},{13,12},{... | collective-permute-start | bytes 52232 | tf_op jit(solution)/shard_map/ppermute | solution.py:19

commit v14 on v13

--- a/solution.py
+++ b/solution.py
@@ -132,21 +132,27 @@
     return jnp.concatenate([low, block, high], axis=dim)
 
 
-def section_conv(block, kernel):
+def section_conv(block, kernel, split_rows):
     reach = (kernel.shape[0] - 1) // 2
-    cols = block.shape[1]
+    rows, cols = block.shape[:2]
     band = 8
     tall = exchange(block, "row", 0, reach)
-    middle = depthwise(tall[None], kernel, band - reach, cols - 2 * band)
+    if split_rows:
+        inner = depthwise(block[band - reach : rows - band + reach][None], kernel, 1, cols - 2 * band)
+        caps = jnp.stack([tall[: band + 2 * reach], tall[rows - band :]], axis=0)
+        caps = depthwise(caps, kernel, band - reach, cols - 2 * band)
+        middle = jnp.concatenate([caps[0], inner[0], caps[1]], axis=0)
+    else:
+        middle = depthwise(tall[None], kernel, band - reach, cols - 2 * band)[0]
     full = exchange(tall, "col", 1, reach)
     ends = jnp.stack([full[:, : band + 2 * reach], full[:, cols - band :]], axis=0)
     edge = depthwise(ends, kernel, 0, band)
-    return jnp.concatenate([edge[0], middle[0], edge[1]], axis=1)
-
-
-def local_section(field, raw, sigma, w_in, w_out):
+    return jnp.concatenate([edge[0], middle, edge[1]], axis=1)
+
+
+def local_section(field, raw, sigma, w_in, w_out, split_rows):
     kernel = masked_kernel(raw, sigma)
-    conv_out = section_conv(field, kernel)
+    conv_out = section_conv(field, kernel, split_rows)
     mean = jnp.mean(conv_out, axis=-1, keepdims=True)
     var = jnp.mean((conv_out - mean) ** 2, axis=-1, keepdims=True)
     normed = ((conv_out - mean) * lax.rsqrt(var + 1e-06)).astype(jnp.bfloat16)
@@ -183,11 +189,11 @@
     in_second,
     out_second,
 ):
-    first = local_section(image, raw_first, sigma_first, in_first, out_first)
+    first = local_section(image, raw_first, sigma_first, in_first, out_first, True)
     first_cycle = padded_2(first, (("row", 0), ("col", 1)), 1)
     first_pooled = blur_down(first_cycle)
     widened = jnp.dot(first_pooled, widen, preferred_element_type=jnp.float32).astype(jnp.bfloat16)
-    second = local_section(widened, raw_second, sigma_second, in_second, out_second)
+    second = local_section(widened, raw_second, sigma_second, in_second, out_second, False)
     second_cycle = padded_2(second, (("row", 0), ("col", 1)), 1)
     return blur_down(second_cycle)
 

time: 266 us -> 276 us (1.038)
  local copies, waits for them, and re-layouts: 10.5 us -> 15 us
  Pallas kernels: 152 us -> 156 us
  waiting for transfers between devices: 24.4 us -> 20.9 us
    pallas_call x4 -> x5, Pallas kernels: 152 us -> 156 us  [depthwise(): pl.pallas_call(body, out_shape=jax.ShapeDtypeStruct((count, rows, cols, c...]
    ppermute x4, waiting for transfers between devices: 7.3 us -> 4.05 us  [exchange(): lax.ppermute(lax.slice_in_dim(block, 0, width, axis=dim), axis, backward)]
    broadcast_in_dim x0 -> x1, local copies, waits for them, and re-layouts: none -> 3.15 us  [section_conv(): block[band - reach:rows - band + reach][None]]
  transfers between devices with their start and end apart: 16 -> 16, of which waited for: 8 -> 6; matrix products, arithmetic and copies ran while one was open for 2% -> 3% of each run, Pallas kernels for 48% -> 48%
where the time goes in v14:
time: 276 us; the launch traced here: 275 us
  Pallas kernels  156 us (57%)
  starting transfers between devices  42.8 us (16%)
  other arithmetic  23.7 us (9%)
  waiting for transfers between devices  20.9 us (8%)
  matrix products  15.6 us (6%)
  local copies, waits for them, and re-layouts  15 us (5%)
    pallas_call x5, Pallas kernels, depthwise(): pl.pallas_call(body, out_shape=jax.ShapeDtypeStruct((count, rows, cols, c...  156 us
    ppermute x4, starting transfers between devices, padded_2(): lax.ppermute(lax.slice_in_dim(block, block.shape[dim] - width, None, axis...  15.4 us
    dot_general x2, matrix products, local_section(): mixed = jnp.dot(hidden, w_out, preferred_element_type=jnp.float32)  15.2 us
    ppermute x4, waiting for transfers between devices, padded_2(): lax.ppermute(lax.slice_in_dim(block, 0, width, axis=dim), axis, backward)  14.6 us
    ppermute x4, starting transfers between devices, exchange(): lax.ppermute(lax.slice_in_dim(block, block.shape[dim] - width, None, axis...  13.8 us
    ppermute x4, starting transfers between devices, padded_2(): lax.ppermute(lax.slice_in_dim(block, 0, width, axis=dim), axis, backward)  7.21 us
    ppermute x4, starting transfers between devices, exchange(): lax.ppermute(lax.slice_in_dim(block, 0, width, axis=dim), axis, backward)  6.41 us
  transfers between devices with their start and end apart: 16, of which 6 were waited for; matrix products, arithmetic and copies ran while one was open for 3% of the time, Pallas kernels for 48%

profile of v14, /device:TPU:3, one launch (start us, length us, event | category | flops | bytes accessed | tf_op | source)
XLA Modules:
  0.0 274.7 jit_solution(1034570463054700798)
XLA Ops:
  0.0 1.1 fusion.91
  1.2 3.8 %collective-permute-start = (bf16[7,128,128]{2,1,0:T(8,128)(2,1)S(1)}, bf16[7,128,128]{2,1,0:T(8,128)(2,1)S(1)}, u32[]{:S(2)}, u32[]{:S(2)}) collective-permute-start(bf16[7,128,128]{2,1,0:T(8,128)(2,1)S(1)} %get-tuple-element.30), channel_id=1, source_target_pairs={{0,4},{4,8},{8,12},{12,16},{16,20},{20,24},{24,28},{1,5},{5,9},{9,... | collective-permute-start | bytes 688136 | tf_op jit(solution)/shard_map/ppermute | solution.py:128
  5.0 1.9 collective-permute-start.1
  6.9 3.2 %slice_bitcast_fusion.x_all = bf16[1,62,128,128]{3,2,1,0:T(8,128)(2,1)} fusion(bf16[64,128,128]{2,1,0:T(8,128)(2,1)} %param.10), kind=kLoop, calls=%fused_computation.39 | loop fusion | bytes 4063232 | tf_op jit(solution)/shard_map/broadcast_in_dim | solution.py:141
  10.2 0.8 fusion.69.k_ref
  10.9 66.0 %shard_map.102 = f32[1,48,112,128]{3,2,1,0:T(8,128)} custom-call(bf16[1,62,128,128]{3,2,1,0:T(8,128)(2,1)} %slice_bitcast_fusion.x_all, f32[15,15,128]{2,1,0:T(8,128)} %fusion.69.k_ref), custom_call_target="tpu_custom_call" | custom-call | flops 309657600 | bytes 4784128 | tf_op jit(solution)/shard_map/pallas_call | solution.py:107
  77.4 3.9 %collective-permute-start.2 = (bf16[78,7,128]{2,1,0:T(8,128)(2,1)S(1)}, bf16[78,7,128]{2,1,0:T(8,128)(2,1)}, u32[]{:S(2)}, u32[]{:S(2)}) collective-permute-start(bf16[78,7,128]{2,1,0:T(8,128)(2,1)S(1)} %get-tuple-element.13), channel_id=1, source_target_pairs={{0,1},{1,2},{2,3},{4,5},{5,6},{6,7},{8,9},{9,10},{10,11},{12,13},{... | collective-permute-start | bytes 419336 | tf_op jit(solution)/shard_map/ppermute | solution.py:128
  81.3 1.3 collective-permute-start.3
  82.7 1.3 pad_maximum_fusion.3.x_all
  84.0 24.6 %shard_map.101 = f32[2,8,112,128]{3,2,1,0:T(8,128)} custom-call(bf16[2,22,128,128]{3,2,1,0:T(8,128)(2,1)} %pad_maximum_fusion.3.x_all, f32[15,15,128]{2,1,0:T(8,128)} %fusion.69.k_ref), custom_call_target="tpu_custom_call" | custom-call | flops 103219200 | bytes 2359296 | tf_op jit(solution)/shard_map/pallas_call | solution.py:107
  108.6 2.2 slice_bitcast_fusion.2
  110.8 1.5 fusion.58
  112.3 1.1 pad_maximum_fusion.5.x_all
  113.4 12.3 %shard_map.100 = f32[2,64,8,128]{3,2,1,0:T(8,128)} custom-call(bf16[2,78,22,128]{3,2,1,0:T(8,128)(2,1)} %pad_maximum_fusion.5.x_all, f32[15,15,128]{2,1,0:T(8,128)} %fusion.69.k_ref), custom_call_target="tpu_custom_call" | custom-call | flops 58982400 | bytes 1402880 | tf_op jit(solution)/shard_map/pallas_call | solution.py:107
  125.7 1.1 slice_bitcast_fusion.6
  126.8 2.4 fusion.80
  129.3 2.6 multiply_reduce_fusion
  131.9 0.6 add_rsqrt_fusion
  132.6 9.8 %add_convert_fusion = bf16[64,128,128]{2,1,0:T(8,128)(2,1)} fusion(bf16[64,128,128]{2,1,0:T(8,128)(2,1)} %param.10, f32[64,128]{1,0:T(8,128)} %add_rsqrt_fusion, f32[64,128]{1,0:T(8,128)} %copy-done.12, bf16[512,128]{1,0:T(8,128)(2,1)} %param.14, bf16[128,512]{1,0:T(8,128)(2,1)} %param.13, f32[64,8,128]{2,1,0:T(8,128)} %copy-done.9, ...), kind=kOutput, calls=%fused_computation.19 | convolution fusion | flops 2195718144 | bytes 8716288 | tf_op jit(solution)/shard_map/dot_general | solution.py:162
  142.3 0.9 fusion.90
  143.3 4.8 %collective-permute-start.4 = (bf16[1,128,128]{2,1,0:T(8,128)(2,1)S(1)}, bf16[1,128,128]{2,1,0:T(8,128)(2,1)S(1)}, u32[]{:S(2)}, u32[]{:S(2)}) collective-permute-start(bf16[1,128,128]{2,1,0:T(8,128)(2,1)S(1)} %get-tuple-element.25), channel_id=1, source_target_pairs={{0,4},{4,8},{8,12},{12,16},{16,20},{20,24},{24,28},{1,5},{5,9},{9,... | collective-permute-start | bytes 98312 | tf_op jit(solution)/shard_map/ppermute | solution.py:16
  148.1 2.1 collective-permute-start.5
  150.2 4.0 %collective-permute-done.5 = bf16[1,128,128]{2,1,0:T(8,128)(2,1)S(1)} collective-permute-done((bf16[1,128,128]{2,1,0:T(8,128)(2,1)S(1)}, bf16[1,128,128]{2,1,0:T(8,128)(2,1)S(1)}, u32[]{:S(2)}, u32[]{:S(2)}) %collective-permute-start.5) | collective-permute-done | bytes 32800 | tf_op jit(solution)/shard_map/ppermute | solution.py:19
  154.2 1.0 pad_maximum_fusion.23
  155.3 4.3 %collective-permute-start.6 = (bf16[66,1,128]{2,1,0:T(2,128)(2,1)S(1)}, bf16[66,1,128]{2,1,0:T(2,128)(2,1)S(1)}, u32[]{:S(2)}, u32[]{:S(2)}) collective-permute-start(bf16[66,1,128]{2,1,0:T(2,128)(2,1)S(1)} %get-tuple-element.21), channel_id=1, source_target_pairs={{0,1},{1,2},{2,3},{4,5},{5,6},{6,7},{8,9},{9,10},{10,11},{12,13},{... | collective-permute-start | bytes 50696 | tf_op jit(solution)/shard_map/ppermute | solution.py:16
  159.5 1.3 collective-permute-start.7
  160.8 3.4 %collective-permute-done.7 = bf16[66,1,128]{2,1,0:T(2,128)(2,1)S(1)} collective-permute-done((bf16[66,1,128]{2,1,0:T(2,128)(2,1)S(1)}, bf16[66,1,128]{2,1,0:T(2,128)(2,1)S(1)}, u32[]{:S(2)}, u32[]{:S(2)}) %collective-permute-start.7) | collective-permute-done | bytes 16928 | tf_op jit(solution)/shard_map/ppermute | solution.py:19
  164.2 0.9 maximum_convert_fusion
  165.1 0.6 fusion.82
  165.7 0.6 fusion.83
  166.2 1.6 fusion.22
  167.8 0.6 fusion.89
  168.4 0.5 fusion.56
  168.9 0.3 copy-done.14
  169.2 0.4 convolution_convert_fusion
  169.7 3.3 %collective-permute-start.8 = (bf16[7,64,256]{2,1,0:T(8,128)(2,1)S(1)}, bf16[7,64,256]{2,1,0:T(8,128)(2,1)S(1)}, u32[]{:S(2)}, u32[]{:S(2)}) collective-permute-start(bf16[7,64,256]{2,1,0:T(8,128)(2,1)S(1)} %get-tuple-element.43), channel_id=1, source_target_pairs={{0,4},{4,8},{8,12},{12,16},{16,20},{20,24},{24,28},{1,5},{5,9},{9,... | collective-permute-start | bytes 688136 | tf_op jit(solution)/shard_map/ppermute | solution.py:128
  173.1 1.9 collective-permute-start.9
  175.0 2.2 collective-permute-done.8
  177.3 4.0 %collective-permute-done.9 = bf16[7,64,256]{2,1,0:T(8,128)(2,1)S(1)} collective-permute-done((bf16[7,64,256]{2,1,0:T(8,128)(2,1)S(1)}, bf16[7,64,256]{2,1,0:T(8,128)(2,1)S(1)}, u32[]{:S(2)}, u32[]{:S(2)}) %collective-permute-start.9) | collective-permute-done | bytes 229408 | tf_op jit(solution)/shard_map/ppermute | solution.py:131
  181.3 1.4 fusion.81
  182.7 2.8 %collective-permute-start.10 = (bf16[46,7,256]{2,1,0:T(8,128)(2,1)S(1)}, bf16[46,7,256]{2,1,0:T(8,128)(2,1)S(1)}, u32[]{:S(2)}, u32[]{:S(2)}) collective-permute-start(bf16[46,7,256]{2,1,0:T(8,128)(2,1)S(1)} %get-tuple-element.35), channel_id=1, source_target_pairs={{0,1},{1,2},{2,3},{4,5},{5,6},{6,7},{8,9},{9,10},{10,11},{12,13},{... | collective-permute-start | bytes 494600 | tf_op jit(solution)/shard_map/ppermute | solution.py:128
  185.5 1.3 collective-permute-start.11
  186.8 0.8 fusion.67.k_ref
  187.7 40.1 %shard_map.104 = f32[1,32,48,256]{3,2,1,0:T(8,128)} custom-call(bf16[1,46,64,256]{3,2,1,0:T(8,128)(2,1)} %get-tuple-element.31.x_all, f32[15,15,256]{2,1,0:T(8,128)} %fusion.67.k_ref), custom_call_target="tpu_custom_call" | custom-call | flops 176947200 | bytes 3080192 | tf_op jit(solution)/shard_map/pallas_call | solution.py:107
  227.8 0.6 fusion.47
  228.4 1.1 pad_maximum_fusion.4.x_all
  229.5 12.8 %shard_map.103 = f32[2,32,8,256]{3,2,1,0:T(8,128)} custom-call(bf16[2,46,22,256]{3,2,1,0:T(8,128)(2,1)} %pad_maximum_fusion.4.x_all, f32[15,15,256]{2,1,0:T(8,128)} %fusion.67.k_ref), custom_call_target="tpu_custom_call" | custom-call | flops 58982400 | bytes 1560576 | tf_op jit(solution)/shard_map/pallas_call | solution.py:107
  242.3 1.1 slice_bitcast_fusion.4
  243.4 0.4 fusion.43
  243.8 0.3 copy-done.10
  244.1 0.6 multiply_reduce_fusion.1
  244.8 5.4 %add_convert_fusion.1 = bf16[32,64,256]{2,1,0:T(8,128)(2,1)} fusion(bf16[32,64,256]{2,1,0:T(8,128)(2,1)S(1)} %convolution_convert_fusion, f32[32,64]{1,0:T(8,128)S(1)} %add_rsqrt_fusion.1, f32[32,64]{1,0:T(8,128)S(1)} %broadcast_multiply_fusion.1, f32[32,8,256]{2,1,0:T(8,128)} %copy-done.10, f32[32,48,256]{2,1,0:T(8,128)S(1)} %bitcast.70, ...), kind=kOutput, calls=%fused_computation.34 | convolution fusion | flops 2170552320 | bytes 5259264 | tf_op jit(solution)/shard_map/dot_general | solution.py:162
  250.2 0.8 fusion.94
  251.0 2.0 collective-permute-start.12
  253.0 2.3 collective-permute-start.13
  255.3 3.8 %collective-permute-done.13 = bf16[1,64,256]{2,1,0:T(8,128)(2,1)S(1)} collective-permute-done((bf16[1,64,256]{2,1,0:T(8,128)(2,1)S(1)}, bf16[1,64,256]{2,1,0:T(8,128)(2,1)S(1)}, u32[]{:S(2)}, u32[]{:S(2)}) %collective-permute-start.13) | collective-permute-done | bytes 32800 | tf_op jit(solution)/shard_map/ppermute | solution.py:19
  259.1 1.0 pad_maximum_fusion.20
  260.2 4.3 %collective-permute-start.14 = (bf16[34,1,256]{2,1,0:T(2,128)(2,1)S(1)}, bf16[34,1,256]{2,1,0:T(2,128)(2,1)S(1)}, u32[]{:S(2)}, u32[]{:S(2)}) collective-permute-start(bf16[34,1,256]{2,1,0:T(2,128)(2,1)S(1)} %get-tuple-element.37), channel_id=1, source_target_pairs={{0,1},{1,2},{2,3},{4,5},{5,6},{6,7},{8,9},{9,10},{10,11},{12,13},{... | collective-permute-start | bytes 52232 | tf_op jit(solution)/shard_map/ppermute | solution.py:16
  264.4 1.5 collective-permute-start.15
  266.0 3.4 %collective-permute-done.15 = bf16[34,1,256]{2,1,0:T(2,128)(2,1)S(1)} collective-permute-done((bf16[34,1,256]{2,1,0:T(2,128)(2,1)S(1)}, bf16[34,1,256]{2,1,0:T(2,128)(2,1)S(1)}, u32[]{:S(2)}, u32[]{:S(2)}) %collective-permute-start.15) | collective-permute-done | bytes 17440 | tf_op jit(solution)/shard_map/ppermute | solution.py:19
  269.4 1.8 maximum_convert_fusion.1
  271.1 0.4 fusion.86
  272.0 1.4 fusion.32
  273.9 0.8 copy.20
  (60 shorter events, 1.7 us)
Async XLA Ops:
  0.0 244.7 %copy-start = (bf16[1024,256]{1,0:T(8,128)(2,1)S(1)}, bf16[1024,256]{1,0:T(8,128)(2,1)}, u32[]{:S(2)}) copy-start(bf16[1024,256]{1,0:T(8,128)(2,1)} %param.19) | copy-start | bytes 1572868
  1.1 9.0 %copy-start.16 = (f32[128]{0:T(128)S(1)}, f32[128]{0:T(128)}, u32[]{:S(2)}) copy-start(f32[128]{0:T(128)} %param.12) | copy-start | bytes 1540
  1.2 9.0 %copy-start.13 = (f32[15,15,128]{2,1,0:T(8,128)S(1)}, f32[15,15,128]{2,1,0:T(8,128)}, u32[]{:S(2)}) copy-start(f32[15,15,128]{2,1,0:T(8,128)} %param.11) | copy-start | bytes 345604
  1.2 75.8 %collective-permute-start = (bf16[7,128,128]{2,1,0:T(8,128)(2,1)S(1)}, bf16[7,128,128]{2,1,0:T(8,128)(2,1)S(1)}, u32[]{:S(2)}, u32[]{:S(2)}) collective-permute-start(bf16[7,128,128]{2,1,0:T(8,128)(2,1)S(1)} %get-tuple-element.30), channel_id=1, source_target_pairs={{0,4},{4,8},{8,12},{12,16},{16,20},{20,24},{24,28},{1,5},{5,9},{9,... | collective-permute-start | bytes 688136 | tf_op jit(solution)/shard_map/ppermute | solution.py:128
  5.0 72.3 %collective-permute-start.1 = (bf16[7,128,128]{2,1,0:T(8,128)(2,1)S(1)}, bf16[7,128,128]{2,1,0:T(8,128)(2,1)S(1)}, u32[]{:S(2)}, u32[]{:S(2)}) collective-permute-start(bf16[7,128,128]{2,1,0:T(8,128)(2,1)S(1)} %get-tuple-element.29), channel_id=1, source_target_pairs={{4,0},{8,4},{12,8},{16,12},{20,16},{24,20},{28,24},{5,1},{9,5},{13... | collective-permute-start | bytes 688136 | tf_op jit(solution)/shard_map/ppermute | solution.py:131
  10.9 66.1 %copy-start.2 = (bf16[64,128,128]{2,1,0:T(8,128)(2,1)S(1)}, bf16[64,128,128]{2,1,0:T(8,128)(2,1)}, u32[]{:S(2)}) copy-start(bf16[64,128,128]{2,1,0:T(8,128)(2,1)} %param.10) | copy-start | bytes 6291460
  77.3 5.4 %copy-start.7 = (bf16[78,128,128]{2,1,0:T(8,128)(2,1)}, bf16[78,128,128]{2,1,0:T(8,128)(2,1)S(1)}, u32[]{:S(2)}) copy-start(bf16[78,128,128]{2,1,0:T(8,128)(2,1)S(1)} %constant_dynamic-update-slice_fusion) | copy-start | bytes 7667716
  77.4 33.4 %collective-permute-start.2 = (bf16[78,7,128]{2,1,0:T(8,128)(2,1)S(1)}, bf16[78,7,128]{2,1,0:T(8,128)(2,1)}, u32[]{:S(2)}, u32[]{:S(2)}) collective-permute-start(bf16[78,7,128]{2,1,0:T(8,128)(2,1)S(1)} %get-tuple-element.13), channel_id=1, source_target_pairs={{0,1},{1,2},{2,3},{4,5},{5,6},{6,7},{8,9},{9,10},{10,11},{12,13},{... | collective-permute-start | bytes 419336 | tf_op jit(solution)/shard_map/ppermute | solution.py:128
  81.3 29.5 %collective-permute-start.3 = (bf16[78,7,128]{2,1,0:T(8,128)(2,1)S(1)}, bf16[78,7,128]{2,1,0:T(8,128)(2,1)}, u32[]{:S(2)}, u32[]{:S(2)}) collective-permute-start(bf16[78,7,128]{2,1,0:T(8,128)(2,1)S(1)} %get-tuple-element.14), channel_id=1, source_target_pairs={{1,0},{2,1},{3,2},{5,4},{6,5},{7,6},{9,8},{10,9},{11,10},{13,12},{... | collective-permute-start | bytes 419336 | tf_op jit(solution)/shard_map/ppermute | solution.py:131
  84.0 26.8 %copy-start.8 = (bf16[78,128,128]{2,1,0:T(8,128)(2,1)S(1)}, bf16[78,128,128]{2,1,0:T(8,128)(2,1)}, u32[]{:S(2)}) copy-start(bf16[78,128,128]{2,1,0:T(8,128)(2,1)} %copy-done.7) | copy-start | bytes 7667716
  112.3 14.5 %copy-start.1 = (f32[1,48,112,128]{3,2,1,0:T(8,128)S(1)}, f32[1,48,112,128]{3,2,1,0:T(8,128)}, u32[]{:S(2)}) copy-start(f32[1,48,112,128]{3,2,1,0:T(8,128)} %shard_map.102) | copy-start | bytes 8257540
  126.8 5.2 %copy-start.9 = (f32[64,8,128]{2,1,0:T(8,128)}, f32[64,8,128]{2,1,0:T(8,128)S(1)}, u32[]{:S(2)}) copy-start(f32[64,8,128]{2,1,0:T(8,128)S(1)} %get-tuple-element.50) | copy-start | bytes 786436
  126.8 2.5 copy-start.5
  126.8 2.5 copy-start.6
  129.3 2.7 copy-start.12
  142.3 21.9 %copy-start.4 = (bf16[64,128,128]{2,1,0:T(8,128)(2,1)S(1)}, bf16[64,128,128]{2,1,0:T(8,128)(2,1)}, u32[]{:S(2)}) copy-start(bf16[64,128,128]{2,1,0:T(8,128)(2,1)} %add_convert_fusion) | copy-start | bytes 6291460
  143.3 6.9 %collective-permute-start.4 = (bf16[1,128,128]{2,1,0:T(8,128)(2,1)S(1)}, bf16[1,128,128]{2,1,0:T(8,128)(2,1)S(1)}, u32[]{:S(2)}, u32[]{:S(2)}) collective-permute-start(bf16[1,128,128]{2,1,0:T(8,128)(2,1)S(1)} %get-tuple-element.25), channel_id=1, source_target_pairs={{0,4},{4,8},{8,12},{12,16},{16,20},{20,24},{24,28},{1,5},{5,9},{9,... | collective-permute-start | bytes 98312 | tf_op jit(solution)/shard_map/ppermute | solution.py:16
  148.1 6.1 %collective-permute-start.5 = (bf16[1,128,128]{2,1,0:T(8,128)(2,1)S(1)}, bf16[1,128,128]{2,1,0:T(8,128)(2,1)S(1)}, u32[]{:S(2)}, u32[]{:S(2)}) collective-permute-start(bf16[1,128,128]{2,1,0:T(8,128)(2,1)S(1)} %get-tuple-element.26), channel_id=1, source_target_pairs={{4,0},{8,4},{12,8},{16,12},{20,16},{24,20},{28,24},{5,1},{9,5},{13... | collective-permute-start | bytes 98312 | tf_op jit(solution)/shard_map/ppermute | solution.py:19
  155.3 5.6 %collective-permute-start.6 = (bf16[66,1,128]{2,1,0:T(2,128)(2,1)S(1)}, bf16[66,1,128]{2,1,0:T(2,128)(2,1)S(1)}, u32[]{:S(2)}, u32[]{:S(2)}) collective-permute-start(bf16[66,1,128]{2,1,0:T(2,128)(2,1)S(1)} %get-tuple-element.21), channel_id=1, source_target_pairs={{0,1},{1,2},{2,3},{4,5},{5,6},{6,7},{8,9},{9,10},{10,11},{12,13},{... | collective-permute-start | bytes 50696 | tf_op jit(solution)/shard_map/ppermute | solution.py:16
  159.5 4.7 %collective-permute-start.7 = (bf16[66,1,128]{2,1,0:T(2,128)(2,1)S(1)}, bf16[66,1,128]{2,1,0:T(2,128)(2,1)S(1)}, u32[]{:S(2)}, u32[]{:S(2)}) collective-permute-start(bf16[66,1,128]{2,1,0:T(2,128)(2,1)S(1)} %get-tuple-element.22), channel_id=1, source_target_pairs={{1,0},{2,1},{3,2},{5,4},{6,5},{7,6},{9,8},{10,9},{11,10},{13,12},{... | collective-permute-start | bytes 50696 | tf_op jit(solution)/shard_map/ppermute | solution.py:19
  168.4 0.8 copy-start.14
  169.2 5.8 %copy-start.15 = (f32[256]{0:T(256)S(1)}, f32[256]{0:T(256)}, u32[]{:S(2)}) copy-start(f32[256]{0:T(256)} %param.17) | copy-start | bytes 3076
  169.7 7.6 %collective-permute-start.8 = (bf16[7,64,256]{2,1,0:T(8,128)(2,1)S(1)}, bf16[7,64,256]{2,1,0:T(8,128)(2,1)S(1)}, u32[]{:S(2)}, u32[]{:S(2)}) collective-permute-start(bf16[7,64,256]{2,1,0:T(8,128)(2,1)S(1)} %get-tuple-element.43), channel_id=1, source_target_pairs={{0,4},{4,8},{8,12},{12,16},{16,20},{20,24},{24,28},{1,5},{5,9},{9,... | collective-permute-start | bytes 688136 | tf_op jit(solution)/shard_map/ppermute | solution.py:128
  173.1 8.2 %collective-permute-start.9 = (bf16[7,64,256]{2,1,0:T(8,128)(2,1)S(1)}, bf16[7,64,256]{2,1,0:T(8,128)(2,1)S(1)}, u32[]{:S(2)}, u32[]{:S(2)}) collective-permute-start(bf16[7,64,256]{2,1,0:T(8,128)(2,1)S(1)} %get-tuple-element.44), channel_id=1, source_target_pairs={{4,0},{8,4},{12,8},{16,12},{20,16},{24,20},{28,24},{5,1},{9,5},{13... | collective-permute-start | bytes 688136 | tf_op jit(solution)/shard_map/ppermute | solution.py:131
  175.0 11.8 %copy-start.11 = (f32[15,15,256]{2,1,0:T(8,128)S(1)}, f32[15,15,256]{2,1,0:T(8,128)}, u32[]{:S(2)}) copy-start(f32[15,15,256]{2,1,0:T(8,128)} %param.16) | copy-start | bytes 691204
  182.7 45.0 %collective-permute-start.10 = (bf16[46,7,256]{2,1,0:T(8,128)(2,1)S(1)}, bf16[46,7,256]{2,1,0:T(8,128)(2,1)S(1)}, u32[]{:S(2)}, u32[]{:S(2)}) collective-permute-start(bf16[46,7,256]{2,1,0:T(8,128)(2,1)S(1)} %get-tuple-element.35), channel_id=1, source_target_pairs={{0,1},{1,2},{2,3},{4,5},{5,6},{6,7},{8,9},{9,10},{10,11},{12,13},{... | collective-permute-start | bytes 494600 | tf_op jit(solution)/shard_map/ppermute | solution.py:128
  185.5 42.2 %collective-permute-start.11 = (bf16[46,7,256]{2,1,0:T(8,128)(2,1)S(1)}, bf16[46,7,256]{2,1,0:T(8,128)(2,1)S(1)}, u32[]{:S(2)}, u32[]{:S(2)}) collective-permute-start(bf16[46,7,256]{2,1,0:T(8,128)(2,1)S(1)} %get-tuple-element.36), channel_id=1, source_target_pairs={{1,0},{2,1},{3,2},{5,4},{6,5},{7,6},{9,8},{10,9},{11,10},{13,12},{... | collective-permute-start | bytes 494600 | tf_op jit(solution)/shard_map/ppermute | solution.py:131
  228.3 15.0 %copy-start.3 = (f32[1,32,48,256]{3,2,1,0:T(8,128)S(1)}, f32[1,32,48,256]{3,2,1,0:T(8,128)}, u32[]{:S(2)}) copy-start(f32[1,32,48,256]{3,2,1,0:T(8,128)} %shard_map.104) | copy-start | bytes 4718596
  243.4 0.7 copy-start.10
  251.0 4.3 %collective-permute-start.12 = (bf16[1,64,256]{2,1,0:T(8,128)(2,1)S(1)}, bf16[1,64,256]{2,1,0:T(8,128)(2,1)S(1)}, u32[]{:S(2)}, u32[]{:S(2)}) collective-permute-start(bf16[1,64,256]{2,1,0:T(8,128)(2,1)S(1)} %get-tuple-element.41), channel_id=1, source_target_pairs={{0,4},{4,8},{8,12},{12,16},{16,20},{20,24},{24,28},{1,5},{5,9},{9,... | collective-permute-start | bytes 98312 | tf_op jit(solution)/shard_map/ppermute | solution.py:16
  253.0 6.1 %collective-permute-start.13 = (bf16[1,64,256]{2,1,0:T(8,128)(2,1)S(1)}, bf16[1,64,256]{2,1,0:T(8,128)(2,1)S(1)}, u32[]{:S(2)}, u32[]{:S(2)}) collective-permute-start(bf16[1,64,256]{2,1,0:T(8,128)(2,1)S(1)} %get-tuple-element.42), channel_id=1, source_target_pairs={{4,0},{8,4},{12,8},{16,12},{20,16},{24,20},{28,24},{5,1},{9,5},{13... | collective-permute-start | bytes 98312 | tf_op jit(solution)/shard_map/ppermute | solution.py:19
  260.2 5.8 %collective-permute-start.14 = (bf16[34,1,256]{2,1,0:T(2,128)(2,1)S(1)}, bf16[34,1,256]{2,1,0:T(2,128)(2,1)S(1)}, u32[]{:S(2)}, u32[]{:S(2)}) collective-permute-start(bf16[34,1,256]{2,1,0:T(2,128)(2,1)S(1)} %get-tuple-element.37), channel_id=1, source_target_pairs={{0,1},{1,2},{2,3},{4,5},{5,6},{6,7},{8,9},{9,10},{10,11},{12,13},{... | collective-permute-start | bytes 52232 | tf_op jit(solution)/shard_map/ppermute | solution.py:16
  264.4 5.0 %collective-permute-start.15 = (bf16[34,1,256]{2,1,0:T(2,128)(2,1)S(1)}, bf16[34,1,256]{2,1,0:T(2,128)(2,1)S(1)}, u32[]{:S(2)}, u32[]{:S(2)}) collective-permute-start(bf16[34,1,256]{2,1,0:T(2,128)(2,1)S(1)} %get-tuple-element.38), channel_id=1, source_target_pairs={{1,0},{2,1},{3,2},{5,4},{6,5},{7,6},{9,8},{10,9},{11,10},{13,12},{... | collective-permute-start | bytes 52232 | tf_op jit(solution)/shard_map/ppermute | solution.py:19

commit v15 on v13

--- a/solution.py
+++ b/solution.py
@@ -28,21 +28,25 @@
     return (raw * mask).astype(jnp.bfloat16)
 
 
-def _dw_body(x_all, k_ref, o_all, xf_ref, xs_ref, *, taps, cbase, rows, cols, chans, rb):
+def _dw_body(*refs, parts, taps, cbase, rows, cols, chans, rb):
+    x_parts = refs[:parts]
+    k_ref, o_all, xf_ref, xs_ref = refs[parts:]
     nlb = chans // 128
     njb = cols // 8
     nrb = rows // rb
     spread = max(1, min(8, 16 // (njb * nlb)))
 
     def one_strip(n, carry):
-        x_ref = x_all.at[n]
         o_ref = o_all.at[n]
-
-        def widen_row(r, c):
-            xf_ref[r] = x_ref[r].astype(jnp.float32)
-            return c
-
-        lax.fori_loop(0, rows + taps - 1, widen_row, 0, unroll=spread)
+        start = 0
+        for x_all in x_parts:
+
+            def widen_row(r, c, x_ref=x_all.at[n], start=start):
+                xf_ref[start + r] = x_ref[r].astype(jnp.float32)
+                return c
+
+            lax.fori_loop(0, x_all.shape[1], widen_row, 0, unroll=spread)
+            start += x_all.shape[1]
         first = True
         for s in range(8):
             if (cbase + s) % 8 == 0:
@@ -92,36 +96,44 @@
                 first = False
         return carry
 
-    lax.fori_loop(0, x_all.shape[0], one_strip, 0)
-
-
-def depthwise(strips, kernel, cbase, cols):
+    lax.fori_loop(0, x_parts[0].shape[0], one_strip, 0)
+
+
+def depthwise(parts, kernel, cbase, cols):
     taps = kernel.shape[0]
-    count = strips.shape[0]
-    rows = strips.shape[1] - taps + 1
-    chans = strips.shape[3]
+    count = parts[0].shape[0]
+    in_rows = sum(p.shape[1] for p in parts)
+    rows = in_rows - taps + 1
+    chans = parts[0].shape[3]
     body = functools.partial(
-        _dw_body, taps=taps, cbase=cbase, rows=rows, cols=cols, chans=chans, rb=8
+        _dw_body,
+        parts=len(parts),
+        taps=taps,
+        cbase=cbase,
+        rows=rows,
+        cols=cols,
+        chans=chans,
+        rb=8,
     )
     vmem = pl.BlockSpec(memory_space=pltpu.VMEM)
     return pl.pallas_call(
         body,
         out_shape=jax.ShapeDtypeStruct((count, rows, cols, chans), jnp.float32),
-        in_specs=[vmem, vmem],
+        in_specs=[vmem] * (len(parts) + 1),
         out_specs=vmem,
         scratch_shapes=[
-            pltpu.VMEM(strips.shape[1:], jnp.float32),
-            pltpu.VMEM((rows + taps - 1, cols + 8, chans), jnp.float32),
+            pltpu.VMEM((in_rows,) + parts[0].shape[2:], jnp.float32),
+            pltpu.VMEM((in_rows, cols + 8, chans), jnp.float32),
         ],
         cost_estimate=pl.CostEstimate(
             flops=2 * count * rows * cols * chans * taps * taps,
             transcendentals=0,
-            bytes_accessed=strips.size * 2 + count * rows * cols * chans * 4,
+            bytes_accessed=sum(p.size for p in parts) * 2 + count * rows * cols * chans * 4,
         ),
-    )(strips, kernel.astype(jnp.float32))
-
-
-def exchange(block, axis, dim, width):
+    )(*parts, kernel.astype(jnp.float32))
+
+
+def halos(block, axis, dim, width):
     count = lax.axis_size(axis)
     forward = [(i, i + 1) for i in range(count - 1)]
     backward = [(target, source) for source, target in forward]
@@ -129,18 +141,33 @@
         lax.slice_in_dim(block, block.shape[dim] - width, None, axis=dim), axis, forward
     )
     high = lax.ppermute(lax.slice_in_dim(block, 0, width, axis=dim), axis, backward)
-    return jnp.concatenate([low, block, high], axis=dim)
+    return low, high
 
 
 def section_conv(block, kernel):
     reach = (kernel.shape[0] - 1) // 2
     cols = block.shape[1]
     band = 8
-    tall = exchange(block, "row", 0, reach)
-    middle = depthwise(tall[None], kernel, band - reach, cols - 2 * band)
-    full = exchange(tall, "col", 1, reach)
-    ends = jnp.stack([full[:, : band + 2 * reach], full[:, cols - band :]], axis=0)
-    edge = depthwise(ends, kernel, 0, band)
+    up, down = halos(block, "row", 0, reach)
+    pieces = [up, block, down]
+    middle = depthwise([p[None] for p in pieces], kernel, band - reach, cols - 2 * band)
+
+    def tall_cols(start, stop):
+        return jnp.concatenate([p[:, start:stop] for p in pieces], axis=0)
+
+    count = lax.axis_size("col")
+    forward = [(i, i + 1) for i in range(count - 1)]
+    backward = [(target, source) for source, target in forward]
+    left = lax.ppermute(tall_cols(cols - reach, cols), "col", forward)
+    right = lax.ppermute(tall_cols(0, reach), "col", backward)
+    ends = jnp.stack(
+        [
+            jnp.concatenate([left, tall_cols(0, band + reach)], axis=1),
+            jnp.concatenate([tall_cols(cols - band - reach, cols), right], axis=1),
+        ],
+        axis=0,
+    )
+    edge = depthwise([ends], kernel, 0, band)
     return jnp.concatenate([edge[0], middle[0], edge[1]], axis=1)
 
 

time: 266 us -> 261 us (0.981)
  other arithmetic: 22.5 us -> 19.1 us
  transfers between devices with their start and end apart: 16 -> 16, of which waited for: 8 -> 7; matrix products, arithmetic and copies ran while one was open for 2% -> 2% of each run, Pallas kernels for 48% -> 49%
where the time goes in v15:
time: 261 us; the launch traced here: 260 us
  Pallas kernels  152 us (58%)
  starting transfers between devices  40.2 us (15%)
  waiting for transfers between devices  22.7 us (9%)
  other arithmetic  19.1 us (7%)
  matrix products  14.5 us (6%)
  local copies, waits for them, and re-layouts  10.7 us (4%)
    pallas_call x4, Pallas kernels, depthwise(): pl.pallas_call(body, out_shape=jax.ShapeDtypeStruct((count, rows, cols, c...  152 us
    dot_general x2, matrix products, local_section(): mixed = jnp.dot(hidden, w_out, preferred_element_type=jnp.float32)  14.1 us
    ppermute x4, waiting for transfers between devices, padded_2(): lax.ppermute(lax.slice_in_dim(block, 0, width, axis=dim), axis, backward)  13.1 us
    ppermute x4, starting transfers between devices, padded_2(): lax.ppermute(lax.slice_in_dim(block, block.shape[dim] - width, None, axis...  12.7 us
    ppermute x4, starting transfers between devices, padded_2(): lax.ppermute(lax.slice_in_dim(block, 0, width, axis=dim), axis, backward)  7.59 us
    ppermute x2, waiting for transfers between devices, halos(): lax.ppermute(lax.slice_in_dim(block, 0, width, axis=dim), axis, backward)  7.48 us
    ppermute x2, starting transfers between devices, halos(): lax.ppermute(lax.slice_in_dim(block, block.shape[dim] - width, None, axis...  7.02 us
    ppermute x2, starting transfers between devices, section_conv(): left = lax.ppermute(tall_cols(cols - reach, cols), 'col', forward)  6.43 us
  transfers between devices with their start and end apart: 16, of which 7 were waited for; matrix products, arithmetic and copies ran while one was open for 2% of the time, Pallas kernels for 49%

profile of v15, /device:TPU:3, one launch (start us, length us, event | category | flops | bytes accessed | tf_op | source)
XLA Modules:
  0.0 260.1 jit_solution(9944364232729833747)
XLA Ops:
  0.0 1.1 fusion.87
  1.2 3.7 %collective-permute-start = (bf16[7,128,128]{2,1,0:T(8,128)(2,1)S(1)}, bf16[7,128,128]{2,1,0:T(8,128)(2,1)S(1)}, u32[]{:S(2)}, u32[]{:S(2)}) collective-permute-start(bf16[7,128,128]{2,1,0:T(8,128)(2,1)S(1)} %get-tuple-element.27), channel_id=1, source_target_pairs={{0,4},{4,8},{8,12},{12,16},{16,20},{20,24},{24,28},{1,5},{5,9},{9,... | collective-permute-start | bytes 688136 | tf_op jit(solution)/shard_map/ppermute | solution.py:140
  4.8 1.9 collective-permute-start.1
  6.8 1.0 fusion.85
  7.8 1.2 fusion.86
  9.0 0.8 fusion.64.refs_1_.refs_3_
  9.8 3.3 %collective-permute-done.1 = bf16[7,128,128]{2,1,0:T(8,128)(2,1)S(1)} collective-permute-done((bf16[7,128,128]{2,1,0:T(8,128)(2,1)S(1)}, bf16[7,128,128]{2,1,0:T(8,128)(2,1)S(1)}, u32[]{:S(2)}, u32[]{:S(2)}) %collective-permute-start.1) | collective-permute-done | bytes 229408 | tf_op jit(solution)/shard_map/ppermute | solution.py:143
  13.2 3.2 %collective-permute-start.2 = (bf16[78,7,128]{2,1,0:T(8,128)(2,1)S(1)}, bf16[78,7,128]{2,1,0:T(8,128)(2,1)S(1)}, u32[]{:S(2)}, u32[]{:S(2)}) collective-permute-start(bf16[78,7,128]{2,1,0:T(8,128)(2,1)S(1)} %pad_maximum_fusion.10), channel_id=1, source_target_pairs={{0,1},{1,2},{2,3},{4,5},{5,6},{6,7},{8,9},{9,10},{10,11},{12,13},{... | collective-permute-start | bytes 419336 | tf_op jit(solution)/shard_map/ppermute | solution.py:161
  16.4 1.3 collective-permute-start.3
  17.8 87.0 %shard_map.101 = f32[1,64,112,128]{3,2,1,0:T(8,128)} custom-call(bf16[1,7,128,128]{3,2,1,0:T(8,128)(2,1)} %bitcast.75, bf16[1,64,128,128]{3,2,1,0:T(8,128)(2,1)} %bitcast.70, bf16[1,7,128,128]{3,2,1,0:T(8,128)(2,1)} %bitcast.76, f32[15,15,128]{2,1,0:T(8,128)} %fusion.64.refs_1_.refs_3_), custom_call_target="tpu_custom_call" | custom-call | flops 412876800 | bytes 6225920 | tf_op jit(solution)/shard_map/pallas_call | solution.py:119
  104.7 0.2 maximum_bitcast_fusion.2
  104.9 0.2 maximum_bitcast_fusion.3
  105.1 1.1 pad_maximum_fusion.5.refs_0_
  106.2 12.3 %shard_map.100 = f32[2,64,8,128]{3,2,1,0:T(8,128)} custom-call(bf16[2,78,22,128]{3,2,1,0:T(8,128)(2,1)} %pad_maximum_fusion.5.refs_0_, f32[15,15,128]{2,1,0:T(8,128)} %fusion.64.refs_1_.refs_3_), custom_call_target="tpu_custom_call" | custom-call | flops 58982400 | bytes 1402880 | tf_op jit(solution)/shard_map/pallas_call | solution.py:119
  118.5 1.1 slice_bitcast_fusion.3
  119.6 3.3 %fusion.29 = f32[64,128]{1,0:T(8,128)S(1)} fusion(f32[64,8,128]{2,1,0:T(8,128)S(1)} %get-tuple-element.44, f32[64,112,128]{2,1,0:T(8,128)} %bitcast.57, f32[64,8,128]{2,1,0:T(8,128)S(1)} %get-tuple-element.43), kind=kLoop, calls=%fused_computation.39 | loop fusion | flops 3137536 | bytes 4227072 | tf_op jit(solution)/shard_map/reduce_sum | solution.py:177
  122.9 2.6 %multiply_reduce_fusion = f32[64,128]{1,0:T(8,128)S(1)} fusion(f32[64,128]{1,0:T(8,128)S(1)} %broadcast_multiply_fusion, f32[64,8,128]{2,1,0:T(8,128)S(1)} %get-tuple-element.44, f32[64,112,128]{2,1,0:T(8,128)S(1)} %bitcast.59, f32[64,8,128]{2,1,0:T(8,128)S(1)} %get-tuple-element.43), kind=kLoop, calls=%fused_computation.21 | loop fusion | flops 5234688 | bytes 4259840 | tf_op jit(solution)/shard_map/reduce_sum | solution.py:178
  125.6 8.6 %add_convert_fusion = bf16[64,128,128]{2,1,0:T(8,128)(2,1)S(1)} fusion(bf16[64,128,128]{2,1,0:T(8,128)(2,1)} %param.10, f32[64,128]{1,0:T(8,128)S(1)} %add_rsqrt_fusion, f32[64,128]{1,0:T(8,128)S(1)} %broadcast_multiply_fusion, f32[64,8,128]{2,1,0:T(8,128)S(1)} %get-tuple-element.44, f32[64,112,128]{2,1,0:T(8,128)} %bitcast.58, ...), kind=kOutput, calls=%fused_computation.19 | convolution fusion | flops 2193620992 | bytes 8716288 | tf_op jit(solution)/shard_map/dot_general | solution.py:183
  134.3 2.2 collective-permute-start.4
  136.5 2.3 collective-permute-start.5
  138.8 3.8 %collective-permute-done.5 = bf16[1,128,128]{2,1,0:T(8,128)(2,1)S(1)} collective-permute-done((bf16[1,128,128]{2,1,0:T(8,128)(2,1)S(1)}, bf16[1,128,128]{2,1,0:T(8,128)(2,1)S(1)}, u32[]{:S(2)}, u32[]{:S(2)}) %collective-permute-start.5) | collective-permute-done | bytes 32800 | tf_op jit(solution)/shard_map/ppermute | solution.py:19
  142.7 4.3 %collective-permute-start.6 = (bf16[66,1,128]{2,1,0:T(2,128)(2,1)S(1)}, bf16[66,1,128]{2,1,0:T(2,128)(2,1)S(1)}, u32[]{:S(2)}, u32[]{:S(2)}) collective-permute-start(bf16[66,1,128]{2,1,0:T(2,128)(2,1)S(1)} %get-tuple-element.17), channel_id=1, source_target_pairs={{0,1},{1,2},{2,3},{4,5},{5,6},{6,7},{8,9},{9,10},{10,11},{12,13},{... | collective-permute-start | bytes 50696 | tf_op jit(solution)/shard_map/ppermute | solution.py:16
  146.9 1.5 collective-permute-start.7
  148.4 0.8 fusion.62.refs_1_.refs_3_
  149.2 2.4 collective-permute-done.7
  151.6 0.8 maximum_convert_fusion
  152.5 0.6 fusion.77
  153.0 0.6 fusion.78
  153.6 1.6 fusion.22
  155.2 0.6 fusion.83
  155.8 0.5 fusion.53
  156.3 0.3 copy-done.12
  156.6 0.4 convolution_convert_fusion
  157.2 3.3 %collective-permute-start.8 = (bf16[7,64,256]{2,1,0:T(8,128)(2,1)S(1)}, bf16[7,64,256]{2,1,0:T(8,128)(2,1)S(1)}, u32[]{:S(2)}, u32[]{:S(2)}) collective-permute-start(bf16[7,64,256]{2,1,0:T(8,128)(2,1)S(1)} %get-tuple-element.39), channel_id=1, source_target_pairs={{0,4},{4,8},{8,12},{12,16},{16,20},{20,24},{24,28},{1,5},{5,9},{9,... | collective-permute-start | bytes 688136 | tf_op jit(solution)/shard_map/ppermute | solution.py:140
  160.6 1.9 collective-permute-start.9
  162.5 2.0 collective-permute-done.8
  164.6 4.2 %collective-permute-done.9 = bf16[7,64,256]{2,1,0:T(8,128)(2,1)S(1)} collective-permute-done((bf16[7,64,256]{2,1,0:T(8,128)(2,1)S(1)}, bf16[7,64,256]{2,1,0:T(8,128)(2,1)S(1)}, u32[]{:S(2)}, u32[]{:S(2)}) %collective-permute-start.9) | collective-permute-done | bytes 229408 | tf_op jit(solution)/shard_map/ppermute | solution.py:143
  168.9 3.2 %collective-permute-start.10 = (bf16[46,7,256]{2,1,0:T(8,128)(2,1)S(1)}, bf16[46,7,256]{2,1,0:T(8,128)(2,1)S(1)}, u32[]{:S(2)}, u32[]{:S(2)}) collective-permute-start(bf16[46,7,256]{2,1,0:T(8,128)(2,1)S(1)} %pad_maximum_fusion.8), channel_id=1, source_target_pairs={{0,1},{1,2},{2,3},{4,5},{5,6},{6,7},{8,9},{9,10},{10,11},{12,13},{... | collective-permute-start | bytes 494600 | tf_op jit(solution)/shard_map/ppermute | solution.py:161
  172.1 1.3 collective-permute-start.11
  173.5 40.1 %shard_map.103 = f32[1,32,48,256]{3,2,1,0:T(8,128)} custom-call(bf16[1,7,64,256]{3,2,1,0:T(8,128)(2,1)} %bitcast.73, bf16[1,32,64,256]{3,2,1,0:T(8,128)(2,1)} %bitcast.65, bf16[1,7,64,256]{3,2,1,0:T(8,128)(2,1)} %bitcast.74, f32[15,15,256]{2,1,0:T(8,128)} %fusion.62.refs_1_.refs_3_), custom_call_target="tpu_custom_call" | custom-call | flops 176947200 | bytes 3080192 | tf_op jit(solution)/shard_map/pallas_call | solution.py:119
  213.7 0.2 maximum_bitcast_fusion
  214.1 1.1 pad_maximum_fusion.4.refs_0_
  215.2 12.8 %shard_map.102 = f32[2,32,8,256]{3,2,1,0:T(8,128)} custom-call(bf16[2,46,22,256]{3,2,1,0:T(8,128)(2,1)} %pad_maximum_fusion.4.refs_0_, f32[15,15,256]{2,1,0:T(8,128)} %fusion.62.refs_1_.refs_3_), custom_call_target="tpu_custom_call" | custom-call | flops 58982400 | bytes 1560576 | tf_op jit(solution)/shard_map/pallas_call | solution.py:119
  228.0 1.1 slice_bitcast_fusion.1
  229.1 0.4 fusion.44
  229.5 0.3 copy-done.5
  229.8 0.6 multiply_reduce_fusion.1
  230.5 5.4 %add_convert_fusion.1 = bf16[32,64,256]{2,1,0:T(8,128)(2,1)} fusion(bf16[32,64,256]{2,1,0:T(8,128)(2,1)S(1)} %copy-done.4, f32[32,64]{1,0:T(8,128)S(1)} %add_rsqrt_fusion.1, f32[32,64]{1,0:T(8,128)S(1)} %broadcast_multiply_fusion.1, f32[32,8,256]{2,1,0:T(8,128)} %copy-done.5, f32[32,48,256]{2,1,0:T(8,128)S(1)} %bitcast.64, ...), kind=kOutput, calls=%fused_computation.34 | convolution fusion | flops 2170552320 | bytes 5259264 | tf_op jit(solution)/shard_map/dot_general | solution.py:183
  235.9 0.8 fusion.89
  236.7 2.0 collective-permute-start.12
  238.7 2.3 collective-permute-start.13
  241.0 3.8 %collective-permute-done.13 = bf16[1,64,256]{2,1,0:T(8,128)(2,1)S(1)} collective-permute-done((bf16[1,64,256]{2,1,0:T(8,128)(2,1)S(1)}, bf16[1,64,256]{2,1,0:T(8,128)(2,1)S(1)}, u32[]{:S(2)}, u32[]{:S(2)}) %collective-permute-start.13) | collective-permute-done | bytes 32800 | tf_op jit(solution)/shard_map/ppermute | solution.py:19
  244.8 1.0 pad_maximum_fusion.14
  245.9 4.3 %collective-permute-start.14 = (bf16[34,1,256]{2,1,0:T(2,128)(2,1)S(1)}, bf16[34,1,256]{2,1,0:T(2,128)(2,1)S(1)}, u32[]{:S(2)}, u32[]{:S(2)}) collective-permute-start(bf16[34,1,256]{2,1,0:T(2,128)(2,1)S(1)} %get-tuple-element.29), channel_id=1, source_target_pairs={{0,1},{1,2},{2,3},{4,5},{5,6},{6,7},{8,9},{9,10},{10,11},{12,13},{... | collective-permute-start | bytes 52232 | tf_op jit(solution)/shard_map/ppermute | solution.py:16
  250.1 1.5 collective-permute-start.15
  251.7 3.1 %collective-permute-done.15 = bf16[34,1,256]{2,1,0:T(2,128)(2,1)S(1)} collective-permute-done((bf16[34,1,256]{2,1,0:T(2,128)(2,1)S(1)}, bf16[34,1,256]{2,1,0:T(2,128)(2,1)S(1)}, u32[]{:S(2)}, u32[]{:S(2)}) %collective-permute-start.15) | collective-permute-done | bytes 17440 | tf_op jit(solution)/shard_map/ppermute | solution.py:19
  254.8 1.8 maximum_convert_fusion.1
  256.6 0.4 fusion.80
  257.0 0.2 fusion.81
  257.2 0.2 fusion.82
  257.4 1.4 fusion.33
  258.8 0.3 fusion.88
  259.1 0.2 fusion.54
  259.3 0.8 copy.20
  (67 shorter events, 0.8 us)
Async XLA Ops:
  0.0 230.4 %copy-start = (bf16[1024,256]{1,0:T(8,128)(2,1)S(1)}, bf16[1024,256]{1,0:T(8,128)(2,1)}, u32[]{:S(2)}) copy-start(bf16[1024,256]{1,0:T(8,128)(2,1)} %param.19) | copy-start | bytes 1572868
  0.0 9.0 %copy-start.16 = (f32[128]{0:T(128)S(1)}, f32[128]{0:T(128)}, u32[]{:S(2)}) copy-start(f32[128]{0:T(128)} %param.12) | copy-start | bytes 1540
  0.0 9.0 %copy-start.11 = (f32[15,15,128]{2,1,0:T(8,128)S(1)}, f32[15,15,128]{2,1,0:T(8,128)}, u32[]{:S(2)}) copy-start(f32[15,15,128]{2,1,0:T(8,128)} %param.11) | copy-start | bytes 345604
  1.2 8.6 %collective-permute-start = (bf16[7,128,128]{2,1,0:T(8,128)(2,1)S(1)}, bf16[7,128,128]{2,1,0:T(8,128)(2,1)S(1)}, u32[]{:S(2)}, u32[]{:S(2)}) collective-permute-start(bf16[7,128,128]{2,1,0:T(8,128)(2,1)S(1)} %get-tuple-element.27), channel_id=1, source_target_pairs={{0,4},{4,8},{8,12},{12,16},{16,20},{20,24},{24,28},{1,5},{5,9},{9,... | collective-permute-start | bytes 688136 | tf_op jit(solution)/shard_map/ppermute | solution.py:140
  4.8 8.2 %collective-permute-start.1 = (bf16[7,128,128]{2,1,0:T(8,128)(2,1)S(1)}, bf16[7,128,128]{2,1,0:T(8,128)(2,1)S(1)}, u32[]{:S(2)}, u32[]{:S(2)}) collective-permute-start(bf16[7,128,128]{2,1,0:T(8,128)(2,1)S(1)} %get-tuple-element.28), channel_id=1, source_target_pairs={{4,0},{8,4},{12,8},{16,12},{20,16},{24,20},{28,24},{5,1},{9,5},{13... | collective-permute-start | bytes 688136 | tf_op jit(solution)/shard_map/ppermute | solution.py:143
  9.8 8.0 %copy-start.8 = (bf16[7,128,128]{2,1,0:T(8,128)(2,1)}, bf16[7,128,128]{2,1,0:T(8,128)(2,1)S(1)}, u32[]{:S(2)}) copy-start(bf16[7,128,128]{2,1,0:T(8,128)(2,1)S(1)} %collective-permute-done) | copy-start | bytes 688132
  13.1 4.7 %copy-start.9 = (bf16[7,128,128]{2,1,0:T(8,128)(2,1)}, bf16[7,128,128]{2,1,0:T(8,128)(2,1)S(1)}, u32[]{:S(2)}) copy-start(bf16[7,128,128]{2,1,0:T(8,128)(2,1)S(1)} %collective-permute-done.1) | copy-start | bytes 688132
  13.2 91.6 %collective-permute-start.2 = (bf16[78,7,128]{2,1,0:T(8,128)(2,1)S(1)}, bf16[78,7,128]{2,1,0:T(8,128)(2,1)S(1)}, u32[]{:S(2)}, u32[]{:S(2)}) collective-permute-start(bf16[78,7,128]{2,1,0:T(8,128)(2,1)S(1)} %pad_maximum_fusion.10), channel_id=1, source_target_pairs={{0,1},{1,2},{2,3},{4,5},{5,6},{6,7},{8,9},{9,10},{10,11},{12,13},{... | collective-permute-start | bytes 419336 | tf_op jit(solution)/shard_map/ppermute | solution.py:161
  16.4 88.5 %collective-permute-start.3 = (bf16[78,7,128]{2,1,0:T(8,128)(2,1)S(1)}, bf16[78,7,128]{2,1,0:T(8,128)(2,1)S(1)}, u32[]{:S(2)}, u32[]{:S(2)}) collective-permute-start(bf16[78,7,128]{2,1,0:T(8,128)(2,1)S(1)} %pad_maximum_fusion.11), channel_id=1, source_target_pairs={{1,0},{2,1},{3,2},{5,4},{6,5},{7,6},{9,8},{10,9},{11,10},{13,12},{... | collective-permute-start | bytes 419336 | tf_op jit(solution)/shard_map/ppermute | solution.py:162
  119.5 3.4 %copy-start.1 = (f32[1,64,112,128]{3,2,1,0:T(8,128)S(1)}, f32[1,64,112,128]{3,2,1,0:T(8,128)}, u32[]{:S(2)}) copy-start(f32[1,64,112,128]{3,2,1,0:T(8,128)} %shard_map.101) | copy-start | bytes 11010052
  122.9 2.7 %copy-start.14 = (bf16[512,128]{1,0:T(8,128)(2,1)S(1)}, bf16[512,128]{1,0:T(8,128)(2,1)}, u32[]{:S(2)}) copy-start(bf16[512,128]{1,0:T(8,128)(2,1)} %param.14) | copy-start | bytes 393220
  122.9 2.7 %copy-start.15 = (bf16[128,512]{1,0:T(8,128)(2,1)S(1)}, bf16[128,512]{1,0:T(8,128)(2,1)}, u32[]{:S(2)}) copy-start(bf16[128,512]{1,0:T(8,128)(2,1)} %param.13) | copy-start | bytes 393220
  125.6 13.2 %copy-start.13 = (f32[256]{0:T(256)S(1)}, f32[256]{0:T(256)}, u32[]{:S(2)}) copy-start(f32[256]{0:T(256)} %param.17) | copy-start | bytes 3076
  134.3 14.2 %copy-start.10 = (f32[15,15,256]{2,1,0:T(8,128)S(1)}, f32[15,15,256]{2,1,0:T(8,128)}, u32[]{:S(2)}) copy-start(f32[15,15,256]{2,1,0:T(8,128)} %param.16) | copy-start | bytes 691204
  134.3 4.5 %collective-permute-start.4 = (bf16[1,128,128]{2,1,0:T(8,128)(2,1)S(1)}, bf16[1,128,128]{2,1,0:T(8,128)(2,1)S(1)}, u32[]{:S(2)}, u32[]{:S(2)}) collective-permute-start(bf16[1,128,128]{2,1,0:T(8,128)(2,1)S(1)} %get-tuple-element.21), channel_id=1, source_target_pairs={{0,4},{4,8},{8,12},{12,16},{16,20},{20,24},{24,28},{1,5},{5,9},{9,... | collective-permute-start | bytes 98312 | tf_op jit(solution)/shard_map/ppermute | solution.py:16
  136.5 6.1 %collective-permute-start.5 = (bf16[1,128,128]{2,1,0:T(8,128)(2,1)S(1)}, bf16[1,128,128]{2,1,0:T(8,128)(2,1)S(1)}, u32[]{:S(2)}, u32[]{:S(2)}) collective-permute-start(bf16[1,128,128]{2,1,0:T(8,128)(2,1)S(1)} %get-tuple-element.22), channel_id=1, source_target_pairs={{4,0},{8,4},{12,8},{16,12},{20,16},{24,20},{28,24},{5,1},{9,5},{13... | collective-permute-start | bytes 98312 | tf_op jit(solution)/shard_map/ppermute | solution.py:19
  142.7 6.6 %collective-permute-start.6 = (bf16[66,1,128]{2,1,0:T(2,128)(2,1)S(1)}, bf16[66,1,128]{2,1,0:T(2,128)(2,1)S(1)}, u32[]{:S(2)}, u32[]{:S(2)}) collective-permute-start(bf16[66,1,128]{2,1,0:T(2,128)(2,1)S(1)} %get-tuple-element.17), channel_id=1, source_target_pairs={{0,1},{1,2},{2,3},{4,5},{5,6},{6,7},{8,9},{9,10},{10,11},{12,13},{... | collective-permute-start | bytes 50696 | tf_op jit(solution)/shard_map/ppermute | solution.py:16
  146.9 4.7 %collective-permute-start.7 = (bf16[66,1,128]{2,1,0:T(2,128)(2,1)S(1)}, bf16[66,1,128]{2,1,0:T(2,128)(2,1)S(1)}, u32[]{:S(2)}, u32[]{:S(2)}) collective-permute-start(bf16[66,1,128]{2,1,0:T(2,128)(2,1)S(1)} %get-tuple-element.18), channel_id=1, source_target_pairs={{1,0},{2,1},{3,2},{5,4},{6,5},{7,6},{9,8},{10,9},{11,10},{13,12},{... | collective-permute-start | bytes 50696 | tf_op jit(solution)/shard_map/ppermute | solution.py:19
  155.8 0.8 copy-start.12
  157.1 16.4 %copy-start.3 = (bf16[32,64,256]{2,1,0:T(8,128)(2,1)}, bf16[32,64,256]{2,1,0:T(8,128)(2,1)S(1)}, u32[]{:S(2)}) copy-start(bf16[32,64,256]{2,1,0:T(8,128)(2,1)S(1)} %convolution_convert_fusion) | copy-start | bytes 3145732
  157.2 7.4 %collective-permute-start.8 = (bf16[7,64,256]{2,1,0:T(8,128)(2,1)S(1)}, bf16[7,64,256]{2,1,0:T(8,128)(2,1)S(1)}, u32[]{:S(2)}, u32[]{:S(2)}) collective-permute-start(bf16[7,64,256]{2,1,0:T(8,128)(2,1)S(1)} %get-tuple-element.39), channel_id=1, source_target_pairs={{0,4},{4,8},{8,12},{12,16},{16,20},{20,24},{24,28},{1,5},{5,9},{9,... | collective-permute-start | bytes 688136 | tf_op jit(solution)/shard_map/ppermute | solution.py:140
  160.6 8.2 %collective-permute-start.9 = (bf16[7,64,256]{2,1,0:T(8,128)(2,1)S(1)}, bf16[7,64,256]{2,1,0:T(8,128)(2,1)S(1)}, u32[]{:S(2)}, u32[]{:S(2)}) collective-permute-start(bf16[7,64,256]{2,1,0:T(8,128)(2,1)S(1)} %get-tuple-element.40), channel_id=1, source_target_pairs={{4,0},{8,4},{12,8},{16,12},{20,16},{24,20},{28,24},{5,1},{9,5},{13... | collective-permute-start | bytes 688136 | tf_op jit(solution)/shard_map/ppermute | solution.py:143
  164.6 8.9 %copy-start.6 = (bf16[7,64,256]{2,1,0:T(8,128)(2,1)}, bf16[7,64,256]{2,1,0:T(8,128)(2,1)S(1)}, u32[]{:S(2)}) copy-start(bf16[7,64,256]{2,1,0:T(8,128)(2,1)S(1)} %collective-permute-done.8) | copy-start | bytes 688132
  168.8 4.7 %copy-start.7 = (bf16[7,64,256]{2,1,0:T(8,128)(2,1)}, bf16[7,64,256]{2,1,0:T(8,128)(2,1)S(1)}, u32[]{:S(2)}) copy-start(bf16[7,64,256]{2,1,0:T(8,128)(2,1)S(1)} %collective-permute-done.9) | copy-start | bytes 688132
  168.9 44.8 %collective-permute-start.10 = (bf16[46,7,256]{2,1,0:T(8,128)(2,1)S(1)}, bf16[46,7,256]{2,1,0:T(8,128)(2,1)S(1)}, u32[]{:S(2)}, u32[]{:S(2)}) collective-permute-start(bf16[46,7,256]{2,1,0:T(8,128)(2,1)S(1)} %pad_maximum_fusion.8), channel_id=1, source_target_pairs={{0,1},{1,2},{2,3},{4,5},{5,6},{6,7},{8,9},{9,10},{10,11},{12,13},{... | collective-permute-start | bytes 494600 | tf_op jit(solution)/shard_map/ppermute | solution.py:161
  172.1 41.8 %collective-permute-start.11 = (bf16[46,7,256]{2,1,0:T(8,128)(2,1)S(1)}, bf16[46,7,256]{2,1,0:T(8,128)(2,1)S(1)}, u32[]{:S(2)}, u32[]{:S(2)}) collective-permute-start(bf16[46,7,256]{2,1,0:T(8,128)(2,1)S(1)} %pad_maximum_fusion.9), channel_id=1, source_target_pairs={{1,0},{2,1},{3,2},{5,4},{6,5},{7,6},{9,8},{10,9},{11,10},{13,12},{... | collective-permute-start | bytes 494600 | tf_op jit(solution)/shard_map/ppermute | solution.py:162
  214.1 15.0 %copy-start.2 = (f32[1,32,48,256]{3,2,1,0:T(8,128)S(1)}, f32[1,32,48,256]{3,2,1,0:T(8,128)}, u32[]{:S(2)}) copy-start(f32[1,32,48,256]{3,2,1,0:T(8,128)} %shard_map.103) | copy-start | bytes 4718596
  229.1 0.7 copy-start.5
  229.1 1.4 copy-start.4
  236.7 4.3 %collective-permute-start.12 = (bf16[1,64,256]{2,1,0:T(8,128)(2,1)S(1)}, bf16[1,64,256]{2,1,0:T(8,128)(2,1)S(1)}, u32[]{:S(2)}, u32[]{:S(2)}) collective-permute-start(bf16[1,64,256]{2,1,0:T(8,128)(2,1)S(1)} %get-tuple-element.33), channel_id=1, source_target_pairs={{0,4},{4,8},{8,12},{12,16},{16,20},{20,24},{24,28},{1,5},{5,9},{9,... | collective-permute-start | bytes 98312 | tf_op jit(solution)/shard_map/ppermute | solution.py:16
  238.7 6.1 %collective-permute-start.13 = (bf16[1,64,256]{2,1,0:T(8,128)(2,1)S(1)}, bf16[1,64,256]{2,1,0:T(8,128)(2,1)S(1)}, u32[]{:S(2)}, u32[]{:S(2)}) collective-permute-start(bf16[1,64,256]{2,1,0:T(8,128)(2,1)S(1)} %get-tuple-element.34), channel_id=1, source_target_pairs={{4,0},{8,4},{12,8},{16,12},{20,16},{24,20},{28,24},{5,1},{9,5},{13... | collective-permute-start | bytes 98312 | tf_op jit(solution)/shard_map/ppermute | solution.py:19
  245.9 5.8 %collective-permute-start.14 = (bf16[34,1,256]{2,1,0:T(2,128)(2,1)S(1)}, bf16[34,1,256]{2,1,0:T(2,128)(2,1)S(1)}, u32[]{:S(2)}, u32[]{:S(2)}) collective-permute-start(bf16[34,1,256]{2,1,0:T(2,128)(2,1)S(1)} %get-tuple-element.29), channel_id=1, source_target_pairs={{0,1},{1,2},{2,3},{4,5},{5,6},{6,7},{8,9},{9,10},{10,11},{12,13},{... | collective-permute-start | bytes 52232 | tf_op jit(solution)/shard_map/ppermute | solution.py:16
  250.1 4.7 %collective-permute-start.15 = (bf16[34,1,256]{2,1,0:T(2,128)(2,1)S(1)}, bf16[34,1,256]{2,1,0:T(2,128)(2,1)S(1)}, u32[]{:S(2)}, u32[]{:S(2)}) collective-permute-start(bf16[34,1,256]{2,1,0:T(2,128)(2,1)S(1)} %get-tuple-element.30), channel_id=1, source_target_pairs={{1,0},{2,1},{3,2},{5,4},{6,5},{7,6},{9,8},{10,9},{11,10},{13,12},{... | collective-permute-start | bytes 52232 | tf_op jit(solution)/shard_map/ppermute | solution.py:19

commit v16 on v15

--- a/solution.py
+++ b/solution.py
@@ -34,7 +34,7 @@
     nlb = chans // 128
     njb = cols // 8
     nrb = rows // rb
-    spread = max(1, min(8, 16 // (njb * nlb)))
+    spread = max(1, min(8, 32 // (njb * nlb)))
 
     def one_strip(n, carry):
         o_ref = o_all.at[n]

time: 261 us -> 259 us (level)
  no operation moved by 1% of the time
where the time goes in v16:
time: 259 us; the launch traced here: 258 us
  Pallas kernels  150 us (58%)
  starting transfers between devices  40.2 us (16%)
  waiting for transfers between devices  22.7 us (9%)
  other arithmetic  19.1 us (7%)
  matrix products  14.5 us (6%)
  local copies, waits for them, and re-layouts  10.7 us (4%)
    pallas_call x4, Pallas kernels, depthwise(): pl.pallas_call(body, out_shape=jax.ShapeDtypeStruct((count, rows, cols, c...  150 us
    dot_general x2, matrix products, local_section(): mixed = jnp.dot(hidden, w_out, preferred_element_type=jnp.float32)  14.1 us
    ppermute x4, waiting for transfers between devices, padded_2(): lax.ppermute(lax.slice_in_dim(block, 0, width, axis=dim), axis, backward)  13.1 us
    ppermute x4, starting transfers between devices, padded_2(): lax.ppermute(lax.slice_in_dim(block, block.shape[dim] - width, None, axis...  12.7 us
    ppermute x4, starting transfers between devices, padded_2(): lax.ppermute(lax.slice_in_dim(block, 0, width, axis=dim), axis, backward)  7.58 us
    ppermute x2, waiting for transfers between devices, halos(): lax.ppermute(lax.slice_in_dim(block, 0, width, axis=dim), axis, backward)  7.46 us
    ppermute x2, starting transfers between devices, halos(): lax.ppermute(lax.slice_in_dim(block, block.shape[dim] - width, None, axis...  7.02 us
    ppermute x2, starting transfers between devices, section_conv(): left = lax.ppermute(tall_cols(cols - reach, cols), 'col', forward)  6.42 us
  transfers between devices with their start and end apart: 16, of which 7 were waited for; matrix products, arithmetic and copies ran while one was open for 2% of the time, Pallas kernels for 49%

profile of v16, /device:TPU:3, one launch (start us, length us, event | category | flops | bytes accessed | tf_op | source)
XLA Modules:
  0.0 258.3 jit_solution(14239555234606733101)
XLA Ops:
  0.0 1.1 fusion.87
  1.2 3.7 %collective-permute-start = (bf16[7,128,128]{2,1,0:T(8,128)(2,1)S(1)}, bf16[7,128,128]{2,1,0:T(8,128)(2,1)S(1)}, u32[]{:S(2)}, u32[]{:S(2)}) collective-permute-start(bf16[7,128,128]{2,1,0:T(8,128)(2,1)S(1)} %get-tuple-element.27), channel_id=1, source_target_pairs={{0,4},{4,8},{8,12},{12,16},{16,20},{20,24},{24,28},{1,5},{5,9},{9,... | collective-permute-start | bytes 688136 | tf_op jit(solution)/shard_map/ppermute | solution.py:140
  4.8 1.9 collective-permute-start.1
  6.8 1.0 fusion.85
  7.8 1.2 fusion.86
  9.0 0.8 fusion.64.refs_1_.refs_3_
  9.8 3.3 %collective-permute-done.1 = bf16[7,128,128]{2,1,0:T(8,128)(2,1)S(1)} collective-permute-done((bf16[7,128,128]{2,1,0:T(8,128)(2,1)S(1)}, bf16[7,128,128]{2,1,0:T(8,128)(2,1)S(1)}, u32[]{:S(2)}, u32[]{:S(2)}) %collective-permute-start.1) | collective-permute-done | bytes 229408 | tf_op jit(solution)/shard_map/ppermute | solution.py:143
  13.2 3.2 %collective-permute-start.2 = (bf16[78,7,128]{2,1,0:T(8,128)(2,1)S(1)}, bf16[78,7,128]{2,1,0:T(8,128)(2,1)S(1)}, u32[]{:S(2)}, u32[]{:S(2)}) collective-permute-start(bf16[78,7,128]{2,1,0:T(8,128)(2,1)S(1)} %pad_maximum_fusion.10), channel_id=1, source_target_pairs={{0,1},{1,2},{2,3},{4,5},{5,6},{6,7},{8,9},{9,10},{10,11},{12,13},{... | collective-permute-start | bytes 419336 | tf_op jit(solution)/shard_map/ppermute | solution.py:161
  16.4 1.3 collective-permute-start.3
  17.8 86.0 %shard_map.101 = f32[1,64,112,128]{3,2,1,0:T(8,128)} custom-call(bf16[1,7,128,128]{3,2,1,0:T(8,128)(2,1)} %bitcast.75, bf16[1,64,128,128]{3,2,1,0:T(8,128)(2,1)} %bitcast.70, bf16[1,7,128,128]{3,2,1,0:T(8,128)(2,1)} %bitcast.76, f32[15,15,128]{2,1,0:T(8,128)} %fusion.64.refs_1_.refs_3_), custom_call_target="tpu_custom_call" | custom-call | flops 412876800 | bytes 6225920 | tf_op jit(solution)/shard_map/pallas_call | solution.py:119
  103.8 0.2 maximum_bitcast_fusion.2
  104.0 0.2 maximum_bitcast_fusion.3
  104.2 1.1 pad_maximum_fusion.5.refs_0_
  105.3 12.3 %shard_map.100 = f32[2,64,8,128]{3,2,1,0:T(8,128)} custom-call(bf16[2,78,22,128]{3,2,1,0:T(8,128)(2,1)} %pad_maximum_fusion.5.refs_0_, f32[15,15,128]{2,1,0:T(8,128)} %fusion.64.refs_1_.refs_3_), custom_call_target="tpu_custom_call" | custom-call | flops 58982400 | bytes 1402880 | tf_op jit(solution)/shard_map/pallas_call | solution.py:119
  117.6 1.1 slice_bitcast_fusion.3
  118.6 3.3 %fusion.29 = f32[64,128]{1,0:T(8,128)S(1)} fusion(f32[64,8,128]{2,1,0:T(8,128)S(1)} %get-tuple-element.44, f32[64,112,128]{2,1,0:T(8,128)} %bitcast.57, f32[64,8,128]{2,1,0:T(8,128)S(1)} %get-tuple-element.43), kind=kLoop, calls=%fused_computation.39 | loop fusion | flops 3137536 | bytes 4227072 | tf_op jit(solution)/shard_map/reduce_sum | solution.py:177
  122.0 2.6 %multiply_reduce_fusion = f32[64,128]{1,0:T(8,128)S(1)} fusion(f32[64,128]{1,0:T(8,128)S(1)} %broadcast_multiply_fusion, f32[64,8,128]{2,1,0:T(8,128)S(1)} %get-tuple-element.44, f32[64,112,128]{2,1,0:T(8,128)S(1)} %bitcast.59, f32[64,8,128]{2,1,0:T(8,128)S(1)} %get-tuple-element.43), kind=kLoop, calls=%fused_computation.21 | loop fusion | flops 5234688 | bytes 4259840 | tf_op jit(solution)/shard_map/reduce_sum | solution.py:178
  124.7 8.7 %add_convert_fusion = bf16[64,128,128]{2,1,0:T(8,128)(2,1)S(1)} fusion(bf16[64,128,128]{2,1,0:T(8,128)(2,1)} %param.10, f32[64,128]{1,0:T(8,128)S(1)} %add_rsqrt_fusion, f32[64,128]{1,0:T(8,128)S(1)} %broadcast_multiply_fusion, f32[64,8,128]{2,1,0:T(8,128)S(1)} %get-tuple-element.44, f32[64,112,128]{2,1,0:T(8,128)} %bitcast.58, ...), kind=kOutput, calls=%fused_computation.19 | convolution fusion | flops 2193620992 | bytes 8716288 | tf_op jit(solution)/shard_map/dot_general | solution.py:183
  133.4 2.2 collective-permute-start.4
  135.5 2.3 collective-permute-start.5
  137.9 3.8 %collective-permute-done.5 = bf16[1,128,128]{2,1,0:T(8,128)(2,1)S(1)} collective-permute-done((bf16[1,128,128]{2,1,0:T(8,128)(2,1)S(1)}, bf16[1,128,128]{2,1,0:T(8,128)(2,1)S(1)}, u32[]{:S(2)}, u32[]{:S(2)}) %collective-permute-start.5) | collective-permute-done | bytes 32800 | tf_op jit(solution)/shard_map/ppermute | solution.py:19
  141.7 4.3 %collective-permute-start.6 = (bf16[66,1,128]{2,1,0:T(2,128)(2,1)S(1)}, bf16[66,1,128]{2,1,0:T(2,128)(2,1)S(1)}, u32[]{:S(2)}, u32[]{:S(2)}) collective-permute-start(bf16[66,1,128]{2,1,0:T(2,128)(2,1)S(1)} %get-tuple-element.17), channel_id=1, source_target_pairs={{0,1},{1,2},{2,3},{4,5},{5,6},{6,7},{8,9},{9,10},{10,11},{12,13},{... | collective-permute-start | bytes 50696 | tf_op jit(solution)/shard_map/ppermute | solution.py:16
  146.0 1.5 collective-permute-start.7
  147.5 0.8 fusion.62.refs_1_.refs_3_
  148.3 2.4 collective-permute-done.7
  150.7 0.8 maximum_convert_fusion
  151.5 0.6 fusion.77
  152.1 0.6 fusion.78
  152.7 1.6 fusion.22
  154.3 0.6 fusion.83
  154.9 0.5 fusion.53
  155.4 0.3 copy-done.12
  155.7 0.4 convolution_convert_fusion
  156.3 3.3 %collective-permute-start.8 = (bf16[7,64,256]{2,1,0:T(8,128)(2,1)S(1)}, bf16[7,64,256]{2,1,0:T(8,128)(2,1)S(1)}, u32[]{:S(2)}, u32[]{:S(2)}) collective-permute-start(bf16[7,64,256]{2,1,0:T(8,128)(2,1)S(1)} %get-tuple-element.39), channel_id=1, source_target_pairs={{0,4},{4,8},{8,12},{12,16},{16,20},{20,24},{24,28},{1,5},{5,9},{9,... | collective-permute-start | bytes 688136 | tf_op jit(solution)/shard_map/ppermute | solution.py:140
  159.6 1.9 collective-permute-start.9
  161.6 2.1 collective-permute-done.8
  163.7 4.2 %collective-permute-done.9 = bf16[7,64,256]{2,1,0:T(8,128)(2,1)S(1)} collective-permute-done((bf16[7,64,256]{2,1,0:T(8,128)(2,1)S(1)}, bf16[7,64,256]{2,1,0:T(8,128)(2,1)S(1)}, u32[]{:S(2)}, u32[]{:S(2)}) %collective-permute-start.9) | collective-permute-done | bytes 229408 | tf_op jit(solution)/shard_map/ppermute | solution.py:143
  167.9 3.2 %collective-permute-start.10 = (bf16[46,7,256]{2,1,0:T(8,128)(2,1)S(1)}, bf16[46,7,256]{2,1,0:T(8,128)(2,1)S(1)}, u32[]{:S(2)}, u32[]{:S(2)}) collective-permute-start(bf16[46,7,256]{2,1,0:T(8,128)(2,1)S(1)} %pad_maximum_fusion.8), channel_id=1, source_target_pairs={{0,1},{1,2},{2,3},{4,5},{5,6},{6,7},{8,9},{9,10},{10,11},{12,13},{... | collective-permute-start | bytes 494600 | tf_op jit(solution)/shard_map/ppermute | solution.py:161
  171.2 1.3 collective-permute-start.11
  172.6 39.3 %shard_map.103 = f32[1,32,48,256]{3,2,1,0:T(8,128)} custom-call(bf16[1,7,64,256]{3,2,1,0:T(8,128)(2,1)} %bitcast.73, bf16[1,32,64,256]{3,2,1,0:T(8,128)(2,1)} %bitcast.65, bf16[1,7,64,256]{3,2,1,0:T(8,128)(2,1)} %bitcast.74, f32[15,15,256]{2,1,0:T(8,128)} %fusion.62.refs_1_.refs_3_), custom_call_target="tpu_custom_call" | custom-call | flops 176947200 | bytes 3080192 | tf_op jit(solution)/shard_map/pallas_call | solution.py:119
  211.9 0.2 maximum_bitcast_fusion
  212.3 1.1 pad_maximum_fusion.4.refs_0_
  213.4 12.8 %shard_map.102 = f32[2,32,8,256]{3,2,1,0:T(8,128)} custom-call(bf16[2,46,22,256]{3,2,1,0:T(8,128)(2,1)} %pad_maximum_fusion.4.refs_0_, f32[15,15,256]{2,1,0:T(8,128)} %fusion.62.refs_1_.refs_3_), custom_call_target="tpu_custom_call" | custom-call | flops 58982400 | bytes 1560576 | tf_op jit(solution)/shard_map/pallas_call | solution.py:119
  226.2 1.1 slice_bitcast_fusion.1
  227.3 0.4 fusion.44
  227.7 0.3 copy-done.5
  228.0 0.6 multiply_reduce_fusion.1
  228.6 5.4 %add_convert_fusion.1 = bf16[32,64,256]{2,1,0:T(8,128)(2,1)} fusion(bf16[32,64,256]{2,1,0:T(8,128)(2,1)S(1)} %copy-done.4, f32[32,64]{1,0:T(8,128)S(1)} %add_rsqrt_fusion.1, f32[32,64]{1,0:T(8,128)S(1)} %broadcast_multiply_fusion.1, f32[32,8,256]{2,1,0:T(8,128)} %copy-done.5, f32[32,48,256]{2,1,0:T(8,128)S(1)} %bitcast.64, ...), kind=kOutput, calls=%fused_computation.34 | convolution fusion | flops 2170552320 | bytes 5259264 | tf_op jit(solution)/shard_map/dot_general | solution.py:183
  234.1 0.8 fusion.89
  234.9 2.0 collective-permute-start.12
  236.9 2.3 collective-permute-start.13
  239.2 3.8 %collective-permute-done.13 = bf16[1,64,256]{2,1,0:T(8,128)(2,1)S(1)} collective-permute-done((bf16[1,64,256]{2,1,0:T(8,128)(2,1)S(1)}, bf16[1,64,256]{2,1,0:T(8,128)(2,1)S(1)}, u32[]{:S(2)}, u32[]{:S(2)}) %collective-permute-start.13) | collective-permute-done | bytes 32800 | tf_op jit(solution)/shard_map/ppermute | solution.py:19
  243.0 1.0 pad_maximum_fusion.14
  244.1 4.3 %collective-permute-start.14 = (bf16[34,1,256]{2,1,0:T(2,128)(2,1)S(1)}, bf16[34,1,256]{2,1,0:T(2,128)(2,1)S(1)}, u32[]{:S(2)}, u32[]{:S(2)}) collective-permute-start(bf16[34,1,256]{2,1,0:T(2,128)(2,1)S(1)} %get-tuple-element.29), channel_id=1, source_target_pairs={{0,1},{1,2},{2,3},{4,5},{5,6},{6,7},{8,9},{9,10},{10,11},{12,13},{... | collective-permute-start | bytes 52232 | tf_op jit(solution)/shard_map/ppermute | solution.py:16
  248.3 1.5 collective-permute-start.15
  249.9 3.1 %collective-permute-done.15 = bf16[34,1,256]{2,1,0:T(2,128)(2,1)S(1)} collective-permute-done((bf16[34,1,256]{2,1,0:T(2,128)(2,1)S(1)}, bf16[34,1,256]{2,1,0:T(2,128)(2,1)S(1)}, u32[]{:S(2)}, u32[]{:S(2)}) %collective-permute-start.15) | collective-permute-done | bytes 17440 | tf_op jit(solution)/shard_map/ppermute | solution.py:19
  253.0 1.8 maximum_convert_fusion.1
  254.8 0.4 fusion.80
  255.2 0.2 fusion.81
  255.4 0.2 fusion.82
  255.6 1.4 fusion.33
  257.0 0.3 fusion.88
  257.3 0.2 fusion.54
  257.5 0.8 copy.20
  (67 shorter events, 0.8 us)
Async XLA Ops:
  0.0 228.6 %copy-start = (bf16[1024,256]{1,0:T(8,128)(2,1)S(1)}, bf16[1024,256]{1,0:T(8,128)(2,1)}, u32[]{:S(2)}) copy-start(bf16[1024,256]{1,0:T(8,128)(2,1)} %param.19) | copy-start | bytes 1572868
  0.0 9.0 %copy-start.16 = (f32[128]{0:T(128)S(1)}, f32[128]{0:T(128)}, u32[]{:S(2)}) copy-start(f32[128]{0:T(128)} %param.12) | copy-start | bytes 1540
  0.0 9.0 %copy-start.11 = (f32[15,15,128]{2,1,0:T(8,128)S(1)}, f32[15,15,128]{2,1,0:T(8,128)}, u32[]{:S(2)}) copy-start(f32[15,15,128]{2,1,0:T(8,128)} %param.11) | copy-start | bytes 345604
  1.2 8.6 %collective-permute-start = (bf16[7,128,128]{2,1,0:T(8,128)(2,1)S(1)}, bf16[7,128,128]{2,1,0:T(8,128)(2,1)S(1)}, u32[]{:S(2)}, u32[]{:S(2)}) collective-permute-start(bf16[7,128,128]{2,1,0:T(8,128)(2,1)S(1)} %get-tuple-element.27), channel_id=1, source_target_pairs={{0,4},{4,8},{8,12},{12,16},{16,20},{20,24},{24,28},{1,5},{5,9},{9,... | collective-permute-start | bytes 688136 | tf_op jit(solution)/shard_map/ppermute | solution.py:140
  4.8 8.2 %collective-permute-start.1 = (bf16[7,128,128]{2,1,0:T(8,128)(2,1)S(1)}, bf16[7,128,128]{2,1,0:T(8,128)(2,1)S(1)}, u32[]{:S(2)}, u32[]{:S(2)}) collective-permute-start(bf16[7,128,128]{2,1,0:T(8,128)(2,1)S(1)} %get-tuple-element.28), channel_id=1, source_target_pairs={{4,0},{8,4},{12,8},{16,12},{20,16},{24,20},{28,24},{5,1},{9,5},{13... | collective-permute-start | bytes 688136 | tf_op jit(solution)/shard_map/ppermute | solution.py:143
  9.8 8.0 %copy-start.8 = (bf16[7,128,128]{2,1,0:T(8,128)(2,1)}, bf16[7,128,128]{2,1,0:T(8,128)(2,1)S(1)}, u32[]{:S(2)}) copy-start(bf16[7,128,128]{2,1,0:T(8,128)(2,1)S(1)} %collective-permute-done) | copy-start | bytes 688132
  13.1 4.7 %copy-start.9 = (bf16[7,128,128]{2,1,0:T(8,128)(2,1)}, bf16[7,128,128]{2,1,0:T(8,128)(2,1)S(1)}, u32[]{:S(2)}) copy-start(bf16[7,128,128]{2,1,0:T(8,128)(2,1)S(1)} %collective-permute-done.1) | copy-start | bytes 688132
  13.2 90.7 %collective-permute-start.2 = (bf16[78,7,128]{2,1,0:T(8,128)(2,1)S(1)}, bf16[78,7,128]{2,1,0:T(8,128)(2,1)S(1)}, u32[]{:S(2)}, u32[]{:S(2)}) collective-permute-start(bf16[78,7,128]{2,1,0:T(8,128)(2,1)S(1)} %pad_maximum_fusion.10), channel_id=1, source_target_pairs={{0,1},{1,2},{2,3},{4,5},{5,6},{6,7},{8,9},{9,10},{10,11},{12,13},{... | collective-permute-start | bytes 419336 | tf_op jit(solution)/shard_map/ppermute | solution.py:161
  16.4 87.6 %collective-permute-start.3 = (bf16[78,7,128]{2,1,0:T(8,128)(2,1)S(1)}, bf16[78,7,128]{2,1,0:T(8,128)(2,1)S(1)}, u32[]{:S(2)}, u32[]{:S(2)}) collective-permute-start(bf16[78,7,128]{2,1,0:T(8,128)(2,1)S(1)} %pad_maximum_fusion.11), channel_id=1, source_target_pairs={{1,0},{2,1},{3,2},{5,4},{6,5},{7,6},{9,8},{10,9},{11,10},{13,12},{... | collective-permute-start | bytes 419336 | tf_op jit(solution)/shard_map/ppermute | solution.py:162
  118.6 3.4 %copy-start.1 = (f32[1,64,112,128]{3,2,1,0:T(8,128)S(1)}, f32[1,64,112,128]{3,2,1,0:T(8,128)}, u32[]{:S(2)}) copy-start(f32[1,64,112,128]{3,2,1,0:T(8,128)} %shard_map.101) | copy-start | bytes 11010052
  122.0 2.7 %copy-start.14 = (bf16[512,128]{1,0:T(8,128)(2,1)S(1)}, bf16[512,128]{1,0:T(8,128)(2,1)}, u32[]{:S(2)}) copy-start(bf16[512,128]{1,0:T(8,128)(2,1)} %param.14) | copy-start | bytes 393220
  122.0 2.7 %copy-start.15 = (bf16[128,512]{1,0:T(8,128)(2,1)S(1)}, bf16[128,512]{1,0:T(8,128)(2,1)}, u32[]{:S(2)}) copy-start(bf16[128,512]{1,0:T(8,128)(2,1)} %param.13) | copy-start | bytes 393220
  124.7 13.2 %copy-start.13 = (f32[256]{0:T(256)S(1)}, f32[256]{0:T(256)}, u32[]{:S(2)}) copy-start(f32[256]{0:T(256)} %param.17) | copy-start | bytes 3076
  133.3 14.1 %copy-start.10 = (f32[15,15,256]{2,1,0:T(8,128)S(1)}, f32[15,15,256]{2,1,0:T(8,128)}, u32[]{:S(2)}) copy-start(f32[15,15,256]{2,1,0:T(8,128)} %param.16) | copy-start | bytes 691204
  133.4 4.5 %collective-permute-start.4 = (bf16[1,128,128]{2,1,0:T(8,128)(2,1)S(1)}, bf16[1,128,128]{2,1,0:T(8,128)(2,1)S(1)}, u32[]{:S(2)}, u32[]{:S(2)}) collective-permute-start(bf16[1,128,128]{2,1,0:T(8,128)(2,1)S(1)} %get-tuple-element.21), channel_id=1, source_target_pairs={{0,4},{4,8},{8,12},{12,16},{16,20},{20,24},{24,28},{1,5},{5,9},{9,... | collective-permute-start | bytes 98312 | tf_op jit(solution)/shard_map/ppermute | solution.py:16
  135.5 6.1 %collective-permute-start.5 = (bf16[1,128,128]{2,1,0:T(8,128)(2,1)S(1)}, bf16[1,128,128]{2,1,0:T(8,128)(2,1)S(1)}, u32[]{:S(2)}, u32[]{:S(2)}) collective-permute-start(bf16[1,128,128]{2,1,0:T(8,128)(2,1)S(1)} %get-tuple-element.22), channel_id=1, source_target_pairs={{4,0},{8,4},{12,8},{16,12},{20,16},{24,20},{28,24},{5,1},{9,5},{13... | collective-permute-start | bytes 98312 | tf_op jit(solution)/shard_map/ppermute | solution.py:19
  141.7 6.6 %collective-permute-start.6 = (bf16[66,1,128]{2,1,0:T(2,128)(2,1)S(1)}, bf16[66,1,128]{2,1,0:T(2,128)(2,1)S(1)}, u32[]{:S(2)}, u32[]{:S(2)}) collective-permute-start(bf16[66,1,128]{2,1,0:T(2,128)(2,1)S(1)} %get-tuple-element.17), channel_id=1, source_target_pairs={{0,1},{1,2},{2,3},{4,5},{5,6},{6,7},{8,9},{9,10},{10,11},{12,13},{... | collective-permute-start | bytes 50696 | tf_op jit(solution)/shard_map/ppermute | solution.py:16
  146.0 4.7 %collective-permute-start.7 = (bf16[66,1,128]{2,1,0:T(2,128)(2,1)S(1)}, bf16[66,1,128]{2,1,0:T(2,128)(2,1)S(1)}, u32[]{:S(2)}, u32[]{:S(2)}) collective-permute-start(bf16[66,1,128]{2,1,0:T(2,128)(2,1)S(1)} %get-tuple-element.18), channel_id=1, source_target_pairs={{1,0},{2,1},{3,2},{5,4},{6,5},{7,6},{9,8},{10,9},{11,10},{13,12},{... | collective-permute-start | bytes 50696 | tf_op jit(solution)/shard_map/ppermute | solution.py:19
  154.9 0.8 copy-start.12
  156.1 16.4 %copy-start.3 = (bf16[32,64,256]{2,1,0:T(8,128)(2,1)}, bf16[32,64,256]{2,1,0:T(8,128)(2,1)S(1)}, u32[]{:S(2)}) copy-start(bf16[32,64,256]{2,1,0:T(8,128)(2,1)S(1)} %convolution_convert_fusion) | copy-start | bytes 3145732
  156.3 7.4 %collective-permute-start.8 = (bf16[7,64,256]{2,1,0:T(8,128)(2,1)S(1)}, bf16[7,64,256]{2,1,0:T(8,128)(2,1)S(1)}, u32[]{:S(2)}, u32[]{:S(2)}) collective-permute-start(bf16[7,64,256]{2,1,0:T(8,128)(2,1)S(1)} %get-tuple-element.39), channel_id=1, source_target_pairs={{0,4},{4,8},{8,12},{12,16},{16,20},{20,24},{24,28},{1,5},{5,9},{9,... | collective-permute-start | bytes 688136 | tf_op jit(solution)/shard_map/ppermute | solution.py:140
  159.6 8.2 %collective-permute-start.9 = (bf16[7,64,256]{2,1,0:T(8,128)(2,1)S(1)}, bf16[7,64,256]{2,1,0:T(8,128)(2,1)S(1)}, u32[]{:S(2)}, u32[]{:S(2)}) collective-permute-start(bf16[7,64,256]{2,1,0:T(8,128)(2,1)S(1)} %get-tuple-element.40), channel_id=1, source_target_pairs={{4,0},{8,4},{12,8},{16,12},{20,16},{24,20},{28,24},{5,1},{9,5},{13... | collective-permute-start | bytes 688136 | tf_op jit(solution)/shard_map/ppermute | solution.py:143
  163.7 8.9 %copy-start.6 = (bf16[7,64,256]{2,1,0:T(8,128)(2,1)}, bf16[7,64,256]{2,1,0:T(8,128)(2,1)S(1)}, u32[]{:S(2)}) copy-start(bf16[7,64,256]{2,1,0:T(8,128)(2,1)S(1)} %collective-permute-done.8) | copy-start | bytes 688132
  167.9 4.7 %copy-start.7 = (bf16[7,64,256]{2,1,0:T(8,128)(2,1)}, bf16[7,64,256]{2,1,0:T(8,128)(2,1)S(1)}, u32[]{:S(2)}) copy-start(bf16[7,64,256]{2,1,0:T(8,128)(2,1)S(1)} %collective-permute-done.9) | copy-start | bytes 688132
  167.9 43.9 %collective-permute-start.10 = (bf16[46,7,256]{2,1,0:T(8,128)(2,1)S(1)}, bf16[46,7,256]{2,1,0:T(8,128)(2,1)S(1)}, u32[]{:S(2)}, u32[]{:S(2)}) collective-permute-start(bf16[46,7,256]{2,1,0:T(8,128)(2,1)S(1)} %pad_maximum_fusion.8), channel_id=1, source_target_pairs={{0,1},{1,2},{2,3},{4,5},{5,6},{6,7},{8,9},{9,10},{10,11},{12,13},{... | collective-permute-start | bytes 494600 | tf_op jit(solution)/shard_map/ppermute | solution.py:161
  171.2 40.9 %collective-permute-start.11 = (bf16[46,7,256]{2,1,0:T(8,128)(2,1)S(1)}, bf16[46,7,256]{2,1,0:T(8,128)(2,1)S(1)}, u32[]{:S(2)}, u32[]{:S(2)}) collective-permute-start(bf16[46,7,256]{2,1,0:T(8,128)(2,1)S(1)} %pad_maximum_fusion.9), channel_id=1, source_target_pairs={{1,0},{2,1},{3,2},{5,4},{6,5},{7,6},{9,8},{10,9},{11,10},{13,12},{... | collective-permute-start | bytes 494600 | tf_op jit(solution)/shard_map/ppermute | solution.py:162
  212.2 15.0 %copy-start.2 = (f32[1,32,48,256]{3,2,1,0:T(8,128)S(1)}, f32[1,32,48,256]{3,2,1,0:T(8,128)}, u32[]{:S(2)}) copy-start(f32[1,32,48,256]{3,2,1,0:T(8,128)} %shard_map.103) | copy-start | bytes 4718596
  227.3 0.7 copy-start.5
  227.3 1.4 copy-start.4
  234.9 4.3 %collective-permute-start.12 = (bf16[1,64,256]{2,1,0:T(8,128)(2,1)S(1)}, bf16[1,64,256]{2,1,0:T(8,128)(2,1)S(1)}, u32[]{:S(2)}, u32[]{:S(2)}) collective-permute-start(bf16[1,64,256]{2,1,0:T(8,128)(2,1)S(1)} %get-tuple-element.33), channel_id=1, source_target_pairs={{0,4},{4,8},{8,12},{12,16},{16,20},{20,24},{24,28},{1,5},{5,9},{9,... | collective-permute-start | bytes 98312 | tf_op jit(solution)/shard_map/ppermute | solution.py:16
  236.9 6.1 %collective-permute-start.13 = (bf16[1,64,256]{2,1,0:T(8,128)(2,1)S(1)}, bf16[1,64,256]{2,1,0:T(8,128)(2,1)S(1)}, u32[]{:S(2)}, u32[]{:S(2)}) collective-permute-start(bf16[1,64,256]{2,1,0:T(8,128)(2,1)S(1)} %get-tuple-element.34), channel_id=1, source_target_pairs={{4,0},{8,4},{12,8},{16,12},{20,16},{24,20},{28,24},{5,1},{9,5},{13... | collective-permute-start | bytes 98312 | tf_op jit(solution)/shard_map/ppermute | solution.py:19
  244.1 5.8 %collective-permute-start.14 = (bf16[34,1,256]{2,1,0:T(2,128)(2,1)S(1)}, bf16[34,1,256]{2,1,0:T(2,128)(2,1)S(1)}, u32[]{:S(2)}, u32[]{:S(2)}) collective-permute-start(bf16[34,1,256]{2,1,0:T(2,128)(2,1)S(1)} %get-tuple-element.29), channel_id=1, source_target_pairs={{0,1},{1,2},{2,3},{4,5},{5,6},{6,7},{8,9},{9,10},{10,11},{12,13},{... | collective-permute-start | bytes 52232 | tf_op jit(solution)/shard_map/ppermute | solution.py:16
  248.3 4.7 %collective-permute-start.15 = (bf16[34,1,256]{2,1,0:T(2,128)(2,1)S(1)}, bf16[34,1,256]{2,1,0:T(2,128)(2,1)S(1)}, u32[]{:S(2)}, u32[]{:S(2)}) collective-permute-start(bf16[34,1,256]{2,1,0:T(2,128)(2,1)S(1)} %get-tuple-element.30), channel_id=1, source_target_pairs={{1,0},{2,1},{3,2},{5,4},{6,5},{7,6},{9,8},{10,9},{11,10},{13,12},{... | collective-permute-start | bytes 52232 | tf_op jit(solution)/shard_map/ppermute | solution.py:19

commit v17 on v16

--- a/solution.py
+++ b/solution.py
@@ -34,7 +34,7 @@
     nlb = chans // 128
     njb = cols // 8
     nrb = rows // rb
-    spread = max(1, min(8, 32 // (njb * nlb)))
+    spread = max(1, min(8, 64 // (njb * nlb)))
 
     def one_strip(n, carry):
         o_ref = o_all.at[n]

time: 259 us -> 258 us (level)
  transfers between devices with their start and end apart: 16 -> 16, of which waited for: 7 -> 7; matrix products, arithmetic and copies ran while one was open for 2% -> 2% of each run, Pallas kernels for 49% -> 48%
where the time goes in v17:
time: 258 us
  Pallas kernels  150 us (58%)
  starting transfers between devices  40.2 us (16%)
  waiting for transfers between devices  22.7 us (9%)
  other arithmetic  19.1 us (7%)
  matrix products  14.5 us (6%)
  local copies, waits for them, and re-layouts  10.7 us (4%)
    pallas_call x4, Pallas kernels, depthwise(): pl.pallas_call(body, out_shape=jax.ShapeDtypeStruct((count, rows, cols, c...  150 us
    dot_general x2, matrix products, local_section(): mixed = jnp.dot(hidden, w_out, preferred_element_type=jnp.float32)  14.1 us
    ppermute x4, waiting for transfers between devices, padded_2(): lax.ppermute(lax.slice_in_dim(block, 0, width, axis=dim), axis, backward)  13.1 us
    ppermute x4, starting transfers between devices, padded_2(): lax.ppermute(lax.slice_in_dim(block, block.shape[dim] - width, None, axis...  12.7 us
    ppermute x4, starting transfers between devices, padded_2(): lax.ppermute(lax.slice_in_dim(block, 0, width, axis=dim), axis, backward)  7.6 us
    ppermute x2, waiting for transfers between devices, halos(): lax.ppermute(lax.slice_in_dim(block, 0, width, axis=dim), axis, backward)  7.46 us
    ppermute x2, starting transfers between devices, halos(): lax.ppermute(lax.slice_in_dim(block, block.shape[dim] - width, None, axis...  7.02 us
    ppermute x2, starting transfers between devices, section_conv(): left = lax.ppermute(tall_cols(cols - reach, cols), 'col', forward)  6.43 us
  transfers between devices with their start and end apart: 16, of which 7 were waited for; matrix products, arithmetic and copies ran while one was open for 2% of the time, Pallas kernels for 48%

profile of v17, /device:TPU:3, one launch (start us, length us, event | category | flops | bytes accessed | tf_op | source)
XLA Modules:
  0.0 257.6 jit_solution(7029747508162602191)
XLA Ops:
  0.0 1.1 fusion.87
  1.2 3.7 %collective-permute-start = (bf16[7,128,128]{2,1,0:T(8,128)(2,1)S(1)}, bf16[7,128,128]{2,1,0:T(8,128)(2,1)S(1)}, u32[]{:S(2)}, u32[]{:S(2)}) collective-permute-start(bf16[7,128,128]{2,1,0:T(8,128)(2,1)S(1)} %get-tuple-element.27), channel_id=1, source_target_pairs={{0,4},{4,8},{8,12},{12,16},{16,20},{20,24},{24,28},{1,5},{5,9},{9,... | collective-permute-start | bytes 688136 | tf_op jit(solution)/shard_map/ppermute | solution.py:140
  4.8 1.9 collective-permute-start.1
  6.8 1.0 fusion.85
  7.8 1.2 fusion.86
  9.0 0.8 fusion.64.refs_1_.refs_3_
  9.8 3.3 %collective-permute-done.1 = bf16[7,128,128]{2,1,0:T(8,128)(2,1)S(1)} collective-permute-done((bf16[7,128,128]{2,1,0:T(8,128)(2,1)S(1)}, bf16[7,128,128]{2,1,0:T(8,128)(2,1)S(1)}, u32[]{:S(2)}, u32[]{:S(2)}) %collective-permute-start.1) | collective-permute-done | bytes 229408 | tf_op jit(solution)/shard_map/ppermute | solution.py:143
  13.2 3.2 %collective-permute-start.2 = (bf16[78,7,128]{2,1,0:T(8,128)(2,1)S(1)}, bf16[78,7,128]{2,1,0:T(8,128)(2,1)S(1)}, u32[]{:S(2)}, u32[]{:S(2)}) collective-permute-start(bf16[78,7,128]{2,1,0:T(8,128)(2,1)S(1)} %pad_maximum_fusion.10), channel_id=1, source_target_pairs={{0,1},{1,2},{2,3},{4,5},{5,6},{6,7},{8,9},{9,10},{10,11},{12,13},{... | collective-permute-start | bytes 419336 | tf_op jit(solution)/shard_map/ppermute | solution.py:161
  16.4 1.3 collective-permute-start.3
  17.8 85.7 %shard_map.101 = f32[1,64,112,128]{3,2,1,0:T(8,128)} custom-call(bf16[1,7,128,128]{3,2,1,0:T(8,128)(2,1)} %bitcast.75, bf16[1,64,128,128]{3,2,1,0:T(8,128)(2,1)} %bitcast.70, bf16[1,7,128,128]{3,2,1,0:T(8,128)(2,1)} %bitcast.76, f32[15,15,128]{2,1,0:T(8,128)} %fusion.64.refs_1_.refs_3_), custom_call_target="tpu_custom_call" | custom-call | flops 412876800 | bytes 6225920 | tf_op jit(solution)/shard_map/pallas_call | solution.py:119
  103.4 0.2 maximum_bitcast_fusion.2
  103.6 0.2 maximum_bitcast_fusion.3
  103.8 1.1 pad_maximum_fusion.5.refs_0_
  104.9 12.3 %shard_map.100 = f32[2,64,8,128]{3,2,1,0:T(8,128)} custom-call(bf16[2,78,22,128]{3,2,1,0:T(8,128)(2,1)} %pad_maximum_fusion.5.refs_0_, f32[15,15,128]{2,1,0:T(8,128)} %fusion.64.refs_1_.refs_3_), custom_call_target="tpu_custom_call" | custom-call | flops 58982400 | bytes 1402880 | tf_op jit(solution)/shard_map/pallas_call | solution.py:119
  117.2 1.1 slice_bitcast_fusion.3
  118.3 3.3 %fusion.29 = f32[64,128]{1,0:T(8,128)S(1)} fusion(f32[64,8,128]{2,1,0:T(8,128)S(1)} %get-tuple-element.44, f32[64,112,128]{2,1,0:T(8,128)} %bitcast.57, f32[64,8,128]{2,1,0:T(8,128)S(1)} %get-tuple-element.43), kind=kLoop, calls=%fused_computation.39 | loop fusion | flops 3137536 | bytes 4227072 | tf_op jit(solution)/shard_map/reduce_sum | solution.py:177
  121.6 2.6 %multiply_reduce_fusion = f32[64,128]{1,0:T(8,128)S(1)} fusion(f32[64,128]{1,0:T(8,128)S(1)} %broadcast_multiply_fusion, f32[64,8,128]{2,1,0:T(8,128)S(1)} %get-tuple-element.44, f32[64,112,128]{2,1,0:T(8,128)S(1)} %bitcast.59, f32[64,8,128]{2,1,0:T(8,128)S(1)} %get-tuple-element.43), kind=kLoop, calls=%fused_computation.21 | loop fusion | flops 5234688 | bytes 4259840 | tf_op jit(solution)/shard_map/reduce_sum | solution.py:178
  124.3 8.7 %add_convert_fusion = bf16[64,128,128]{2,1,0:T(8,128)(2,1)S(1)} fusion(bf16[64,128,128]{2,1,0:T(8,128)(2,1)} %param.10, f32[64,128]{1,0:T(8,128)S(1)} %add_rsqrt_fusion, f32[64,128]{1,0:T(8,128)S(1)} %broadcast_multiply_fusion, f32[64,8,128]{2,1,0:T(8,128)S(1)} %get-tuple-element.44, f32[64,112,128]{2,1,0:T(8,128)} %bitcast.58, ...), kind=kOutput, calls=%fused_computation.19 | convolution fusion | flops 2193620992 | bytes 8716288 | tf_op jit(solution)/shard_map/dot_general | solution.py:183
  133.0 2.1 collective-permute-start.4
  135.2 2.3 collective-permute-start.5
  137.5 3.8 %collective-permute-done.5 = bf16[1,128,128]{2,1,0:T(8,128)(2,1)S(1)} collective-permute-done((bf16[1,128,128]{2,1,0:T(8,128)(2,1)S(1)}, bf16[1,128,128]{2,1,0:T(8,128)(2,1)S(1)}, u32[]{:S(2)}, u32[]{:S(2)}) %collective-permute-start.5) | collective-permute-done | bytes 32800 | tf_op jit(solution)/shard_map/ppermute | solution.py:19
  141.4 4.3 %collective-permute-start.6 = (bf16[66,1,128]{2,1,0:T(2,128)(2,1)S(1)}, bf16[66,1,128]{2,1,0:T(2,128)(2,1)S(1)}, u32[]{:S(2)}, u32[]{:S(2)}) collective-permute-start(bf16[66,1,128]{2,1,0:T(2,128)(2,1)S(1)} %get-tuple-element.17), channel_id=1, source_target_pairs={{0,1},{1,2},{2,3},{4,5},{5,6},{6,7},{8,9},{9,10},{10,11},{12,13},{... | collective-permute-start | bytes 50696 | tf_op jit(solution)/shard_map/ppermute | solution.py:16
  145.6 1.5 collective-permute-start.7
  147.1 0.8 fusion.62.refs_1_.refs_3_
  147.9 2.4 collective-permute-done.7
  150.3 0.8 maximum_convert_fusion
  151.2 0.6 fusion.77
  151.7 0.6 fusion.78
  152.3 1.6 fusion.22
  153.9 0.6 fusion.83
  154.5 0.5 fusion.53
  155.0 0.3 copy-done.12
  155.3 0.4 convolution_convert_fusion
  155.9 3.3 %collective-permute-start.8 = (bf16[7,64,256]{2,1,0:T(8,128)(2,1)S(1)}, bf16[7,64,256]{2,1,0:T(8,128)(2,1)S(1)}, u32[]{:S(2)}, u32[]{:S(2)}) collective-permute-start(bf16[7,64,256]{2,1,0:T(8,128)(2,1)S(1)} %get-tuple-element.39), channel_id=1, source_target_pairs={{0,4},{4,8},{8,12},{12,16},{16,20},{20,24},{24,28},{1,5},{5,9},{9,... | collective-permute-start | bytes 688136 | tf_op jit(solution)/shard_map/ppermute | solution.py:140
  159.3 1.9 collective-permute-start.9
  161.2 2.1 collective-permute-done.8
  163.3 4.2 %collective-permute-done.9 = bf16[7,64,256]{2,1,0:T(8,128)(2,1)S(1)} collective-permute-done((bf16[7,64,256]{2,1,0:T(8,128)(2,1)S(1)}, bf16[7,64,256]{2,1,0:T(8,128)(2,1)S(1)}, u32[]{:S(2)}, u32[]{:S(2)}) %collective-permute-start.9) | collective-permute-done | bytes 229408 | tf_op jit(solution)/shard_map/ppermute | solution.py:143
  167.6 3.2 %collective-permute-start.10 = (bf16[46,7,256]{2,1,0:T(8,128)(2,1)S(1)}, bf16[46,7,256]{2,1,0:T(8,128)(2,1)S(1)}, u32[]{:S(2)}, u32[]{:S(2)}) collective-permute-start(bf16[46,7,256]{2,1,0:T(8,128)(2,1)S(1)} %pad_maximum_fusion.8), channel_id=1, source_target_pairs={{0,1},{1,2},{2,3},{4,5},{5,6},{6,7},{8,9},{9,10},{10,11},{12,13},{... | collective-permute-start | bytes 494600 | tf_op jit(solution)/shard_map/ppermute | solution.py:161
  170.8 1.3 collective-permute-start.11
  172.2 38.9 %shard_map.103 = f32[1,32,48,256]{3,2,1,0:T(8,128)} custom-call(bf16[1,7,64,256]{3,2,1,0:T(8,128)(2,1)} %bitcast.73, bf16[1,32,64,256]{3,2,1,0:T(8,128)(2,1)} %bitcast.65, bf16[1,7,64,256]{3,2,1,0:T(8,128)(2,1)} %bitcast.74, f32[15,15,256]{2,1,0:T(8,128)} %fusion.62.refs_1_.refs_3_), custom_call_target="tpu_custom_call" | custom-call | flops 176947200 | bytes 3080192 | tf_op jit(solution)/shard_map/pallas_call | solution.py:119
  211.1 0.2 maximum_bitcast_fusion
  211.5 1.1 pad_maximum_fusion.4.refs_0_
  212.6 12.8 %shard_map.102 = f32[2,32,8,256]{3,2,1,0:T(8,128)} custom-call(bf16[2,46,22,256]{3,2,1,0:T(8,128)(2,1)} %pad_maximum_fusion.4.refs_0_, f32[15,15,256]{2,1,0:T(8,128)} %fusion.62.refs_1_.refs_3_), custom_call_target="tpu_custom_call" | custom-call | flops 58982400 | bytes 1560576 | tf_op jit(solution)/shard_map/pallas_call | solution.py:119
  225.5 1.1 slice_bitcast_fusion.1
  226.6 0.4 fusion.44
  226.9 0.3 copy-done.5
  227.2 0.6 multiply_reduce_fusion.1
  227.9 5.4 %add_convert_fusion.1 = bf16[32,64,256]{2,1,0:T(8,128)(2,1)} fusion(bf16[32,64,256]{2,1,0:T(8,128)(2,1)S(1)} %copy-done.4, f32[32,64]{1,0:T(8,128)S(1)} %add_rsqrt_fusion.1, f32[32,64]{1,0:T(8,128)S(1)} %broadcast_multiply_fusion.1, f32[32,8,256]{2,1,0:T(8,128)} %copy-done.5, f32[32,48,256]{2,1,0:T(8,128)S(1)} %bitcast.64, ...), kind=kOutput, calls=%fused_computation.34 | convolution fusion | flops 2170552320 | bytes 5259264 | tf_op jit(solution)/shard_map/dot_general | solution.py:183
  233.4 0.8 fusion.89
  234.1 2.0 collective-permute-start.12
  236.2 2.3 collective-permute-start.13
  238.5 3.8 %collective-permute-done.13 = bf16[1,64,256]{2,1,0:T(8,128)(2,1)S(1)} collective-permute-done((bf16[1,64,256]{2,1,0:T(8,128)(2,1)S(1)}, bf16[1,64,256]{2,1,0:T(8,128)(2,1)S(1)}, u32[]{:S(2)}, u32[]{:S(2)}) %collective-permute-start.13) | collective-permute-done | bytes 32800 | tf_op jit(solution)/shard_map/ppermute | solution.py:19
  242.3 1.0 pad_maximum_fusion.14
  243.3 4.3 %collective-permute-start.14 = (bf16[34,1,256]{2,1,0:T(2,128)(2,1)S(1)}, bf16[34,1,256]{2,1,0:T(2,128)(2,1)S(1)}, u32[]{:S(2)}, u32[]{:S(2)}) collective-permute-start(bf16[34,1,256]{2,1,0:T(2,128)(2,1)S(1)} %get-tuple-element.29), channel_id=1, source_target_pairs={{0,1},{1,2},{2,3},{4,5},{5,6},{6,7},{8,9},{9,10},{10,11},{12,13},{... | collective-permute-start | bytes 52232 | tf_op jit(solution)/shard_map/ppermute | solution.py:16
  247.6 1.5 collective-permute-start.15
  249.1 3.1 %collective-permute-done.15 = bf16[34,1,256]{2,1,0:T(2,128)(2,1)S(1)} collective-permute-done((bf16[34,1,256]{2,1,0:T(2,128)(2,1)S(1)}, bf16[34,1,256]{2,1,0:T(2,128)(2,1)S(1)}, u32[]{:S(2)}, u32[]{:S(2)}) %collective-permute-start.15) | collective-permute-done | bytes 17440 | tf_op jit(solution)/shard_map/ppermute | solution.py:19
  252.3 1.8 maximum_convert_fusion.1
  254.0 0.4 fusion.80
  254.4 0.2 fusion.81
  254.6 0.2 fusion.82
  254.9 1.4 fusion.33
  256.3 0.3 fusion.88
  256.5 0.2 fusion.54
  256.8 0.8 copy.20
  (67 shorter events, 0.8 us)
Async XLA Ops:
  0.0 227.9 %copy-start = (bf16[1024,256]{1,0:T(8,128)(2,1)S(1)}, bf16[1024,256]{1,0:T(8,128)(2,1)}, u32[]{:S(2)}) copy-start(bf16[1024,256]{1,0:T(8,128)(2,1)} %param.19) | copy-start | bytes 1572868
  0.0 9.0 %copy-start.16 = (f32[128]{0:T(128)S(1)}, f32[128]{0:T(128)}, u32[]{:S(2)}) copy-start(f32[128]{0:T(128)} %param.12) | copy-start | bytes 1540
  0.0 9.0 %copy-start.11 = (f32[15,15,128]{2,1,0:T(8,128)S(1)}, f32[15,15,128]{2,1,0:T(8,128)}, u32[]{:S(2)}) copy-start(f32[15,15,128]{2,1,0:T(8,128)} %param.11) | copy-start | bytes 345604
  1.2 8.6 %collective-permute-start = (bf16[7,128,128]{2,1,0:T(8,128)(2,1)S(1)}, bf16[7,128,128]{2,1,0:T(8,128)(2,1)S(1)}, u32[]{:S(2)}, u32[]{:S(2)}) collective-permute-start(bf16[7,128,128]{2,1,0:T(8,128)(2,1)S(1)} %get-tuple-element.27), channel_id=1, source_target_pairs={{0,4},{4,8},{8,12},{12,16},{16,20},{20,24},{24,28},{1,5},{5,9},{9,... | collective-permute-start | bytes 688136 | tf_op jit(solution)/shard_map/ppermute | solution.py:140
  4.8 8.2 %collective-permute-start.1 = (bf16[7,128,128]{2,1,0:T(8,128)(2,1)S(1)}, bf16[7,128,128]{2,1,0:T(8,128)(2,1)S(1)}, u32[]{:S(2)}, u32[]{:S(2)}) collective-permute-start(bf16[7,128,128]{2,1,0:T(8,128)(2,1)S(1)} %get-tuple-element.28), channel_id=1, source_target_pairs={{4,0},{8,4},{12,8},{16,12},{20,16},{24,20},{28,24},{5,1},{9,5},{13... | collective-permute-start | bytes 688136 | tf_op jit(solution)/shard_map/ppermute | solution.py:143
  9.8 8.0 %copy-start.8 = (bf16[7,128,128]{2,1,0:T(8,128)(2,1)}, bf16[7,128,128]{2,1,0:T(8,128)(2,1)S(1)}, u32[]{:S(2)}) copy-start(bf16[7,128,128]{2,1,0:T(8,128)(2,1)S(1)} %collective-permute-done) | copy-start | bytes 688132
  13.1 4.7 %copy-start.9 = (bf16[7,128,128]{2,1,0:T(8,128)(2,1)}, bf16[7,128,128]{2,1,0:T(8,128)(2,1)S(1)}, u32[]{:S(2)}) copy-start(bf16[7,128,128]{2,1,0:T(8,128)(2,1)S(1)} %collective-permute-done.1) | copy-start | bytes 688132
  13.2 90.3 %collective-permute-start.2 = (bf16[78,7,128]{2,1,0:T(8,128)(2,1)S(1)}, bf16[78,7,128]{2,1,0:T(8,128)(2,1)S(1)}, u32[]{:S(2)}, u32[]{:S(2)}) collective-permute-start(bf16[78,7,128]{2,1,0:T(8,128)(2,1)S(1)} %pad_maximum_fusion.10), channel_id=1, source_target_pairs={{0,1},{1,2},{2,3},{4,5},{5,6},{6,7},{8,9},{9,10},{10,11},{12,13},{... | collective-permute-start | bytes 419336 | tf_op jit(solution)/shard_map/ppermute | solution.py:161
  16.4 87.2 %collective-permute-start.3 = (bf16[78,7,128]{2,1,0:T(8,128)(2,1)S(1)}, bf16[78,7,128]{2,1,0:T(8,128)(2,1)S(1)}, u32[]{:S(2)}, u32[]{:S(2)}) collective-permute-start(bf16[78,7,128]{2,1,0:T(8,128)(2,1)S(1)} %pad_maximum_fusion.11), channel_id=1, source_target_pairs={{1,0},{2,1},{3,2},{5,4},{6,5},{7,6},{9,8},{10,9},{11,10},{13,12},{... | collective-permute-start | bytes 419336 | tf_op jit(solution)/shard_map/ppermute | solution.py:162
  118.2 3.4 %copy-start.1 = (f32[1,64,112,128]{3,2,1,0:T(8,128)S(1)}, f32[1,64,112,128]{3,2,1,0:T(8,128)}, u32[]{:S(2)}) copy-start(f32[1,64,112,128]{3,2,1,0:T(8,128)} %shard_map.101) | copy-start | bytes 11010052
  121.6 2.7 %copy-start.14 = (bf16[512,128]{1,0:T(8,128)(2,1)S(1)}, bf16[512,128]{1,0:T(8,128)(2,1)}, u32[]{:S(2)}) copy-start(bf16[512,128]{1,0:T(8,128)(2,1)} %param.14) | copy-start | bytes 393220
  121.6 2.7 %copy-start.15 = (bf16[128,512]{1,0:T(8,128)(2,1)S(1)}, bf16[128,512]{1,0:T(8,128)(2,1)}, u32[]{:S(2)}) copy-start(bf16[128,512]{1,0:T(8,128)(2,1)} %param.13) | copy-start | bytes 393220
  124.3 13.2 %copy-start.13 = (f32[256]{0:T(256)S(1)}, f32[256]{0:T(256)}, u32[]{:S(2)}) copy-start(f32[256]{0:T(256)} %param.17) | copy-start | bytes 3076
  133.0 14.1 %copy-start.10 = (f32[15,15,256]{2,1,0:T(8,128)S(1)}, f32[15,15,256]{2,1,0:T(8,128)}, u32[]{:S(2)}) copy-start(f32[15,15,256]{2,1,0:T(8,128)} %param.16) | copy-start | bytes 691204
  133.0 4.5 %collective-permute-start.4 = (bf16[1,128,128]{2,1,0:T(8,128)(2,1)S(1)}, bf16[1,128,128]{2,1,0:T(8,128)(2,1)S(1)}, u32[]{:S(2)}, u32[]{:S(2)}) collective-permute-start(bf16[1,128,128]{2,1,0:T(8,128)(2,1)S(1)} %get-tuple-element.21), channel_id=1, source_target_pairs={{0,4},{4,8},{8,12},{12,16},{16,20},{20,24},{24,28},{1,5},{5,9},{9,... | collective-permute-start | bytes 98312 | tf_op jit(solution)/shard_map/ppermute | solution.py:16
  135.2 6.1 %collective-permute-start.5 = (bf16[1,128,128]{2,1,0:T(8,128)(2,1)S(1)}, bf16[1,128,128]{2,1,0:T(8,128)(2,1)S(1)}, u32[]{:S(2)}, u32[]{:S(2)}) collective-permute-start(bf16[1,128,128]{2,1,0:T(8,128)(2,1)S(1)} %get-tuple-element.22), channel_id=1, source_target_pairs={{4,0},{8,4},{12,8},{16,12},{20,16},{24,20},{28,24},{5,1},{9,5},{13... | collective-permute-start | bytes 98312 | tf_op jit(solution)/shard_map/ppermute | solution.py:19
  141.4 6.6 %collective-permute-start.6 = (bf16[66,1,128]{2,1,0:T(2,128)(2,1)S(1)}, bf16[66,1,128]{2,1,0:T(2,128)(2,1)S(1)}, u32[]{:S(2)}, u32[]{:S(2)}) collective-permute-start(bf16[66,1,128]{2,1,0:T(2,128)(2,1)S(1)} %get-tuple-element.17), channel_id=1, source_target_pairs={{0,1},{1,2},{2,3},{4,5},{5,6},{6,7},{8,9},{9,10},{10,11},{12,13},{... | collective-permute-start | bytes 50696 | tf_op jit(solution)/shard_map/ppermute | solution.py:16
  145.6 4.7 %collective-permute-start.7 = (bf16[66,1,128]{2,1,0:T(2,128)(2,1)S(1)}, bf16[66,1,128]{2,1,0:T(2,128)(2,1)S(1)}, u32[]{:S(2)}, u32[]{:S(2)}) collective-permute-start(bf16[66,1,128]{2,1,0:T(2,128)(2,1)S(1)} %get-tuple-element.18), channel_id=1, source_target_pairs={{1,0},{2,1},{3,2},{5,4},{6,5},{7,6},{9,8},{10,9},{11,10},{13,12},{... | collective-permute-start | bytes 50696 | tf_op jit(solution)/shard_map/ppermute | solution.py:19
  154.5 0.8 copy-start.12
  155.8 16.4 %copy-start.3 = (bf16[32,64,256]{2,1,0:T(8,128)(2,1)}, bf16[32,64,256]{2,1,0:T(8,128)(2,1)S(1)}, u32[]{:S(2)}) copy-start(bf16[32,64,256]{2,1,0:T(8,128)(2,1)S(1)} %convolution_convert_fusion) | copy-start | bytes 3145732
  155.9 7.4 %collective-permute-start.8 = (bf16[7,64,256]{2,1,0:T(8,128)(2,1)S(1)}, bf16[7,64,256]{2,1,0:T(8,128)(2,1)S(1)}, u32[]{:S(2)}, u32[]{:S(2)}) collective-permute-start(bf16[7,64,256]{2,1,0:T(8,128)(2,1)S(1)} %get-tuple-element.39), channel_id=1, source_target_pairs={{0,4},{4,8},{8,12},{12,16},{16,20},{20,24},{24,28},{1,5},{5,9},{9,... | collective-permute-start | bytes 688136 | tf_op jit(solution)/shard_map/ppermute | solution.py:140
  159.3 8.2 %collective-permute-start.9 = (bf16[7,64,256]{2,1,0:T(8,128)(2,1)S(1)}, bf16[7,64,256]{2,1,0:T(8,128)(2,1)S(1)}, u32[]{:S(2)}, u32[]{:S(2)}) collective-permute-start(bf16[7,64,256]{2,1,0:T(8,128)(2,1)S(1)} %get-tuple-element.40), channel_id=1, source_target_pairs={{4,0},{8,4},{12,8},{16,12},{20,16},{24,20},{28,24},{5,1},{9,5},{13... | collective-permute-start | bytes 688136 | tf_op jit(solution)/shard_map/ppermute | solution.py:143
  163.3 8.9 %copy-start.6 = (bf16[7,64,256]{2,1,0:T(8,128)(2,1)}, bf16[7,64,256]{2,1,0:T(8,128)(2,1)S(1)}, u32[]{:S(2)}) copy-start(bf16[7,64,256]{2,1,0:T(8,128)(2,1)S(1)} %collective-permute-done.8) | copy-start | bytes 688132
  167.5 4.7 %copy-start.7 = (bf16[7,64,256]{2,1,0:T(8,128)(2,1)}, bf16[7,64,256]{2,1,0:T(8,128)(2,1)S(1)}, u32[]{:S(2)}) copy-start(bf16[7,64,256]{2,1,0:T(8,128)(2,1)S(1)} %collective-permute-done.9) | copy-start | bytes 688132
  167.6 43.5 %collective-permute-start.10 = (bf16[46,7,256]{2,1,0:T(8,128)(2,1)S(1)}, bf16[46,7,256]{2,1,0:T(8,128)(2,1)S(1)}, u32[]{:S(2)}, u32[]{:S(2)}) collective-permute-start(bf16[46,7,256]{2,1,0:T(8,128)(2,1)S(1)} %pad_maximum_fusion.8), channel_id=1, source_target_pairs={{0,1},{1,2},{2,3},{4,5},{5,6},{6,7},{8,9},{9,10},{10,11},{12,13},{... | collective-permute-start | bytes 494600 | tf_op jit(solution)/shard_map/ppermute | solution.py:161
  170.8 40.5 %collective-permute-start.11 = (bf16[46,7,256]{2,1,0:T(8,128)(2,1)S(1)}, bf16[46,7,256]{2,1,0:T(8,128)(2,1)S(1)}, u32[]{:S(2)}, u32[]{:S(2)}) collective-permute-start(bf16[46,7,256]{2,1,0:T(8,128)(2,1)S(1)} %pad_maximum_fusion.9), channel_id=1, source_target_pairs={{1,0},{2,1},{3,2},{5,4},{6,5},{7,6},{9,8},{10,9},{11,10},{13,12},{... | collective-permute-start | bytes 494600 | tf_op jit(solution)/shard_map/ppermute | solution.py:162
  211.5 15.0 %copy-start.2 = (f32[1,32,48,256]{3,2,1,0:T(8,128)S(1)}, f32[1,32,48,256]{3,2,1,0:T(8,128)}, u32[]{:S(2)}) copy-start(f32[1,32,48,256]{3,2,1,0:T(8,128)} %shard_map.103) | copy-start | bytes 4718596
  226.5 0.7 copy-start.5
  226.5 1.4 copy-start.4
  234.1 4.3 %collective-permute-start.12 = (bf16[1,64,256]{2,1,0:T(8,128)(2,1)S(1)}, bf16[1,64,256]{2,1,0:T(8,128)(2,1)S(1)}, u32[]{:S(2)}, u32[]{:S(2)}) collective-permute-start(bf16[1,64,256]{2,1,0:T(8,128)(2,1)S(1)} %get-tuple-element.33), channel_id=1, source_target_pairs={{0,4},{4,8},{8,12},{12,16},{16,20},{20,24},{24,28},{1,5},{5,9},{9,... | collective-permute-start | bytes 98312 | tf_op jit(solution)/shard_map/ppermute | solution.py:16
  236.2 6.1 %collective-permute-start.13 = (bf16[1,64,256]{2,1,0:T(8,128)(2,1)S(1)}, bf16[1,64,256]{2,1,0:T(8,128)(2,1)S(1)}, u32[]{:S(2)}, u32[]{:S(2)}) collective-permute-start(bf16[1,64,256]{2,1,0:T(8,128)(2,1)S(1)} %get-tuple-element.34), channel_id=1, source_target_pairs={{4,0},{8,4},{12,8},{16,12},{20,16},{24,20},{28,24},{5,1},{9,5},{13... | collective-permute-start | bytes 98312 | tf_op jit(solution)/shard_map/ppermute | solution.py:19
  243.3 5.8 %collective-permute-start.14 = (bf16[34,1,256]{2,1,0:T(2,128)(2,1)S(1)}, bf16[34,1,256]{2,1,0:T(2,128)(2,1)S(1)}, u32[]{:S(2)}, u32[]{:S(2)}) collective-permute-start(bf16[34,1,256]{2,1,0:T(2,128)(2,1)S(1)} %get-tuple-element.29), channel_id=1, source_target_pairs={{0,1},{1,2},{2,3},{4,5},{5,6},{6,7},{8,9},{9,10},{10,11},{12,13},{... | collective-permute-start | bytes 52232 | tf_op jit(solution)/shard_map/ppermute | solution.py:16
  247.6 4.7 %collective-permute-start.15 = (bf16[34,1,256]{2,1,0:T(2,128)(2,1)S(1)}, bf16[34,1,256]{2,1,0:T(2,128)(2,1)S(1)}, u32[]{:S(2)}, u32[]{:S(2)}) collective-permute-start(bf16[34,1,256]{2,1,0:T(2,128)(2,1)S(1)} %get-tuple-element.30), channel_id=1, source_target_pairs={{1,0},{2,1},{3,2},{5,4},{6,5},{7,6},{9,8},{10,9},{11,10},{13,12},{... | collective-permute-start | bytes 52232 | tf_op jit(solution)/shard_map/ppermute | solution.py:19

commit v18 on v17

--- a/solution.py
+++ b/solution.py
@@ -34,7 +34,8 @@
     nlb = chans // 128
     njb = cols // 8
     nrb = rows // rb
-    spread = max(1, min(8, 64 // (njb * nlb)))
+    spread = max(1, min(16, 64 // (njb * nlb)))
+    deep = 2
 
     def one_strip(n, carry):
         o_ref = o_all.at[n]
@@ -92,7 +93,7 @@
                         o_ref[pl.ds(r0, rb), pl.ds(j0, 8), lanes] = acc
                         return c
 
-                    lax.fori_loop(0, nrb * njb, body, 0, unroll=2)
+                    lax.fori_loop(0, nrb * njb, body, 0, unroll=deep)
                 first = False
         return carry
 

time: 258 us -> 259 us (level)
  no operation moved by 1% of the time
where the time goes in v18:
time: 259 us; the launch traced here: 258 us
  Pallas kernels  151 us (58%)
  starting transfers between devices  40.1 us (15%)
  waiting for transfers between devices  22.7 us (9%)
  other arithmetic  19.1 us (7%)
  matrix products  14.5 us (6%)
  local copies, waits for them, and re-layouts  10.7 us (4%)
    pallas_call x4, Pallas kernels, depthwise(): pl.pallas_call(body, out_shape=jax.ShapeDtypeStruct((count, rows, cols, c...  151 us
    dot_general x2, matrix products, local_section(): mixed = jnp.dot(hidden, w_out, preferred_element_type=jnp.float32)  14.1 us
    ppermute x4, waiting for transfers between devices, padded_2(): lax.ppermute(lax.slice_in_dim(block, 0, width, axis=dim), axis, backward)  13.1 us
    ppermute x4, starting transfers between devices, padded_2(): lax.ppermute(lax.slice_in_dim(block, block.shape[dim] - width, None, axis...  12.7 us
    ppermute x4, starting transfers between devices, padded_2(): lax.ppermute(lax.slice_in_dim(block, 0, width, axis=dim), axis, backward)  7.58 us
    ppermute x2, waiting for transfers between devices, halos(): lax.ppermute(lax.slice_in_dim(block, 0, width, axis=dim), axis, backward)  7.46 us
    ppermute x2, starting transfers between devices, halos(): lax.ppermute(lax.slice_in_dim(block, block.shape[dim] - width, None, axis...  7.02 us
    ppermute x2, starting transfers between devices, section_conv(): left = lax.ppermute(tall_cols(cols - reach, cols), 'col', forward)  6.42 us
  transfers between devices with their start and end apart: 16, of which 7 were waited for; matrix products, arithmetic and copies ran while one was open for 2% of the time, Pallas kernels for 48%

profile of v18, /device:TPU:3, one launch (start us, length us, event | category | flops | bytes accessed | tf_op | source)
XLA Modules:
  0.0 258.4 jit_solution(2747089104059740472)
XLA Ops:
  0.0 1.1 fusion.87
  1.2 3.7 %collective-permute-start = (bf16[7,128,128]{2,1,0:T(8,128)(2,1)S(1)}, bf16[7,128,128]{2,1,0:T(8,128)(2,1)S(1)}, u32[]{:S(2)}, u32[]{:S(2)}) collective-permute-start(bf16[7,128,128]{2,1,0:T(8,128)(2,1)S(1)} %get-tuple-element.27), channel_id=1, source_target_pairs={{0,4},{4,8},{8,12},{12,16},{16,20},{20,24},{24,28},{1,5},{5,9},{9,... | collective-permute-start | bytes 688136 | tf_op jit(solution)/shard_map/ppermute | solution.py:141
  4.8 1.9 collective-permute-start.1
  6.8 1.0 fusion.85
  7.8 1.2 fusion.86
  9.0 0.8 fusion.64.refs_1_.refs_3_
  9.8 3.3 %collective-permute-done.1 = bf16[7,128,128]{2,1,0:T(8,128)(2,1)S(1)} collective-permute-done((bf16[7,128,128]{2,1,0:T(8,128)(2,1)S(1)}, bf16[7,128,128]{2,1,0:T(8,128)(2,1)S(1)}, u32[]{:S(2)}, u32[]{:S(2)}) %collective-permute-start.1) | collective-permute-done | bytes 229408 | tf_op jit(solution)/shard_map/ppermute | solution.py:144
  13.2 3.2 %collective-permute-start.2 = (bf16[78,7,128]{2,1,0:T(8,128)(2,1)S(1)}, bf16[78,7,128]{2,1,0:T(8,128)(2,1)S(1)}, u32[]{:S(2)}, u32[]{:S(2)}) collective-permute-start(bf16[78,7,128]{2,1,0:T(8,128)(2,1)S(1)} %pad_maximum_fusion.10), channel_id=1, source_target_pairs={{0,1},{1,2},{2,3},{4,5},{5,6},{6,7},{8,9},{9,10},{10,11},{12,13},{... | collective-permute-start | bytes 419336 | tf_op jit(solution)/shard_map/ppermute | solution.py:162
  16.4 1.3 collective-permute-start.3
  17.8 85.7 %shard_map.101 = f32[1,64,112,128]{3,2,1,0:T(8,128)} custom-call(bf16[1,7,128,128]{3,2,1,0:T(8,128)(2,1)} %bitcast.75, bf16[1,64,128,128]{3,2,1,0:T(8,128)(2,1)} %bitcast.70, bf16[1,7,128,128]{3,2,1,0:T(8,128)(2,1)} %bitcast.76, f32[15,15,128]{2,1,0:T(8,128)} %fusion.64.refs_1_.refs_3_), custom_call_target="tpu_custom_call" | custom-call | flops 412876800 | bytes 6225920 | tf_op jit(solution)/shard_map/pallas_call | solution.py:120
  103.4 0.2 maximum_bitcast_fusion.2
  103.6 0.2 maximum_bitcast_fusion.3
  103.8 1.1 pad_maximum_fusion.5.refs_0_
  104.9 12.8 %shard_map.100 = f32[2,64,8,128]{3,2,1,0:T(8,128)} custom-call(bf16[2,78,22,128]{3,2,1,0:T(8,128)(2,1)} %pad_maximum_fusion.5.refs_0_, f32[15,15,128]{2,1,0:T(8,128)} %fusion.64.refs_1_.refs_3_), custom_call_target="tpu_custom_call" | custom-call | flops 58982400 | bytes 1402880 | tf_op jit(solution)/shard_map/pallas_call | solution.py:120
  117.7 1.1 slice_bitcast_fusion.3
  118.7 3.3 %fusion.29 = f32[64,128]{1,0:T(8,128)S(1)} fusion(f32[64,8,128]{2,1,0:T(8,128)S(1)} %get-tuple-element.44, f32[64,112,128]{2,1,0:T(8,128)} %bitcast.57, f32[64,8,128]{2,1,0:T(8,128)S(1)} %get-tuple-element.43), kind=kLoop, calls=%fused_computation.39 | loop fusion | flops 3137536 | bytes 4227072 | tf_op jit(solution)/shard_map/reduce_sum | solution.py:178
  122.1 2.6 %multiply_reduce_fusion = f32[64,128]{1,0:T(8,128)S(1)} fusion(f32[64,128]{1,0:T(8,128)S(1)} %broadcast_multiply_fusion, f32[64,8,128]{2,1,0:T(8,128)S(1)} %get-tuple-element.44, f32[64,112,128]{2,1,0:T(8,128)S(1)} %bitcast.59, f32[64,8,128]{2,1,0:T(8,128)S(1)} %get-tuple-element.43), kind=kLoop, calls=%fused_computation.21 | loop fusion | flops 5234688 | bytes 4259840 | tf_op jit(solution)/shard_map/reduce_sum | solution.py:179
  124.8 8.7 %add_convert_fusion = bf16[64,128,128]{2,1,0:T(8,128)(2,1)S(1)} fusion(bf16[64,128,128]{2,1,0:T(8,128)(2,1)} %param.10, f32[64,128]{1,0:T(8,128)S(1)} %add_rsqrt_fusion, f32[64,128]{1,0:T(8,128)S(1)} %broadcast_multiply_fusion, f32[64,8,128]{2,1,0:T(8,128)S(1)} %get-tuple-element.44, f32[64,112,128]{2,1,0:T(8,128)} %bitcast.58, ...), kind=kOutput, calls=%fused_computation.19 | convolution fusion | flops 2193620992 | bytes 8716288 | tf_op jit(solution)/shard_map/dot_general | solution.py:184
  133.5 2.2 collective-permute-start.4
  135.7 2.3 collective-permute-start.5
  138.0 3.8 %collective-permute-done.5 = bf16[1,128,128]{2,1,0:T(8,128)(2,1)S(1)} collective-permute-done((bf16[1,128,128]{2,1,0:T(8,128)(2,1)S(1)}, bf16[1,128,128]{2,1,0:T(8,128)(2,1)S(1)}, u32[]{:S(2)}, u32[]{:S(2)}) %collective-permute-start.5) | collective-permute-done | bytes 32800 | tf_op jit(solution)/shard_map/ppermute | solution.py:19
  141.8 4.3 %collective-permute-start.6 = (bf16[66,1,128]{2,1,0:T(2,128)(2,1)S(1)}, bf16[66,1,128]{2,1,0:T(2,128)(2,1)S(1)}, u32[]{:S(2)}, u32[]{:S(2)}) collective-permute-start(bf16[66,1,128]{2,1,0:T(2,128)(2,1)S(1)} %get-tuple-element.17), channel_id=1, source_target_pairs={{0,1},{1,2},{2,3},{4,5},{5,6},{6,7},{8,9},{9,10},{10,11},{12,13},{... | collective-permute-start | bytes 50696 | tf_op jit(solution)/shard_map/ppermute | solution.py:16
  146.1 1.5 collective-permute-start.7
  147.6 0.8 fusion.62.refs_1_.refs_3_
  148.4 2.4 collective-permute-done.7
  150.8 0.8 maximum_convert_fusion
  151.6 0.6 fusion.77
  152.2 0.6 fusion.78
  152.8 1.6 fusion.22
  154.4 0.6 fusion.83
  155.0 0.5 fusion.53
  155.5 0.3 copy-done.12
  155.8 0.4 convolution_convert_fusion
  156.4 3.3 %collective-permute-start.8 = (bf16[7,64,256]{2,1,0:T(8,128)(2,1)S(1)}, bf16[7,64,256]{2,1,0:T(8,128)(2,1)S(1)}, u32[]{:S(2)}, u32[]{:S(2)}) collective-permute-start(bf16[7,64,256]{2,1,0:T(8,128)(2,1)S(1)} %get-tuple-element.39), channel_id=1, source_target_pairs={{0,4},{4,8},{8,12},{12,16},{16,20},{20,24},{24,28},{1,5},{5,9},{9,... | collective-permute-start | bytes 688136 | tf_op jit(solution)/shard_map/ppermute | solution.py:141
  159.7 1.9 collective-permute-start.9
  161.7 2.1 collective-permute-done.8
  163.8 4.2 %collective-permute-done.9 = bf16[7,64,256]{2,1,0:T(8,128)(2,1)S(1)} collective-permute-done((bf16[7,64,256]{2,1,0:T(8,128)(2,1)S(1)}, bf16[7,64,256]{2,1,0:T(8,128)(2,1)S(1)}, u32[]{:S(2)}, u32[]{:S(2)}) %collective-permute-start.9) | collective-permute-done | bytes 229408 | tf_op jit(solution)/shard_map/ppermute | solution.py:144
  168.0 3.2 %collective-permute-start.10 = (bf16[46,7,256]{2,1,0:T(8,128)(2,1)S(1)}, bf16[46,7,256]{2,1,0:T(8,128)(2,1)S(1)}, u32[]{:S(2)}, u32[]{:S(2)}) collective-permute-start(bf16[46,7,256]{2,1,0:T(8,128)(2,1)S(1)} %pad_maximum_fusion.8), channel_id=1, source_target_pairs={{0,1},{1,2},{2,3},{4,5},{5,6},{6,7},{8,9},{9,10},{10,11},{12,13},{... | collective-permute-start | bytes 494600 | tf_op jit(solution)/shard_map/ppermute | solution.py:162
  171.3 1.3 collective-permute-start.11
  172.7 38.9 %shard_map.103 = f32[1,32,48,256]{3,2,1,0:T(8,128)} custom-call(bf16[1,7,64,256]{3,2,1,0:T(8,128)(2,1)} %bitcast.73, bf16[1,32,64,256]{3,2,1,0:T(8,128)(2,1)} %bitcast.65, bf16[1,7,64,256]{3,2,1,0:T(8,128)(2,1)} %bitcast.74, f32[15,15,256]{2,1,0:T(8,128)} %fusion.62.refs_1_.refs_3_), custom_call_target="tpu_custom_call" | custom-call | flops 176947200 | bytes 3080192 | tf_op jit(solution)/shard_map/pallas_call | solution.py:120
  211.6 0.2 maximum_bitcast_fusion
  212.0 1.1 pad_maximum_fusion.4.refs_0_
  213.1 13.2 %shard_map.102 = f32[2,32,8,256]{3,2,1,0:T(8,128)} custom-call(bf16[2,46,22,256]{3,2,1,0:T(8,128)(2,1)} %pad_maximum_fusion.4.refs_0_, f32[15,15,256]{2,1,0:T(8,128)} %fusion.62.refs_1_.refs_3_), custom_call_target="tpu_custom_call" | custom-call | flops 58982400 | bytes 1560576 | tf_op jit(solution)/shard_map/pallas_call | solution.py:120
  226.3 1.1 slice_bitcast_fusion.1
  227.4 0.4 fusion.44
  227.8 0.3 copy-done.5
  228.1 0.6 multiply_reduce_fusion.1
  228.8 5.4 %add_convert_fusion.1 = bf16[32,64,256]{2,1,0:T(8,128)(2,1)} fusion(bf16[32,64,256]{2,1,0:T(8,128)(2,1)S(1)} %copy-done.4, f32[32,64]{1,0:T(8,128)S(1)} %add_rsqrt_fusion.1, f32[32,64]{1,0:T(8,128)S(1)} %broadcast_multiply_fusion.1, f32[32,8,256]{2,1,0:T(8,128)} %copy-done.5, f32[32,48,256]{2,1,0:T(8,128)S(1)} %bitcast.64, ...), kind=kOutput, calls=%fused_computation.34 | convolution fusion | flops 2170552320 | bytes 5259264 | tf_op jit(solution)/shard_map/dot_general | solution.py:184
  234.2 0.8 fusion.89
  235.0 2.0 collective-permute-start.12
  237.0 2.3 collective-permute-start.13
  239.4 3.8 %collective-permute-done.13 = bf16[1,64,256]{2,1,0:T(8,128)(2,1)S(1)} collective-permute-done((bf16[1,64,256]{2,1,0:T(8,128)(2,1)S(1)}, bf16[1,64,256]{2,1,0:T(8,128)(2,1)S(1)}, u32[]{:S(2)}, u32[]{:S(2)}) %collective-permute-start.13) | collective-permute-done | bytes 32800 | tf_op jit(solution)/shard_map/ppermute | solution.py:19
  243.2 1.0 pad_maximum_fusion.14
  244.2 4.3 %collective-permute-start.14 = (bf16[34,1,256]{2,1,0:T(2,128)(2,1)S(1)}, bf16[34,1,256]{2,1,0:T(2,128)(2,1)S(1)}, u32[]{:S(2)}, u32[]{:S(2)}) collective-permute-start(bf16[34,1,256]{2,1,0:T(2,128)(2,1)S(1)} %get-tuple-element.29), channel_id=1, source_target_pairs={{0,1},{1,2},{2,3},{4,5},{5,6},{6,7},{8,9},{9,10},{10,11},{12,13},{... | collective-permute-start | bytes 52232 | tf_op jit(solution)/shard_map/ppermute | solution.py:16
  248.5 1.5 collective-permute-start.15
  250.0 3.1 %collective-permute-done.15 = bf16[34,1,256]{2,1,0:T(2,128)(2,1)S(1)} collective-permute-done((bf16[34,1,256]{2,1,0:T(2,128)(2,1)S(1)}, bf16[34,1,256]{2,1,0:T(2,128)(2,1)S(1)}, u32[]{:S(2)}, u32[]{:S(2)}) %collective-permute-start.15) | collective-permute-done | bytes 17440 | tf_op jit(solution)/shard_map/ppermute | solution.py:19
  253.2 1.8 maximum_convert_fusion.1
  254.9 0.4 fusion.80
  255.3 0.2 fusion.81
  255.5 0.2 fusion.82
  255.7 1.4 fusion.33
  257.1 0.3 fusion.88
  257.4 0.2 fusion.54
  257.6 0.8 copy.20
  (67 shorter events, 0.8 us)
Async XLA Ops:
  0.0 228.8 %copy-start = (bf16[1024,256]{1,0:T(8,128)(2,1)S(1)}, bf16[1024,256]{1,0:T(8,128)(2,1)}, u32[]{:S(2)}) copy-start(bf16[1024,256]{1,0:T(8,128)(2,1)} %param.19) | copy-start | bytes 1572868
  0.0 9.0 %copy-start.16 = (f32[128]{0:T(128)S(1)}, f32[128]{0:T(128)}, u32[]{:S(2)}) copy-start(f32[128]{0:T(128)} %param.12) | copy-start | bytes 1540
  0.0 9.0 %copy-start.11 = (f32[15,15,128]{2,1,0:T(8,128)S(1)}, f32[15,15,128]{2,1,0:T(8,128)}, u32[]{:S(2)}) copy-start(f32[15,15,128]{2,1,0:T(8,128)} %param.11) | copy-start | bytes 345604
  1.2 8.6 %collective-permute-start = (bf16[7,128,128]{2,1,0:T(8,128)(2,1)S(1)}, bf16[7,128,128]{2,1,0:T(8,128)(2,1)S(1)}, u32[]{:S(2)}, u32[]{:S(2)}) collective-permute-start(bf16[7,128,128]{2,1,0:T(8,128)(2,1)S(1)} %get-tuple-element.27), channel_id=1, source_target_pairs={{0,4},{4,8},{8,12},{12,16},{16,20},{20,24},{24,28},{1,5},{5,9},{9,... | collective-permute-start | bytes 688136 | tf_op jit(solution)/shard_map/ppermute | solution.py:141
  4.8 8.2 %collective-permute-start.1 = (bf16[7,128,128]{2,1,0:T(8,128)(2,1)S(1)}, bf16[7,128,128]{2,1,0:T(8,128)(2,1)S(1)}, u32[]{:S(2)}, u32[]{:S(2)}) collective-permute-start(bf16[7,128,128]{2,1,0:T(8,128)(2,1)S(1)} %get-tuple-element.28), channel_id=1, source_target_pairs={{4,0},{8,4},{12,8},{16,12},{20,16},{24,20},{28,24},{5,1},{9,5},{13... | collective-permute-start | bytes 688136 | tf_op jit(solution)/shard_map/ppermute | solution.py:144
  9.8 8.0 %copy-start.8 = (bf16[7,128,128]{2,1,0:T(8,128)(2,1)}, bf16[7,128,128]{2,1,0:T(8,128)(2,1)S(1)}, u32[]{:S(2)}) copy-start(bf16[7,128,128]{2,1,0:T(8,128)(2,1)S(1)} %collective-permute-done) | copy-start | bytes 688132
  13.1 4.7 %copy-start.9 = (bf16[7,128,128]{2,1,0:T(8,128)(2,1)}, bf16[7,128,128]{2,1,0:T(8,128)(2,1)S(1)}, u32[]{:S(2)}) copy-start(bf16[7,128,128]{2,1,0:T(8,128)(2,1)S(1)} %collective-permute-done.1) | copy-start | bytes 688132
  13.2 90.3 %collective-permute-start.2 = (bf16[78,7,128]{2,1,0:T(8,128)(2,1)S(1)}, bf16[78,7,128]{2,1,0:T(8,128)(2,1)S(1)}, u32[]{:S(2)}, u32[]{:S(2)}) collective-permute-start(bf16[78,7,128]{2,1,0:T(8,128)(2,1)S(1)} %pad_maximum_fusion.10), channel_id=1, source_target_pairs={{0,1},{1,2},{2,3},{4,5},{5,6},{6,7},{8,9},{9,10},{10,11},{12,13},{... | collective-permute-start | bytes 419336 | tf_op jit(solution)/shard_map/ppermute | solution.py:162
  16.4 87.2 %collective-permute-start.3 = (bf16[78,7,128]{2,1,0:T(8,128)(2,1)S(1)}, bf16[78,7,128]{2,1,0:T(8,128)(2,1)S(1)}, u32[]{:S(2)}, u32[]{:S(2)}) collective-permute-start(bf16[78,7,128]{2,1,0:T(8,128)(2,1)S(1)} %pad_maximum_fusion.11), channel_id=1, source_target_pairs={{1,0},{2,1},{3,2},{5,4},{6,5},{7,6},{9,8},{10,9},{11,10},{13,12},{... | collective-permute-start | bytes 419336 | tf_op jit(solution)/shard_map/ppermute | solution.py:163
  118.7 3.4 %copy-start.1 = (f32[1,64,112,128]{3,2,1,0:T(8,128)S(1)}, f32[1,64,112,128]{3,2,1,0:T(8,128)}, u32[]{:S(2)}) copy-start(f32[1,64,112,128]{3,2,1,0:T(8,128)} %shard_map.101) | copy-start | bytes 11010052
  122.1 2.7 %copy-start.14 = (bf16[512,128]{1,0:T(8,128)(2,1)S(1)}, bf16[512,128]{1,0:T(8,128)(2,1)}, u32[]{:S(2)}) copy-start(bf16[512,128]{1,0:T(8,128)(2,1)} %param.14) | copy-start | bytes 393220
  122.1 2.7 %copy-start.15 = (bf16[128,512]{1,0:T(8,128)(2,1)S(1)}, bf16[128,512]{1,0:T(8,128)(2,1)}, u32[]{:S(2)}) copy-start(bf16[128,512]{1,0:T(8,128)(2,1)} %param.13) | copy-start | bytes 393220
  124.8 13.2 %copy-start.13 = (f32[256]{0:T(256)S(1)}, f32[256]{0:T(256)}, u32[]{:S(2)}) copy-start(f32[256]{0:T(256)} %param.17) | copy-start | bytes 3076
  133.5 14.1 %copy-start.10 = (f32[15,15,256]{2,1,0:T(8,128)S(1)}, f32[15,15,256]{2,1,0:T(8,128)}, u32[]{:S(2)}) copy-start(f32[15,15,256]{2,1,0:T(8,128)} %param.16) | copy-start | bytes 691204
  133.5 4.5 %collective-permute-start.4 = (bf16[1,128,128]{2,1,0:T(8,128)(2,1)S(1)}, bf16[1,128,128]{2,1,0:T(8,128)(2,1)S(1)}, u32[]{:S(2)}, u32[]{:S(2)}) collective-permute-start(bf16[1,128,128]{2,1,0:T(8,128)(2,1)S(1)} %get-tuple-element.21), channel_id=1, source_target_pairs={{0,4},{4,8},{8,12},{12,16},{16,20},{20,24},{24,28},{1,5},{5,9},{9,... | collective-permute-start | bytes 98312 | tf_op jit(solution)/shard_map/ppermute | solution.py:16
  135.7 6.1 %collective-permute-start.5 = (bf16[1,128,128]{2,1,0:T(8,128)(2,1)S(1)}, bf16[1,128,128]{2,1,0:T(8,128)(2,1)S(1)}, u32[]{:S(2)}, u32[]{:S(2)}) collective-permute-start(bf16[1,128,128]{2,1,0:T(8,128)(2,1)S(1)} %get-tuple-element.22), channel_id=1, source_target_pairs={{4,0},{8,4},{12,8},{16,12},{20,16},{24,20},{28,24},{5,1},{9,5},{13... | collective-permute-start | bytes 98312 | tf_op jit(solution)/shard_map/ppermute | solution.py:19
  141.8 6.6 %collective-permute-start.6 = (bf16[66,1,128]{2,1,0:T(2,128)(2,1)S(1)}, bf16[66,1,128]{2,1,0:T(2,128)(2,1)S(1)}, u32[]{:S(2)}, u32[]{:S(2)}) collective-permute-start(bf16[66,1,128]{2,1,0:T(2,128)(2,1)S(1)} %get-tuple-element.17), channel_id=1, source_target_pairs={{0,1},{1,2},{2,3},{4,5},{5,6},{6,7},{8,9},{9,10},{10,11},{12,13},{... | collective-permute-start | bytes 50696 | tf_op jit(solution)/shard_map/ppermute | solution.py:16
  146.1 4.7 %collective-permute-start.7 = (bf16[66,1,128]{2,1,0:T(2,128)(2,1)S(1)}, bf16[66,1,128]{2,1,0:T(2,128)(2,1)S(1)}, u32[]{:S(2)}, u32[]{:S(2)}) collective-permute-start(bf16[66,1,128]{2,1,0:T(2,128)(2,1)S(1)} %get-tuple-element.18), channel_id=1, source_target_pairs={{1,0},{2,1},{3,2},{5,4},{6,5},{7,6},{9,8},{10,9},{11,10},{13,12},{... | collective-permute-start | bytes 50696 | tf_op jit(solution)/shard_map/ppermute | solution.py:19
  155.0 0.8 copy-start.12
  156.3 16.4 %copy-start.3 = (bf16[32,64,256]{2,1,0:T(8,128)(2,1)}, bf16[32,64,256]{2,1,0:T(8,128)(2,1)S(1)}, u32[]{:S(2)}) copy-start(bf16[32,64,256]{2,1,0:T(8,128)(2,1)S(1)} %convolution_convert_fusion) | copy-start | bytes 3145732
  156.4 7.4 %collective-permute-start.8 = (bf16[7,64,256]{2,1,0:T(8,128)(2,1)S(1)}, bf16[7,64,256]{2,1,0:T(8,128)(2,1)S(1)}, u32[]{:S(2)}, u32[]{:S(2)}) collective-permute-start(bf16[7,64,256]{2,1,0:T(8,128)(2,1)S(1)} %get-tuple-element.39), channel_id=1, source_target_pairs={{0,4},{4,8},{8,12},{12,16},{16,20},{20,24},{24,28},{1,5},{5,9},{9,... | collective-permute-start | bytes 688136 | tf_op jit(solution)/shard_map/ppermute | solution.py:141
  159.7 8.2 %collective-permute-start.9 = (bf16[7,64,256]{2,1,0:T(8,128)(2,1)S(1)}, bf16[7,64,256]{2,1,0:T(8,128)(2,1)S(1)}, u32[]{:S(2)}, u32[]{:S(2)}) collective-permute-start(bf16[7,64,256]{2,1,0:T(8,128)(2,1)S(1)} %get-tuple-element.40), channel_id=1, source_target_pairs={{4,0},{8,4},{12,8},{16,12},{20,16},{24,20},{28,24},{5,1},{9,5},{13... | collective-permute-start | bytes 688136 | tf_op jit(solution)/shard_map/ppermute | solution.py:144
  163.8 8.9 %copy-start.6 = (bf16[7,64,256]{2,1,0:T(8,128)(2,1)}, bf16[7,64,256]{2,1,0:T(8,128)(2,1)S(1)}, u32[]{:S(2)}) copy-start(bf16[7,64,256]{2,1,0:T(8,128)(2,1)S(1)} %collective-permute-done.8) | copy-start | bytes 688132
  168.0 4.7 %copy-start.7 = (bf16[7,64,256]{2,1,0:T(8,128)(2,1)}, bf16[7,64,256]{2,1,0:T(8,128)(2,1)S(1)}, u32[]{:S(2)}) copy-start(bf16[7,64,256]{2,1,0:T(8,128)(2,1)S(1)} %collective-permute-done.9) | copy-start | bytes 688132
  168.0 43.5 %collective-permute-start.10 = (bf16[46,7,256]{2,1,0:T(8,128)(2,1)S(1)}, bf16[46,7,256]{2,1,0:T(8,128)(2,1)S(1)}, u32[]{:S(2)}, u32[]{:S(2)}) collective-permute-start(bf16[46,7,256]{2,1,0:T(8,128)(2,1)S(1)} %pad_maximum_fusion.8), channel_id=1, source_target_pairs={{0,1},{1,2},{2,3},{4,5},{5,6},{6,7},{8,9},{9,10},{10,11},{12,13},{... | collective-permute-start | bytes 494600 | tf_op jit(solution)/shard_map/ppermute | solution.py:162
  171.3 40.5 %collective-permute-start.11 = (bf16[46,7,256]{2,1,0:T(8,128)(2,1)S(1)}, bf16[46,7,256]{2,1,0:T(8,128)(2,1)S(1)}, u32[]{:S(2)}, u32[]{:S(2)}) collective-permute-start(bf16[46,7,256]{2,1,0:T(8,128)(2,1)S(1)} %pad_maximum_fusion.9), channel_id=1, source_target_pairs={{1,0},{2,1},{3,2},{5,4},{6,5},{7,6},{9,8},{10,9},{11,10},{13,12},{... | collective-permute-start | bytes 494600 | tf_op jit(solution)/shard_map/ppermute | solution.py:163
  212.0 15.4 %copy-start.2 = (f32[1,32,48,256]{3,2,1,0:T(8,128)S(1)}, f32[1,32,48,256]{3,2,1,0:T(8,128)}, u32[]{:S(2)}) copy-start(f32[1,32,48,256]{3,2,1,0:T(8,128)} %shard_map.103) | copy-start | bytes 4718596
  227.4 0.7 copy-start.5
  227.4 1.4 copy-start.4
  235.0 4.3 %collective-permute-start.12 = (bf16[1,64,256]{2,1,0:T(8,128)(2,1)S(1)}, bf16[1,64,256]{2,1,0:T(8,128)(2,1)S(1)}, u32[]{:S(2)}, u32[]{:S(2)}) collective-permute-start(bf16[1,64,256]{2,1,0:T(8,128)(2,1)S(1)} %get-tuple-element.33), channel_id=1, source_target_pairs={{0,4},{4,8},{8,12},{12,16},{16,20},{20,24},{24,28},{1,5},{5,9},{9,... | collective-permute-start | bytes 98312 | tf_op jit(solution)/shard_map/ppermute | solution.py:16
  237.0 6.1 %collective-permute-start.13 = (bf16[1,64,256]{2,1,0:T(8,128)(2,1)S(1)}, bf16[1,64,256]{2,1,0:T(8,128)(2,1)S(1)}, u32[]{:S(2)}, u32[]{:S(2)}) collective-permute-start(bf16[1,64,256]{2,1,0:T(8,128)(2,1)S(1)} %get-tuple-element.34), channel_id=1, source_target_pairs={{4,0},{8,4},{12,8},{16,12},{20,16},{24,20},{28,24},{5,1},{9,5},{13... | collective-permute-start | bytes 98312 | tf_op jit(solution)/shard_map/ppermute | solution.py:19
  244.2 5.8 %collective-permute-start.14 = (bf16[34,1,256]{2,1,0:T(2,128)(2,1)S(1)}, bf16[34,1,256]{2,1,0:T(2,128)(2,1)S(1)}, u32[]{:S(2)}, u32[]{:S(2)}) collective-permute-start(bf16[34,1,256]{2,1,0:T(2,128)(2,1)S(1)} %get-tuple-element.29), channel_id=1, source_target_pairs={{0,1},{1,2},{2,3},{4,5},{5,6},{6,7},{8,9},{9,10},{10,11},{12,13},{... | collective-permute-start | bytes 52232 | tf_op jit(solution)/shard_map/ppermute | solution.py:16
  248.5 4.7 %collective-permute-start.15 = (bf16[34,1,256]{2,1,0:T(2,128)(2,1)S(1)}, bf16[34,1,256]{2,1,0:T(2,128)(2,1)S(1)}, u32[]{:S(2)}, u32[]{:S(2)}) collective-permute-start(bf16[34,1,256]{2,1,0:T(2,128)(2,1)S(1)} %get-tuple-element.30), channel_id=1, source_target_pairs={{1,0},{2,1},{3,2},{5,4},{6,5},{7,6},{9,8},{10,9},{11,10},{13,12},{... | collective-permute-start | bytes 52232 | tf_op jit(solution)/shard_map/ppermute | solution.py:19

commit v19 on v17

--- a/solution.py
+++ b/solution.py
@@ -34,7 +34,7 @@
     nlb = chans // 128
     njb = cols // 8
     nrb = rows // rb
-    spread = max(1, min(8, 64 // (njb * nlb)))
+    spread = max(1, min(8, 128 // (njb * nlb)))
 
     def one_strip(n, carry):
         o_ref = o_all.at[n]

time: 258 us -> 258 us (level)
  no operation moved by 1% of the time
where the time goes in v19:
time: 258 us
  Pallas kernels  150 us (58%)
  starting transfers between devices  40.2 us (16%)
  waiting for transfers between devices  22.7 us (9%)
  other arithmetic  19.1 us (7%)
  matrix products  14.5 us (6%)
  local copies, waits for them, and re-layouts  10.7 us (4%)
    pallas_call x4, Pallas kernels, depthwise(): pl.pallas_call(body, out_shape=jax.ShapeDtypeStruct((count, rows, cols, c...  150 us
    dot_general x2, matrix products, local_section(): mixed = jnp.dot(hidden, w_out, preferred_element_type=jnp.float32)  14.1 us
    ppermute x4, waiting for transfers between devices, padded_2(): lax.ppermute(lax.slice_in_dim(block, 0, width, axis=dim), axis, backward)  13.1 us
    ppermute x4, starting transfers between devices, padded_2(): lax.ppermute(lax.slice_in_dim(block, block.shape[dim] - width, None, axis...  12.7 us
    ppermute x4, starting transfers between devices, padded_2(): lax.ppermute(lax.slice_in_dim(block, 0, width, axis=dim), axis, backward)  7.58 us
    ppermute x2, waiting for transfers between devices, halos(): lax.ppermute(lax.slice_in_dim(block, 0, width, axis=dim), axis, backward)  7.44 us
    ppermute x2, starting transfers between devices, halos(): lax.ppermute(lax.slice_in_dim(block, block.shape[dim] - width, None, axis...  7.02 us
    ppermute x2, starting transfers between devices, section_conv(): left = lax.ppermute(tall_cols(cols - reach, cols), 'col', forward)  6.41 us
  transfers between devices with their start and end apart: 16, of which 7 were waited for; matrix products, arithmetic and copies ran while one was open for 2% of the time, Pallas kernels for 48%

profile of v19, /device:TPU:3, one launch (start us, length us, event | category | flops | bytes accessed | tf_op | source)
XLA Modules:
  0.0 257.5 jit_solution(12901680740530466406)
XLA Ops:
  0.0 1.1 fusion.87
  1.2 3.7 %collective-permute-start = (bf16[7,128,128]{2,1,0:T(8,128)(2,1)S(1)}, bf16[7,128,128]{2,1,0:T(8,128)(2,1)S(1)}, u32[]{:S(2)}, u32[]{:S(2)}) collective-permute-start(bf16[7,128,128]{2,1,0:T(8,128)(2,1)S(1)} %get-tuple-element.27), channel_id=1, source_target_pairs={{0,4},{4,8},{8,12},{12,16},{16,20},{20,24},{24,28},{1,5},{5,9},{9,... | collective-permute-start | bytes 688136 | tf_op jit(solution)/shard_map/ppermute | solution.py:140
  4.8 1.9 collective-permute-start.1
  6.8 1.0 fusion.85
  7.8 1.2 fusion.86
  9.0 0.8 fusion.64.refs_1_.refs_3_
  9.8 3.3 %collective-permute-done.1 = bf16[7,128,128]{2,1,0:T(8,128)(2,1)S(1)} collective-permute-done((bf16[7,128,128]{2,1,0:T(8,128)(2,1)S(1)}, bf16[7,128,128]{2,1,0:T(8,128)(2,1)S(1)}, u32[]{:S(2)}, u32[]{:S(2)}) %collective-permute-start.1) | collective-permute-done | bytes 229408 | tf_op jit(solution)/shard_map/ppermute | solution.py:143
  13.2 3.2 %collective-permute-start.2 = (bf16[78,7,128]{2,1,0:T(8,128)(2,1)S(1)}, bf16[78,7,128]{2,1,0:T(8,128)(2,1)S(1)}, u32[]{:S(2)}, u32[]{:S(2)}) collective-permute-start(bf16[78,7,128]{2,1,0:T(8,128)(2,1)S(1)} %pad_maximum_fusion.10), channel_id=1, source_target_pairs={{0,1},{1,2},{2,3},{4,5},{5,6},{6,7},{8,9},{9,10},{10,11},{12,13},{... | collective-permute-start | bytes 419336 | tf_op jit(solution)/shard_map/ppermute | solution.py:161
  16.4 1.3 collective-permute-start.3
  17.8 85.6 %shard_map.101 = f32[1,64,112,128]{3,2,1,0:T(8,128)} custom-call(bf16[1,7,128,128]{3,2,1,0:T(8,128)(2,1)} %bitcast.75, bf16[1,64,128,128]{3,2,1,0:T(8,128)(2,1)} %bitcast.70, bf16[1,7,128,128]{3,2,1,0:T(8,128)(2,1)} %bitcast.76, f32[15,15,128]{2,1,0:T(8,128)} %fusion.64.refs_1_.refs_3_), custom_call_target="tpu_custom_call" | custom-call | flops 412876800 | bytes 6225920 | tf_op jit(solution)/shard_map/pallas_call | solution.py:119
  103.4 0.2 maximum_bitcast_fusion.2
  103.6 0.2 maximum_bitcast_fusion.3
  103.7 1.1 pad_maximum_fusion.5.refs_0_
  104.8 12.3 %shard_map.100 = f32[2,64,8,128]{3,2,1,0:T(8,128)} custom-call(bf16[2,78,22,128]{3,2,1,0:T(8,128)(2,1)} %pad_maximum_fusion.5.refs_0_, f32[15,15,128]{2,1,0:T(8,128)} %fusion.64.refs_1_.refs_3_), custom_call_target="tpu_custom_call" | custom-call | flops 58982400 | bytes 1402880 | tf_op jit(solution)/shard_map/pallas_call | solution.py:119
  117.1 1.1 slice_bitcast_fusion.3
  118.2 3.3 %fusion.29 = f32[64,128]{1,0:T(8,128)S(1)} fusion(f32[64,8,128]{2,1,0:T(8,128)S(1)} %get-tuple-element.44, f32[64,112,128]{2,1,0:T(8,128)} %bitcast.57, f32[64,8,128]{2,1,0:T(8,128)S(1)} %get-tuple-element.43), kind=kLoop, calls=%fused_computation.39 | loop fusion | flops 3137536 | bytes 4227072 | tf_op jit(solution)/shard_map/reduce_sum | solution.py:177
  121.6 2.6 %multiply_reduce_fusion = f32[64,128]{1,0:T(8,128)S(1)} fusion(f32[64,128]{1,0:T(8,128)S(1)} %broadcast_multiply_fusion, f32[64,8,128]{2,1,0:T(8,128)S(1)} %get-tuple-element.44, f32[64,112,128]{2,1,0:T(8,128)S(1)} %bitcast.59, f32[64,8,128]{2,1,0:T(8,128)S(1)} %get-tuple-element.43), kind=kLoop, calls=%fused_computation.21 | loop fusion | flops 5234688 | bytes 4259840 | tf_op jit(solution)/shard_map/reduce_sum | solution.py:178
  124.2 8.6 %add_convert_fusion = bf16[64,128,128]{2,1,0:T(8,128)(2,1)S(1)} fusion(bf16[64,128,128]{2,1,0:T(8,128)(2,1)} %param.10, f32[64,128]{1,0:T(8,128)S(1)} %add_rsqrt_fusion, f32[64,128]{1,0:T(8,128)S(1)} %broadcast_multiply_fusion, f32[64,8,128]{2,1,0:T(8,128)S(1)} %get-tuple-element.44, f32[64,112,128]{2,1,0:T(8,128)} %bitcast.58, ...), kind=kOutput, calls=%fused_computation.19 | convolution fusion | flops 2193620992 | bytes 8716288 | tf_op jit(solution)/shard_map/dot_general | solution.py:183
  132.9 2.2 collective-permute-start.4
  135.1 2.3 collective-permute-start.5
  137.4 3.8 %collective-permute-done.5 = bf16[1,128,128]{2,1,0:T(8,128)(2,1)S(1)} collective-permute-done((bf16[1,128,128]{2,1,0:T(8,128)(2,1)S(1)}, bf16[1,128,128]{2,1,0:T(8,128)(2,1)S(1)}, u32[]{:S(2)}, u32[]{:S(2)}) %collective-permute-start.5) | collective-permute-done | bytes 32800 | tf_op jit(solution)/shard_map/ppermute | solution.py:19
  141.3 4.3 %collective-permute-start.6 = (bf16[66,1,128]{2,1,0:T(2,128)(2,1)S(1)}, bf16[66,1,128]{2,1,0:T(2,128)(2,1)S(1)}, u32[]{:S(2)}, u32[]{:S(2)}) collective-permute-start(bf16[66,1,128]{2,1,0:T(2,128)(2,1)S(1)} %get-tuple-element.17), channel_id=1, source_target_pairs={{0,1},{1,2},{2,3},{4,5},{5,6},{6,7},{8,9},{9,10},{10,11},{12,13},{... | collective-permute-start | bytes 50696 | tf_op jit(solution)/shard_map/ppermute | solution.py:16
  145.5 1.5 collective-permute-start.7
  147.0 0.8 fusion.62.refs_1_.refs_3_
  147.8 2.4 collective-permute-done.7
  150.2 0.8 maximum_convert_fusion
  151.1 0.6 fusion.77
  151.7 0.6 fusion.78
  152.2 1.6 fusion.22
  153.8 0.6 fusion.83
  154.4 0.5 fusion.53
  154.9 0.3 copy-done.12
  155.3 0.4 convolution_convert_fusion
  155.8 3.3 %collective-permute-start.8 = (bf16[7,64,256]{2,1,0:T(8,128)(2,1)S(1)}, bf16[7,64,256]{2,1,0:T(8,128)(2,1)S(1)}, u32[]{:S(2)}, u32[]{:S(2)}) collective-permute-start(bf16[7,64,256]{2,1,0:T(8,128)(2,1)S(1)} %get-tuple-element.39), channel_id=1, source_target_pairs={{0,4},{4,8},{8,12},{12,16},{16,20},{20,24},{24,28},{1,5},{5,9},{9,... | collective-permute-start | bytes 688136 | tf_op jit(solution)/shard_map/ppermute | solution.py:140
  159.2 1.9 collective-permute-start.9
  161.1 2.1 collective-permute-done.8
  163.2 4.2 %collective-permute-done.9 = bf16[7,64,256]{2,1,0:T(8,128)(2,1)S(1)} collective-permute-done((bf16[7,64,256]{2,1,0:T(8,128)(2,1)S(1)}, bf16[7,64,256]{2,1,0:T(8,128)(2,1)S(1)}, u32[]{:S(2)}, u32[]{:S(2)}) %collective-permute-start.9) | collective-permute-done | bytes 229408 | tf_op jit(solution)/shard_map/ppermute | solution.py:143
  167.5 3.2 %collective-permute-start.10 = (bf16[46,7,256]{2,1,0:T(8,128)(2,1)S(1)}, bf16[46,7,256]{2,1,0:T(8,128)(2,1)S(1)}, u32[]{:S(2)}, u32[]{:S(2)}) collective-permute-start(bf16[46,7,256]{2,1,0:T(8,128)(2,1)S(1)} %pad_maximum_fusion.8), channel_id=1, source_target_pairs={{0,1},{1,2},{2,3},{4,5},{5,6},{6,7},{8,9},{9,10},{10,11},{12,13},{... | collective-permute-start | bytes 494600 | tf_op jit(solution)/shard_map/ppermute | solution.py:161
  170.7 1.3 collective-permute-start.11
  172.1 39.0 %shard_map.103 = f32[1,32,48,256]{3,2,1,0:T(8,128)} custom-call(bf16[1,7,64,256]{3,2,1,0:T(8,128)(2,1)} %bitcast.73, bf16[1,32,64,256]{3,2,1,0:T(8,128)(2,1)} %bitcast.65, bf16[1,7,64,256]{3,2,1,0:T(8,128)(2,1)} %bitcast.74, f32[15,15,256]{2,1,0:T(8,128)} %fusion.62.refs_1_.refs_3_), custom_call_target="tpu_custom_call" | custom-call | flops 176947200 | bytes 3080192 | tf_op jit(solution)/shard_map/pallas_call | solution.py:119
  211.1 0.2 maximum_bitcast_fusion
  211.5 1.1 pad_maximum_fusion.4.refs_0_
  212.6 12.8 %shard_map.102 = f32[2,32,8,256]{3,2,1,0:T(8,128)} custom-call(bf16[2,46,22,256]{3,2,1,0:T(8,128)(2,1)} %pad_maximum_fusion.4.refs_0_, f32[15,15,256]{2,1,0:T(8,128)} %fusion.62.refs_1_.refs_3_), custom_call_target="tpu_custom_call" | custom-call | flops 58982400 | bytes 1560576 | tf_op jit(solution)/shard_map/pallas_call | solution.py:119
  225.4 1.1 slice_bitcast_fusion.1
  226.5 0.4 fusion.44
  226.9 0.3 copy-done.5
  227.2 0.6 multiply_reduce_fusion.1
  227.9 5.4 %add_convert_fusion.1 = bf16[32,64,256]{2,1,0:T(8,128)(2,1)} fusion(bf16[32,64,256]{2,1,0:T(8,128)(2,1)S(1)} %copy-done.4, f32[32,64]{1,0:T(8,128)S(1)} %add_rsqrt_fusion.1, f32[32,64]{1,0:T(8,128)S(1)} %broadcast_multiply_fusion.1, f32[32,8,256]{2,1,0:T(8,128)} %copy-done.5, f32[32,48,256]{2,1,0:T(8,128)S(1)} %bitcast.64, ...), kind=kOutput, calls=%fused_computation.34 | convolution fusion | flops 2170552320 | bytes 5259264 | tf_op jit(solution)/shard_map/dot_general | solution.py:183
  233.3 0.8 fusion.89
  234.1 2.0 collective-permute-start.12
  236.1 2.3 collective-permute-start.13
  238.5 3.8 %collective-permute-done.13 = bf16[1,64,256]{2,1,0:T(8,128)(2,1)S(1)} collective-permute-done((bf16[1,64,256]{2,1,0:T(8,128)(2,1)S(1)}, bf16[1,64,256]{2,1,0:T(8,128)(2,1)S(1)}, u32[]{:S(2)}, u32[]{:S(2)}) %collective-permute-start.13) | collective-permute-done | bytes 32800 | tf_op jit(solution)/shard_map/ppermute | solution.py:19
  242.3 1.0 pad_maximum_fusion.14
  243.3 4.3 %collective-permute-start.14 = (bf16[34,1,256]{2,1,0:T(2,128)(2,1)S(1)}, bf16[34,1,256]{2,1,0:T(2,128)(2,1)S(1)}, u32[]{:S(2)}, u32[]{:S(2)}) collective-permute-start(bf16[34,1,256]{2,1,0:T(2,128)(2,1)S(1)} %get-tuple-element.29), channel_id=1, source_target_pairs={{0,1},{1,2},{2,3},{4,5},{5,6},{6,7},{8,9},{9,10},{10,11},{12,13},{... | collective-permute-start | bytes 52232 | tf_op jit(solution)/shard_map/ppermute | solution.py:16
  247.6 1.5 collective-permute-start.15
  249.1 3.1 %collective-permute-done.15 = bf16[34,1,256]{2,1,0:T(2,128)(2,1)S(1)} collective-permute-done((bf16[34,1,256]{2,1,0:T(2,128)(2,1)S(1)}, bf16[34,1,256]{2,1,0:T(2,128)(2,1)S(1)}, u32[]{:S(2)}, u32[]{:S(2)}) %collective-permute-start.15) | collective-permute-done | bytes 17440 | tf_op jit(solution)/shard_map/ppermute | solution.py:19
  252.3 1.8 maximum_convert_fusion.1
  254.0 0.4 fusion.80
  254.4 0.2 fusion.81
  254.6 0.2 fusion.82
  254.8 1.4 fusion.33
  256.2 0.3 fusion.88
  256.5 0.2 fusion.54
  256.8 0.8 copy.20
  (67 shorter events, 0.8 us)
Async XLA Ops:
  0.0 227.9 %copy-start = (bf16[1024,256]{1,0:T(8,128)(2,1)S(1)}, bf16[1024,256]{1,0:T(8,128)(2,1)}, u32[]{:S(2)}) copy-start(bf16[1024,256]{1,0:T(8,128)(2,1)} %param.19) | copy-start | bytes 1572868
  0.0 9.0 %copy-start.16 = (f32[128]{0:T(128)S(1)}, f32[128]{0:T(128)}, u32[]{:S(2)}) copy-start(f32[128]{0:T(128)} %param.12) | copy-start | bytes 1540
  0.0 9.0 %copy-start.11 = (f32[15,15,128]{2,1,0:T(8,128)S(1)}, f32[15,15,128]{2,1,0:T(8,128)}, u32[]{:S(2)}) copy-start(f32[15,15,128]{2,1,0:T(8,128)} %param.11) | copy-start | bytes 345604
  1.2 8.6 %collective-permute-start = (bf16[7,128,128]{2,1,0:T(8,128)(2,1)S(1)}, bf16[7,128,128]{2,1,0:T(8,128)(2,1)S(1)}, u32[]{:S(2)}, u32[]{:S(2)}) collective-permute-start(bf16[7,128,128]{2,1,0:T(8,128)(2,1)S(1)} %get-tuple-element.27), channel_id=1, source_target_pairs={{0,4},{4,8},{8,12},{12,16},{16,20},{20,24},{24,28},{1,5},{5,9},{9,... | collective-permute-start | bytes 688136 | tf_op jit(solution)/shard_map/ppermute | solution.py:140
  4.8 8.2 %collective-permute-start.1 = (bf16[7,128,128]{2,1,0:T(8,128)(2,1)S(1)}, bf16[7,128,128]{2,1,0:T(8,128)(2,1)S(1)}, u32[]{:S(2)}, u32[]{:S(2)}) collective-permute-start(bf16[7,128,128]{2,1,0:T(8,128)(2,1)S(1)} %get-tuple-element.28), channel_id=1, source_target_pairs={{4,0},{8,4},{12,8},{16,12},{20,16},{24,20},{28,24},{5,1},{9,5},{13... | collective-permute-start | bytes 688136 | tf_op jit(solution)/shard_map/ppermute | solution.py:143
  9.8 8.0 %copy-start.8 = (bf16[7,128,128]{2,1,0:T(8,128)(2,1)}, bf16[7,128,128]{2,1,0:T(8,128)(2,1)S(1)}, u32[]{:S(2)}) copy-start(bf16[7,128,128]{2,1,0:T(8,128)(2,1)S(1)} %collective-permute-done) | copy-start | bytes 688132
  13.1 4.7 %copy-start.9 = (bf16[7,128,128]{2,1,0:T(8,128)(2,1)}, bf16[7,128,128]{2,1,0:T(8,128)(2,1)S(1)}, u32[]{:S(2)}) copy-start(bf16[7,128,128]{2,1,0:T(8,128)(2,1)S(1)} %collective-permute-done.1) | copy-start | bytes 688132
  13.2 90.2 %collective-permute-start.2 = (bf16[78,7,128]{2,1,0:T(8,128)(2,1)S(1)}, bf16[78,7,128]{2,1,0:T(8,128)(2,1)S(1)}, u32[]{:S(2)}, u32[]{:S(2)}) collective-permute-start(bf16[78,7,128]{2,1,0:T(8,128)(2,1)S(1)} %pad_maximum_fusion.10), channel_id=1, source_target_pairs={{0,1},{1,2},{2,3},{4,5},{5,6},{6,7},{8,9},{9,10},{10,11},{12,13},{... | collective-permute-start | bytes 419336 | tf_op jit(solution)/shard_map/ppermute | solution.py:161
  16.4 87.1 %collective-permute-start.3 = (bf16[78,7,128]{2,1,0:T(8,128)(2,1)S(1)}, bf16[78,7,128]{2,1,0:T(8,128)(2,1)S(1)}, u32[]{:S(2)}, u32[]{:S(2)}) collective-permute-start(bf16[78,7,128]{2,1,0:T(8,128)(2,1)S(1)} %pad_maximum_fusion.11), channel_id=1, source_target_pairs={{1,0},{2,1},{3,2},{5,4},{6,5},{7,6},{9,8},{10,9},{11,10},{13,12},{... | collective-permute-start | bytes 419336 | tf_op jit(solution)/shard_map/ppermute | solution.py:162
  118.2 3.4 %copy-start.1 = (f32[1,64,112,128]{3,2,1,0:T(8,128)S(1)}, f32[1,64,112,128]{3,2,1,0:T(8,128)}, u32[]{:S(2)}) copy-start(f32[1,64,112,128]{3,2,1,0:T(8,128)} %shard_map.101) | copy-start | bytes 11010052
  121.5 2.7 %copy-start.14 = (bf16[512,128]{1,0:T(8,128)(2,1)S(1)}, bf16[512,128]{1,0:T(8,128)(2,1)}, u32[]{:S(2)}) copy-start(bf16[512,128]{1,0:T(8,128)(2,1)} %param.14) | copy-start | bytes 393220
  121.5 2.7 %copy-start.15 = (bf16[128,512]{1,0:T(8,128)(2,1)S(1)}, bf16[128,512]{1,0:T(8,128)(2,1)}, u32[]{:S(2)}) copy-start(bf16[128,512]{1,0:T(8,128)(2,1)} %param.13) | copy-start | bytes 393220
  124.2 13.2 %copy-start.13 = (f32[256]{0:T(256)S(1)}, f32[256]{0:T(256)}, u32[]{:S(2)}) copy-start(f32[256]{0:T(256)} %param.17) | copy-start | bytes 3076
  132.9 14.2 %copy-start.10 = (f32[15,15,256]{2,1,0:T(8,128)S(1)}, f32[15,15,256]{2,1,0:T(8,128)}, u32[]{:S(2)}) copy-start(f32[15,15,256]{2,1,0:T(8,128)} %param.16) | copy-start | bytes 691204
  132.9 4.5 %collective-permute-start.4 = (bf16[1,128,128]{2,1,0:T(8,128)(2,1)S(1)}, bf16[1,128,128]{2,1,0:T(8,128)(2,1)S(1)}, u32[]{:S(2)}, u32[]{:S(2)}) collective-permute-start(bf16[1,128,128]{2,1,0:T(8,128)(2,1)S(1)} %get-tuple-element.21), channel_id=1, source_target_pairs={{0,4},{4,8},{8,12},{12,16},{16,20},{20,24},{24,28},{1,5},{5,9},{9,... | collective-permute-start | bytes 98312 | tf_op jit(solution)/shard_map/ppermute | solution.py:16
  135.1 6.1 %collective-permute-start.5 = (bf16[1,128,128]{2,1,0:T(8,128)(2,1)S(1)}, bf16[1,128,128]{2,1,0:T(8,128)(2,1)S(1)}, u32[]{:S(2)}, u32[]{:S(2)}) collective-permute-start(bf16[1,128,128]{2,1,0:T(8,128)(2,1)S(1)} %get-tuple-element.22), channel_id=1, source_target_pairs={{4,0},{8,4},{12,8},{16,12},{20,16},{24,20},{28,24},{5,1},{9,5},{13... | collective-permute-start | bytes 98312 | tf_op jit(solution)/shard_map/ppermute | solution.py:19
  141.3 6.6 %collective-permute-start.6 = (bf16[66,1,128]{2,1,0:T(2,128)(2,1)S(1)}, bf16[66,1,128]{2,1,0:T(2,128)(2,1)S(1)}, u32[]{:S(2)}, u32[]{:S(2)}) collective-permute-start(bf16[66,1,128]{2,1,0:T(2,128)(2,1)S(1)} %get-tuple-element.17), channel_id=1, source_target_pairs={{0,1},{1,2},{2,3},{4,5},{5,6},{6,7},{8,9},{9,10},{10,11},{12,13},{... | collective-permute-start | bytes 50696 | tf_op jit(solution)/shard_map/ppermute | solution.py:16
  145.5 4.7 %collective-permute-start.7 = (bf16[66,1,128]{2,1,0:T(2,128)(2,1)S(1)}, bf16[66,1,128]{2,1,0:T(2,128)(2,1)S(1)}, u32[]{:S(2)}, u32[]{:S(2)}) collective-permute-start(bf16[66,1,128]{2,1,0:T(2,128)(2,1)S(1)} %get-tuple-element.18), channel_id=1, source_target_pairs={{1,0},{2,1},{3,2},{5,4},{6,5},{7,6},{9,8},{10,9},{11,10},{13,12},{... | collective-permute-start | bytes 50696 | tf_op jit(solution)/shard_map/ppermute | solution.py:19
  154.4 0.8 copy-start.12
  155.7 16.4 %copy-start.3 = (bf16[32,64,256]{2,1,0:T(8,128)(2,1)}, bf16[32,64,256]{2,1,0:T(8,128)(2,1)S(1)}, u32[]{:S(2)}) copy-start(bf16[32,64,256]{2,1,0:T(8,128)(2,1)S(1)} %convolution_convert_fusion) | copy-start | bytes 3145732
  155.8 7.4 %collective-permute-start.8 = (bf16[7,64,256]{2,1,0:T(8,128)(2,1)S(1)}, bf16[7,64,256]{2,1,0:T(8,128)(2,1)S(1)}, u32[]{:S(2)}, u32[]{:S(2)}) collective-permute-start(bf16[7,64,256]{2,1,0:T(8,128)(2,1)S(1)} %get-tuple-element.39), channel_id=1, source_target_pairs={{0,4},{4,8},{8,12},{12,16},{16,20},{20,24},{24,28},{1,5},{5,9},{9,... | collective-permute-start | bytes 688136 | tf_op jit(solution)/shard_map/ppermute | solution.py:140
  159.2 8.2 %collective-permute-start.9 = (bf16[7,64,256]{2,1,0:T(8,128)(2,1)S(1)}, bf16[7,64,256]{2,1,0:T(8,128)(2,1)S(1)}, u32[]{:S(2)}, u32[]{:S(2)}) collective-permute-start(bf16[7,64,256]{2,1,0:T(8,128)(2,1)S(1)} %get-tuple-element.40), channel_id=1, source_target_pairs={{4,0},{8,4},{12,8},{16,12},{20,16},{24,20},{28,24},{5,1},{9,5},{13... | collective-permute-start | bytes 688136 | tf_op jit(solution)/shard_map/ppermute | solution.py:143
  163.2 8.9 %copy-start.6 = (bf16[7,64,256]{2,1,0:T(8,128)(2,1)}, bf16[7,64,256]{2,1,0:T(8,128)(2,1)S(1)}, u32[]{:S(2)}) copy-start(bf16[7,64,256]{2,1,0:T(8,128)(2,1)S(1)} %collective-permute-done.8) | copy-start | bytes 688132
  167.4 4.7 %copy-start.7 = (bf16[7,64,256]{2,1,0:T(8,128)(2,1)}, bf16[7,64,256]{2,1,0:T(8,128)(2,1)S(1)}, u32[]{:S(2)}) copy-start(bf16[7,64,256]{2,1,0:T(8,128)(2,1)S(1)} %collective-permute-done.9) | copy-start | bytes 688132
  167.5 43.6 %collective-permute-start.10 = (bf16[46,7,256]{2,1,0:T(8,128)(2,1)S(1)}, bf16[46,7,256]{2,1,0:T(8,128)(2,1)S(1)}, u32[]{:S(2)}, u32[]{:S(2)}) collective-permute-start(bf16[46,7,256]{2,1,0:T(8,128)(2,1)S(1)} %pad_maximum_fusion.8), channel_id=1, source_target_pairs={{0,1},{1,2},{2,3},{4,5},{5,6},{6,7},{8,9},{9,10},{10,11},{12,13},{... | collective-permute-start | bytes 494600 | tf_op jit(solution)/shard_map/ppermute | solution.py:161
  170.7 40.6 %collective-permute-start.11 = (bf16[46,7,256]{2,1,0:T(8,128)(2,1)S(1)}, bf16[46,7,256]{2,1,0:T(8,128)(2,1)S(1)}, u32[]{:S(2)}, u32[]{:S(2)}) collective-permute-start(bf16[46,7,256]{2,1,0:T(8,128)(2,1)S(1)} %pad_maximum_fusion.9), channel_id=1, source_target_pairs={{1,0},{2,1},{3,2},{5,4},{6,5},{7,6},{9,8},{10,9},{11,10},{13,12},{... | collective-permute-start | bytes 494600 | tf_op jit(solution)/shard_map/ppermute | solution.py:162
  211.5 15.0 %copy-start.2 = (f32[1,32,48,256]{3,2,1,0:T(8,128)S(1)}, f32[1,32,48,256]{3,2,1,0:T(8,128)}, u32[]{:S(2)}) copy-start(f32[1,32,48,256]{3,2,1,0:T(8,128)} %shard_map.103) | copy-start | bytes 4718596
  226.5 0.7 copy-start.5
  226.5 1.4 copy-start.4
  234.1 4.3 %collective-permute-start.12 = (bf16[1,64,256]{2,1,0:T(8,128)(2,1)S(1)}, bf16[1,64,256]{2,1,0:T(8,128)(2,1)S(1)}, u32[]{:S(2)}, u32[]{:S(2)}) collective-permute-start(bf16[1,64,256]{2,1,0:T(8,128)(2,1)S(1)} %get-tuple-element.33), channel_id=1, source_target_pairs={{0,4},{4,8},{8,12},{12,16},{16,20},{20,24},{24,28},{1,5},{5,9},{9,... | collective-permute-start | bytes 98312 | tf_op jit(solution)/shard_map/ppermute | solution.py:16
  236.1 6.1 %collective-permute-start.13 = (bf16[1,64,256]{2,1,0:T(8,128)(2,1)S(1)}, bf16[1,64,256]{2,1,0:T(8,128)(2,1)S(1)}, u32[]{:S(2)}, u32[]{:S(2)}) collective-permute-start(bf16[1,64,256]{2,1,0:T(8,128)(2,1)S(1)} %get-tuple-element.34), channel_id=1, source_target_pairs={{4,0},{8,4},{12,8},{16,12},{20,16},{24,20},{28,24},{5,1},{9,5},{13... | collective-permute-start | bytes 98312 | tf_op jit(solution)/shard_map/ppermute | solution.py:19
  243.3 5.8 %collective-permute-start.14 = (bf16[34,1,256]{2,1,0:T(2,128)(2,1)S(1)}, bf16[34,1,256]{2,1,0:T(2,128)(2,1)S(1)}, u32[]{:S(2)}, u32[]{:S(2)}) collective-permute-start(bf16[34,1,256]{2,1,0:T(2,128)(2,1)S(1)} %get-tuple-element.29), channel_id=1, source_target_pairs={{0,1},{1,2},{2,3},{4,5},{5,6},{6,7},{8,9},{9,10},{10,11},{12,13},{... | collective-permute-start | bytes 52232 | tf_op jit(solution)/shard_map/ppermute | solution.py:16
  247.6 4.7 %collective-permute-start.15 = (bf16[34,1,256]{2,1,0:T(2,128)(2,1)S(1)}, bf16[34,1,256]{2,1,0:T(2,128)(2,1)S(1)}, u32[]{:S(2)}, u32[]{:S(2)}) collective-permute-start(bf16[34,1,256]{2,1,0:T(2,128)(2,1)S(1)} %get-tuple-element.30), channel_id=1, source_target_pairs={{1,0},{2,1},{3,2},{5,4},{6,5},{7,6},{9,8},{10,9},{11,10},{13,12},{... | collective-permute-start | bytes 52232 | tf_op jit(solution)/shard_map/ppermute | solution.py:19
